TPU v7x, 32 devices: a whole 2x2x4 slice. The times are simulated.
32 devices in a mesh: visit: 8 (over z, x), sky: 4 (over y, core).
Axes of the slice: x: 2, y: 2, z: 4, core: 2. Of those that a mesh axis runs over, the one named last changes fastest.
Arguments:
- warped: bfloat16 [16, 512, 2048], P('visit', 'sky'), may hold values from -11 to 21
- inv_var: bfloat16 [16, 512, 2048], P('visit', 'sky'), may hold values from 0.19921875 to 5
- intersection: int32 [8, 4, 4], P('visit', 'sky'), may hold values from 0 to 3, as said below
- col_start: int32 [8, 4], P('visit', 'sky'), may hold values from 0 to 1536, as said below
- row_interp: bfloat16 [8, 4, 512, 512], P('visit', 'sky'), may hold values from -0.22 to 1.4, as said below
- col_interp: bfloat16 [8, 4, 512, 512], P('visit', 'sky'), may hold values from -0.22 to 1.4, as said below
- cell_ids: int32 [8, 4, 4, 4], P('visit', 'sky'), may hold values from 0 to 15
- kernels: bfloat16 [8, 4, 16, 121], P('visit', 'sky'), may hold values from -0.59765625 to 0.59765625
- science: bfloat16 [8, 4, 512, 512], P('visit', 'sky'), may hold values from -8 to 8
- inv_sigma: bfloat16 [8, 4, 512, 512], P('visit', 'sky'), may hold values from 0.29882812 to 1
Outputs:
- coadd: float32 [512, 2048], P('sky')
- outlier_weight: float32 [8, 4, 512, 512], P('visit', 'sky')
Inputs may be any that keep to these rules, and one draw needn't show every extreme that they name: `intersection`: the 4 strip numbers of one tile are distinct. `col_start`: a multiple of 128. `row_interp`: nonzero only within two places of the diagonal, each row's diagonal entry larger than the sum of its other magnitudes. `col_interp`: nonzero only within two places of the diagonal, each row's diagonal entry larger than the sum of its other magnitudes.
All inputs are finite; a program needn't handle non-finite values.
Results may differ from a plain program's by a relative error of at most 0.0017.
Values may be sent and summed in bfloat16 or wider, within the bound.
No kernel may reach another device: no remote copies, remote signals or barrier semaphores. Data moves between devices by JAX's collectives and lax.ppermute only.
A program may use at most 64 MiB of HBM per device.

v0:
```python
import jax
import jax.numpy as jnp
from jax import lax
from jax.sharding import PartitionSpec as P

STRIP = 128
NOV = 4
TILE = 512
KSIZE = 11
CELL = 128
NCELL = 16
PASSES = 3


CAUCHY = 2.0
OUTLIER = 3.0


def local_coadd(warped_all, var_all):
    values = warped_all.astype(jnp.float32)
    weights = var_all.astype(jnp.float32)
    root_weight = jnp.sqrt(weights)
    coadd_field = jnp.sum(weights * values, axis=0) / jnp.sum(weights, axis=0)
    for pass_index in range(PASSES):
        scaled = (values - coadd_field[None]) * root_weight / CAUCHY
        cauchy = weights / (1.0 + scaled * scaled)
        coadd_field = jnp.sum(cauchy * values, axis=0) / jnp.sum(cauchy, axis=0)
    return coadd_field


def psf_match(blotted, cell_grid, kernel_table):
    tile_side = blotted.shape[1]
    blocks = tile_side // CELL
    half_width = KSIZE // 2
    window = CELL + KSIZE - 1
    picker = (cell_grid.reshape(-1)[:, None] == jnp.arange(NCELL, dtype=jnp.int32)[None, :]).astype(
        jnp.bfloat16
    )
    tap_rows = jnp.dot(picker, kernel_table, preferred_element_type=jnp.float32)
    tap_rows = tap_rows.reshape(blocks, blocks, KSIZE, KSIZE)
    source = jnp.arange(window, dtype=jnp.int32)[:, None]
    target = jnp.arange(CELL, dtype=jnp.int32)[None, :]
    diagonal = (
        (source - target)[None] == jnp.arange(KSIZE, dtype=jnp.int32)[:, None, None]
    ).astype(jnp.float32)
    banded_all = jnp.einsum(
        "xyab,bcl->xyacl", tap_rows, diagonal, precision=lax.Precision.HIGHEST
    ).astype(jnp.bfloat16)
    padded = jnp.pad(blotted, ((half_width, half_width), (half_width, half_width)))
    row_parts = []
    for row_block in range(blocks):
        rows_window = lax.slice_in_dim(padded, row_block * CELL, row_block * CELL + window, axis=0)
        col_parts = []
        for col_block in range(blocks):
            cols_window = lax.slice_in_dim(
                rows_window, col_block * CELL, col_block * CELL + window, axis=1
            )
            horizontal = jnp.einsum(
                "rc,acl->arl",
                cols_window,
                banded_all[row_block, col_block],
                preferred_element_type=jnp.float32,
            )
            summed = horizontal[0, 0:CELL, :]
            for tap_row in range(1, KSIZE):
                summed = summed + horizontal[tap_row, tap_row : tap_row + CELL, :]
            col_parts.append(summed)
        row_parts.append(jnp.concatenate(col_parts, axis=1))
    return jnp.concatenate(row_parts, axis=0)


def shards(
    warped,
    inv_var,
    intersection,
    col_start,
    row_interp,
    col_interp,
    cell_ids,
    kernels,
    science,
    inv_sigma,
):
    warped_all, var_all = (
        lax.all_to_all(warped, "visit", split_axis=2, concat_axis=0, tiled=True),
        lax.all_to_all(inv_var, "visit", split_axis=2, concat_axis=0, tiled=True),
    )
    column_share = local_coadd(warped_all, var_all)
    coadd_field = lax.all_gather(column_share, "visit", axis=1, tiled=True)
    coadd_low = coadd_field.astype(jnp.bfloat16)
    strips = intersection[0, 0]
    start_col = col_start[0, 0]
    rows_map = row_interp[0, 0]
    shard_rows = lax.all_gather(coadd_low, "sky", axis=0, tiled=True)
    first_row = jnp.int32(0)
    row_count = shard_rows.shape[0]
    block_rows = min(row_count, STRIP)
    total = jnp.zeros((TILE, TILE), jnp.float32)
    for block_index in range(row_count // block_rows):
        block_first = first_row + block_index * block_rows
        strip_of = block_first // STRIP
        inside = block_first % STRIP
        matches = strips == strip_of
        slot_index = jnp.sum(jnp.where(matches, jnp.arange(NOV, dtype=jnp.int32), 0))
        present = jnp.any(matches)
        block_data = shard_rows[block_index * block_rows : (block_index + 1) * block_rows]

        def add_block(current):
            chosen = lax.dynamic_slice_in_dim(rows_map, slot_index * STRIP + inside, block_rows, 1)
            columns = lax.dynamic_slice_in_dim(block_data, start_col, TILE, 1)
            return current + jnp.dot(chosen, columns, preferred_element_type=jnp.float32)

        total = lax.cond(present, add_block, lambda current: current, total)
    blotted = jnp.dot(
        total.astype(jnp.bfloat16), col_interp[0, 0], preferred_element_type=jnp.float32
    ).astype(jnp.bfloat16)
    matched = psf_match(blotted, cell_ids[0, 0], kernels[0, 0])
    residual = (
        (science[0, 0].astype(jnp.float32) - matched)
        * inv_sigma[0, 0].astype(jnp.float32)
        / OUTLIER
    )
    outlier = 1.0 / (1.0 + residual * residual)
    return (coadd_field, outlier[None, None])


def solution(mesh):
    in_specs = (
        P("visit", "sky", None),
        P("visit", "sky", None),
        P("visit", "sky", None),
        P("visit", "sky"),
        P("visit", "sky", None, None),
        P("visit", "sky", None, None),
        P("visit", "sky", None, None),
        P("visit", "sky", None, None),
        P("visit", "sky", None, None),
        P("visit", "sky", None, None),
    )
    out_specs = (P("sky", None), P("visit", "sky", None, None))
    return jax.shard_map(shards, mesh=mesh, in_specs=in_specs, out_specs=out_specs, check_vma=False)
```

profile of v0, /device:TPU:0, one launch (start us, length us, event | category | flops | bytes accessed | tf_op | source)
XLA Modules:
  0.0 203.1 jit_solution(12061333700261532114)
XLA Ops:
  7.2 3.8 %copy.119 = bf16[2,128,2048]{1,0,2:T(2,128)(2,1)} copy(bf16[2,128,2048]{2,1,0:T(8,128)(2,1)} %param.18) | data formatting | bytes 2097152 | tf_op args[0]
  11.0 7.3 %all-to-all-start.1 = ((bf16[2,128,2048]{1,0,2:T(2,128)(2,1)}), bf16[2,128,2048]{1,0,2:T(2,128)(2,1)S(1)}, u32[]{:S(2)}, u32[]{:S(2)}) async-start(bf16[2,128,2048]{1,0,2:T(2,128)(2,1)} %copy.119), calls=%async_computation.1 | async-start | bytes 2097152 | tf_op jit(solution)/shard_map/all_to_all | solution.py:85
  18.3 2.0 copy.116
  20.3 23.8 %all-to-all-done.1 = bf16[2,128,2048]{1,0,2:T(2,128)(2,1)S(1)} async-done(((bf16[2,128,2048]{1,0,2:T(2,128)(2,1)}), bf16[2,128,2048]{1,0,2:T(2,128)(2,1)S(1)}, u32[]{:S(2)}, u32[]{:S(2)}) %all-to-all-start.1) | async-done | bytes 1048608 | tf_op jit(solution)/shard_map/all_to_all | solution.py:85
  44.0 4.2 %all-to-all-start = ((bf16[2,128,2048]{1,0,2:T(2,128)(2,1)}), bf16[2,128,2048]{1,0,2:T(2,128)(2,1)}, u32[]{:S(2)}, u32[]{:S(2)}) async-start(bf16[2,128,2048]{1,0,2:T(2,128)(2,1)} %copy.116), calls=%async_computation | async-start | bytes 2097152 | tf_op jit(solution)/shard_map/all_to_all | solution.py:86
  48.3 1.1 copy.120
  49.4 1.5 copy.121
  50.9 22.9 %all-to-all-done = bf16[2,128,2048]{1,0,2:T(2,128)(2,1)} async-done(((bf16[2,128,2048]{1,0,2:T(2,128)(2,1)}), bf16[2,128,2048]{1,0,2:T(2,128)(2,1)}, u32[]{:S(2)}, u32[]{:S(2)}) %all-to-all-start) | async-done | bytes 1048608 | tf_op jit(solution)/shard_map/all_to_all | solution.py:86
  73.8 2.3 %copy.117 = bf16[2,128,2048]{1,2,0:T(8,128)(2,1)} copy(bf16[2,128,2048]{1,0,2:T(2,128)(2,1)} %all-to-all-done) | data formatting | bytes 2097152 | tf_op jit(solution)/shard_map/all_to_all | solution.py:86
  76.2 2.6 %copy.118 = f32[2,128,8,256]{3,1,0,2:T(8,128)} copy(bf16[2,128,8,256]{1,3,2,0:T(8,128)(2,1)} %bitcast.283) | data formatting | bytes 3145728 | tf_op jit(solution)/shard_map/convert_element_type | solution.py:21
  78.8 2.0 %bitcast_reduce_fusion = (f32[128,256]{1,0:T(8,128)S(1)}, f32[128,256]{1,0:T(8,128)S(1)}) fusion(f32[2,128,8,256]{3,1,0,2:T(8,128)} %copy.118, f32[2,128,8,256]{3,1,0,2:T(8,128)S(1)} %copy.121), kind=kLoop, calls=%fused_computation.52 | loop fusion | flops 1507328 | bytes 4456448 | tf_op jit(solution)/shard_map/reduce_sum | solution.py:23
  81.0 1.2 fusion.106
  82.2 1.2 fusion.105
  83.5 1.2 fusion.104
  85.0 0.7 div.72
  85.7 39.2 %all-gather.3.cloned.1.call-done = f32[128,2048]{0,1:T(8,128)} async-done(((f32[128,256]{0,1:T(8,128)}), f32[128,2048]{0,1:T(8,128)}) %all-gather.3.cloned.1.call-update) | async-done | bytes 1048592 | tf_op jit(solution)/shard_map/all_gather | solution.py:89
  124.9 2.1 %convert_element_type.88 = bf16[128,2048]{0,1:T(8,128)(2,1)} convert(f32[128,2048]{0,1:T(8,128)} %all-gather.3.cloned.1.call-done) | non-fusion elementwise | flops 262144 | bytes 1572864 | tf_op jit(solution)/shard_map/convert_element_type | solution.py:90
  127.0 0.7 fusion.125
  130.9 7.5 %convolution_convert_fusion = bf16[4,4,11,138,128]{4,2,3,1,0:T(8,128)(2,1)S(1)} fusion(s32[138,128]{1,0:T(8,128)S(1)} %iota_subtract_fusion, f32[4,4,11,11,1]{3,1,2,0,4:T(4,128)S(1)} %convolution_bitcast_fusion.16), kind=kOutput, calls=%fused_computation.24 | convolution fusion | flops 413673216 | bytes 6296128 | tf_op jit(solution)/shard_map/xyab,bcl->xyacl/dot_general | solution.py:46
  138.4 3.4 %slice_bitcast_fusion.15 = (bf16[11,138,128]{2,0,1:T(8,128)(2,1)}, bf16[11,138,128]{2,0,1:T(8,128)(2,1)}, bf16[11,138,128]{2,0,1:T(8,128)(2,1)}, bf16[11,138,128...) fusion(bf16[4,4,11,138,128]{4,2,3,1,0:T(8,128)(2,1)S(1)} %convo, ...), kind=kLoop, calls=%fused_computation.106 | loop fusion | bytes 12435456 | tf_op jit(solution)/shard_map/squeeze | solution.py:61
  141.8 1.3 copy.146
  143.1 5.7 %all-gather.5.cloned.1.call-done = bf16[512,2048]{0,1:T(8,128)(2,1)} async-done(((bf16[128,2048]{0,1:T(8,128)(2,1)}), bf16[512,2048]{0,1:T(8,128)(2,1)}) %all-gather.5.cloned.1.call-update) | async-done | bytes 2097168 | tf_op jit(solution)/shard_map/all_gather | solution.py:94
  148.7 7.5 %conditional.4 = (f32[512,512]{1,0:T(8,128)S(1)}) conditional(s32[]{:T(128)} %convert_element_type.87, () %tuple.44, (pred[1,1,4]{2,1,0:T(4,128)(4,1)S(1)}, bf16[512,512]{1,0:T(8,128)(2,1)}, s32[]{:T(128)}, bf16[512,2048]{0,1:T(8,128)(2,1)}, s32[]{:T(128)}, /*index=5*/s32[4]{0:T(128)S(1)}, s32[4]{0:T(128)S(1)}) %tuple.105), branch_computations={%region_13.14_spmd, %region_14.15_spmd} | conditional | flops 67108880 | bytes 6553740 | solution.py:113
  150.7 0.7 fusion.3
  152.0 2.9 %copy.126 = bf16[512,2048]{1,0:T(8,128)(2,1)S(1)} copy(bf16[512,2048]{0,1:T(8,128)(2,1)} %get-tuple-element.197) | data formatting | bytes 4194304 | tf_op jit(solution)/shard_map
  155.0 1.3 fusion
  156.3 9.5 %conditional.5 = (f32[512,512]{1,0:T(8,128)S(1)}) conditional(s32[]{:T(128)} %convert_element_type.86, f32[512,512]{1,0:T(8,128)S(1)} %get-tuple-element.261, (pred[1,1,4]{2,1,0:T(4,128)(4,1)S(1)}, bf16[512,512]{1,0:T(8,128)(2,1)}, s32[]{:T(128)}, bf16[512,2048]{0,1:T(8,128)(2,1)}, f32[512,512]{1,0:T(8,128)S(1)}, /*index=5*/s32[]{:T(128)}, ...), branch_computations={%region_16.17_spmd, %region_17.18_spmd} | conditional | flops 67371024 | bytes 7602316 | solution.py:113
  158.2 0.6 fusion.7
  159.4 4.0 %copy.127 = bf16[512,2048]{1,0:T(8,128)(2,1)} copy(bf16[512,2048]{0,1:T(8,128)(2,1)} %get-tuple-element.204) | data formatting | bytes 4194304 | tf_op jit(solution)/shard_map
  163.4 1.1 slice.877
  164.5 1.3 convolution_add_fusion
  165.8 9.6 %conditional.6 = (f32[512,512]{1,0:T(8,128)S(1)}) conditional(s32[]{:T(128)} %convert_element_type.85, f32[512,512]{1,0:T(8,128)S(1)} %get-tuple-element.262, (pred[1,1,4]{2,1,0:T(4,128)(4,1)S(1)}, bf16[512,512]{1,0:T(8,128)(2,1)}, s32[]{:T(128)}, bf16[512,2048]{0,1:T(8,128)(2,1)}, f32[512,512]{1,0:T(8,128)S(1)}, /*index=5*/s32[]{:T(128)}, ...), branch_computations={%region_19.20_spmd, %region_20.21_spmd} | conditional | flops 67371024 | bytes 7602316 | solution.py:113
  167.9 0.6 fusion.11
  169.1 4.0 %copy.128 = bf16[512,2048]{1,0:T(8,128)(2,1)} copy(bf16[512,2048]{0,1:T(8,128)(2,1)} %get-tuple-element.212) | data formatting | bytes 4194304 | tf_op jit(solution)/shard_map
  173.0 1.1 slice.878
  174.1 1.3 convolution_add_fusion.1
  175.4 9.4 %conditional.7 = (f32[512,512]{1,0:T(8,128)S(1)}) conditional(s32[]{:T(128)} %convert_element_type.84, f32[512,512]{1,0:T(8,128)S(1)} %get-tuple-element.263, (pred[1,1,4]{2,1,0:T(4,128)(4,1)S(1)}, s32[4]{0:T(128)S(1)}, bf16[512,512]{1,0:T(8,128)(2,1)}, bf16[512,2048]{0,1:T(8,128)(2,1)}, s32[]{:T(128)}, /*index=5*/f32[512,512]{1,0:T(8,128)S(1)}) %tuple.108), branch_computations={%region_21.22_spmd, %region_22.24_spmd} | conditional | flops 67371024 | bytes 7602296 | solution.py:113
  177.4 0.6 fusion.15
  178.5 4.0 %copy.129 = bf16[512,2048]{1,0:T(8,128)(2,1)} copy(bf16[512,2048]{0,1:T(8,128)(2,1)} %get-tuple-element.220) | data formatting | bytes 4194304 | tf_op jit(solution)/shard_map
  182.5 1.1 slice.879
  183.6 1.3 convolution_add_fusion.2
  184.9 0.4 convolution_convert_fusion.1
  185.3 0.6 copy-done.17
  185.9 0.3 convolution_bitcast_fusion.15
  186.4 0.3 convolution_bitcast_fusion
  186.8 0.3 copy-done.15
  187.0 0.3 convolution_bitcast_fusion.1
  187.4 0.3 convolution_bitcast_fusion.2
  187.8 0.3 copy-done.13
  188.1 0.3 convolution_bitcast_fusion.3
  188.5 0.3 convolution_bitcast_fusion.4
  189.2 0.3 convolution_bitcast_fusion.5
  189.6 0.3 convolution_bitcast_fusion.6
  190.1 0.3 convolution_bitcast_fusion.7
  190.7 0.3 convolution_bitcast_fusion.8
  191.2 0.3 convolution_bitcast_fusion.9
  191.8 0.3 convolution_bitcast_fusion.10
  192.3 0.3 convolution_bitcast_fusion.11
  192.7 0.3 copy-done.4
  192.9 0.3 convolution_bitcast_fusion.12
  193.4 0.3 convolution_bitcast_fusion.13
  193.8 0.3 convolution_bitcast_fusion.14
  194.3 0.5 copy-done.19
  195.0 1.3 fusion.42
  (80 shorter events, 3.4 us)
Async XLA Ops:
  7.2 177.7 %copy-start = (bf16[1,1,512,512]{3,2,1,0:T(8,128)(2,1)S(1)}, bf16[1,1,512,512]{3,2,1,0:T(8,128)(2,1)}, u32[]{:S(2)}) copy-start(bf16[1,1,512,512]{3,2,1,0:T(8,128)(2,1)} %param.23) | copy-start | bytes 1572868
  7.2 11.1 %copy-start.18 = (bf16[2,128,2048]{2,1,0:T(8,128)(2,1)S(1)}, bf16[2,128,2048]{2,1,0:T(8,128)(2,1)}, u32[]{:S(2)}) copy-start(bf16[2,128,2048]{2,1,0:T(8,128)(2,1)} %param.19) | copy-start | bytes 3145732
  11.0 33.0 %all-to-all-start.1 = ((bf16[2,128,2048]{1,0,2:T(2,128)(2,1)}), bf16[2,128,2048]{1,0,2:T(2,128)(2,1)S(1)}, u32[]{:S(2)}, u32[]{:S(2)}) async-start(bf16[2,128,2048]{1,0,2:T(2,128)(2,1)} %copy.119), calls=%async_computation.1 | async-start | bytes 2097152 | tf_op jit(solution)/shard_map/all_to_all | solution.py:85
  44.0 29.8 %all-to-all-start = ((bf16[2,128,2048]{1,0,2:T(2,128)(2,1)}), bf16[2,128,2048]{1,0,2:T(2,128)(2,1)}, u32[]{:S(2)}, u32[]{:S(2)}) async-start(bf16[2,128,2048]{1,0,2:T(2,128)(2,1)} %copy.116), calls=%async_computation | async-start | bytes 2097152 | tf_op jit(solution)/shard_map/all_to_all | solution.py:86
  48.3 76.7 %all-gather.3.cloned.1.call-start = ((), (), s32[]{:S(2)}) async-start(), calls=%async_computation.2 | async-start | bytes 1179648 | tf_op jit(solution)/shard_map/all_gather | solution.py:89
  78.8 2.2 %copy-start.1 = (f32[2,128,8,256]{3,1,0,2:T(8,128)S(1)}, f32[2,128,8,256]{3,1,0,2:T(8,128)}, u32[]{:S(2)}) copy-start(f32[2,128,8,256]{3,1,0,2:T(8,128)} %copy.118) | copy-start | bytes 6291460
  84.7 42.3 %copy-start.23 = (s32[1,1,4]{2,1,0:T(1,128)S(1)}, s32[1,1,4]{2,1,0:T(1,128)}, u32[]{:S(2)}) copy-start(s32[1,1,4]{2,1,0:T(1,128)} %param.20) | copy-start | bytes 52
  84.7 45.6 %copy-start.21 = (bf16[1,1,16,121]{3,2,1,0:T(8,128)(2,1)S(1)}, bf16[1,1,16,121]{3,2,1,0:T(8,128)(2,1)}, u32[]{:S(2)}) copy-start(bf16[1,1,16,121]{3,2,1,0:T(8,128)(2,1)} %param.25) | copy-start | bytes 11620
  84.7 45.9 %copy-start.22 = (s32[1,1,4,4]{3,2,1,0:T(4,128)S(1)}, s32[1,1,4,4]{3,2,1,0:T(4,128)}, u32[]{:S(2)}) copy-start(s32[1,1,4,4]{3,2,1,0:T(4,128)} %param.24) | copy-start | bytes 196
  85.7 63.1 %all-gather.5.cloned.1.call-start = ((), (), s32[]{:S(2)}) async-start(), calls=%async_computation.3 | async-start | bytes 2621440 | tf_op jit(solution)/shard_map/all_gather | solution.py:94
  138.4 3.4 %copy-start.2 = (f32[128,2048]{0,1:T(8,128)S(1)}, f32[128,2048]{0,1:T(8,128)}, u32[]{:S(2)}) copy-start(f32[128,2048]{0,1:T(8,128)} %all-gather.3.cloned.1.call-done) | copy-start | bytes 3145732
  184.9 1.1 copy-start.17
  184.9 1.4 copy-start.16
  185.9 1.1 copy-start.15
  186.3 1.1 copy-start.14
  187.0 1.1 copy-start.13
  187.4 1.1 copy-start.12
  188.1 1.1 copy-start.11
  188.5 1.1 copy-start.10
  189.0 1.1 copy-start.9
  189.6 1.1 copy-start.8
  190.1 1.1 copy-start.7
  190.7 1.1 copy-start.6
  191.1 1.1 copy-start.5
  191.8 1.1 copy-start.4
  192.3 1.1 copy-start.3
  193.8 1.0 copy-start.19
  193.8 1.2 copy-start.20
Sparse Core Ops, SparseCore 0:
  85.8 39.1 all-gather.2
  127.2 21.5 all-gather.4
where the time goes:
time: 204 us; the launch traced here: 203 us
  waiting for transfers between devices  91.6 us (45%)
  local copies, waits for them, and re-layouts  39.7 us (19%)
  matrix products  18.5 us (9%)
  between operations  17.1 us (8%)
  other arithmetic  14.2 us (7%)
  starting transfers between devices  11.6 us (6%)
  loops' own time  10.3 us (5%)
    all_gather x1, waiting for transfers between devices, shards(): coadd_field = lax.all_gather(column_share, 'visit', axis=1, tiled=True)  39.2 us
    all_to_all x1, waiting for transfers between devices, shards(): lax.all_to_all(warped, 'visit', split_axis=2, concat_axis=0, tiled=True)  23.8 us
    all_to_all x1, waiting for transfers between devices, shards(): lax.all_to_all(inv_var, 'visit', split_axis=2, concat_axis=0, tiled=True)  22.9 us
    another operation x4, local copies, waits for them, and re-layouts  14.8 us
    unnamed x53, local copies, waits for them, and re-layouts  10.5 us
    another operation x4, loops' own time, shards(): total = lax.cond(present, add_block, lambda current: current, total)  10.3 us
    dot_general x1, matrix products, psf_match(): jnp.einsum('xyab,bcl->xyacl', tap_rows, diagonal, precision=lax.Precision...  7.51 us
    all_to_all x1, starting transfers between devices, shards(): lax.all_to_all(warped, 'visit', split_axis=2, concat_axis=0, tiled=True)  7.28 us
  transfers between devices with their start and end apart: 4, of which 4 were waited for; matrix products, arithmetic and copies ran while one was open for 9% of the time, Pallas kernels for 0%

commit v1 on v0

--- a/solution.py
+++ b/solution.py
@@ -16,9 +16,7 @@
 OUTLIER = 3.0
 
 
-def local_coadd(warped_all, var_all):
-    values = warped_all.astype(jnp.float32)
-    weights = var_all.astype(jnp.float32)
+def local_coadd(values, weights):
     root_weight = jnp.sqrt(weights)
     coadd_field = jnp.sum(weights * values, axis=0) / jnp.sum(weights, axis=0)
     for pass_index in range(PASSES):
@@ -81,39 +79,36 @@
     science,
     inv_sigma,
 ):
-    warped_all, var_all = (
-        lax.all_to_all(warped, "visit", split_axis=2, concat_axis=0, tiled=True),
-        lax.all_to_all(inv_var, "visit", split_axis=2, concat_axis=0, tiled=True),
+    n_visit = lax.axis_size("visit")
+    n_sky = lax.axis_size("sky")
+    local_visits, strip_rows, sky_w = warped.shape
+    stacked = jnp.stack([warped, inv_var], axis=0)
+    chunk = strip_rows // n_visit
+    stacked = stacked.reshape(2, local_visits, n_visit, chunk, sky_w)
+    gathered = lax.all_to_all(stacked, "visit", split_axis=2, concat_axis=1, tiled=True)
+    gathered = gathered.reshape(2, local_visits * n_visit, chunk, sky_w)
+    row_share = local_coadd(gathered[0].astype(jnp.float32), gathered[1].astype(jnp.float32))
+    coadd_field = lax.all_gather(row_share, "visit", axis=0, tiled=True)
+    coadd_low = coadd_field.astype(jnp.bfloat16)
+
+    start_col = col_start[0, 0]
+    all_starts = lax.all_gather(col_start[0], "sky", axis=0, tiled=True)
+    windows = jnp.stack(
+        [lax.dynamic_slice_in_dim(coadd_low, all_starts[peer], TILE, 1) for peer in range(n_sky)],
+        axis=0,
     )
-    column_share = local_coadd(warped_all, var_all)
-    coadd_field = lax.all_gather(column_share, "visit", axis=1, tiled=True)
-    coadd_low = coadd_field.astype(jnp.bfloat16)
+    strips_here = lax.all_to_all(windows, "sky", split_axis=0, concat_axis=0, tiled=True)
     strips = intersection[0, 0]
-    start_col = col_start[0, 0]
-    rows_map = row_interp[0, 0]
-    shard_rows = lax.all_gather(coadd_low, "sky", axis=0, tiled=True)
-    first_row = jnp.int32(0)
-    row_count = shard_rows.shape[0]
-    block_rows = min(row_count, STRIP)
-    total = jnp.zeros((TILE, TILE), jnp.float32)
-    for block_index in range(row_count // block_rows):
-        block_first = first_row + block_index * block_rows
-        strip_of = block_first // STRIP
-        inside = block_first % STRIP
-        matches = strips == strip_of
-        slot_index = jnp.sum(jnp.where(matches, jnp.arange(NOV, dtype=jnp.int32), 0))
-        present = jnp.any(matches)
-        block_data = shard_rows[block_index * block_rows : (block_index + 1) * block_rows]
-
-        def add_block(current):
-            chosen = lax.dynamic_slice_in_dim(rows_map, slot_index * STRIP + inside, block_rows, 1)
-            columns = lax.dynamic_slice_in_dim(block_data, start_col, TILE, 1)
-            return current + jnp.dot(chosen, columns, preferred_element_type=jnp.float32)
-
-        total = lax.cond(present, add_block, lambda current: current, total)
-    blotted = jnp.dot(
-        total.astype(jnp.bfloat16), col_interp[0, 0], preferred_element_type=jnp.float32
-    ).astype(jnp.bfloat16)
+    footprint = jnp.concatenate(
+        [lax.dynamic_index_in_dim(strips_here, strips[slot], 0, keepdims=False) for slot in range(NOV)],
+        axis=0,
+    )
+    projected = jnp.dot(row_interp[0, 0], footprint, preferred_element_type=jnp.float32).astype(
+        jnp.bfloat16
+    )
+    blotted = jnp.dot(projected, col_interp[0, 0], preferred_element_type=jnp.float32).astype(
+        jnp.bfloat16
+    )
     matched = psf_match(blotted, cell_ids[0, 0], kernels[0, 0])
     residual = (
         (science[0, 0].astype(jnp.float32) - matched)

time: 204 us -> 147 us (0.72)
  waiting for transfers between devices: 91.6 us -> 8.24 us
  blocking collectives: 0 us -> 60.3 us
  local copies, waits for them, and re-layouts: 39.7 us -> 13.7 us
  between operations: 17.1 us -> 30.3 us
  loops' own time: 10.3 us -> 0 us
  starting transfers between devices: 11.6 us -> 3.69 us
  other arithmetic: 14.2 us -> 11.5 us
    all_to_all x0 -> x1, blocking collectives: none -> 55.3 us  [shards(): lax.all_to_all(stacked, 'visit', split_axis=2, concat_axis=1, tiled=True)]
    all_to_all x2 -> x1, waiting for transfers between devices: 46.7 us -> 2.12 us  [shards(): lax.all_to_all(windows, 'sky', split_axis=0, concat_axis=0, tiled=True)]
    all_gather x2 -> x1, waiting for transfers between devices: 44.9 us -> 6.1 us  [shards(): coadd_field = lax.all_gather(row_share, 'visit', axis=0, tiled=True)]
    another operation x4 -> x2, local copies, waits for them, and re-layouts: 14.8 us -> 0.55 us  [the longest x1 0.31 us: shards(): jnp.stack([lax.dynamic_slice_in_dim(coadd_low, all_starts[peer], TILE, 1)...]
    another operation x4 -> x0, loops' own time: 10.3 us -> none  [shards(): total = lax.cond(present, add_block, lambda current: current, total)]
    all_to_all x2 -> x1, starting transfers between devices: 11.5 us -> 3.65 us  [shards(): lax.all_to_all(windows, 'sky', split_axis=0, concat_axis=0, tiled=True)]
    unnamed x53 -> x42, local copies, waits for them, and re-layouts: 10.5 us -> 4.36 us
    unnamed x0 -> x1, blocking collectives: none -> 4.97 us
  transfers between devices with their start and end apart: 4 -> 2, of which waited for: 4 -> 2; matrix products, arithmetic and copies ran while one was open for 9% -> 13% of each run, Pallas kernels for 0% -> 0%
where the time goes in v1:
time: 147 us; the launch traced here: 146 us
  blocking collectives  60.3 us (41%)
  between operations  30.3 us (21%)
  matrix products  18.2 us (12%)
  local copies, waits for them, and re-layouts  13.7 us (9%)
  other arithmetic  11.5 us (8%)
  waiting for transfers between devices  8.24 us (6%)
  starting transfers between devices  3.69 us (3%)
    all_to_all x1, blocking collectives, shards(): lax.all_to_all(stacked, 'visit', split_axis=2, concat_axis=1, tiled=True)  55.3 us
    dot_general x1, matrix products, psf_match(): jnp.einsum('xyab,bcl->xyacl', tap_rows, diagonal, precision=lax.Precision...  9.57 us
    squeeze x1, local copies, waits for them, and re-layouts, psf_match(): banded_all[row_block, col_block]  6.48 us
    dot_general x16, matrix products, psf_match(): jnp.einsum('rc,acl->arl', cols_window, banded_all[row_block, col_block],...  6.3 us
    all_gather x1, waiting for transfers between devices, shards(): coadd_field = lax.all_gather(row_share, 'visit', axis=0, tiled=True)  6.1 us
    unnamed x1, blocking collectives  4.97 us
    unnamed x42, local copies, waits for them, and re-layouts  4.36 us
    reduce_sum x3, other arithmetic, local_coadd(): coadd_field = jnp.sum(cauchy * values, axis=0) / jnp.sum(cauchy, axis=0)  3.95 us
  transfers between devices with their start and end apart: 2, of which 2 were waited for; matrix products, arithmetic and copies ran while one was open for 13% of the time, Pallas kernels for 0%

profile of v1, /device:TPU:0, one launch (start us, length us, event | category | flops | bytes accessed | tf_op | source)
XLA Modules:
  0.0 145.9 jit_solution(5891192401278518905)
XLA Ops:
  7.2 1.8 %pad_maximum_fusion = bf16[2,2,8,16,2048]{4,3,2,1,0:T(8,128)(2,1)S(1)} fusion(bf16[1,2,8,16,2048]{4,3,2,1,0:T(8,128)(2,1)} %bitcast.217, bf16[1,2,8,16,2048]{4,3,2,1,0:T(8,128)(2,1)} %bitcast.218), kind=kLoop, calls=%fused_computation.29 | loop fusion | flops 1048576 | bytes 4194304 | tf_op jit(solution)/shard_map/stack | solution.py:85
  9.0 0.2 copy.62
  9.3 55.3 %all_to_all.20 = bf16[2,2,8,16,2048]{4,3,1,0,2:T(8,128)(2,1)S(1)} all-to-all(bf16[2,2,8,16,2048]{4,3,1,0,2:T(8,128)(2,1)S(1)} %copy.62), channel_id=1, replica_groups=mesh['visit'=8,'sky'=4] {'visit'}, dimensions={2} | all-to-all | bytes 4194304 | tf_op jit(solution)/shard_map/all_to_all | solution.py:88
  64.6 0.4 convert_reduce_fusion
  65.0 1.3 fusion.23
  66.3 1.3 fusion.24
  67.7 1.3 fusion.25
  69.1 0.7 div.67
  70.4 0.6 dynamic-slice
  71.0 0.7 bitcast_dynamic-update-slice_fusion
  71.7 5.0 %all-reduce.1 = s32[4]{0:T(128)S(1)} all-reduce(s32[4]{0:T(128)S(1)} %bitcast_dynamic-update-slice_fusion), channel_id=2, replica_groups=mesh['visit'=8,'sky'=4] {'sky'}, use_global_device_ids=true, to_apply=%add.1 | all-reduce | flops 4 | bytes 32
  76.7 0.7 fusion.120
  82.5 0.6 fusion.119
  88.0 0.1 dot_general.65
  88.2 0.2 copy.63
  93.4 0.2 convolution_bitcast_fusion.16
  93.6 9.6 %convolution_convert_fusion = bf16[4,4,11,138,128]{4,2,3,1,0:T(8,128)(2,1)} fusion(s32[138,128]{1,0:T(8,128)S(1)} %iota_subtract_fusion, f32[4,4,11,11,1]{3,1,2,0,4:T(4,128)S(1)} %convolution_bitcast_fusion.16), kind=kOutput, calls=%fused_computation | convolution fusion | flops 413673216 | bytes 6296128 | tf_op jit(solution)/shard_map/xyab,bcl->xyacl/dot_general | solution.py:44
  103.2 6.1 %all-gather.3.cloned.1.call-done = f32[128,2048]{1,0:T(8,128)} async-done(((f32[16,2048]{1,0:T(8,128)}), f32[128,2048]{1,0:T(8,128)}) %all-gather.3.cloned.1.call-update) | async-done | bytes 1048592 | tf_op jit(solution)/shard_map/all_gather | solution.py:91
  109.3 1.3 convert_element_type.50
  110.6 0.3 dynamic-slice_bitcast_fusion.7
  110.9 0.9 pad_maximum_fusion.1
  111.8 3.6 %all-to-all-start.1 = ((bf16[4,128,512]{2,1,0:T(8,128)(2,1)}), bf16[4,128,512]{2,1,0:T(8,128)(2,1)S(1)}, u32[]{:S(2)}, u32[]{:S(2)}) async-start(bf16[4,128,512]{2,1,0:T(8,128)(2,1)} %pad_maximum_fusion.1), calls=%async_computation.1 | async-start | bytes 1048576 | tf_op jit(solution)/shard_map/all_to_all | solution.py:100
  115.5 6.5 %slice_bitcast_fusion.15 = (bf16[11,138,128]{2,0,1:T(8,128)(2,1)}, bf16[11,138,128]{2,0,1:T(8,128)(2,1)}, bf16[11,138,128]{2,0,1:T(8,128)(2,1)}, bf16[11,138,128...) fusion(bf16[4,4,11,138,128]{4,2,3,1,0:T(8,128)(2,1)} %convoluti, ...), kind=kLoop, calls=%fused_computation.87 | loop fusion | bytes 12435456 | tf_op jit(solution)/shard_map/squeeze | solution.py:59
  122.0 2.1 %all-to-all-done.1 = bf16[4,128,512]{2,1,0:T(8,128)(2,1)S(1)} async-done(((bf16[4,128,512]{2,1,0:T(8,128)(2,1)}), bf16[4,128,512]{2,1,0:T(8,128)(2,1)S(1)}, u32[]{:S(2)}, u32[]{:S(2)}) %all-to-all-start.1) | async-done | bytes 524320 | tf_op jit(solution)/shard_map/all_to_all | solution.py:100
  124.1 0.8 dynamic-slice_bitcast_fusion.3
  124.8 2.1 %convolution_convert_fusion.1 = bf16[512,512]{1,0:T(8,128)(2,1)S(1)} fusion(bf16[128,512]{1,0:T(8,128)(2,1)} %get-tuple-element.27, bf16[128,512]{1,0:T(8,128)(2,1)} %get-tuple-element.28, bf16[128,512]{1,0:T(8,128)(2,1)} %get-tuple-element.29, bf16[128,512]{1,0:T(8,128)(2,1)S(1)} %get-tuple-element.26, bf16[1,1,512,512]{3,2,1,0:T(8,128)(2,1)S(1)} %copy-done, ...), kind=kOutput, calls=%fused_computation.46 | convolution fusion | flops 539492352 | bytes 2097152 | tf_op jit(solution)/shard_map/dot_general | solution.py:109
  127.0 1.5 %convolution_bitcast_fusion.15 = f32[11,138,128]{2,1,0:T(8,128)S(1)} fusion(bf16[11,138,128]{2,0,1:T(8,128)(2,1)} %get-tuple-element.10, bf16[512,512]{1,0:T(8,128)(2,1)S(1)} %convolution_convert_fusion.1), kind=kOutput, calls=%fused_computation.45 | convolution fusion | flops 53627904 | bytes 1690112 | tf_op jit(solution)/shard_map/rc,acl->arl/dot_general | solution.py:56
  128.4 0.1 fusion.100
  128.5 0.3 convolution_bitcast_fusion
  128.9 0.1 fusion.85
  129.0 0.3 convolution_bitcast_fusion.1
  129.3 0.1 fusion.86
  129.3 0.2 copy-done.10
  129.6 0.3 convolution_bitcast_fusion.2
  129.9 0.1 fusion.87
  130.0 0.3 convolution_bitcast_fusion.3
  130.4 0.1 fusion.88
  130.4 0.2 copy-done.8
  130.7 0.3 convolution_bitcast_fusion.4
  131.0 0.1 fusion.89
  131.1 0.3 convolution_bitcast_fusion.5
  131.5 0.1 fusion.90
  131.5 0.2 copy-done.6
  131.8 0.3 convolution_bitcast_fusion.6
  132.1 0.1 fusion.91
  132.2 0.3 convolution_bitcast_fusion.7
  132.5 0.1 fusion.92
  132.6 0.3 copy-done.4
  132.9 0.3 convolution_bitcast_fusion.8
  133.2 0.1 fusion.93
  133.3 0.3 convolution_bitcast_fusion.9
  133.6 0.1 fusion.94
  133.7 0.3 copy-done.2
  134.0 0.3 convolution_bitcast_fusion.10
  134.3 0.1 fusion.95
  134.4 0.3 convolution_bitcast_fusion.11
  134.8 0.3 convolution_bitcast_fusion.12
  135.1 0.1 fusion.97
  135.2 0.3 convolution_bitcast_fusion.13
  135.6 0.3 convolution_bitcast_fusion.14
  136.1 0.5 copy-done.13
  136.6 0.2 copy-done.14
  136.8 1.3 fusion.22
  138.1 1.0 copy.123
  (43 shorter events, 0.6 us)
Async XLA Ops:
  7.2 117.7 %copy-start = (bf16[1,1,512,512]{3,2,1,0:T(8,128)(2,1)S(1)}, bf16[1,1,512,512]{3,2,1,0:T(8,128)(2,1)}, u32[]{:S(2)}) copy-start(bf16[1,1,512,512]{3,2,1,0:T(8,128)(2,1)} %param.15) | copy-start | bytes 1572868
  7.2 102.1 %all-gather.3.cloned.1.call-start = ((), (), s32[]{:S(2)}) async-start(), calls=%async_computation.2 | async-start | bytes 1179648 | tf_op jit(solution)/shard_map/all_gather | solution.py:91
  67.7 2.8 %copy-start.18 = (u32[32]{0:T(128)S(1)}, u32[32]{0:T(128)}, u32[]{:S(2)}) copy-start(u32[32]{0:T(128)} %constant.44) | copy-start | bytes 388
  67.7 14.8 %copy-start.15 = (s32[1,1,4]{2,1,0:T(1,128)S(1)}, s32[1,1,4]{2,1,0:T(1,128)}, u32[]{:S(2)}) copy-start(s32[1,1,4]{2,1,0:T(1,128)} %param.12) | copy-start | bytes 52
  67.7 20.4 %copy-start.16 = (bf16[1,1,16,121]{3,2,1,0:T(8,128)(2,1)S(1)}, bf16[1,1,16,121]{3,2,1,0:T(8,128)(2,1)}, u32[]{:S(2)}) copy-start(bf16[1,1,16,121]{3,2,1,0:T(8,128)(2,1)} %param.17) | copy-start | bytes 11620
  67.7 25.7 %copy-start.17 = (s32[1,1,4,4]{3,2,1,0:T(4,128)S(1)}, s32[1,1,4,4]{3,2,1,0:T(4,128)}, u32[]{:S(2)}) copy-start(s32[1,1,4,4]{3,2,1,0:T(4,128)} %param.16) | copy-start | bytes 196
  111.8 12.3 %all-to-all-start.1 = ((bf16[4,128,512]{2,1,0:T(8,128)(2,1)}), bf16[4,128,512]{2,1,0:T(8,128)(2,1)S(1)}, u32[]{:S(2)}, u32[]{:S(2)}) async-start(bf16[4,128,512]{2,1,0:T(8,128)(2,1)} %pad_maximum_fusion.1), calls=%async_computation.1 | async-start | bytes 1048576 | tf_op jit(solution)/shard_map/all_to_all | solution.py:100
  126.9 1.6 %copy-start.12 = (bf16[11,138,128]{2,0,1:T(8,128)(2,1)S(1)}, bf16[11,138,128]{2,0,1:T(8,128)(2,1)}, u32[]{:S(2)}) copy-start(bf16[11,138,128]{2,0,1:T(8,128)(2,1)} %get-tuple-element.11) | copy-start | bytes 1165828
  127.0 2.0 %copy-start.11 = (bf16[11,138,128]{2,0,1:T(8,128)(2,1)S(1)}, bf16[11,138,128]{2,0,1:T(8,128)(2,1)}, u32[]{:S(2)}) copy-start(bf16[11,138,128]{2,0,1:T(8,128)(2,1)} %get-tuple-element.12) | copy-start | bytes 1165828
  128.5 1.1 copy-start.10
  128.9 1.1 copy-start.9
  129.6 1.1 copy-start.8
  130.0 1.1 copy-start.7
  130.7 1.1 copy-start.6
  131.1 1.1 copy-start.5
  131.8 1.1 copy-start.4
  132.2 1.1 copy-start.3
  132.9 1.1 copy-start.2
  135.6 1.0 copy-start.13
  135.6 1.2 copy-start.14
  136.1 2.0 %copy-start.1 = (f32[128,2048]{1,0:T(8,128)S(1)}, f32[128,2048]{1,0:T(8,128)}, u32[]{:S(2)}) copy-start(f32[128,2048]{1,0:T(8,128)} %all-gather.3.cloned.1.call-done) | copy-start | bytes 3145732
Sparse Core Ops, SparseCore 0:
  69.9 39.3 all-gather.2

commit v2 on v1

--- a/solution.py
+++ b/solution.py
@@ -88,7 +88,9 @@
     gathered = lax.all_to_all(stacked, "visit", split_axis=2, concat_axis=1, tiled=True)
     gathered = gathered.reshape(2, local_visits * n_visit, chunk, sky_w)
     row_share = local_coadd(gathered[0].astype(jnp.float32), gathered[1].astype(jnp.float32))
-    coadd_field = lax.all_gather(row_share, "visit", axis=0, tiled=True)
+    copies = jnp.broadcast_to(row_share[None], (n_visit,) + row_share.shape)
+    coadd_field = lax.all_to_all(copies, "visit", split_axis=0, concat_axis=0, tiled=True)
+    coadd_field = coadd_field.reshape(n_visit * chunk, sky_w)
     coadd_low = coadd_field.astype(jnp.bfloat16)
 
     start_col = col_start[0, 0]

time: 147 us -> 130 us (0.88)
  between operations: 30.3 us -> 16.9 us
  waiting for transfers between devices: 8.24 us -> 2.08 us
  starting transfers between devices: 3.69 us -> 7.24 us
  other arithmetic: 11.5 us -> 9.59 us
    all_gather x1 -> x0, waiting for transfers between devices: 6.1 us -> none  [shards(): coadd_field = lax.all_gather(row_share, 'visit', axis=0, tiled=True)]
    all_to_all x0 -> x1, starting transfers between devices: none -> 3.59 us  [shards(): lax.all_to_all(copies, 'visit', split_axis=0, concat_axis=0, tiled=True)]
    unnamed x42 -> x44, local copies, waits for them, and re-layouts: 4.36 us -> 4.64 us
  transfers between devices with their start and end apart: 2 -> 2, of which waited for: 2 -> 1; matrix products, arithmetic and copies ran while one was open for 13% -> 15% of each run, Pallas kernels for 0% -> 0%
where the time goes in v2:
time: 130 us; the launch traced here: 129 us
  blocking collectives  60.3 us (46%)
  matrix products  18.1 us (14%)
  between operations  16.9 us (13%)
  local copies, waits for them, and re-layouts  15 us (12%)
  other arithmetic  9.59 us (7%)
  starting transfers between devices  7.24 us (6%)
  waiting for transfers between devices  2.08 us (2%)
    all_to_all x1, blocking collectives, shards(): lax.all_to_all(stacked, 'visit', split_axis=2, concat_axis=1, tiled=True)  55.3 us
    dot_general x1, matrix products, psf_match(): jnp.einsum('xyab,bcl->xyacl', tap_rows, diagonal, precision=lax.Precision...  9.57 us
    squeeze x1, local copies, waits for them, and re-layouts, psf_match(): banded_all[row_block, col_block]  6.52 us
    dot_general x16, matrix products, psf_match(): jnp.einsum('rc,acl->arl', cols_window, banded_all[row_block, col_block],...  6.3 us
    unnamed x1, blocking collectives  4.97 us
    unnamed x44, local copies, waits for them, and re-layouts  4.64 us
    reduce_sum x3, other arithmetic, local_coadd(): coadd_field = jnp.sum(cauchy * values, axis=0) / jnp.sum(cauchy, axis=0)  3.96 us
    all_to_all x1, starting transfers between devices, shards(): lax.all_to_all(windows, 'sky', split_axis=0, concat_axis=0, tiled=True)  3.65 us
  transfers between devices with their start and end apart: 2, of which 1 were waited for; matrix products, arithmetic and copies ran while one was open for 15% of the time, Pallas kernels for 0%

profile of v2, /device:TPU:0, one launch (start us, length us, event | category | flops | bytes accessed | tf_op | source)
XLA Modules:
  0.0 129.3 jit_solution(13960027414776677944)
XLA Ops:
  0.6 1.8 %pad_maximum_fusion = bf16[2,2,8,16,2048]{4,3,2,1,0:T(8,128)(2,1)S(1)} fusion(bf16[1,2,8,16,2048]{4,3,2,1,0:T(8,128)(2,1)} %bitcast.220, bf16[1,2,8,16,2048]{4,3,2,1,0:T(8,128)(2,1)} %bitcast.221), kind=kLoop, calls=%fused_computation.29 | loop fusion | flops 1048576 | bytes 4194304 | tf_op jit(solution)/shard_map/stack | solution.py:85
  2.4 0.2 copy.62
  2.7 55.3 %all_to_all.25 = bf16[2,2,8,16,2048]{4,3,1,0,2:T(8,128)(2,1)S(1)} all-to-all(bf16[2,2,8,16,2048]{4,3,1,0,2:T(8,128)(2,1)S(1)} %copy.62), channel_id=1, replica_groups=mesh['visit'=8,'sky'=4] {'visit'}, dimensions={2} | all-to-all | bytes 4194304 | tf_op jit(solution)/shard_map/all_to_all | solution.py:88
  58.0 0.4 convert_reduce_fusion
  58.4 1.3 %fusion.23 = (f32[16,2048]{1,0:T(8,128)S(1)}, f32[16,2048]{1,0:T(8,128)S(1)}) fusion(f32[16,2048]{1,0:T(8,128)S(1)} %div.62, bf16[2,8,2,1,16,2048]{5,4,2,0,1,3:T(8,128)(2,1)S(1)} %bitcast.216), kind=kLoop, calls=%fused_computation.69 | loop fusion | flops 5701632 | bytes 2490368 | tf_op jit(solution)/shard_map/reduce_sum | solution.py:25
  59.8 1.3 %fusion.24 = (f32[16,2048]{1,0:T(8,128)S(1)}, f32[16,2048]{1,0:T(8,128)S(1)}) fusion(f32[16,2048]{1,0:T(8,128)S(1)} %div.65, bf16[2,8,2,1,16,2048]{5,4,2,0,1,3:T(8,128)(2,1)S(1)} %bitcast.217), kind=kLoop, calls=%fused_computation.70 | loop fusion | flops 5701632 | bytes 2490368 | tf_op jit(solution)/shard_map/reduce_sum | solution.py:25
  61.1 1.3 %fusion.25 = (f32[16,2048]{1,0:T(8,128)S(1)}, f32[16,2048]{1,0:T(8,128)S(1)}) fusion(f32[16,2048]{1,0:T(8,128)S(1)} %div.68, bf16[2,8,2,1,16,2048]{5,4,2,0,1,3:T(8,128)(2,1)S(1)} %bitcast.218), kind=kLoop, calls=%fused_computation.71 | loop fusion | flops 5701632 | bytes 2490368 | tf_op jit(solution)/shard_map/reduce_sum | solution.py:25
  62.5 1.1 broadcast_in_dim.2
  63.6 3.6 %all-to-all-start.1 = ((f32[8,16,2048]{2,1,0:T(8,128)}), f32[8,16,2048]{2,1,0:T(8,128)S(1)}, u32[]{:S(2)}, u32[]{:S(2)}) async-start(f32[8,16,2048]{2,1,0:T(8,128)} %broadcast_in_dim.2), calls=%async_computation.1 | async-start | bytes 2097152 | tf_op jit(solution)/shard_map/all_to_all | solution.py:92
  67.9 0.6 dynamic-slice
  68.4 0.7 bitcast_dynamic-update-slice_fusion
  69.1 5.0 %all-reduce.1 = s32[4]{0:T(128)S(1)} all-reduce(s32[4]{0:T(128)S(1)} %bitcast_dynamic-update-slice_fusion), channel_id=2, replica_groups=mesh['visit'=8,'sky'=4] {'sky'}, use_global_device_ids=true, to_apply=%add.1 | all-reduce | flops 4 | bytes 32
  74.1 0.7 fusion.120
  79.9 0.6 fusion.119
  85.5 0.1 dot_general.65
  85.6 0.2 copy.63
  90.8 0.2 convolution_bitcast_fusion.16
  91.1 9.6 %convolution_convert_fusion = bf16[4,4,11,138,128]{4,2,3,1,0:T(8,128)(2,1)} fusion(s32[138,128]{1,0:T(8,128)S(1)} %iota_subtract_fusion, f32[4,4,11,11,1]{3,1,2,0,4:T(4,128)S(1)} %convolution_bitcast_fusion.16), kind=kOutput, calls=%fused_computation | convolution fusion | flops 413673216 | bytes 6296128 | tf_op jit(solution)/shard_map/xyab,bcl->xyacl/dot_general | solution.py:44
  100.7 0.3 dynamic-slice_bitcast_fusion.7
  101.0 0.9 pad_maximum_fusion.1
  101.9 3.6 %all-to-all-start.2 = ((bf16[4,128,512]{2,1,0:T(8,128)(2,1)}), bf16[4,128,512]{2,1,0:T(8,128)(2,1)S(1)}, u32[]{:S(2)}, u32[]{:S(2)}) async-start(bf16[4,128,512]{2,1,0:T(8,128)(2,1)} %pad_maximum_fusion.1), calls=%async_computation.2 | async-start | bytes 1048576 | tf_op jit(solution)/shard_map/all_to_all | solution.py:102
  105.5 6.5 %slice_bitcast_fusion.15 = (bf16[11,138,128]{2,0,1:T(8,128)(2,1)}, bf16[11,138,128]{2,0,1:T(8,128)(2,1)}, bf16[11,138,128]{2,0,1:T(8,128)(2,1)}, bf16[11,138,128...) fusion(bf16[4,4,11,138,128]{4,2,3,1,0:T(8,128)(2,1)} %convoluti, ...), kind=kLoop, calls=%fused_computation.87 | loop fusion | bytes 12435456 | tf_op jit(solution)/shard_map/squeeze | solution.py:59
  112.1 2.1 %all-to-all-done.2 = bf16[4,128,512]{2,1,0:T(8,128)(2,1)S(1)} async-done(((bf16[4,128,512]{2,1,0:T(8,128)(2,1)}), bf16[4,128,512]{2,1,0:T(8,128)(2,1)S(1)}, u32[]{:S(2)}, u32[]{:S(2)}) %all-to-all-start.2) | async-done | bytes 524320 | tf_op jit(solution)/shard_map/all_to_all | solution.py:102
  114.1 0.7 dynamic-slice_bitcast_fusion.3
  114.9 2.0 %convolution_convert_fusion.1 = bf16[512,512]{1,0:T(8,128)(2,1)S(1)} fusion(bf16[128,512]{1,0:T(8,128)(2,1)S(1)} %get-tuple-element.27, bf16[128,512]{1,0:T(8,128)(2,1)} %get-tuple-element.28, bf16[128,512]{1,0:T(8,128)(2,1)} %get-tuple-element.29, bf16[128,512]{1,0:T(8,128)(2,1)S(1)} %get-tuple-element.26, bf16[1,1,512,512]{3,2,1,0:T(8,128)(2,1)S(1)} %copy-done, ...), kind=kOutput, calls=%fused_computation.46 | convolution fusion | flops 539492352 | bytes 2097152 | tf_op jit(solution)/shard_map/dot_general | solution.py:111
  116.9 1.5 %convolution_bitcast_fusion.15 = f32[11,138,128]{2,1,0:T(8,128)S(1)} fusion(bf16[11,138,128]{2,0,1:T(8,128)(2,1)} %get-tuple-element.10, bf16[512,512]{1,0:T(8,128)(2,1)S(1)} %convolution_convert_fusion.1), kind=kOutput, calls=%fused_computation.45 | convolution fusion | flops 53627904 | bytes 1690112 | tf_op jit(solution)/shard_map/rc,acl->arl/dot_general | solution.py:56
  118.4 0.1 fusion.100
  118.5 0.3 convolution_bitcast_fusion
  118.8 0.1 fusion.85
  118.9 0.3 convolution_bitcast_fusion.1
  119.2 0.1 fusion.86
  119.3 0.2 copy-done.11
  119.5 0.3 convolution_bitcast_fusion.2
  119.9 0.1 fusion.87
  120.0 0.3 convolution_bitcast_fusion.3
  120.3 0.1 fusion.88
  120.4 0.2 copy-done.9
  120.6 0.3 convolution_bitcast_fusion.4
  121.0 0.1 fusion.89
  121.1 0.3 convolution_bitcast_fusion.5
  121.4 0.1 fusion.90
  121.5 0.2 copy-done.7
  121.7 0.3 convolution_bitcast_fusion.6
  122.1 0.1 fusion.91
  122.2 0.3 convolution_bitcast_fusion.7
  122.5 0.1 fusion.92
  122.6 0.3 copy-done.5
  122.8 0.3 convolution_bitcast_fusion.8
  123.2 0.1 fusion.93
  123.3 0.3 convolution_bitcast_fusion.9
  123.6 0.1 fusion.94
  123.7 0.3 copy-done.3
  123.9 0.3 convolution_bitcast_fusion.10
  124.3 0.1 fusion.95
  124.3 0.3 convolution_bitcast_fusion.11
  124.7 0.1 fusion.96
  124.8 0.3 copy-done.1
  125.0 0.3 convolution_bitcast_fusion.12
  125.4 0.3 convolution_bitcast_fusion.13
  125.9 0.3 convolution_bitcast_fusion.14
  126.4 0.5 copy-done.14
  126.9 0.2 copy-done.15
  127.0 1.3 fusion.22
  128.3 1.0 copy.123
  (45 shorter events, 0.7 us)
Async XLA Ops:
  0.6 114.2 %copy-start = (bf16[1,1,512,512]{3,2,1,0:T(8,128)(2,1)S(1)}, bf16[1,1,512,512]{3,2,1,0:T(8,128)(2,1)}, u32[]{:S(2)}) copy-start(bf16[1,1,512,512]{3,2,1,0:T(8,128)(2,1)} %param.15) | copy-start | bytes 1572868
  62.4 5.4 %copy-start.19 = (u32[32]{0:T(128)S(1)}, u32[32]{0:T(128)}, u32[]{:S(2)}) copy-start(u32[32]{0:T(128)} %constant.44) | copy-start | bytes 388
  62.5 17.5 %copy-start.16 = (s32[1,1,4]{2,1,0:T(1,128)S(1)}, s32[1,1,4]{2,1,0:T(1,128)}, u32[]{:S(2)}) copy-start(s32[1,1,4]{2,1,0:T(1,128)} %param.12) | copy-start | bytes 52
  62.5 23.0 %copy-start.17 = (bf16[1,1,16,121]{3,2,1,0:T(8,128)(2,1)S(1)}, bf16[1,1,16,121]{3,2,1,0:T(8,128)(2,1)}, u32[]{:S(2)}) copy-start(bf16[1,1,16,121]{3,2,1,0:T(8,128)(2,1)} %param.17) | copy-start | bytes 11620
  62.5 28.3 %copy-start.18 = (s32[1,1,4,4]{3,2,1,0:T(4,128)S(1)}, s32[1,1,4,4]{3,2,1,0:T(4,128)}, u32[]{:S(2)}) copy-start(s32[1,1,4,4]{3,2,1,0:T(4,128)} %param.16) | copy-start | bytes 196
  63.6 37.0 %all-to-all-start.1 = ((f32[8,16,2048]{2,1,0:T(8,128)}), f32[8,16,2048]{2,1,0:T(8,128)S(1)}, u32[]{:S(2)}, u32[]{:S(2)}) async-start(f32[8,16,2048]{2,1,0:T(8,128)} %broadcast_in_dim.2), calls=%async_computation.1 | async-start | bytes 2097152 | tf_op jit(solution)/shard_map/all_to_all | solution.py:92
  101.9 12.3 %all-to-all-start.2 = ((bf16[4,128,512]{2,1,0:T(8,128)(2,1)}), bf16[4,128,512]{2,1,0:T(8,128)(2,1)S(1)}, u32[]{:S(2)}, u32[]{:S(2)}) async-start(bf16[4,128,512]{2,1,0:T(8,128)(2,1)} %pad_maximum_fusion.1), calls=%async_computation.2 | async-start | bytes 1048576 | tf_op jit(solution)/shard_map/all_to_all | solution.py:102
  116.9 1.6 %copy-start.13 = (bf16[11,138,128]{2,0,1:T(8,128)(2,1)S(1)}, bf16[11,138,128]{2,0,1:T(8,128)(2,1)}, u32[]{:S(2)}) copy-start(bf16[11,138,128]{2,0,1:T(8,128)(2,1)} %get-tuple-element.11) | copy-start | bytes 1165828
  116.9 2.0 %copy-start.12 = (bf16[11,138,128]{2,0,1:T(8,128)(2,1)S(1)}, bf16[11,138,128]{2,0,1:T(8,128)(2,1)}, u32[]{:S(2)}) copy-start(bf16[11,138,128]{2,0,1:T(8,128)(2,1)} %get-tuple-element.12) | copy-start | bytes 1165828
  118.5 1.1 copy-start.11
  118.9 1.1 copy-start.10
  119.5 1.1 copy-start.9
  120.0 1.1 copy-start.8
  120.6 1.1 copy-start.7
  121.0 1.1 copy-start.6
  121.7 1.1 copy-start.5
  122.2 1.1 copy-start.4
  122.8 1.1 copy-start.3
  123.2 1.1 copy-start.2
  123.9 1.1 copy-start.1
  125.8 1.0 copy-start.14
  125.9 1.2 copy-start.15

commit v3 on v2

--- a/solution.py
+++ b/solution.py
@@ -35,15 +35,16 @@
         jnp.bfloat16
     )
     tap_rows = jnp.dot(picker, kernel_table, preferred_element_type=jnp.float32)
-    tap_rows = tap_rows.reshape(blocks, blocks, KSIZE, KSIZE)
+    tap_rows = tap_rows.astype(jnp.bfloat16).reshape(blocks * blocks, KSIZE, KSIZE)
     source = jnp.arange(window, dtype=jnp.int32)[:, None]
     target = jnp.arange(CELL, dtype=jnp.int32)[None, :]
     diagonal = (
         (source - target)[None] == jnp.arange(KSIZE, dtype=jnp.int32)[:, None, None]
-    ).astype(jnp.float32)
+    ).astype(jnp.bfloat16)
     banded_all = jnp.einsum(
-        "xyab,bcl->xyacl", tap_rows, diagonal, precision=lax.Precision.HIGHEST
+        "kab,bcl->kcal", tap_rows, diagonal, preferred_element_type=jnp.float32
     ).astype(jnp.bfloat16)
+    banded_all = banded_all.reshape(blocks * blocks, window, KSIZE * CELL)
     padded = jnp.pad(blotted, ((half_width, half_width), (half_width, half_width)))
     row_parts = []
     for row_block in range(blocks):
@@ -53,15 +54,14 @@
             cols_window = lax.slice_in_dim(
                 rows_window, col_block * CELL, col_block * CELL + window, axis=1
             )
-            horizontal = jnp.einsum(
-                "rc,acl->arl",
+            horizontal = jnp.dot(
                 cols_window,
-                banded_all[row_block, col_block],
+                banded_all[row_block * blocks + col_block],
                 preferred_element_type=jnp.float32,
-            )
-            summed = horizontal[0, 0:CELL, :]
+            ).reshape(window, KSIZE, CELL)
+            summed = horizontal[0:CELL, 0, :]
             for tap_row in range(1, KSIZE):
-                summed = summed + horizontal[tap_row, tap_row : tap_row + CELL, :]
+                summed = summed + horizontal[tap_row : tap_row + CELL, tap_row, :]
             col_parts.append(summed)
         row_parts.append(jnp.concatenate(col_parts, axis=1))
     return jnp.concatenate(row_parts, axis=0)
@@ -84,9 +84,11 @@
     local_visits, strip_rows, sky_w = warped.shape
     stacked = jnp.stack([warped, inv_var], axis=0)
     chunk = strip_rows // n_visit
-    stacked = stacked.reshape(2, local_visits, n_visit, chunk, sky_w)
-    gathered = lax.all_to_all(stacked, "visit", split_axis=2, concat_axis=1, tiled=True)
-    gathered = gathered.reshape(2, local_visits * n_visit, chunk, sky_w)
+    stacked = stacked.reshape(2, local_visits, n_visit, chunk, sky_w).transpose(2, 0, 1, 3, 4)
+    stacked = stacked.reshape(n_visit, 2 * local_visits * chunk, sky_w)
+    gathered = lax.all_to_all(stacked, "visit", split_axis=0, concat_axis=0, tiled=True)
+    gathered = gathered.reshape(n_visit, 2, local_visits, chunk, sky_w)
+    gathered = gathered.transpose(1, 0, 2, 3, 4).reshape(2, n_visit * local_visits, chunk, sky_w)
     row_share = local_coadd(gathered[0].astype(jnp.float32), gathered[1].astype(jnp.float32))
     copies = jnp.broadcast_to(row_share[None], (n_visit,) + row_share.shape)
     coadd_field = lax.all_to_all(copies, "visit", split_axis=0, concat_axis=0, tiled=True)

time: 130 us -> 229 us (1.76)
  local copies, waits for them, and re-layouts: 15 us -> 115 us
  matrix products: 18.1 us -> 11.7 us
  waiting for transfers between devices: 2.08 us -> 5.6 us
    slice x0 -> x1, local copies, waits for them, and re-layouts: none -> 46.7 us  [psf_match(): banded_all[row_block * blocks + col_block]]
    dot_general x2 -> x16, local copies, waits for them, and re-layouts: 0.26 us -> 30.4 us  [psf_match(): jnp.dot(cols_window, banded_all[row_block * blocks + col_block], preferre...]
    unnamed x44 -> x80, local copies, waits for them, and re-layouts: 4.64 us -> 33.3 us
    squeeze x1 -> x0, local copies, waits for them, and re-layouts: 6.52 us -> none  [psf_match(): banded_all[row_block, col_block]]
    dot_general x17, matrix products: 15.9 us -> 9.45 us  [the longest x16 5.06 us: psf_match(): jnp.dot(cols_window, banded_all[row_block * blocks + col_block], preferre...]
    all_to_all x1, waiting for transfers between devices: 0.01 us -> 5.6 us  [shards(): lax.all_to_all(copies, 'visit', split_axis=0, concat_axis=0, tiled=True)]
  transfers between devices with their start and end apart: 2 -> 2, of which waited for: 1 -> 1; matrix products, arithmetic and copies ran while one was open for 15% -> 49% of each run, Pallas kernels for 0% -> 0%
where the time goes in v3:
time: 229 us; the launch traced here: 227 us
  local copies, waits for them, and re-layouts  115 us (50%)
  blocking collectives  60.3 us (26%)
  between operations  16.8 us (7%)
  matrix products  11.7 us (5%)
  other arithmetic  9.64 us (4%)
  starting transfers between devices  7.91 us (3%)
  waiting for transfers between devices  5.6 us (2%)
    all_to_all x1, blocking collectives, shards(): lax.all_to_all(stacked, 'visit', split_axis=0, concat_axis=0, tiled=True)  55.3 us
    slice x1, local copies, waits for them, and re-layouts, psf_match(): banded_all[row_block * blocks + col_block]  46.7 us
    unnamed x80, local copies, waits for them, and re-layouts  33.3 us
    dot_general x16, local copies, waits for them, and re-layouts, psf_match(): jnp.dot(cols_window, banded_all[row_block * blocks + col_block], preferre...  30.4 us
    all_to_all x1, waiting for transfers between devices, shards(): lax.all_to_all(copies, 'visit', split_axis=0, concat_axis=0, tiled=True)  5.6 us
    dot_general x16, matrix products, psf_match(): jnp.dot(cols_window, banded_all[row_block * blocks + col_block], preferre...  5.06 us
    unnamed x1, blocking collectives  4.97 us
  transfers between devices with their start and end apart: 2, of which 1 were waited for; matrix products, arithmetic and copies ran while one was open for 49% of the time, Pallas kernels for 0%

profile of v3, /device:TPU:0, one launch (start us, length us, event | category | flops | bytes accessed | tf_op | source)
XLA Modules:
  0.0 227.3 jit_solution(4613131695956559904)
XLA Ops:
  0.6 1.8 maximum_bitcast_fusion
  2.7 55.3 %all_to_all.15 = bf16[8,64,2048]{2,1,0:T(8,128)(2,1)S(1)} all-to-all(bf16[8,64,2048]{2,1,0:T(8,128)(2,1)S(1)} %bitcast.262), channel_id=1, replica_groups=mesh['visit'=8,'sky'=4] {'visit'}, dimensions={0} | all-to-all | bytes 4194304 | tf_op jit(solution)/shard_map/all_to_all | solution.py:89
  58.4 1.3 fusion.23
  59.8 1.3 fusion.24
  61.1 1.3 fusion.25
  62.5 1.1 broadcast_in_dim.2
  63.6 3.6 %all-to-all-start.1 = ((f32[8,16,2048]{2,1,0:T(8,128)}), f32[8,16,2048]{2,1,0:T(8,128)S(1)}, u32[]{:S(2)}, u32[]{:S(2)}) async-start(f32[8,16,2048]{2,1,0:T(8,128)} %broadcast_in_dim.2), calls=%async_computation.1 | async-start | bytes 2097152 | tf_op jit(solution)/shard_map/all_to_all | solution.py:94
  68.4 0.7 bitcast_dynamic-update-slice_fusion
  69.1 5.0 %all-reduce.1 = s32[4]{0:T(128)S(1)} all-reduce(s32[4]{0:T(128)S(1)} %bitcast_dynamic-update-slice_fusion), channel_id=2, replica_groups=mesh['visit'=8,'sky'=4] {'sky'}, use_global_device_ids=true, to_apply=%add.1 | all-reduce | flops 4 | bytes 32
  74.1 0.7 fusion.135
  82.8 4.4 %convert_bitcast_fusion = bf16[16,138,11,128]{3,0,2,1:T(8,128)(2,1)} fusion(s32[138,128]{1,0:T(8,128)S(1)} %iota_subtract_fusion, bf16[16,11,11]{2,1,0:T(8,128)(2,1)S(1)} %reshape.203), kind=kOutput, calls=%fused_computation | convolution fusion | flops 71698176 | bytes 6292256 | tf_op jit(solution)/shard_map/kab,bcl->kcal/dot_general | solution.py:44
  87.2 5.6 %all-to-all-done.1 = f32[8,16,2048]{2,1,0:T(8,128)S(1)} async-done(((f32[8,16,2048]{2,1,0:T(8,128)}), f32[8,16,2048]{2,1,0:T(8,128)S(1)}, u32[]{:S(2)}, u32[]{:S(2)}) %all-to-all-start.1) | async-done | bytes 1048608 | tf_op jit(solution)/shard_map/all_to_all | solution.py:94
  93.1 0.9 pad_maximum_fusion
  94.0 4.3 %all-to-all-start.2 = ((bf16[4,128,512]{2,1,0:T(8,128)(2,1)}), bf16[4,128,512]{2,1,0:T(8,128)(2,1)}, u32[]{:S(2)}, u32[]{:S(2)}) async-start(bf16[4,128,512]{2,1,0:T(8,128)(2,1)} %pad_maximum_fusion), calls=%async_computation.2 | async-start | bytes 1048576 | tf_op jit(solution)/shard_map/all_to_all | solution.py:104
  98.4 46.7 %slice_reduce_fusion.15 = (bf16[138,11,128]{2,1,0:T(8,128)(2,1)}, bf16[138,11,128]{2,1,0:T(8,128)(2,1)}, bf16[138,11,128]{2,1,0:T(8,128)(2,1)}, bf16[138,11,128]...) fusion(bf16[16,138,11,128]{3,0,2,1:T(8,128)(2,1)} %convert_bitc, ...), kind=kLoop, calls=%fused_computation.56 | loop fusion | bytes 12435456 | tf_op jit(solution)/shard_map/slice | solution.py:59
  145.1 0.6 fusion.134
  150.4 1.2 pad.35
  151.6 0.9 copy.49
  152.5 2.1 dot_general.129
  154.5 1.2 pad.50
  155.7 0.9 copy.64
  156.6 2.1 dot_general.174
  158.6 1.2 pad.49
  159.8 0.9 copy.63
  160.7 2.1 dot_general.171
  162.8 1.2 pad.48
  163.9 0.9 copy.62
  164.8 2.1 dot_general.168
  166.9 1.2 pad.47
  168.0 0.9 copy.61
  168.9 2.1 dot_general.165
  171.0 1.2 pad.46
  172.1 0.9 copy.60
  173.0 2.1 dot_general.162
  175.1 1.2 pad.45
  176.2 0.9 copy.59
  177.1 2.1 dot_general.159
  179.2 1.2 pad.44
  180.3 0.9 copy.58
  181.2 2.1 dot_general.156
  183.3 1.2 pad.43
  184.5 0.9 copy.57
  185.3 2.1 dot_general.153
  187.4 1.2 pad.42
  188.6 0.9 copy.56
  189.4 2.1 dot_general.150
  191.5 1.2 pad.41
  192.7 0.9 copy.55
  193.6 2.1 dot_general.147
  195.6 1.2 pad.40
  196.8 0.9 copy.54
  197.7 2.1 dot_general.144
  199.8 1.2 pad.39
  200.9 0.9 copy.53
  201.8 2.1 dot_general.141
  204.0 0.9 copy.52
  204.9 1.3 dot_general.138
  206.6 1.1 dot_general.132
  207.7 1.1 dot_general.135
  211.2 1.8 dynamic-slice_bitcast_fusion.3
  213.0 2.1 convolution_convert_fusion
  215.5 0.6 copy-done.2
  225.0 1.3 fusion.22
  226.3 1.0 copy.104
  (97 shorter events, 11.4 us)
Async XLA Ops:
  0.6 212.4 %copy-start = (bf16[1,1,512,512]{3,2,1,0:T(8,128)(2,1)S(1)}, bf16[1,1,512,512]{3,2,1,0:T(8,128)(2,1)}, u32[]{:S(2)}) copy-start(bf16[1,1,512,512]{3,2,1,0:T(8,128)(2,1)} %param.15) | copy-start | bytes 1572868
  62.4 5.4 %copy-start.21 = (u32[32]{0:T(128)S(1)}, u32[32]{0:T(128)}, u32[]{:S(2)}) copy-start(u32[32]{0:T(128)} %constant.44) | copy-start | bytes 388
  62.5 17.4 %copy-start.19 = (s32[1,1,4,4]{3,2,1,0:T(4,128)S(1)}, s32[1,1,4,4]{3,2,1,0:T(4,128)}, u32[]{:S(2)}) copy-start(s32[1,1,4,4]{3,2,1,0:T(4,128)} %param.16) | copy-start | bytes 196
  62.5 17.4 %copy-start.20 = (bf16[1,1,16,121]{3,2,1,0:T(8,128)(2,1)S(1)}, bf16[1,1,16,121]{3,2,1,0:T(8,128)(2,1)}, u32[]{:S(2)}) copy-start(bf16[1,1,16,121]{3,2,1,0:T(8,128)(2,1)} %param.17) | copy-start | bytes 11620
  63.6 29.2 %all-to-all-start.1 = ((f32[8,16,2048]{2,1,0:T(8,128)}), f32[8,16,2048]{2,1,0:T(8,128)S(1)}, u32[]{:S(2)}, u32[]{:S(2)}) async-start(f32[8,16,2048]{2,1,0:T(8,128)} %broadcast_in_dim.2), calls=%async_computation.1 | async-start | bytes 2097152 | tf_op jit(solution)/shard_map/all_to_all | solution.py:94
  94.0 117.1 %all-to-all-start.2 = ((bf16[4,128,512]{2,1,0:T(8,128)(2,1)}), bf16[4,128,512]{2,1,0:T(8,128)(2,1)}, u32[]{:S(2)}, u32[]{:S(2)}) async-start(bf16[4,128,512]{2,1,0:T(8,128)(2,1)} %pad_maximum_fusion), calls=%async_computation.2 | async-start | bytes 1048576 | tf_op jit(solution)/shard_map/all_to_all | solution.py:104
  98.4 46.7 %copy-start.18 = (s32[1,1,4]{2,1,0:T(1,128)S(1)}, s32[1,1,4]{2,1,0:T(1,128)}, u32[]{:S(2)}) copy-start(s32[1,1,4]{2,1,0:T(1,128)} %param.12) | copy-start | bytes 52
  213.0 2.1 copy-start.1
  215.1 1.1 copy-start.2
  215.1 1.4 copy-start.3
  216.2 1.1 copy-start.4
  216.6 1.1 copy-start.5
  217.3 1.1 copy-start.6
  217.7 1.1 copy-start.7
  218.4 1.1 copy-start.8
  219.0 1.1 copy-start.9
  219.5 1.1 copy-start.10
  220.1 1.1 copy-start.11
  220.6 1.1 copy-start.12
  221.2 1.1 copy-start.13
  222.3 1.1 copy-start.15
  222.7 1.1 copy-start.14
  223.8 1.0 copy-start.16
  223.8 1.2 copy-start.17

commit v4 on v2

--- a/solution.py
+++ b/solution.py
@@ -35,14 +35,14 @@
         jnp.bfloat16
     )
     tap_rows = jnp.dot(picker, kernel_table, preferred_element_type=jnp.float32)
-    tap_rows = tap_rows.reshape(blocks, blocks, KSIZE, KSIZE)
-    source = jnp.arange(window, dtype=jnp.int32)[:, None]
-    target = jnp.arange(CELL, dtype=jnp.int32)[None, :]
+    tap_rows = tap_rows.astype(jnp.bfloat16).reshape(blocks * blocks, KSIZE, KSIZE)
+    target = jnp.arange(CELL, dtype=jnp.int32)[:, None]
+    source = jnp.arange(window, dtype=jnp.int32)[None, :]
     diagonal = (
         (source - target)[None] == jnp.arange(KSIZE, dtype=jnp.int32)[:, None, None]
-    ).astype(jnp.float32)
-    banded_all = jnp.einsum(
-        "xyab,bcl->xyacl", tap_rows, diagonal, precision=lax.Precision.HIGHEST
+    ).astype(jnp.bfloat16)
+    vertical = jnp.einsum(
+        "kab,ais->kbis", tap_rows, diagonal, preferred_element_type=jnp.float32
     ).astype(jnp.bfloat16)
     padded = jnp.pad(blotted, ((half_width, half_width), (half_width, half_width)))
     row_parts = []
@@ -53,15 +53,12 @@
             cols_window = lax.slice_in_dim(
                 rows_window, col_block * CELL, col_block * CELL + window, axis=1
             )
-            horizontal = jnp.einsum(
-                "rc,acl->arl",
-                cols_window,
-                banded_all[row_block, col_block],
-                preferred_element_type=jnp.float32,
-            )
-            summed = horizontal[0, 0:CELL, :]
-            for tap_row in range(1, KSIZE):
-                summed = summed + horizontal[tap_row, tap_row : tap_row + CELL, :]
+            stacked = vertical[row_block * blocks + col_block].reshape(KSIZE * CELL, window)
+            partial = jnp.dot(stacked, cols_window, preferred_element_type=jnp.float32)
+            partial = partial.reshape(KSIZE, CELL, window)
+            summed = partial[0, :, 0:CELL]
+            for tap_col in range(1, KSIZE):
+                summed = summed + partial[tap_col, :, tap_col : tap_col + CELL]
             col_parts.append(summed)
         row_parts.append(jnp.concatenate(col_parts, axis=1))
     return jnp.concatenate(row_parts, axis=0)

time: 130 us -> 152 us (1.17)
  local copies, waits for them, and re-layouts: 15 us -> 38.7 us
  matrix products: 18.1 us -> 14 us
  waiting for transfers between devices: 2.08 us -> 5.41 us
    slice x0 -> x1, local copies, waits for them, and re-layouts: none -> 26.6 us  [psf_match(): vertical[row_block * blocks + col_block].reshape(KSIZE * CELL, window)]
    squeeze x1 -> x0, local copies, waits for them, and re-layouts: 6.52 us -> none  [psf_match(): banded_all[row_block, col_block]]
    all_to_all x1, waiting for transfers between devices: 0.01 us -> 5.41 us  [shards(): lax.all_to_all(copies, 'visit', split_axis=0, concat_axis=0, tiled=True)]
    unnamed x44 -> x51, local copies, waits for them, and re-layouts: 4.64 us -> 8.71 us
    dot_general x17, matrix products: 15.9 us -> 11.9 us  [the longest x16 7.57 us: psf_match(): partial = jnp.dot(stacked, cols_window, preferred_element_type=jnp.float32)]
    all_to_all x1, waiting for transfers between devices: 2.07 us -> 0.01 us  [shards(): lax.all_to_all(windows, 'sky', split_axis=0, concat_axis=0, tiled=True)]
  transfers between devices with their start and end apart: 2 -> 2, of which waited for: 1 -> 1; matrix products, arithmetic and copies ran while one was open for 15% -> 25% of each run, Pallas kernels for 0% -> 0%
where the time goes in v4:
time: 152 us; the launch traced here: 151 us
  blocking collectives  60.3 us (40%)
  local copies, waits for them, and re-layouts  38.7 us (25%)
  between operations  17.1 us (11%)
  matrix products  14 us (9%)
  other arithmetic  8.64 us (6%)
  starting transfers between devices  7.24 us (5%)
  waiting for transfers between devices  5.41 us (4%)
    all_to_all x1, blocking collectives, shards(): lax.all_to_all(stacked, 'visit', split_axis=2, concat_axis=1, tiled=True)  55.3 us
    slice x1, local copies, waits for them, and re-layouts, psf_match(): vertical[row_block * blocks + col_block].reshape(KSIZE * CELL, window)  26.6 us
    unnamed x51, local copies, waits for them, and re-layouts  8.71 us
    dot_general x16, matrix products, psf_match(): partial = jnp.dot(stacked, cols_window, preferred_element_type=jnp.float32)  7.57 us
    all_to_all x1, waiting for transfers between devices, shards(): lax.all_to_all(copies, 'visit', split_axis=0, concat_axis=0, tiled=True)  5.41 us
    unnamed x1, blocking collectives  4.97 us
    dot_general x1, matrix products, psf_match(): jnp.einsum('kab,ais->kbis', tap_rows, diagonal, preferred_element_type=jn...  4.34 us
    reduce_sum x3, other arithmetic, local_coadd(): coadd_field = jnp.sum(cauchy * values, axis=0) / jnp.sum(cauchy, axis=0)  3.96 us
  transfers between devices with their start and end apart: 2, of which 1 were waited for; matrix products, arithmetic and copies ran while one was open for 25% of the time, Pallas kernels for 0%

profile of v4, /device:TPU:0, one launch (start us, length us, event | category | flops | bytes accessed | tf_op | source)
XLA Modules:
  0.0 151.4 jit_solution(11395953809913051559)
XLA Ops:
  0.6 1.8 %pad_maximum_fusion = bf16[2,2,8,16,2048]{4,3,2,1,0:T(8,128)(2,1)S(1)} fusion(bf16[1,2,8,16,2048]{4,3,2,1,0:T(8,128)(2,1)} %bitcast.190, bf16[1,2,8,16,2048]{4,3,2,1,0:T(8,128)(2,1)} %bitcast.191), kind=kLoop, calls=%fused_computation.29 | loop fusion | flops 1048576 | bytes 4194304 | tf_op jit(solution)/shard_map/stack | solution.py:82
  2.4 0.2 copy.72
  2.7 55.3 %all_to_all.25 = bf16[2,2,8,16,2048]{4,3,1,0,2:T(8,128)(2,1)S(1)} all-to-all(bf16[2,2,8,16,2048]{4,3,1,0,2:T(8,128)(2,1)S(1)} %copy.72), channel_id=1, replica_groups=mesh['visit'=8,'sky'=4] {'visit'}, dimensions={2} | all-to-all | bytes 4194304 | tf_op jit(solution)/shard_map/all_to_all | solution.py:85
  58.0 0.4 convert_reduce_fusion
  58.4 1.3 fusion.23
  59.8 1.3 fusion.24
  61.1 1.3 fusion.25
  62.5 1.1 broadcast_in_dim.2
  63.6 3.6 %all-to-all-start.1 = ((f32[8,16,2048]{2,1,0:T(8,128)}), f32[8,16,2048]{2,1,0:T(8,128)S(1)}, u32[]{:S(2)}, u32[]{:S(2)}) async-start(f32[8,16,2048]{2,1,0:T(8,128)} %broadcast_in_dim.2), calls=%async_computation.1 | async-start | bytes 2097152 | tf_op jit(solution)/shard_map/all_to_all | solution.py:89
  67.8 0.6 dynamic-slice
  68.4 0.7 bitcast_dynamic-update-slice_fusion
  69.1 5.0 %all-reduce.1 = s32[4]{0:T(128)S(1)} all-reduce(s32[4]{0:T(128)S(1)} %bitcast_dynamic-update-slice_fusion), channel_id=2, replica_groups=mesh['visit'=8,'sky'=4] {'sky'}, use_global_device_ids=true, to_apply=%add.1 | all-reduce | flops 4 | bytes 32
  74.1 0.7 fusion.150
  79.8 0.1 eq.28
  79.9 0.2 convolution_convert_fusion.3
  80.1 0.1 reshape.179
  80.2 0.2 copy.93
  83.0 4.3 %convolution_convert_fusion = bf16[16,11,128,138]{2,0,3,1:T(8,128)(2,1)} fusion(bf16[16,11,11,1]{1,0,3,2:T(8,128)(2,1)S(1)} %copy.93, s32[128,138]{0,1:T(8,128)S(1)} %iota_subtract_fusion), kind=kOutput, calls=%fused_computation.12 | convolution fusion | flops 71698176 | bytes 6292256 | tf_op jit(solution)/shard_map/kab,ais->kbis/dot_general | solution.py:44
  87.3 5.4 %all-to-all-done.1 = f32[8,16,2048]{2,1,0:T(8,128)S(1)} async-done(((f32[8,16,2048]{2,1,0:T(8,128)}), f32[8,16,2048]{2,1,0:T(8,128)S(1)}, u32[]{:S(2)}, u32[]{:S(2)}) %all-to-all-start.1) | async-done | bytes 1048608 | tf_op jit(solution)/shard_map/all_to_all | solution.py:89
  92.8 0.3 dynamic-slice_bitcast_fusion.7
  93.1 0.9 pad_maximum_fusion.1
  94.0 3.6 %all-to-all-start.2 = ((bf16[4,128,512]{2,1,0:T(8,128)(2,1)}), bf16[4,128,512]{2,1,0:T(8,128)(2,1)S(1)}, u32[]{:S(2)}, u32[]{:S(2)}) async-start(bf16[4,128,512]{2,1,0:T(8,128)(2,1)} %pad_maximum_fusion.1), calls=%async_computation.2 | async-start | bytes 1048576 | tf_op jit(solution)/shard_map/all_to_all | solution.py:99
  97.7 26.6 %fusion.148 = (bf16[1,11,128,138]{2,0,3,1:T(2,128)(2,1)}, bf16[1,11,128,138]{2,0,3,1:T(2,128)(2,1)}, bf16[1,11,128,138]{2,0,3,1:T(2,128)(2,1)}, bf16[1,11,128,13...) fusion(bf16[16,11,128,138]{2,0,3,1:T(8,128)(2,1)} %convolution_, ...), kind=kLoop, calls=%fused_computation.337 | loop fusion | bytes 12435456 | tf_op jit(solution)/shard_map/slice | solution.py:56
  124.3 0.7 fusion.149
  130.2 1.0 copy.73
  131.2 2.1 %copy.91 = bf16[1,1,512,512]{2,3,1,0:T(8,128)(2,1)} copy(bf16[1,1,512,512]{3,2,1,0:T(8,128)(2,1)} %param.19) | data formatting | bytes 1048576 | tf_op args[9]
  135.9 1.9 %convolution_convert_fusion.1 = bf16[512,512]{1,0:T(8,128)(2,1)S(1)} fusion(bf16[128,512]{1,0:T(8,128)(2,1)S(1)} %get-tuple-element.35, bf16[128,512]{1,0:T(8,128)(2,1)S(1)} %get-tuple-element.36, bf16[128,512]{1,0:T(8,128)(2,1)S(1)} %get-tuple-element.37, bf16[128,512]{1,0:T(8,128)(2,1)S(1)} %get-tuple-element.34, ...), kind=kOutput, calls=%fused_computation.30 | convolution fusion | flops 539492352 | bytes 2097152 | tf_op jit(solution)/shard_map/dot_general | solution.py:108
  137.8 1.6 %fusion.77 = f32[11,128,138]{1,2,0:T(8,128)S(1)} fusion(bf16[1,11,128,138]{2,0,3,1:T(2,128)(2,1)} %get-tuple-element.30, bf16[512,512]{1,0:T(8,128)(2,1)S(1)} %convolution_convert_fusion.1), kind=kOutput, calls=%fused_computation.100 | convolution fusion | flops 53627904 | bytes 1690112 | tf_op jit(solution)/shard_map/dot_general | solution.py:57
  139.5 0.1 fusion.127
  139.6 0.4 fusion.74
  140.0 0.1 fusion.126
  140.1 0.4 fusion.71
  140.5 0.1 fusion.125
  140.5 0.1 copy-done.14
  140.7 0.4 fusion.68
  141.1 0.1 fusion.124
  141.1 0.1 copy-done.13
  141.2 0.4 fusion.89
  141.7 0.1 copy-done.12
  141.9 0.4 fusion.86
  142.3 0.1 copy-done.11
  142.4 0.4 fusion.83
  142.9 0.1 copy-done.10
  143.0 0.4 fusion.80
  143.5 0.1 copy-done.9
  143.6 0.4 fusion.53
  144.1 0.1 copy-done.8
  144.2 0.4 fusion.50
  144.7 0.1 copy-done.7
  144.8 0.4 fusion.47
  145.3 0.1 copy-done.6
  145.4 0.4 fusion.44
  145.9 0.1 copy-done.5
  146.0 0.4 fusion.65
  146.5 0.1 copy-done.4
  146.6 0.4 fusion.62
  147.1 0.1 copy-done.3
  147.2 0.4 fusion.59
  147.7 0.4 fusion.56
  148.2 0.5 copy-done.1
  148.7 0.2 copy-done.2
  148.9 0.3 fusion.22
  149.1 1.3 copy.92
  150.4 1.0 copy.211
  (53 shorter events, 1.2 us)
Async XLA Ops:
  0.6 135.3 %copy-start = (bf16[1,1,512,512]{3,2,1,0:T(8,128)(2,1)S(1)}, bf16[1,1,512,512]{3,2,1,0:T(8,128)(2,1)}, u32[]{:S(2)}) copy-start(bf16[1,1,512,512]{3,2,1,0:T(8,128)(2,1)} %param.15) | copy-start | bytes 1572868
  62.4 5.4 %copy-start.21 = (u32[32]{0:T(128)S(1)}, u32[32]{0:T(128)}, u32[]{:S(2)}) copy-start(u32[32]{0:T(128)} %constant.44) | copy-start | bytes 388
  62.5 17.4 %copy-start.19 = (s32[1,1,4,4]{3,2,1,0:T(4,128)S(1)}, s32[1,1,4,4]{3,2,1,0:T(4,128)}, u32[]{:S(2)}) copy-start(s32[1,1,4,4]{3,2,1,0:T(4,128)} %param.16) | copy-start | bytes 196
  62.5 17.4 %copy-start.20 = (bf16[1,1,16,121]{3,2,1,0:T(8,128)(2,1)S(1)}, bf16[1,1,16,121]{3,2,1,0:T(8,128)(2,1)}, u32[]{:S(2)}) copy-start(bf16[1,1,16,121]{3,2,1,0:T(8,128)(2,1)} %param.17) | copy-start | bytes 11620
  63.6 29.2 %all-to-all-start.1 = ((f32[8,16,2048]{2,1,0:T(8,128)}), f32[8,16,2048]{2,1,0:T(8,128)S(1)}, u32[]{:S(2)}, u32[]{:S(2)}) async-start(f32[8,16,2048]{2,1,0:T(8,128)} %broadcast_in_dim.2), calls=%async_computation.1 | async-start | bytes 2097152 | tf_op jit(solution)/shard_map/all_to_all | solution.py:89
  94.0 41.8 %all-to-all-start.2 = ((bf16[4,128,512]{2,1,0:T(8,128)(2,1)}), bf16[4,128,512]{2,1,0:T(8,128)(2,1)S(1)}, u32[]{:S(2)}, u32[]{:S(2)}) async-start(bf16[4,128,512]{2,1,0:T(8,128)(2,1)} %pad_maximum_fusion.1), calls=%async_computation.2 | async-start | bytes 1048576 | tf_op jit(solution)/shard_map/all_to_all | solution.py:99
  97.7 26.6 %copy-start.18 = (s32[1,1,4]{2,1,0:T(1,128)S(1)}, s32[1,1,4]{2,1,0:T(1,128)}, u32[]{:S(2)}) copy-start(s32[1,1,4]{2,1,0:T(1,128)} %param.12) | copy-start | bytes 52
  97.7 32.5 %copy-start.17 = (bf16[1,1,512,512]{3,2,1,0:T(8,128)(2,1)S(1)}, bf16[1,1,512,512]{3,2,1,0:T(8,128)(2,1)}, u32[]{:S(2)}) copy-start(bf16[1,1,512,512]{3,2,1,0:T(8,128)(2,1)} %param.18) | copy-start | bytes 1572868
  137.8 1.8 %copy-start.16 = (bf16[1,11,128,138]{2,0,3,1:T(2,128)(2,1)S(1)}, bf16[1,11,128,138]{2,0,3,1:T(2,128)(2,1)}, u32[]{:S(2)}) copy-start(bf16[1,11,128,138]{2,0,3,1:T(2,128)(2,1)} %get-tuple-element.29) | copy-start | bytes 1165828
  137.8 2.2 %copy-start.15 = (bf16[1,11,128,138]{2,0,3,1:T(2,128)(2,1)S(1)}, bf16[1,11,128,138]{2,0,3,1:T(2,128)(2,1)}, u32[]{:S(2)}) copy-start(bf16[1,11,128,138]{2,0,3,1:T(2,128)(2,1)} %get-tuple-element.28) | copy-start | bytes 1165828
  139.5 1.1 copy-start.14
  140.0 1.2 copy-start.13
  140.7 1.2 copy-start.12
  141.2 1.2 copy-start.11
  141.9 1.2 copy-start.10
  142.4 1.2 copy-start.9
  143.0 1.2 copy-start.8
  143.6 1.2 copy-start.7
  144.2 1.2 copy-start.6
  144.8 1.2 copy-start.5
  145.4 1.2 copy-start.4
  146.0 1.2 copy-start.3
  147.7 1.0 copy-start.1
  147.7 1.2 copy-start.2

commit v5 on v2

--- a/solution.py
+++ b/solution.py
@@ -35,14 +35,14 @@
         jnp.bfloat16
     )
     tap_rows = jnp.dot(picker, kernel_table, preferred_element_type=jnp.float32)
-    tap_rows = tap_rows.reshape(blocks, blocks, KSIZE, KSIZE)
+    tap_rows = tap_rows.astype(jnp.bfloat16).reshape(blocks, blocks, KSIZE, KSIZE)
     source = jnp.arange(window, dtype=jnp.int32)[:, None]
     target = jnp.arange(CELL, dtype=jnp.int32)[None, :]
     diagonal = (
         (source - target)[None] == jnp.arange(KSIZE, dtype=jnp.int32)[:, None, None]
-    ).astype(jnp.float32)
+    ).astype(jnp.bfloat16)
     banded_all = jnp.einsum(
-        "xyab,bcl->xyacl", tap_rows, diagonal, precision=lax.Precision.HIGHEST
+        "xyab,bcl->xyacl", tap_rows, diagonal, preferred_element_type=jnp.float32
     ).astype(jnp.bfloat16)
     padded = jnp.pad(blotted, ((half_width, half_width), (half_width, half_width)))
     row_parts = []

time: 130 us -> 126 us (0.969)
  matrix products: 18.1 us -> 14.5 us
    dot_general x1, matrix products: 9.57 us -> 5.99 us  [psf_match(): jnp.einsum('xyab,bcl->xyacl', tap_rows, diagonal, preferred_element_type=...]
  transfers between devices with their start and end apart: 2 -> 2, of which waited for: 1 -> 1; matrix products, arithmetic and copies ran while one was open for 15% -> 12% of each run, Pallas kernels for 0% -> 0%
where the time goes in v5:
time: 126 us
  blocking collectives  60.3 us (48%)
  between operations  16.9 us (13%)
  local copies, waits for them, and re-layouts  15 us (12%)
  matrix products  14.5 us (12%)
  other arithmetic  9.59 us (8%)
  starting transfers between devices  7.24 us (6%)
  waiting for transfers between devices  2.08 us (2%)
    all_to_all x1, blocking collectives, shards(): lax.all_to_all(stacked, 'visit', split_axis=2, concat_axis=1, tiled=True)  55.3 us
    squeeze x1, local copies, waits for them, and re-layouts, psf_match(): banded_all[row_block, col_block]  6.52 us
    dot_general x16, matrix products, psf_match(): jnp.einsum('rc,acl->arl', cols_window, banded_all[row_block, col_block],...  6.3 us
    dot_general x1, matrix products, psf_match(): jnp.einsum('xyab,bcl->xyacl', tap_rows, diagonal, preferred_element_type=...  5.99 us
    unnamed x1, blocking collectives  4.97 us
    unnamed x44, local copies, waits for them, and re-layouts  4.64 us
    reduce_sum x3, other arithmetic, local_coadd(): coadd_field = jnp.sum(cauchy * values, axis=0) / jnp.sum(cauchy, axis=0)  3.96 us
    all_to_all x1, starting transfers between devices, shards(): lax.all_to_all(windows, 'sky', split_axis=0, concat_axis=0, tiled=True)  3.65 us
  transfers between devices with their start and end apart: 2, of which 1 were waited for; matrix products, arithmetic and copies ran while one was open for 12% of the time, Pallas kernels for 0%

profile of v5, /device:TPU:0, one launch (start us, length us, event | category | flops | bytes accessed | tf_op | source)
XLA Modules:
  0.0 125.5 jit_solution(1441015139237149059)
XLA Ops:
  0.6 1.8 %pad_maximum_fusion = bf16[2,2,8,16,2048]{4,3,2,1,0:T(8,128)(2,1)S(1)} fusion(bf16[1,2,8,16,2048]{4,3,2,1,0:T(8,128)(2,1)} %bitcast.209, bf16[1,2,8,16,2048]{4,3,2,1,0:T(8,128)(2,1)} %bitcast.210), kind=kLoop, calls=%fused_computation.29 | loop fusion | flops 1048576 | bytes 4194304 | tf_op jit(solution)/shard_map/stack | solution.py:85
  2.4 0.2 copy.60
  2.7 55.3 %all_to_all.25 = bf16[2,2,8,16,2048]{4,3,1,0,2:T(8,128)(2,1)S(1)} all-to-all(bf16[2,2,8,16,2048]{4,3,1,0,2:T(8,128)(2,1)S(1)} %copy.60), channel_id=1, replica_groups=mesh['visit'=8,'sky'=4] {'visit'}, dimensions={2} | all-to-all | bytes 4194304 | tf_op jit(solution)/shard_map/all_to_all | solution.py:88
  58.0 0.4 convert_reduce_fusion
  58.4 1.3 %fusion.23 = (f32[16,2048]{1,0:T(8,128)S(1)}, f32[16,2048]{1,0:T(8,128)S(1)}) fusion(f32[16,2048]{1,0:T(8,128)S(1)} %div.62, bf16[2,8,2,1,16,2048]{5,4,2,0,1,3:T(8,128)(2,1)S(1)} %bitcast.205), kind=kLoop, calls=%fused_computation.69 | loop fusion | flops 5701632 | bytes 2490368 | tf_op jit(solution)/shard_map/reduce_sum | solution.py:25
  59.8 1.3 %fusion.24 = (f32[16,2048]{1,0:T(8,128)S(1)}, f32[16,2048]{1,0:T(8,128)S(1)}) fusion(f32[16,2048]{1,0:T(8,128)S(1)} %div.65, bf16[2,8,2,1,16,2048]{5,4,2,0,1,3:T(8,128)(2,1)S(1)} %bitcast.206), kind=kLoop, calls=%fused_computation.70 | loop fusion | flops 5701632 | bytes 2490368 | tf_op jit(solution)/shard_map/reduce_sum | solution.py:25
  61.1 1.3 %fusion.25 = (f32[16,2048]{1,0:T(8,128)S(1)}, f32[16,2048]{1,0:T(8,128)S(1)}) fusion(f32[16,2048]{1,0:T(8,128)S(1)} %div.68, bf16[2,8,2,1,16,2048]{5,4,2,0,1,3:T(8,128)(2,1)S(1)} %bitcast.207), kind=kLoop, calls=%fused_computation.71 | loop fusion | flops 5701632 | bytes 2490368 | tf_op jit(solution)/shard_map/reduce_sum | solution.py:25
  62.5 1.1 broadcast_in_dim.2
  63.6 3.6 %all-to-all-start.1 = ((f32[8,16,2048]{2,1,0:T(8,128)}), f32[8,16,2048]{2,1,0:T(8,128)S(1)}, u32[]{:S(2)}, u32[]{:S(2)}) async-start(f32[8,16,2048]{2,1,0:T(8,128)} %broadcast_in_dim.2), calls=%async_computation.1 | async-start | bytes 2097152 | tf_op jit(solution)/shard_map/all_to_all | solution.py:92
  67.9 0.6 dynamic-slice
  68.4 0.7 bitcast_dynamic-update-slice_fusion
  69.1 5.0 %all-reduce.1 = s32[4]{0:T(128)S(1)} all-reduce(s32[4]{0:T(128)S(1)} %bitcast_dynamic-update-slice_fusion), channel_id=2, replica_groups=mesh['visit'=8,'sky'=4] {'sky'}, use_global_device_ids=true, to_apply=%add.1 | all-reduce | flops 4 | bytes 32
  74.1 0.7 fusion.118
  79.9 0.6 fusion.117
  85.5 0.1 eq.28
  85.6 0.2 convolution_convert_fusion.3
  85.7 0.1 reshape.250
  90.9 6.0 %convolution_convert_fusion = bf16[4,4,11,138,128]{4,2,3,1,0:T(8,128)(2,1)} fusion(s32[138,128]{1,0:T(8,128)S(1)} %iota_subtract_fusion, bf16[4,4,11,11,1]{3,2,1,0,4:T(8,128)(2,1)S(1)} %reshape.250), kind=kOutput, calls=%fused_computation | convolution fusion | flops 71698176 | bytes 6292256 | tf_op jit(solution)/shard_map/xyab,bcl->xyacl/dot_general | solution.py:44
  97.0 0.3 dynamic-slice_bitcast_fusion.7
  97.3 0.9 pad_maximum_fusion.1
  98.1 3.6 %all-to-all-start.2 = ((bf16[4,128,512]{2,1,0:T(8,128)(2,1)}), bf16[4,128,512]{2,1,0:T(8,128)(2,1)S(1)}, u32[]{:S(2)}, u32[]{:S(2)}) async-start(bf16[4,128,512]{2,1,0:T(8,128)(2,1)} %pad_maximum_fusion.1), calls=%async_computation.2 | async-start | bytes 1048576 | tf_op jit(solution)/shard_map/all_to_all | solution.py:102
  101.8 6.5 %slice_bitcast_fusion.15 = (bf16[11,138,128]{2,0,1:T(8,128)(2,1)}, bf16[11,138,128]{2,0,1:T(8,128)(2,1)}, bf16[11,138,128]{2,0,1:T(8,128)(2,1)}, bf16[11,138,128...) fusion(bf16[4,4,11,138,128]{4,2,3,1,0:T(8,128)(2,1)} %convoluti, ...), kind=kLoop, calls=%fused_computation.87 | loop fusion | bytes 12435456 | tf_op jit(solution)/shard_map/squeeze | solution.py:59
  108.3 2.1 %all-to-all-done.2 = bf16[4,128,512]{2,1,0:T(8,128)(2,1)S(1)} async-done(((bf16[4,128,512]{2,1,0:T(8,128)(2,1)}), bf16[4,128,512]{2,1,0:T(8,128)(2,1)S(1)}, u32[]{:S(2)}, u32[]{:S(2)}) %all-to-all-start.2) | async-done | bytes 524320 | tf_op jit(solution)/shard_map/all_to_all | solution.py:102
  110.4 0.7 dynamic-slice_bitcast_fusion.3
  111.1 2.0 %convolution_convert_fusion.1 = bf16[512,512]{1,0:T(8,128)(2,1)S(1)} fusion(bf16[128,512]{1,0:T(8,128)(2,1)S(1)} %get-tuple-element.27, bf16[128,512]{1,0:T(8,128)(2,1)} %get-tuple-element.28, bf16[128,512]{1,0:T(8,128)(2,1)} %get-tuple-element.29, bf16[128,512]{1,0:T(8,128)(2,1)S(1)} %get-tuple-element.26, bf16[1,1,512,512]{3,2,1,0:T(8,128)(2,1)S(1)} %copy-done, ...), kind=kOutput, calls=%fused_computation.46 | convolution fusion | flops 539492352 | bytes 2097152 | tf_op jit(solution)/shard_map/dot_general | solution.py:111
  113.2 1.5 %convolution_bitcast_fusion.15 = f32[11,138,128]{2,1,0:T(8,128)S(1)} fusion(bf16[11,138,128]{2,0,1:T(8,128)(2,1)} %get-tuple-element.10, bf16[512,512]{1,0:T(8,128)(2,1)S(1)} %convolution_convert_fusion.1), kind=kOutput, calls=%fused_computation.45 | convolution fusion | flops 53627904 | bytes 1690112 | tf_op jit(solution)/shard_map/rc,acl->arl/dot_general | solution.py:56
  114.7 0.1 fusion.99
  114.8 0.3 convolution_bitcast_fusion
  115.1 0.1 fusion.84
  115.2 0.3 convolution_bitcast_fusion.1
  115.5 0.1 fusion.85
  115.6 0.2 copy-done.11
  115.8 0.3 convolution_bitcast_fusion.2
  116.1 0.1 fusion.86
  116.3 0.3 convolution_bitcast_fusion.3
  116.6 0.1 fusion.87
  116.7 0.2 copy-done.9
  116.9 0.3 convolution_bitcast_fusion.4
  117.2 0.1 fusion.88
  117.4 0.3 convolution_bitcast_fusion.5
  117.7 0.1 fusion.89
  117.8 0.2 copy-done.7
  118.0 0.3 convolution_bitcast_fusion.6
  118.3 0.1 fusion.90
  118.4 0.3 convolution_bitcast_fusion.7
  118.8 0.1 fusion.91
  118.8 0.3 copy-done.5
  119.1 0.3 convolution_bitcast_fusion.8
  119.4 0.1 fusion.92
  119.5 0.3 convolution_bitcast_fusion.9
  119.8 0.1 fusion.93
  119.9 0.3 copy-done.3
  120.2 0.3 convolution_bitcast_fusion.10
  120.5 0.1 fusion.94
  120.6 0.3 convolution_bitcast_fusion.11
  120.9 0.1 fusion.95
  121.0 0.3 copy-done.1
  121.3 0.3 convolution_bitcast_fusion.12
  121.7 0.3 convolution_bitcast_fusion.13
  122.1 0.3 convolution_bitcast_fusion.14
  122.6 0.5 copy-done.14
  123.1 0.2 copy-done.15
  123.3 1.3 %fusion.22 = f32[1,1,512,512]{3,2,1,0:T(8,128)} fusion(f32[1,1,128,512]{3,2,1,0:T(8,128)S(1)} %get-tuple-element.45, f32[1,1,128,512]{3,2,1,0:T(8,128)S(1)} %get-tuple-element.44, f32[1,1,128,512]{3,2,1,0:T(8,128)S(1)} %get-tuple-element.43, f32[1,1,128,512]{3,2,1,0:T(8,128)S(1)} %get-tuple-element.42, bf16[1,1,512,512]{3,2,1,0:T(8,128)(2,1)S(1)} %copy-done.14, ...), kind=kLoop, calls=%fused_computation.56 | loop fusion | flops 2883584 | bytes 3145728 | tf_op jit(solution)/shard_map/div | solution.py:120
  124.6 1.0 copy.114
  (45 shorter events, 0.7 us)
Async XLA Ops:
  0.6 110.5 %copy-start = (bf16[1,1,512,512]{3,2,1,0:T(8,128)(2,1)S(1)}, bf16[1,1,512,512]{3,2,1,0:T(8,128)(2,1)}, u32[]{:S(2)}) copy-start(bf16[1,1,512,512]{3,2,1,0:T(8,128)(2,1)} %param.15) | copy-start | bytes 1572868
  62.4 5.4 %copy-start.19 = (u32[32]{0:T(128)S(1)}, u32[32]{0:T(128)}, u32[]{:S(2)}) copy-start(u32[32]{0:T(128)} %constant.44) | copy-start | bytes 388
  62.5 17.5 %copy-start.16 = (s32[1,1,4]{2,1,0:T(1,128)S(1)}, s32[1,1,4]{2,1,0:T(1,128)}, u32[]{:S(2)}) copy-start(s32[1,1,4]{2,1,0:T(1,128)} %param.12) | copy-start | bytes 52
  62.5 23.0 %copy-start.17 = (s32[1,1,4,4]{3,2,1,0:T(4,128)S(1)}, s32[1,1,4,4]{3,2,1,0:T(4,128)}, u32[]{:S(2)}) copy-start(s32[1,1,4,4]{3,2,1,0:T(4,128)} %param.16) | copy-start | bytes 196
  62.5 23.1 %copy-start.18 = (bf16[1,1,16,121]{3,2,1,0:T(8,128)(2,1)S(1)}, bf16[1,1,16,121]{3,2,1,0:T(8,128)(2,1)}, u32[]{:S(2)}) copy-start(bf16[1,1,16,121]{3,2,1,0:T(8,128)(2,1)} %param.17) | copy-start | bytes 11620
  63.6 33.3 %all-to-all-start.1 = ((f32[8,16,2048]{2,1,0:T(8,128)}), f32[8,16,2048]{2,1,0:T(8,128)S(1)}, u32[]{:S(2)}, u32[]{:S(2)}) async-start(f32[8,16,2048]{2,1,0:T(8,128)} %broadcast_in_dim.2), calls=%async_computation.1 | async-start | bytes 2097152 | tf_op jit(solution)/shard_map/all_to_all | solution.py:92
  98.1 12.3 %all-to-all-start.2 = ((bf16[4,128,512]{2,1,0:T(8,128)(2,1)}), bf16[4,128,512]{2,1,0:T(8,128)(2,1)S(1)}, u32[]{:S(2)}, u32[]{:S(2)}) async-start(bf16[4,128,512]{2,1,0:T(8,128)(2,1)} %pad_maximum_fusion.1), calls=%async_computation.2 | async-start | bytes 1048576 | tf_op jit(solution)/shard_map/all_to_all | solution.py:102
  113.2 1.6 %copy-start.13 = (bf16[11,138,128]{2,0,1:T(8,128)(2,1)S(1)}, bf16[11,138,128]{2,0,1:T(8,128)(2,1)}, u32[]{:S(2)}) copy-start(bf16[11,138,128]{2,0,1:T(8,128)(2,1)} %get-tuple-element.11) | copy-start | bytes 1165828
  113.2 2.0 %copy-start.12 = (bf16[11,138,128]{2,0,1:T(8,128)(2,1)S(1)}, bf16[11,138,128]{2,0,1:T(8,128)(2,1)}, u32[]{:S(2)}) copy-start(bf16[11,138,128]{2,0,1:T(8,128)(2,1)} %get-tuple-element.12) | copy-start | bytes 1165828
  114.7 1.1 copy-start.11
  115.2 1.1 copy-start.10
  115.8 1.1 copy-start.9
  116.3 1.1 copy-start.8
  116.9 1.1 copy-start.7
  117.3 1.1 copy-start.6
  118.0 1.1 copy-start.5
  118.4 1.1 copy-start.4
  119.1 1.1 copy-start.3
  119.5 1.1 copy-start.2
  120.2 1.1 copy-start.1
  122.1 1.0 copy-start.14
  122.1 1.2 copy-start.15

commit v6 on v5

--- a/solution.py
+++ b/solution.py
@@ -83,6 +83,10 @@
     n_sky = lax.axis_size("sky")
     local_visits, strip_rows, sky_w = warped.shape
     stacked = jnp.stack([warped, inv_var], axis=0)
+    all_starts = lax.all_gather(col_start[0], "sky", axis=0, tiled=True)
+    peer_starts = tuple(all_starts[peer] for peer in range(n_sky))
+    strip_ids = tuple(intersection[0, 0, slot] for slot in range(NOV))
+    stacked, peer_starts, strip_ids = lax.optimization_barrier((stacked, peer_starts, strip_ids))
     chunk = strip_rows // n_visit
     stacked = stacked.reshape(2, local_visits, n_visit, chunk, sky_w)
     gathered = lax.all_to_all(stacked, "visit", split_axis=2, concat_axis=1, tiled=True)
@@ -93,16 +97,13 @@
     coadd_field = coadd_field.reshape(n_visit * chunk, sky_w)
     coadd_low = coadd_field.astype(jnp.bfloat16)
 
-    start_col = col_start[0, 0]
-    all_starts = lax.all_gather(col_start[0], "sky", axis=0, tiled=True)
     windows = jnp.stack(
-        [lax.dynamic_slice_in_dim(coadd_low, all_starts[peer], TILE, 1) for peer in range(n_sky)],
+        [lax.dynamic_slice_in_dim(coadd_low, peer_starts[peer], TILE, 1) for peer in range(n_sky)],
         axis=0,
     )
     strips_here = lax.all_to_all(windows, "sky", split_axis=0, concat_axis=0, tiled=True)
-    strips = intersection[0, 0]
     footprint = jnp.concatenate(
-        [lax.dynamic_index_in_dim(strips_here, strips[slot], 0, keepdims=False) for slot in range(NOV)],
+        [lax.dynamic_index_in_dim(strips_here, strip_ids[slot], 0, keepdims=False) for slot in range(NOV)],
         axis=0,
     )
     projected = jnp.dot(row_interp[0, 0], footprint, preferred_element_type=jnp.float32).astype(

time: 126 us -> 131 us (1.040)
  waiting for transfers between devices: 2.08 us -> 5.84 us
  local copies, waits for them, and re-layouts: 15 us -> 16.5 us
    all_to_all x1, waiting for transfers between devices: 0.01 us -> 3.79 us  [shards(): lax.all_to_all(copies, 'visit', split_axis=0, concat_axis=0, tiled=True)]
    all_to_all x1, blocking collectives: 55.3 us -> 53.3 us  [shards(): lax.all_to_all(stacked, 'visit', split_axis=2, concat_axis=1, tiled=True)]
    unnamed x1, blocking collectives: 4.97 us -> 6.44 us
    unnamed x44 -> x40, local copies, waits for them, and re-layouts: 4.64 us -> 5.29 us
  transfers between devices with their start and end apart: 2 -> 2, of which waited for: 1 -> 2; matrix products, arithmetic and copies ran while one was open for 12% -> 10% of each run, Pallas kernels for 0% -> 0%
where the time goes in v6:
time: 131 us; the launch traced here: 130 us
  blocking collectives  59.7 us (46%)
  between operations  17.1 us (13%)
  local copies, waits for them, and re-layouts  16.5 us (13%)
  matrix products  14.5 us (11%)
  other arithmetic  9.57 us (7%)
  starting transfers between devices  7.21 us (6%)
  waiting for transfers between devices  5.84 us (4%)
    all_to_all x1, blocking collectives, shards(): lax.all_to_all(stacked, 'visit', split_axis=2, concat_axis=1, tiled=True)  53.3 us
    squeeze x1, local copies, waits for them, and re-layouts, psf_match(): banded_all[row_block, col_block]  6.54 us
    unnamed x1, blocking collectives  6.44 us
    dot_general x16, matrix products, psf_match(): jnp.einsum('rc,acl->arl', cols_window, banded_all[row_block, col_block],...  6.31 us
    dot_general x1, matrix products, psf_match(): jnp.einsum('xyab,bcl->xyacl', tap_rows, diagonal, preferred_element_type=...  5.99 us
    unnamed x40, local copies, waits for them, and re-layouts  5.29 us
    reduce_sum x3, other arithmetic, local_coadd(): coadd_field = jnp.sum(cauchy * values, axis=0) / jnp.sum(cauchy, axis=0)  3.96 us
    all_to_all x1, waiting for transfers between devices, shards(): lax.all_to_all(copies, 'visit', split_axis=0, concat_axis=0, tiled=True)  3.79 us
  transfers between devices with their start and end apart: 2, of which 2 were waited for; matrix products, arithmetic and copies ran while one was open for 10% of the time, Pallas kernels for 0%

profile of v6, /device:TPU:0, one launch (start us, length us, event | category | flops | bytes accessed | tf_op | source)
XLA Modules:
  0.0 130.4 jit_solution(17344391547304786158)
XLA Ops:
  1.4 1.2 dynamic-slice
  2.6 0.7 bitcast_dynamic-update-slice_fusion
  3.3 6.4 %all-reduce.1 = s32[4]{0:T(128)S(1)} all-reduce(s32[4]{0:T(128)S(1)} %bitcast_dynamic-update-slice_fusion), channel_id=2, replica_groups=mesh['visit'=8,'sky'=4] {'sky'}, use_global_device_ids=true, to_apply=%add.1 | all-reduce | flops 4 | bytes 32
  9.7 0.7 fusion.118
  10.4 1.5 %fusion.117 = (s32[1,1,1]{2,1,0:T(1,128)}, s32[1,1,1]{2,1,0:T(1,128)}, s32[1,1,1]{2,1,0:T(1,128)}, s32[1,1,1]{2,1,0:T(1,128)}) fusion(s32[1,1,4]{2,1,0:T(1,128)} %param.12), kind=kLoop, calls=%fused_computation.338 | loop fusion | bytes 32 | tf_op jit(solution)/shard_map/slice | solution.py:88
  11.8 1.7 %pad_maximum_fusion = bf16[2,2,128,2048]{3,2,1,0:T(8,128)(2,1)S(1)} fusion(bf16[1,2,128,2048]{3,2,1,0:T(8,128)(2,1)} %bitcast.211, bf16[1,2,128,2048]{3,2,1,0:T(8,128)(2,1)} %bitcast.212), kind=kLoop, calls=%fused_computation.29 | loop fusion | flops 1048576 | bytes 4194304 | tf_op jit(solution)/shard_map/stack | solution.py:85
  13.6 0.2 copy.60
  13.8 53.3 %all_to_all.25 = bf16[2,2,8,16,2048]{4,3,1,0,2:T(8,128)(2,1)S(1)} all-to-all(bf16[2,2,8,16,2048]{4,3,1,0,2:T(8,128)(2,1)S(1)} %copy.60), channel_id=1, replica_groups=mesh['visit'=8,'sky'=4] {'visit'}, dimensions={2} | all-to-all | bytes 4194304 | tf_op jit(solution)/shard_map/all_to_all | solution.py:92
  67.1 0.4 convert_reduce_fusion
  67.5 1.3 %fusion.23 = (f32[16,2048]{1,0:T(8,128)S(1)}, f32[16,2048]{1,0:T(8,128)S(1)}) fusion(f32[16,2048]{1,0:T(8,128)S(1)} %div.62, bf16[2,8,2,1,16,2048]{5,4,2,0,1,3:T(8,128)(2,1)S(1)} %bitcast.206), kind=kLoop, calls=%fused_computation.69 | loop fusion | flops 5701632 | bytes 2490368 | tf_op jit(solution)/shard_map/reduce_sum | solution.py:25
  68.8 1.3 %fusion.24 = (f32[16,2048]{1,0:T(8,128)S(1)}, f32[16,2048]{1,0:T(8,128)S(1)}) fusion(f32[16,2048]{1,0:T(8,128)S(1)} %div.65, bf16[2,8,2,1,16,2048]{5,4,2,0,1,3:T(8,128)(2,1)S(1)} %bitcast.207), kind=kLoop, calls=%fused_computation.70 | loop fusion | flops 5701632 | bytes 2490368 | tf_op jit(solution)/shard_map/reduce_sum | solution.py:25
  70.2 1.3 %fusion.25 = (f32[16,2048]{1,0:T(8,128)S(1)}, f32[16,2048]{1,0:T(8,128)S(1)}) fusion(f32[16,2048]{1,0:T(8,128)S(1)} %div.68, bf16[2,8,2,1,16,2048]{5,4,2,0,1,3:T(8,128)(2,1)S(1)} %bitcast.208), kind=kLoop, calls=%fused_computation.71 | loop fusion | flops 5701632 | bytes 2490368 | tf_op jit(solution)/shard_map/reduce_sum | solution.py:25
  71.6 1.1 broadcast_in_dim.2
  72.7 3.6 %all-to-all-start.1 = ((f32[8,16,2048]{2,1,0:T(8,128)}), f32[8,16,2048]{2,1,0:T(8,128)S(1)}, u32[]{:S(2)}, u32[]{:S(2)}) async-start(f32[8,16,2048]{2,1,0:T(8,128)} %broadcast_in_dim.2), calls=%async_computation.1 | async-start | bytes 2097152 | tf_op jit(solution)/shard_map/all_to_all | solution.py:96
  86.4 0.1 eq.28
  86.5 0.2 convolution_convert_fusion.3
  86.7 0.1 reshape.241
  91.9 6.0 %convolution_convert_fusion = bf16[4,4,11,138,128]{4,2,3,1,0:T(8,128)(2,1)} fusion(s32[138,128]{1,0:T(8,128)S(1)} %iota_subtract_fusion, bf16[4,4,11,11,1]{3,2,1,0,4:T(8,128)(2,1)S(1)} %reshape.241), kind=kOutput, calls=%fused_computation | convolution fusion | flops 71698176 | bytes 6292256 | tf_op jit(solution)/shard_map/xyab,bcl->xyacl/dot_general | solution.py:44
  97.9 3.8 %all-to-all-done.1 = f32[8,16,2048]{2,1,0:T(8,128)S(1)} async-done(((f32[8,16,2048]{2,1,0:T(8,128)}), f32[8,16,2048]{2,1,0:T(8,128)S(1)}, u32[]{:S(2)}, u32[]{:S(2)}) %all-to-all-start.1) | async-done | bytes 1048608 | tf_op jit(solution)/shard_map/all_to_all | solution.py:96
  101.7 0.3 dynamic-slice_bitcast_fusion.7
  102.1 0.9 pad_maximum_fusion.1
  103.0 3.6 %all-to-all-start.2 = ((bf16[4,128,512]{2,1,0:T(8,128)(2,1)}), bf16[4,128,512]{2,1,0:T(8,128)(2,1)S(1)}, u32[]{:S(2)}, u32[]{:S(2)}) async-start(bf16[4,128,512]{2,1,0:T(8,128)(2,1)} %pad_maximum_fusion.1), calls=%async_computation.2 | async-start | bytes 1048576 | tf_op jit(solution)/shard_map/all_to_all | solution.py:104
  106.6 6.5 %slice_bitcast_fusion.15 = (bf16[11,138,128]{2,0,1:T(8,128)(2,1)}, bf16[11,138,128]{2,0,1:T(8,128)(2,1)}, bf16[11,138,128]{2,0,1:T(8,128)(2,1)}, bf16[11,138,128...) fusion(bf16[4,4,11,138,128]{4,2,3,1,0:T(8,128)(2,1)} %convoluti, ...), kind=kLoop, calls=%fused_computation.87 | loop fusion | bytes 12435456 | tf_op jit(solution)/shard_map/squeeze | solution.py:59
  113.2 2.1 %all-to-all-done.2 = bf16[4,128,512]{2,1,0:T(8,128)(2,1)S(1)} async-done(((bf16[4,128,512]{2,1,0:T(8,128)(2,1)}), bf16[4,128,512]{2,1,0:T(8,128)(2,1)S(1)}, u32[]{:S(2)}, u32[]{:S(2)}) %all-to-all-start.2) | async-done | bytes 524320 | tf_op jit(solution)/shard_map/all_to_all | solution.py:104
  115.2 0.7 dynamic-slice_bitcast_fusion.3
  116.0 2.0 %convolution_convert_fusion.1 = bf16[512,512]{1,0:T(8,128)(2,1)S(1)} fusion(bf16[128,512]{1,0:T(8,128)(2,1)S(1)} %get-tuple-element.45, bf16[128,512]{1,0:T(8,128)(2,1)} %get-tuple-element.46, bf16[128,512]{1,0:T(8,128)(2,1)} %get-tuple-element.47, bf16[128,512]{1,0:T(8,128)(2,1)S(1)} %get-tuple-element.44, bf16[1,1,512,512]{3,2,1,0:T(8,128)(2,1)S(1)} %copy-done, ...), kind=kOutput, calls=%fused_computation.46 | convolution fusion | flops 539492352 | bytes 2097152 | tf_op jit(solution)/shard_map/dot_general | solution.py:112
  118.0 1.5 %convolution_bitcast_fusion.15 = f32[11,138,128]{2,1,0:T(8,128)S(1)} fusion(bf16[11,138,128]{2,0,1:T(8,128)(2,1)} %get-tuple-element.28, bf16[512,512]{1,0:T(8,128)(2,1)S(1)} %convolution_convert_fusion.1), kind=kOutput, calls=%fused_computation.45 | convolution fusion | flops 53627904 | bytes 1690112 | tf_op jit(solution)/shard_map/rc,acl->arl/dot_general | solution.py:56
  119.5 0.1 fusion.99
  119.6 0.3 convolution_bitcast_fusion
  119.9 0.1 fusion.84
  120.0 0.3 convolution_bitcast_fusion.1
  120.3 0.1 fusion.85
  120.4 0.2 copy-done.11
  120.6 0.3 convolution_bitcast_fusion.2
  121.0 0.1 fusion.86
  121.1 0.3 convolution_bitcast_fusion.3
  121.4 0.1 fusion.87
  121.5 0.2 copy-done.9
  121.7 0.3 convolution_bitcast_fusion.4
  122.1 0.1 fusion.88
  122.2 0.3 convolution_bitcast_fusion.5
  122.5 0.1 fusion.89
  122.6 0.2 copy-done.7
  122.8 0.3 convolution_bitcast_fusion.6
  123.2 0.1 fusion.90
  123.3 0.3 convolution_bitcast_fusion.7
  123.6 0.1 fusion.91
  123.7 0.3 copy-done.5
  123.9 0.3 convolution_bitcast_fusion.8
  124.3 0.1 fusion.92
  124.4 0.3 convolution_bitcast_fusion.9
  124.7 0.1 fusion.93
  124.8 0.3 copy-done.3
  125.0 0.3 convolution_bitcast_fusion.10
  125.4 0.3 convolution_bitcast_fusion.11
  125.8 0.3 copy-done.1
  126.1 0.3 convolution_bitcast_fusion.12
  126.5 0.1 fusion.96
  126.5 0.3 convolution_bitcast_fusion.13
  127.0 0.3 convolution_bitcast_fusion.14
  127.5 0.5 copy-done.14
  128.0 0.2 copy-done.15
  128.1 1.3 fusion.22
  129.4 1.0 copy.114
  (41 shorter events, 0.7 us)
Async XLA Ops:
  0.6 115.3 %copy-start = (bf16[1,1,512,512]{3,2,1,0:T(8,128)(2,1)S(1)}, bf16[1,1,512,512]{3,2,1,0:T(8,128)(2,1)}, u32[]{:S(2)}) copy-start(bf16[1,1,512,512]{3,2,1,0:T(8,128)(2,1)} %param.15) | copy-start | bytes 1572868
  71.5 14.9 %copy-start.16 = (s32[1,1,4,4]{3,2,1,0:T(4,128)S(1)}, s32[1,1,4,4]{3,2,1,0:T(4,128)}, u32[]{:S(2)}) copy-start(s32[1,1,4,4]{3,2,1,0:T(4,128)} %param.16) | copy-start | bytes 196
  71.5 15.0 %copy-start.17 = (bf16[1,1,16,121]{3,2,1,0:T(8,128)(2,1)S(1)}, bf16[1,1,16,121]{3,2,1,0:T(8,128)(2,1)}, u32[]{:S(2)}) copy-start(bf16[1,1,16,121]{3,2,1,0:T(8,128)(2,1)} %param.17) | copy-start | bytes 11620
  72.7 29.0 %all-to-all-start.1 = ((f32[8,16,2048]{2,1,0:T(8,128)}), f32[8,16,2048]{2,1,0:T(8,128)S(1)}, u32[]{:S(2)}, u32[]{:S(2)}) async-start(f32[8,16,2048]{2,1,0:T(8,128)} %broadcast_in_dim.2), calls=%async_computation.1 | async-start | bytes 2097152 | tf_op jit(solution)/shard_map/all_to_all | solution.py:96
  103.0 12.3 %all-to-all-start.2 = ((bf16[4,128,512]{2,1,0:T(8,128)(2,1)}), bf16[4,128,512]{2,1,0:T(8,128)(2,1)S(1)}, u32[]{:S(2)}, u32[]{:S(2)}) async-start(bf16[4,128,512]{2,1,0:T(8,128)(2,1)} %pad_maximum_fusion.1), calls=%async_computation.2 | async-start | bytes 1048576 | tf_op jit(solution)/shard_map/all_to_all | solution.py:104
  118.0 1.6 %copy-start.13 = (bf16[11,138,128]{2,0,1:T(8,128)(2,1)S(1)}, bf16[11,138,128]{2,0,1:T(8,128)(2,1)}, u32[]{:S(2)}) copy-start(bf16[11,138,128]{2,0,1:T(8,128)(2,1)} %get-tuple-element.29) | copy-start | bytes 1165828
  118.0 2.0 %copy-start.12 = (bf16[11,138,128]{2,0,1:T(8,128)(2,1)S(1)}, bf16[11,138,128]{2,0,1:T(8,128)(2,1)}, u32[]{:S(2)}) copy-start(bf16[11,138,128]{2,0,1:T(8,128)(2,1)} %get-tuple-element.30) | copy-start | bytes 1165828
  119.6 1.1 copy-start.11
  120.0 1.1 copy-start.10
  120.6 1.1 copy-start.9
  121.1 1.1 copy-start.8
  121.7 1.1 copy-start.7
  122.1 1.1 copy-start.6
  122.8 1.1 copy-start.5
  123.3 1.1 copy-start.4
  123.9 1.1 copy-start.3
  124.3 1.1 copy-start.2
  125.0 1.1 copy-start.1
  126.9 1.0 copy-start.14
  126.9 1.2 copy-start.15

commit v7 on v5

--- a/solution.py
+++ b/solution.py
@@ -3,7 +3,7 @@
 from jax import lax
 from jax.sharding import PartitionSpec as P
 
-STRIP = 128
+
 NOV = 4
 TILE = 512
 KSIZE = 11
@@ -19,17 +19,15 @@
 def local_coadd(values, weights):
     root_weight = jnp.sqrt(weights)
     coadd_field = jnp.sum(weights * values, axis=0) / jnp.sum(weights, axis=0)
-    for pass_index in range(PASSES):
+    for _ in range(PASSES):
         scaled = (values - coadd_field[None]) * root_weight / CAUCHY
         cauchy = weights / (1.0 + scaled * scaled)
         coadd_field = jnp.sum(cauchy * values, axis=0) / jnp.sum(cauchy, axis=0)
     return coadd_field
 
 
-def psf_match(blotted, cell_grid, kernel_table):
-    tile_side = blotted.shape[1]
-    blocks = tile_side // CELL
-    half_width = KSIZE // 2
+def psf_bands(cell_grid, kernel_table):
+    blocks = TILE // CELL
     window = CELL + KSIZE - 1
     picker = (cell_grid.reshape(-1)[:, None] == jnp.arange(NCELL, dtype=jnp.int32)[None, :]).astype(
         jnp.bfloat16
@@ -44,6 +42,14 @@
     banded_all = jnp.einsum(
         "xyab,bcl->xyacl", tap_rows, diagonal, preferred_element_type=jnp.float32
     ).astype(jnp.bfloat16)
+    return tuple(banded_all[r, c] for r in range(blocks) for c in range(blocks))
+
+
+def psf_match(blotted, bands):
+    tile_side = blotted.shape[1]
+    blocks = tile_side // CELL
+    half_width = KSIZE // 2
+    window = CELL + KSIZE - 1
     padded = jnp.pad(blotted, ((half_width, half_width), (half_width, half_width)))
     row_parts = []
     for row_block in range(blocks):
@@ -56,7 +62,7 @@
             horizontal = jnp.einsum(
                 "rc,acl->arl",
                 cols_window,
-                banded_all[row_block, col_block],
+                bands[row_block * blocks + col_block],
                 preferred_element_type=jnp.float32,
             )
             summed = horizontal[0, 0:CELL, :]
@@ -81,19 +87,18 @@
 ):
     n_visit = lax.axis_size("visit")
     n_sky = lax.axis_size("sky")
-    local_visits, strip_rows, sky_w = warped.shape
-    stacked = jnp.stack([warped, inv_var], axis=0)
+    _, strip_rows, sky_w = warped.shape
     chunk = strip_rows // n_visit
-    stacked = stacked.reshape(2, local_visits, n_visit, chunk, sky_w)
-    gathered = lax.all_to_all(stacked, "visit", split_axis=2, concat_axis=1, tiled=True)
-    gathered = gathered.reshape(2, local_visits * n_visit, chunk, sky_w)
-    row_share = local_coadd(gathered[0].astype(jnp.float32), gathered[1].astype(jnp.float32))
+    values_all = lax.all_to_all(warped, "visit", split_axis=1, concat_axis=0, tiled=True)
+    bands = psf_bands(cell_ids[0, 0], kernels[0, 0])
+    weights_all = lax.all_to_all(inv_var, "visit", split_axis=1, concat_axis=0, tiled=True)
+    values_all, bands = lax.optimization_barrier((values_all, bands))
+    row_share = local_coadd(values_all.astype(jnp.float32), weights_all.astype(jnp.float32))
     copies = jnp.broadcast_to(row_share[None], (n_visit,) + row_share.shape)
     coadd_field = lax.all_to_all(copies, "visit", split_axis=0, concat_axis=0, tiled=True)
     coadd_field = coadd_field.reshape(n_visit * chunk, sky_w)
     coadd_low = coadd_field.astype(jnp.bfloat16)
 
-    start_col = col_start[0, 0]
     all_starts = lax.all_gather(col_start[0], "sky", axis=0, tiled=True)
     windows = jnp.stack(
         [lax.dynamic_slice_in_dim(coadd_low, all_starts[peer], TILE, 1) for peer in range(n_sky)],
@@ -111,7 +116,7 @@
     blotted = jnp.dot(projected, col_interp[0, 0], preferred_element_type=jnp.float32).astype(
         jnp.bfloat16
     )
-    matched = psf_match(blotted, cell_ids[0, 0], kernels[0, 0])
+    matched = psf_match(blotted, bands)
     residual = (
         (science[0, 0].astype(jnp.float32) - matched)
         * inv_sigma[0, 0].astype(jnp.float32)

time: 126 us -> 138 us (1.095)
  blocking collectives: 60.3 us -> 4.97 us
  waiting for transfers between devices: 2.08 us -> 52.5 us
  starting transfers between devices: 7.24 us -> 18.3 us
  local copies, waits for them, and re-layouts: 15 us -> 20.5 us
  matrix products: 14.5 us -> 10.9 us
  other arithmetic: 9.59 us -> 12 us
    all_to_all x1 -> x0, blocking collectives: 55.3 us -> none  [shards(): lax.all_to_all(stacked, 'visit', split_axis=2, concat_axis=1, tiled=True)]
    all_to_all x0 -> x2, waiting for transfers between devices: none -> 41.9 us  [the longest x1 23.7 us: shards(): lax.all_to_all(warped, 'visit', split_axis=1, concat_axis=0, tiled=True)]
    all_to_all x0 -> x2, starting transfers between devices: none -> 11 us  [the longest x1 7.28 us: shards(): lax.all_to_all(warped, 'visit', split_axis=1, concat_axis=0, tiled=True)]
    all_to_all x1, waiting for transfers between devices: 0.01 us -> 10.5 us  [shards(): lax.all_to_all(copies, 'visit', split_axis=0, concat_axis=0, tiled=True)]
    unnamed x44 -> x58, local copies, waits for them, and re-layouts: 4.64 us -> 12.7 us
    dot_general x18, matrix products: 12.5 us -> 8.98 us  [the longest x16 6.3 us: psf_match(): jnp.einsum('rc,acl->arl', cols_window, bands[row_block * blocks + col_blo...]
    squeeze x1, local copies, waits for them, and re-layouts: 6.52 us -> 3.33 us  [psf_bands(): banded_all[r, c]]
    reduce_sum x1 -> x3, other arithmetic: 0.38 us -> 3.01 us  [local_coadd(): coadd_field = jnp.sum(weights * values, axis=0) / jnp.sum(weights, axis=0)]
  transfers between devices with their start and end apart: 2 -> 4, of which waited for: 1 -> 4; matrix products, arithmetic and copies ran while one was open for 12% -> 9% of each run, Pallas kernels for 0% -> 0%
where the time goes in v7:
time: 138 us; the launch traced here: 137 us
  waiting for transfers between devices  52.5 us (38%)
  local copies, waits for them, and re-layouts  20.5 us (15%)
  starting transfers between devices  18.3 us (13%)
  between operations  17.4 us (13%)
  other arithmetic  12 us (9%)
  matrix products  10.9 us (8%)
  blocking collectives  4.97 us (4%)
    all_to_all x1, waiting for transfers between devices, shards(): lax.all_to_all(warped, 'visit', split_axis=1, concat_axis=0, tiled=True)  23.7 us
    all_to_all x1, waiting for transfers between devices, shards(): lax.all_to_all(inv_var, 'visit', split_axis=1, concat_axis=0, tiled=True)  18.2 us
    unnamed x58, local copies, waits for them, and re-layouts  12.7 us
    all_to_all x1, waiting for transfers between devices, shards(): lax.all_to_all(copies, 'visit', split_axis=0, concat_axis=0, tiled=True)  10.5 us
    all_to_all x1, starting transfers between devices, shards(): lax.all_to_all(warped, 'visit', split_axis=1, concat_axis=0, tiled=True)  7.28 us
    dot_general x16, matrix products, psf_match(): jnp.einsum('rc,acl->arl', cols_window, bands[row_block * blocks + col_blo...  6.3 us
    reduce_sum x3, other arithmetic, local_coadd(): coadd_field = jnp.sum(cauchy * values, axis=0) / jnp.sum(cauchy, axis=0)  5.17 us
    unnamed x1, blocking collectives  4.97 us
  transfers between devices with their start and end apart: 4, of which 4 were waited for; matrix products, arithmetic and copies ran while one was open for 9% of the time, Pallas kernels for 0%

profile of v7, /device:TPU:0, one launch (start us, length us, event | category | flops | bytes accessed | tf_op | source)
XLA Modules:
  0.0 136.7 jit_solution(8739915835200353286)
XLA Ops:
  0.7 3.4 %copy.87 = bf16[2,128,2048]{2,0,1:T(2,128)(2,1)} copy(bf16[2,128,2048]{2,1,0:T(8,128)(2,1)} %param.10) | data formatting | bytes 2097152 | tf_op args[0]
  4.0 7.3 %all-to-all-start.1 = ((bf16[2,128,2048]{2,0,1:T(2,128)(2,1)}), bf16[2,128,2048]{2,0,1:T(2,128)(2,1)S(1)}, u32[]{:S(2)}, u32[]{:S(2)}) async-start(bf16[2,128,2048]{2,0,1:T(2,128)(2,1)} %copy.87), calls=%async_computation.1 | async-start | bytes 2097152 | tf_op jit(solution)/shard_map/all_to_all | solution.py:92
  11.4 2.0 %copy.84 = bf16[2,128,2048]{2,0,1:T(2,128)(2,1)} copy(bf16[2,128,2048]{2,1,0:T(8,128)(2,1)S(1)} %copy-done.19) | data formatting | bytes 2097152 | tf_op args[1]
  13.4 23.7 %all-to-all-done.1 = bf16[2,128,2048]{2,0,1:T(2,128)(2,1)S(1)} async-done(((bf16[2,128,2048]{2,0,1:T(2,128)(2,1)}), bf16[2,128,2048]{2,0,1:T(2,128)(2,1)S(1)}, u32[]{:S(2)}, u32[]{:S(2)}) %all-to-all-start.1) | async-done | bytes 1048608 | tf_op jit(solution)/shard_map/all_to_all | solution.py:92
  37.1 3.7 %all-to-all-start = ((bf16[2,128,2048]{2,0,1:T(2,128)(2,1)}), bf16[2,128,2048]{2,0,1:T(2,128)(2,1)S(1)}, u32[]{:S(2)}, u32[]{:S(2)}) async-start(bf16[2,128,2048]{2,0,1:T(2,128)(2,1)} %copy.84), calls=%async_computation | async-start | bytes 2097152 | tf_op jit(solution)/shard_map/all_to_all | solution.py:94
  40.9 0.1 eq.28
  40.9 0.2 convolution_convert_fusion.3
  41.1 0.1 reshape.247
  41.3 2.5 %convolution_convert_fusion = bf16[4,4,11,138,128]{4,2,3,1,0:T(8,128)(2,1)S(1)} fusion(s32[138,128]{1,0:T(8,128)S(1)} %iota_subtract_fusion, bf16[4,4,11,11,1]{3,2,1,0,4:T(8,128)(2,1)S(1)} %reshape.247), kind=kOutput, calls=%fused_computation | convolution fusion | flops 71698176 | bytes 6292256 | tf_op jit(solution)/shard_map/xyab,bcl->xyacl/dot_general | solution.py:42
  43.8 3.3 %slice_bitcast_fusion = (bf16[11,138,128]{2,0,1:T(8,128)(2,1)}, bf16[11,138,128]{2,0,1:T(8,128)(2,1)}, bf16[11,138,128]{2,0,1:T(8,128)(2,1)}, bf16[11,138,128]{2...) fusion(bf16[4,4,11,138,128]{4,2,3,1,0:T(8,128)(2,1)S(1)} %convo, ...), kind=kLoop, calls=%fused_computation.68 | loop fusion | bytes 12435456 | tf_op jit(solution)/shard_map/squeeze | solution.py:45
  47.1 0.3 copy.88
  47.4 1.0 copy.89
  48.5 18.2 %all-to-all-done = bf16[2,128,2048]{2,0,1:T(2,128)(2,1)S(1)} async-done(((bf16[2,128,2048]{2,0,1:T(2,128)(2,1)}), bf16[2,128,2048]{2,0,1:T(2,128)(2,1)S(1)}, u32[]{:S(2)}, u32[]{:S(2)}) %all-to-all-start) | async-done | bytes 1048608 | tf_op jit(solution)/shard_map/all_to_all | solution.py:94
  66.7 0.4 copy_convert_fusion
  67.1 0.6 copy-done.3
  67.7 0.2 copy.86
  67.9 1.0 copy-done.1
  68.9 0.3 fusion
  69.2 0.9 copy-done.4
  70.1 1.4 %fusion.60 = f32[128,2048]{1,0:T(8,128)} fusion(bf16[2,128,2048]{2,0,1:T(2,128)(2,1)S(1)} %copy-done.4), kind=kLoop, calls=%fused_computation.111 | loop fusion | flops 786432 | bytes 2097152 | tf_op jit(solution)/shard_map/reduce_sum | solution.py:21
  71.5 1.3 reduce_sum.82
  72.9 2.6 %fusion.104 = (f32[16,2048]{1,0:T(8,128)S(1)}, f32[16,2048]{1,0:T(8,128)S(1)}) fusion(f32[16,2048]{1,0:T(8,128)S(1)} %div.56, bf16[16,16,2048]{2,1,0:T(8,128)(2,1)} %bitcast.231, f32[8,2,16,2048]{3,2,1,0:T(8,128)S(1)} %copy.86), kind=kLoop, calls=%fused_computation.320 | loop fusion | flops 5177344 | bytes 3538944 | tf_op jit(solution)/shard_map/reduce_sum | solution.py:25
  75.5 1.3 fusion.103
  76.8 1.3 fusion.102
  78.2 1.1 broadcast_in_dim.2
  79.2 3.6 %all-to-all-start.2 = ((f32[8,16,2048]{2,1,0:T(8,128)}), f32[8,16,2048]{2,1,0:T(8,128)S(1)}, u32[]{:S(2)}, u32[]{:S(2)}) async-start(f32[8,16,2048]{2,1,0:T(8,128)} %broadcast_in_dim.2), calls=%async_computation.2 | async-start | bytes 2097152 | tf_op jit(solution)/shard_map/all_to_all | solution.py:98
  83.5 0.6 dynamic-slice
  84.1 0.7 bitcast_dynamic-update-slice_fusion
  84.8 5.0 %all-reduce.1 = s32[4]{0:T(128)S(1)} all-reduce(s32[4]{0:T(128)S(1)} %bitcast_dynamic-update-slice_fusion), channel_id=2, replica_groups=mesh['visit'=8,'sky'=4] {'sky'}, use_global_device_ids=true, to_apply=%add.1 | all-reduce | flops 4 | bytes 32
  89.7 0.7 fusion.122
  98.2 10.5 %all-to-all-done.2 = f32[8,16,2048]{2,1,0:T(8,128)S(1)} async-done(((f32[8,16,2048]{2,1,0:T(8,128)}), f32[8,16,2048]{2,1,0:T(8,128)S(1)}, u32[]{:S(2)}, u32[]{:S(2)}) %all-to-all-start.2) | async-done | bytes 1048608 | tf_op jit(solution)/shard_map/all_to_all | solution.py:98
  108.8 0.3 dynamic-slice_bitcast_fusion.7
  109.1 0.9 pad_maximum_fusion
  110.0 3.7 %all-to-all-start.3 = ((bf16[4,128,512]{2,1,0:T(8,128)(2,1)}), bf16[4,128,512]{2,1,0:T(8,128)(2,1)S(1)}, u32[]{:S(2)}, u32[]{:S(2)}) async-start(bf16[4,128,512]{2,1,0:T(8,128)(2,1)} %pad_maximum_fusion), calls=%async_computation.3 | async-start | bytes 1048576 | tf_op jit(solution)/shard_map/all_to_all | solution.py:107
  113.7 0.7 fusion.121
  122.3 1.9 %convolution_convert_fusion.1 = bf16[512,512]{1,0:T(8,128)(2,1)S(1)} fusion(bf16[128,512]{1,0:T(8,128)(2,1)S(1)} %get-tuple-element.59, bf16[128,512]{1,0:T(8,128)(2,1)S(1)} %get-tuple-element.60, bf16[128,512]{1,0:T(8,128)(2,1)S(1)} %get-tuple-element.61, bf16[128,512]{1,0:T(8,128)(2,1)S(1)} %get-tuple-element.58, ...), kind=kOutput, calls=%fused_computation.44 | convolution fusion | flops 539492352 | bytes 2097152 | tf_op jit(solution)/shard_map/dot_general | solution.py:116
  124.2 1.5 %convolution_bitcast_fusion.11 = f32[11,138,128]{2,1,0:T(8,128)S(1)} fusion(bf16[11,138,128]{2,0,1:T(8,128)(2,1)} %get-tuple-element.24, bf16[512,512]{1,0:T(8,128)(2,1)S(1)} %convolution_convert_fusion.1), kind=kOutput, calls=%fused_computation.39 | convolution fusion | flops 53627904 | bytes 1690112 | tf_op jit(solution)/shard_map/rc,acl->arl/dot_general | solution.py:62
  125.7 0.1 fusion.96
  125.8 0.3 convolution_bitcast_fusion.10
  126.2 0.3 convolution_bitcast_fusion.9
  126.6 0.2 copy-done.16
  126.9 0.3 convolution_bitcast_fusion.8
  127.3 0.3 convolution_bitcast_fusion.15
  127.7 0.2 copy-done.14
  128.0 0.3 convolution_bitcast_fusion.14
  128.4 0.3 convolution_bitcast_fusion.13
  128.8 0.2 copy-done.12
  129.1 0.3 convolution_bitcast_fusion.12
  129.5 0.3 convolution_bitcast_fusion.3
  129.9 0.2 copy-done.10
  130.2 0.3 convolution_bitcast_fusion.2
  130.6 0.3 convolution_bitcast_fusion.1
  131.0 0.2 copy-done.8
  131.3 0.3 convolution_bitcast_fusion
  131.7 0.3 convolution_bitcast_fusion.7
  132.1 0.2 copy-done.6
  132.3 0.3 convolution_bitcast_fusion.6
  132.8 0.3 convolution_bitcast_fusion.5
  133.1 0.1 fusion.90
  133.2 0.3 convolution_bitcast_fusion.4
  133.7 0.5 copy-done.20
  134.3 0.2 copy-done.21
  134.4 1.3 fusion.25
  135.7 1.0 copy.146
  (66 shorter events, 1.7 us)
Async XLA Ops:
  0.6 121.7 %copy-start = (bf16[1,1,512,512]{3,2,1,0:T(8,128)(2,1)S(1)}, bf16[1,1,512,512]{3,2,1,0:T(8,128)(2,1)}, u32[]{:S(2)}) copy-start(bf16[1,1,512,512]{3,2,1,0:T(8,128)(2,1)} %param.15) | copy-start | bytes 1572868
  0.6 10.7 %copy-start.19 = (bf16[2,128,2048]{2,1,0:T(8,128)(2,1)S(1)}, bf16[2,128,2048]{2,1,0:T(8,128)(2,1)}, u32[]{:S(2)}) copy-start(bf16[2,128,2048]{2,1,0:T(8,128)(2,1)} %param.11) | copy-start | bytes 3145732
  4.0 33.0 %all-to-all-start.1 = ((bf16[2,128,2048]{2,0,1:T(2,128)(2,1)}), bf16[2,128,2048]{2,0,1:T(2,128)(2,1)S(1)}, u32[]{:S(2)}, u32[]{:S(2)}) async-start(bf16[2,128,2048]{2,0,1:T(2,128)(2,1)} %copy.87), calls=%async_computation.1 | async-start | bytes 2097152 | tf_op jit(solution)/shard_map/all_to_all | solution.py:92
  11.3 29.5 %copy-start.23 = (s32[1,1,4,4]{3,2,1,0:T(4,128)S(1)}, s32[1,1,4,4]{3,2,1,0:T(4,128)}, u32[]{:S(2)}) copy-start(s32[1,1,4,4]{3,2,1,0:T(4,128)} %param.16) | copy-start | bytes 196
  11.3 29.6 %copy-start.24 = (bf16[1,1,16,121]{3,2,1,0:T(8,128)(2,1)S(1)}, bf16[1,1,16,121]{3,2,1,0:T(8,128)(2,1)}, u32[]{:S(2)}) copy-start(bf16[1,1,16,121]{3,2,1,0:T(8,128)(2,1)} %param.17) | copy-start | bytes 11620
  37.1 29.6 %all-to-all-start = ((bf16[2,128,2048]{2,0,1:T(2,128)(2,1)}), bf16[2,128,2048]{2,0,1:T(2,128)(2,1)S(1)}, u32[]{:S(2)}, u32[]{:S(2)}) async-start(bf16[2,128,2048]{2,0,1:T(2,128)(2,1)} %copy.84), calls=%async_computation | async-start | bytes 2097152 | tf_op jit(solution)/shard_map/all_to_all | solution.py:94
  66.7 1.0 copy-start.3
  67.7 1.2 copy-start.1
  68.9 1.2 copy-start.4
  72.8 2.7 %copy-start.2 = (bf16[8,2,16,2048]{3,2,1,0:T(8,128)(2,1)S(1)}, bf16[8,2,16,2048]{3,2,1,0:T(8,128)(2,1)}, u32[]{:S(2)}) copy-start(bf16[8,2,16,2048]{3,2,1,0:T(8,128)(2,1)} %copy.89) | copy-start | bytes 3145732
  78.1 5.4 %copy-start.25 = (u32[32]{0:T(128)S(1)}, u32[32]{0:T(128)}, u32[]{:S(2)}) copy-start(u32[32]{0:T(128)} %constant.44) | copy-start | bytes 388
  79.2 29.5 %all-to-all-start.2 = ((f32[8,16,2048]{2,1,0:T(8,128)}), f32[8,16,2048]{2,1,0:T(8,128)S(1)}, u32[]{:S(2)}, u32[]{:S(2)}) async-start(f32[8,16,2048]{2,1,0:T(8,128)} %broadcast_in_dim.2), calls=%async_computation.2 | async-start | bytes 2097152 | tf_op jit(solution)/shard_map/all_to_all | solution.py:98
  98.2 15.5 %copy-start.22 = (s32[1,1,4]{2,1,0:T(1,128)S(1)}, s32[1,1,4]{2,1,0:T(1,128)}, u32[]{:S(2)}) copy-start(s32[1,1,4]{2,1,0:T(1,128)} %param.12) | copy-start | bytes 52
  110.0 12.3 %all-to-all-start.3 = ((bf16[4,128,512]{2,1,0:T(8,128)(2,1)}), bf16[4,128,512]{2,1,0:T(8,128)(2,1)S(1)}, u32[]{:S(2)}, u32[]{:S(2)}) async-start(bf16[4,128,512]{2,1,0:T(8,128)(2,1)} %pad_maximum_fusion), calls=%async_computation.3 | async-start | bytes 1048576 | tf_op jit(solution)/shard_map/all_to_all | solution.py:107
  124.2 1.6 %copy-start.18 = (bf16[11,138,128]{2,0,1:T(8,128)(2,1)S(1)}, bf16[11,138,128]{2,0,1:T(8,128)(2,1)}, u32[]{:S(2)}) copy-start(bf16[11,138,128]{2,0,1:T(8,128)(2,1)} %get-tuple-element.25) | copy-start | bytes 1165828
  124.2 2.0 %copy-start.17 = (bf16[11,138,128]{2,0,1:T(8,128)(2,1)S(1)}, bf16[11,138,128]{2,0,1:T(8,128)(2,1)}, u32[]{:S(2)}) copy-start(bf16[11,138,128]{2,0,1:T(8,128)(2,1)} %get-tuple-element.26) | copy-start | bytes 1165828
  125.8 1.1 copy-start.16
  126.2 1.1 copy-start.15
  126.9 1.1 copy-start.14
  127.3 1.1 copy-start.13
  128.0 1.1 copy-start.12
  128.4 1.1 copy-start.11
  129.1 1.1 copy-start.10
  129.5 1.1 copy-start.9
  130.2 1.1 copy-start.8
  130.6 1.1 copy-start.7
  131.2 1.1 copy-start.6
  131.7 1.1 copy-start.5
  133.2 1.0 copy-start.20
  133.2 1.2 copy-start.21

commit v8 on v7

--- a/solution.py
+++ b/solution.py
@@ -26,14 +26,18 @@
     return coadd_field
 
 
-def psf_bands(cell_grid, kernel_table):
+def psf_taps(cell_grid, kernel_table):
     blocks = TILE // CELL
-    window = CELL + KSIZE - 1
     picker = (cell_grid.reshape(-1)[:, None] == jnp.arange(NCELL, dtype=jnp.int32)[None, :]).astype(
         jnp.bfloat16
     )
     tap_rows = jnp.dot(picker, kernel_table, preferred_element_type=jnp.float32)
-    tap_rows = tap_rows.astype(jnp.bfloat16).reshape(blocks, blocks, KSIZE, KSIZE)
+    return tap_rows.astype(jnp.bfloat16).reshape(blocks, blocks, KSIZE, KSIZE)
+
+
+def psf_bands(tap_rows):
+    blocks = TILE // CELL
+    window = CELL + KSIZE - 1
     source = jnp.arange(window, dtype=jnp.int32)[:, None]
     target = jnp.arange(CELL, dtype=jnp.int32)[None, :]
     diagonal = (
@@ -87,15 +91,18 @@
 ):
     n_visit = lax.axis_size("visit")
     n_sky = lax.axis_size("sky")
-    _, strip_rows, sky_w = warped.shape
+    local_visits, strip_rows, sky_w = warped.shape
+    stacked = jnp.stack([warped, inv_var], axis=0)
+    tap_rows = psf_taps(cell_ids[0, 0], kernels[0, 0])
+    stacked, tap_rows = lax.optimization_barrier((stacked, tap_rows))
     chunk = strip_rows // n_visit
-    values_all = lax.all_to_all(warped, "visit", split_axis=1, concat_axis=0, tiled=True)
-    bands = psf_bands(cell_ids[0, 0], kernels[0, 0])
-    weights_all = lax.all_to_all(inv_var, "visit", split_axis=1, concat_axis=0, tiled=True)
-    values_all, bands = lax.optimization_barrier((values_all, bands))
-    row_share = local_coadd(values_all.astype(jnp.float32), weights_all.astype(jnp.float32))
+    stacked = stacked.reshape(2, local_visits, n_visit, chunk, sky_w)
+    gathered = lax.all_to_all(stacked, "visit", split_axis=2, concat_axis=1, tiled=True)
+    gathered = gathered.reshape(2, local_visits * n_visit, chunk, sky_w)
+    row_share = local_coadd(gathered[0].astype(jnp.float32), gathered[1].astype(jnp.float32))
     copies = jnp.broadcast_to(row_share[None], (n_visit,) + row_share.shape)
     coadd_field = lax.all_to_all(copies, "visit", split_axis=0, concat_axis=0, tiled=True)
+    bands = psf_bands(tap_rows)
     coadd_field = coadd_field.reshape(n_visit * chunk, sky_w)
     coadd_low = coadd_field.astype(jnp.bfloat16)
 

time: 138 us -> 128 us (0.928)
  blocking collectives: 4.97 us -> 60.3 us
  waiting for transfers between devices: 52.5 us -> 2.06 us
  starting transfers between devices: 18.3 us -> 7.24 us
  local copies, waits for them, and re-layouts: 20.5 us -> 15.8 us
  matrix products: 10.9 us -> 15.2 us
  other arithmetic: 12 us -> 9.57 us
    all_to_all x0 -> x1, blocking collectives: none -> 55.3 us  [shards(): lax.all_to_all(stacked, 'visit', split_axis=2, concat_axis=1, tiled=True)]
    all_to_all x2 -> x0, waiting for transfers between devices: 41.9 us -> none  [the longest x1 23.7 us: shards(): lax.all_to_all(warped, 'visit', split_axis=1, concat_axis=0, tiled=True)]
    all_to_all x2 -> x0, starting transfers between devices: 11 us -> none  [the longest x1 7.28 us: shards(): lax.all_to_all(warped, 'visit', split_axis=1, concat_axis=0, tiled=True)]
    all_to_all x1, waiting for transfers between devices: 10.5 us -> 0.01 us  [shards(): lax.all_to_all(copies, 'visit', split_axis=0, concat_axis=0, tiled=True)]
    unnamed x58 -> x40, local copies, waits for them, and re-layouts: 12.7 us -> 4.63 us
    dot_general x1, matrix products: 2.49 us -> 5.98 us  [psf_bands(): jnp.einsum('xyab,bcl->xyacl', tap_rows, diagonal, preferred_element_type=...]
    squeeze x1, local copies, waits for them, and re-layouts: 3.33 us -> 6.54 us  [psf_bands(): banded_all[r, c]]
    reduce_sum x3 -> x1, other arithmetic: 3.01 us -> 0.38 us  [local_coadd(): coadd_field = jnp.sum(weights * values, axis=0) / jnp.sum(weights, axis=0)]
  transfers between devices with their start and end apart: 4 -> 2, of which waited for: 4 -> 1; matrix products, arithmetic and copies ran while one was open for 9% -> 12% of each run, Pallas kernels for 0% -> 0%
where the time goes in v8:
time: 128 us; the launch traced here: 127 us
  blocking collectives  60.3 us (47%)
  between operations  17 us (13%)
  local copies, waits for them, and re-layouts  15.8 us (12%)
  matrix products  15.2 us (12%)
  other arithmetic  9.57 us (7%)
  starting transfers between devices  7.24 us (6%)
  waiting for transfers between devices  2.06 us (2%)
    all_to_all x1, blocking collectives, shards(): lax.all_to_all(stacked, 'visit', split_axis=2, concat_axis=1, tiled=True)  55.3 us
    squeeze x1, local copies, waits for them, and re-layouts, psf_bands(): banded_all[r, c]  6.54 us
    dot_general x16, matrix products, psf_match(): jnp.einsum('rc,acl->arl', cols_window, bands[row_block * blocks + col_blo...  6.3 us
    dot_general x1, matrix products, psf_bands(): jnp.einsum('xyab,bcl->xyacl', tap_rows, diagonal, preferred_element_type=...  5.98 us
    unnamed x1, blocking collectives  4.97 us
    unnamed x40, local copies, waits for them, and re-layouts  4.63 us
    reduce_sum x3, other arithmetic, local_coadd(): coadd_field = jnp.sum(cauchy * values, axis=0) / jnp.sum(cauchy, axis=0)  3.96 us
    all_to_all x1, starting transfers between devices, shards(): lax.all_to_all(windows, 'sky', split_axis=0, concat_axis=0, tiled=True)  3.65 us
  transfers between devices with their start and end apart: 2, of which 1 were waited for; matrix products, arithmetic and copies ran while one was open for 12% of the time, Pallas kernels for 0%

profile of v8, /device:TPU:0, one launch (start us, length us, event | category | flops | bytes accessed | tf_op | source)
XLA Modules:
  0.0 127.1 jit_solution(2123147829218668663)
XLA Ops:
  0.6 0.8 eq.28
  1.5 0.9 convolution_convert_fusion.3
  2.3 0.1 reshape.128
  2.4 1.7 %pad_maximum_fusion = bf16[2,2,128,2048]{3,2,1,0:T(8,128)(2,1)S(1)} fusion(bf16[1,2,128,2048]{3,2,1,0:T(8,128)(2,1)} %bitcast.213, bf16[1,2,128,2048]{3,2,1,0:T(8,128)(2,1)} %bitcast.214), kind=kLoop, calls=%fused_computation.29 | loop fusion | flops 1048576 | bytes 4194304 | tf_op jit(solution)/shard_map/stack | solution.py:95
  4.2 0.2 copy.60
  4.4 55.3 %all_to_all.25 = bf16[2,2,8,16,2048]{4,3,1,0,2:T(8,128)(2,1)S(1)} all-to-all(bf16[2,2,8,16,2048]{4,3,1,0,2:T(8,128)(2,1)S(1)} %copy.60), channel_id=1, replica_groups=mesh['visit'=8,'sky'=4] {'visit'}, dimensions={2} | all-to-all | bytes 4194304 | tf_op jit(solution)/shard_map/all_to_all | solution.py:100
  59.7 0.4 convert_reduce_fusion
  60.2 1.3 %fusion.23 = (f32[16,2048]{1,0:T(8,128)S(1)}, f32[16,2048]{1,0:T(8,128)S(1)}) fusion(f32[16,2048]{1,0:T(8,128)S(1)} %div.62, bf16[2,8,2,1,16,2048]{5,4,2,0,1,3:T(8,128)(2,1)S(1)} %bitcast.208), kind=kLoop, calls=%fused_computation.69 | loop fusion | flops 5701632 | bytes 2490368 | tf_op jit(solution)/shard_map/reduce_sum | solution.py:25
  61.5 1.3 %fusion.24 = (f32[16,2048]{1,0:T(8,128)S(1)}, f32[16,2048]{1,0:T(8,128)S(1)}) fusion(f32[16,2048]{1,0:T(8,128)S(1)} %div.65, bf16[2,8,2,1,16,2048]{5,4,2,0,1,3:T(8,128)(2,1)S(1)} %bitcast.209), kind=kLoop, calls=%fused_computation.70 | loop fusion | flops 5701632 | bytes 2490368 | tf_op jit(solution)/shard_map/reduce_sum | solution.py:25
  62.9 1.3 %fusion.25 = (f32[16,2048]{1,0:T(8,128)S(1)}, f32[16,2048]{1,0:T(8,128)S(1)}) fusion(f32[16,2048]{1,0:T(8,128)S(1)} %div.68, bf16[2,8,2,1,16,2048]{5,4,2,0,1,3:T(8,128)(2,1)S(1)} %bitcast.210), kind=kLoop, calls=%fused_computation.71 | loop fusion | flops 5701632 | bytes 2490368 | tf_op jit(solution)/shard_map/reduce_sum | solution.py:25
  64.3 1.1 broadcast_in_dim.2
  65.3 3.6 %all-to-all-start.1 = ((f32[8,16,2048]{2,1,0:T(8,128)}), f32[8,16,2048]{2,1,0:T(8,128)S(1)}, u32[]{:S(2)}, u32[]{:S(2)}) async-start(f32[8,16,2048]{2,1,0:T(8,128)} %broadcast_in_dim.2), calls=%async_computation.1 | async-start | bytes 2097152 | tf_op jit(solution)/shard_map/all_to_all | solution.py:104
  69.6 0.6 dynamic-slice
  70.2 0.7 bitcast_dynamic-update-slice_fusion
  70.9 5.0 %all-reduce.1 = s32[4]{0:T(128)S(1)} all-reduce(s32[4]{0:T(128)S(1)} %bitcast_dynamic-update-slice_fusion), channel_id=2, replica_groups=mesh['visit'=8,'sky'=4] {'sky'}, use_global_device_ids=true, to_apply=%add.1 | all-reduce | flops 4 | bytes 32
  75.8 0.7 fusion.118
  81.7 0.7 fusion.117
  92.5 6.0 %convolution_convert_fusion = bf16[4,4,11,138,128]{4,2,3,1,0:T(8,128)(2,1)} fusion(s32[138,128]{1,0:T(8,128)S(1)} %iota_subtract_fusion, bf16[4,4,11,11]{3,2,1,0:T(8,128)(2,1)S(1)} %reshape.128), kind=kOutput, calls=%fused_computation | convolution fusion | flops 71698176 | bytes 6292256 | tf_op jit(solution)/shard_map/xyab,bcl->xyacl/dot_general | solution.py:46
  98.5 0.3 dynamic-slice_bitcast_fusion.7
  98.8 0.9 pad_maximum_fusion.1
  99.7 3.6 %all-to-all-start.2 = ((bf16[4,128,512]{2,1,0:T(8,128)(2,1)}), bf16[4,128,512]{2,1,0:T(8,128)(2,1)S(1)}, u32[]{:S(2)}, u32[]{:S(2)}) async-start(bf16[4,128,512]{2,1,0:T(8,128)(2,1)} %pad_maximum_fusion.1), calls=%async_computation.2 | async-start | bytes 1048576 | tf_op jit(solution)/shard_map/all_to_all | solution.py:114
  103.4 6.5 %slice_bitcast_fusion.15 = (bf16[11,138,128]{2,0,1:T(8,128)(2,1)}, bf16[11,138,128]{2,0,1:T(8,128)(2,1)}, bf16[11,138,128]{2,0,1:T(8,128)(2,1)}, bf16[11,138,128...) fusion(bf16[4,4,11,138,128]{4,2,3,1,0:T(8,128)(2,1)} %convoluti, ...), kind=kLoop, calls=%fused_computation.87 | loop fusion | bytes 12435456 | tf_op jit(solution)/shard_map/squeeze | solution.py:49
  109.9 2.1 %all-to-all-done.2 = bf16[4,128,512]{2,1,0:T(8,128)(2,1)S(1)} async-done(((bf16[4,128,512]{2,1,0:T(8,128)(2,1)}), bf16[4,128,512]{2,1,0:T(8,128)(2,1)S(1)}, u32[]{:S(2)}, u32[]{:S(2)}) %all-to-all-start.2) | async-done | bytes 524320 | tf_op jit(solution)/shard_map/all_to_all | solution.py:114
  112.0 0.7 dynamic-slice_bitcast_fusion.3
  112.7 2.0 %convolution_convert_fusion.1 = bf16[512,512]{1,0:T(8,128)(2,1)S(1)} fusion(bf16[128,512]{1,0:T(8,128)(2,1)S(1)} %get-tuple-element.31, bf16[128,512]{1,0:T(8,128)(2,1)} %get-tuple-element.32, bf16[128,512]{1,0:T(8,128)(2,1)} %get-tuple-element.33, bf16[128,512]{1,0:T(8,128)(2,1)S(1)} %get-tuple-element.30, bf16[1,1,512,512]{3,2,1,0:T(8,128)(2,1)S(1)} %copy-done, ...), kind=kOutput, calls=%fused_computation.46 | convolution fusion | flops 539492352 | bytes 2097152 | tf_op jit(solution)/shard_map/dot_general | solution.py:123
  114.8 1.5 %convolution_bitcast_fusion.15 = f32[11,138,128]{2,1,0:T(8,128)S(1)} fusion(bf16[11,138,128]{2,0,1:T(8,128)(2,1)} %get-tuple-element.14, bf16[512,512]{1,0:T(8,128)(2,1)S(1)} %convolution_convert_fusion.1), kind=kOutput, calls=%fused_computation.45 | convolution fusion | flops 53627904 | bytes 1690112 | tf_op jit(solution)/shard_map/rc,acl->arl/dot_general | solution.py:66
  116.2 0.1 fusion.99
  116.3 0.3 convolution_bitcast_fusion
  116.7 0.1 fusion.84
  116.8 0.3 convolution_bitcast_fusion.1
  117.1 0.1 fusion.85
  117.2 0.2 copy-done.11
  117.4 0.3 convolution_bitcast_fusion.2
  117.7 0.1 fusion.86
  117.8 0.3 convolution_bitcast_fusion.3
  118.2 0.1 fusion.87
  118.3 0.2 copy-done.9
  118.5 0.3 convolution_bitcast_fusion.4
  118.8 0.1 fusion.88
  118.9 0.3 convolution_bitcast_fusion.5
  119.3 0.1 fusion.89
  119.3 0.2 copy-done.7
  119.6 0.3 convolution_bitcast_fusion.6
  119.9 0.1 fusion.90
  120.0 0.3 convolution_bitcast_fusion.7
  120.3 0.1 fusion.91
  120.4 0.3 copy-done.5
  120.7 0.3 convolution_bitcast_fusion.8
  121.0 0.1 fusion.92
  121.1 0.3 convolution_bitcast_fusion.9
  121.4 0.1 fusion.93
  121.5 0.3 copy-done.3
  121.8 0.3 convolution_bitcast_fusion.10
  122.1 0.1 fusion.94
  122.2 0.3 convolution_bitcast_fusion.11
  122.5 0.1 fusion.95
  122.6 0.3 copy-done.1
  122.9 0.3 convolution_bitcast_fusion.12
  123.3 0.3 convolution_bitcast_fusion.13
  123.7 0.3 convolution_bitcast_fusion.14
  124.2 0.5 copy-done.14
  124.7 0.2 copy-done.15
  124.9 1.3 fusion.22
  126.2 1.0 copy.114
  (41 shorter events, 0.7 us)
Async XLA Ops:
  0.6 112.1 %copy-start = (bf16[1,1,512,512]{3,2,1,0:T(8,128)(2,1)S(1)}, bf16[1,1,512,512]{3,2,1,0:T(8,128)(2,1)}, u32[]{:S(2)}) copy-start(bf16[1,1,512,512]{3,2,1,0:T(8,128)(2,1)} %param.15) | copy-start | bytes 1572868
  64.2 5.4 %copy-start.17 = (u32[32]{0:T(128)S(1)}, u32[32]{0:T(128)}, u32[]{:S(2)}) copy-start(u32[32]{0:T(128)} %constant.44) | copy-start | bytes 388
  64.2 17.4 %copy-start.16 = (s32[1,1,4]{2,1,0:T(1,128)S(1)}, s32[1,1,4]{2,1,0:T(1,128)}, u32[]{:S(2)}) copy-start(s32[1,1,4]{2,1,0:T(1,128)} %param.12) | copy-start | bytes 52
  65.3 33.1 %all-to-all-start.1 = ((f32[8,16,2048]{2,1,0:T(8,128)}), f32[8,16,2048]{2,1,0:T(8,128)S(1)}, u32[]{:S(2)}, u32[]{:S(2)}) async-start(f32[8,16,2048]{2,1,0:T(8,128)} %broadcast_in_dim.2), calls=%async_computation.1 | async-start | bytes 2097152 | tf_op jit(solution)/shard_map/all_to_all | solution.py:104
  99.7 12.3 %all-to-all-start.2 = ((bf16[4,128,512]{2,1,0:T(8,128)(2,1)}), bf16[4,128,512]{2,1,0:T(8,128)(2,1)S(1)}, u32[]{:S(2)}, u32[]{:S(2)}) async-start(bf16[4,128,512]{2,1,0:T(8,128)(2,1)} %pad_maximum_fusion.1), calls=%async_computation.2 | async-start | bytes 1048576 | tf_op jit(solution)/shard_map/all_to_all | solution.py:114
  114.7 1.6 %copy-start.13 = (bf16[11,138,128]{2,0,1:T(8,128)(2,1)S(1)}, bf16[11,138,128]{2,0,1:T(8,128)(2,1)}, u32[]{:S(2)}) copy-start(bf16[11,138,128]{2,0,1:T(8,128)(2,1)} %get-tuple-element.15) | copy-start | bytes 1165828
  114.8 2.0 %copy-start.12 = (bf16[11,138,128]{2,0,1:T(8,128)(2,1)S(1)}, bf16[11,138,128]{2,0,1:T(8,128)(2,1)}, u32[]{:S(2)}) copy-start(bf16[11,138,128]{2,0,1:T(8,128)(2,1)} %get-tuple-element.16) | copy-start | bytes 1165828
  116.3 1.1 copy-start.11
  116.7 1.1 copy-start.10
  117.4 1.1 copy-start.9
  117.8 1.1 copy-start.8
  118.5 1.1 copy-start.7
  118.9 1.1 copy-start.6
  119.6 1.1 copy-start.5
  120.0 1.1 copy-start.4
  120.7 1.1 copy-start.3
  121.1 1.1 copy-start.2
  121.8 1.1 copy-start.1
  123.7 1.0 copy-start.14
  123.7 1.2 copy-start.15

commit v9 on v8

--- a/solution.py
+++ b/solution.py
@@ -94,7 +94,8 @@
     local_visits, strip_rows, sky_w = warped.shape
     stacked = jnp.stack([warped, inv_var], axis=0)
     tap_rows = psf_taps(cell_ids[0, 0], kernels[0, 0])
-    stacked, tap_rows = lax.optimization_barrier((stacked, tap_rows))
+    strip_ids = tuple(intersection[0, 0, slot] for slot in range(NOV))
+    stacked, tap_rows, strip_ids = lax.optimization_barrier((stacked, tap_rows, strip_ids))
     chunk = strip_rows // n_visit
     stacked = stacked.reshape(2, local_visits, n_visit, chunk, sky_w)
     gathered = lax.all_to_all(stacked, "visit", split_axis=2, concat_axis=1, tiled=True)
@@ -112,9 +113,8 @@
         axis=0,
     )
     strips_here = lax.all_to_all(windows, "sky", split_axis=0, concat_axis=0, tiled=True)
-    strips = intersection[0, 0]
     footprint = jnp.concatenate(
-        [lax.dynamic_index_in_dim(strips_here, strips[slot], 0, keepdims=False) for slot in range(NOV)],
+        [lax.dynamic_index_in_dim(strips_here, strip_ids[slot], 0, keepdims=False) for slot in range(NOV)],
         axis=0,
     )
     projected = jnp.dot(row_interp[0, 0], footprint, preferred_element_type=jnp.float32).astype(

time: 128 us -> 128 us (level)
    unnamed x40 -> x38, local copies, waits for them, and re-layouts: 4.63 us -> 4.62 us
  transfers between devices with their start and end apart: 2 -> 2, of which waited for: 1 -> 1; matrix products, arithmetic and copies ran while one was open for 12% -> 11% of each run, Pallas kernels for 0% -> 0%
where the time goes in v9:
time: 128 us
  blocking collectives  60.3 us (47%)
  between operations  16.8 us (13%)
  local copies, waits for them, and re-layouts  16.6 us (13%)
  matrix products  15.2 us (12%)
  other arithmetic  9.57 us (7%)
  starting transfers between devices  7.24 us (6%)
  waiting for transfers between devices  2.06 us (2%)
    all_to_all x1, blocking collectives, shards(): lax.all_to_all(stacked, 'visit', split_axis=2, concat_axis=1, tiled=True)  55.3 us
    squeeze x1, local copies, waits for them, and re-layouts, psf_bands(): banded_all[r, c]  6.54 us
    dot_general x16, matrix products, psf_match(): jnp.einsum('rc,acl->arl', cols_window, bands[row_block * blocks + col_blo...  6.3 us
    dot_general x1, matrix products, psf_bands(): jnp.einsum('xyab,bcl->xyacl', tap_rows, diagonal, preferred_element_type=...  5.97 us
    unnamed x1, blocking collectives  4.97 us
    unnamed x38, local copies, waits for them, and re-layouts  4.62 us
    reduce_sum x3, other arithmetic, local_coadd(): coadd_field = jnp.sum(cauchy * values, axis=0) / jnp.sum(cauchy, axis=0)  3.96 us
    all_to_all x1, starting transfers between devices, shards(): lax.all_to_all(windows, 'sky', split_axis=0, concat_axis=0, tiled=True)  3.65 us
  transfers between devices with their start and end apart: 2, of which 1 were waited for; matrix products, arithmetic and copies ran while one was open for 11% of the time, Pallas kernels for 0%

profile of v9, /device:TPU:0, one launch (start us, length us, event | category | flops | bytes accessed | tf_op | source)
XLA Modules:
  0.0 127.6 jit_solution(12639824491055405023)
XLA Ops:
  0.6 0.8 eq.28
  1.5 1.5 %fusion.118 = (s32[1,1,1]{2,1,0:T(1,128)}, s32[1,1,1]{2,1,0:T(1,128)}, s32[1,1,1]{2,1,0:T(1,128)}, s32[1,1,1]{2,1,0:T(1,128)}) fusion(s32[1,1,4]{2,1,0:T(1,128)} %param.12), kind=kLoop, calls=%fused_computation.339 | loop fusion | bytes 32 | tf_op jit(solution)/shard_map/slice | solution.py:97
  2.9 0.9 convolution_convert_fusion.3
  3.8 0.1 reshape.120
  3.9 1.7 %pad_maximum_fusion = bf16[2,2,128,2048]{3,2,1,0:T(8,128)(2,1)S(1)} fusion(bf16[1,2,128,2048]{3,2,1,0:T(8,128)(2,1)} %bitcast.213, bf16[1,2,128,2048]{3,2,1,0:T(8,128)(2,1)} %bitcast.214), kind=kLoop, calls=%fused_computation.29 | loop fusion | flops 1048576 | bytes 4194304 | tf_op jit(solution)/shard_map/stack | solution.py:95
  5.7 0.2 copy.60
  5.9 55.3 %all_to_all.25 = bf16[2,2,8,16,2048]{4,3,1,0,2:T(8,128)(2,1)S(1)} all-to-all(bf16[2,2,8,16,2048]{4,3,1,0,2:T(8,128)(2,1)S(1)} %copy.60), channel_id=1, replica_groups=mesh['visit'=8,'sky'=4] {'visit'}, dimensions={2} | all-to-all | bytes 4194304 | tf_op jit(solution)/shard_map/all_to_all | solution.py:101
  61.2 0.4 convert_reduce_fusion
  61.6 1.3 %fusion.23 = (f32[16,2048]{1,0:T(8,128)S(1)}, f32[16,2048]{1,0:T(8,128)S(1)}) fusion(f32[16,2048]{1,0:T(8,128)S(1)} %div.62, bf16[2,8,2,1,16,2048]{5,4,2,0,1,3:T(8,128)(2,1)S(1)} %bitcast.208), kind=kLoop, calls=%fused_computation.69 | loop fusion | flops 5701632 | bytes 2490368 | tf_op jit(solution)/shard_map/reduce_sum | solution.py:25
  63.0 1.3 %fusion.24 = (f32[16,2048]{1,0:T(8,128)S(1)}, f32[16,2048]{1,0:T(8,128)S(1)}) fusion(f32[16,2048]{1,0:T(8,128)S(1)} %div.65, bf16[2,8,2,1,16,2048]{5,4,2,0,1,3:T(8,128)(2,1)S(1)} %bitcast.209), kind=kLoop, calls=%fused_computation.70 | loop fusion | flops 5701632 | bytes 2490368 | tf_op jit(solution)/shard_map/reduce_sum | solution.py:25
  64.3 1.3 %fusion.25 = (f32[16,2048]{1,0:T(8,128)S(1)}, f32[16,2048]{1,0:T(8,128)S(1)}) fusion(f32[16,2048]{1,0:T(8,128)S(1)} %div.68, bf16[2,8,2,1,16,2048]{5,4,2,0,1,3:T(8,128)(2,1)S(1)} %bitcast.210), kind=kLoop, calls=%fused_computation.71 | loop fusion | flops 5701632 | bytes 2490368 | tf_op jit(solution)/shard_map/reduce_sum | solution.py:25
  65.7 1.1 broadcast_in_dim.2
  66.8 3.6 %all-to-all-start.1 = ((f32[8,16,2048]{2,1,0:T(8,128)}), f32[8,16,2048]{2,1,0:T(8,128)S(1)}, u32[]{:S(2)}, u32[]{:S(2)}) async-start(f32[8,16,2048]{2,1,0:T(8,128)} %broadcast_in_dim.2), calls=%async_computation.1 | async-start | bytes 2097152 | tf_op jit(solution)/shard_map/all_to_all | solution.py:105
  71.0 0.6 dynamic-slice
  71.6 0.7 bitcast_dynamic-update-slice_fusion
  72.3 5.0 %all-reduce.1 = s32[4]{0:T(128)S(1)} all-reduce(s32[4]{0:T(128)S(1)} %bitcast_dynamic-update-slice_fusion), channel_id=2, replica_groups=mesh['visit'=8,'sky'=4] {'sky'}, use_global_device_ids=true, to_apply=%add.1 | all-reduce | flops 4 | bytes 32
  77.3 0.7 fusion.117
  93.0 6.0 %convolution_convert_fusion = bf16[4,4,11,138,128]{4,2,3,1,0:T(8,128)(2,1)} fusion(s32[138,128]{1,0:T(8,128)S(1)} %iota_subtract_fusion, bf16[4,4,11,11]{3,2,1,0:T(8,128)(2,1)S(1)} %reshape.120), kind=kOutput, calls=%fused_computation | convolution fusion | flops 71698176 | bytes 6292256 | tf_op jit(solution)/shard_map/xyab,bcl->xyacl/dot_general | solution.py:46
  99.0 0.3 dynamic-slice_bitcast_fusion.7
  99.3 0.9 pad_maximum_fusion.1
  100.2 3.6 %all-to-all-start.2 = ((bf16[4,128,512]{2,1,0:T(8,128)(2,1)}), bf16[4,128,512]{2,1,0:T(8,128)(2,1)S(1)}, u32[]{:S(2)}, u32[]{:S(2)}) async-start(bf16[4,128,512]{2,1,0:T(8,128)(2,1)} %pad_maximum_fusion.1), calls=%async_computation.2 | async-start | bytes 1048576 | tf_op jit(solution)/shard_map/all_to_all | solution.py:115
  103.9 6.5 %slice_bitcast_fusion.15 = (bf16[11,138,128]{2,0,1:T(8,128)(2,1)}, bf16[11,138,128]{2,0,1:T(8,128)(2,1)}, bf16[11,138,128]{2,0,1:T(8,128)(2,1)}, bf16[11,138,128...) fusion(bf16[4,4,11,138,128]{4,2,3,1,0:T(8,128)(2,1)} %convoluti, ...), kind=kLoop, calls=%fused_computation.87 | loop fusion | bytes 12435456 | tf_op jit(solution)/shard_map/squeeze | solution.py:49
  110.4 2.1 %all-to-all-done.2 = bf16[4,128,512]{2,1,0:T(8,128)(2,1)S(1)} async-done(((bf16[4,128,512]{2,1,0:T(8,128)(2,1)}), bf16[4,128,512]{2,1,0:T(8,128)(2,1)S(1)}, u32[]{:S(2)}, u32[]{:S(2)}) %all-to-all-start.2) | async-done | bytes 524320 | tf_op jit(solution)/shard_map/all_to_all | solution.py:115
  112.5 0.7 dynamic-slice_bitcast_fusion.3
  113.2 2.0 %convolution_convert_fusion.1 = bf16[512,512]{1,0:T(8,128)(2,1)S(1)} fusion(bf16[128,512]{1,0:T(8,128)(2,1)S(1)} %get-tuple-element.39, bf16[128,512]{1,0:T(8,128)(2,1)} %get-tuple-element.40, bf16[128,512]{1,0:T(8,128)(2,1)} %get-tuple-element.41, bf16[128,512]{1,0:T(8,128)(2,1)S(1)} %get-tuple-element.38, bf16[1,1,512,512]{3,2,1,0:T(8,128)(2,1)S(1)} %copy-done, ...), kind=kOutput, calls=%fused_computation.46 | convolution fusion | flops 539492352 | bytes 2097152 | tf_op jit(solution)/shard_map/dot_general | solution.py:123
  115.3 1.5 %convolution_bitcast_fusion.15 = f32[11,138,128]{2,1,0:T(8,128)S(1)} fusion(bf16[11,138,128]{2,0,1:T(8,128)(2,1)} %get-tuple-element.22, bf16[512,512]{1,0:T(8,128)(2,1)S(1)} %convolution_convert_fusion.1), kind=kOutput, calls=%fused_computation.45 | convolution fusion | flops 53627904 | bytes 1690112 | tf_op jit(solution)/shard_map/rc,acl->arl/dot_general | solution.py:66
  116.8 0.1 fusion.99
  116.9 0.3 convolution_bitcast_fusion
  117.2 0.1 fusion.84
  117.3 0.3 convolution_bitcast_fusion.1
  117.6 0.1 fusion.85
  117.7 0.2 copy-done.11
  117.9 0.3 convolution_bitcast_fusion.2
  118.2 0.1 fusion.86
  118.4 0.3 convolution_bitcast_fusion.3
  118.7 0.1 fusion.87
  118.8 0.2 copy-done.9
  119.0 0.3 convolution_bitcast_fusion.4
  119.3 0.1 fusion.88
  119.5 0.3 convolution_bitcast_fusion.5
  119.8 0.1 fusion.89
  119.9 0.2 copy-done.7
  120.1 0.3 convolution_bitcast_fusion.6
  120.4 0.1 fusion.90
  120.5 0.3 convolution_bitcast_fusion.7
  120.9 0.1 fusion.91
  120.9 0.3 copy-done.5
  121.2 0.3 convolution_bitcast_fusion.8
  121.5 0.1 fusion.92
  121.6 0.3 convolution_bitcast_fusion.9
  122.0 0.1 fusion.93
  122.0 0.3 copy-done.3
  122.3 0.3 convolution_bitcast_fusion.10
  122.6 0.1 fusion.94
  122.7 0.3 convolution_bitcast_fusion.11
  123.0 0.1 fusion.95
  123.1 0.3 copy-done.1
  123.4 0.3 convolution_bitcast_fusion.12
  123.8 0.3 convolution_bitcast_fusion.13
  124.2 0.3 convolution_bitcast_fusion.14
  124.7 0.5 copy-done.14
  125.3 0.2 copy-done.15
  125.4 1.3 fusion.22
  126.7 1.0 copy.114
  (39 shorter events, 0.6 us)
Async XLA Ops:
  0.6 112.6 %copy-start = (bf16[1,1,512,512]{3,2,1,0:T(8,128)(2,1)S(1)}, bf16[1,1,512,512]{3,2,1,0:T(8,128)(2,1)}, u32[]{:S(2)}) copy-start(bf16[1,1,512,512]{3,2,1,0:T(8,128)(2,1)} %param.15) | copy-start | bytes 1572868
  65.7 5.4 %copy-start.16 = (u32[32]{0:T(128)S(1)}, u32[32]{0:T(128)}, u32[]{:S(2)}) copy-start(u32[32]{0:T(128)} %constant.44) | copy-start | bytes 388
  66.8 32.2 %all-to-all-start.1 = ((f32[8,16,2048]{2,1,0:T(8,128)}), f32[8,16,2048]{2,1,0:T(8,128)S(1)}, u32[]{:S(2)}, u32[]{:S(2)}) async-start(f32[8,16,2048]{2,1,0:T(8,128)} %broadcast_in_dim.2), calls=%async_computation.1 | async-start | bytes 2097152 | tf_op jit(solution)/shard_map/all_to_all | solution.py:105
  100.2 12.3 %all-to-all-start.2 = ((bf16[4,128,512]{2,1,0:T(8,128)(2,1)}), bf16[4,128,512]{2,1,0:T(8,128)(2,1)S(1)}, u32[]{:S(2)}, u32[]{:S(2)}) async-start(bf16[4,128,512]{2,1,0:T(8,128)(2,1)} %pad_maximum_fusion.1), calls=%async_computation.2 | async-start | bytes 1048576 | tf_op jit(solution)/shard_map/all_to_all | solution.py:115
  115.3 1.6 %copy-start.13 = (bf16[11,138,128]{2,0,1:T(8,128)(2,1)S(1)}, bf16[11,138,128]{2,0,1:T(8,128)(2,1)}, u32[]{:S(2)}) copy-start(bf16[11,138,128]{2,0,1:T(8,128)(2,1)} %get-tuple-element.23) | copy-start | bytes 1165828
  115.3 2.0 %copy-start.12 = (bf16[11,138,128]{2,0,1:T(8,128)(2,1)S(1)}, bf16[11,138,128]{2,0,1:T(8,128)(2,1)}, u32[]{:S(2)}) copy-start(bf16[11,138,128]{2,0,1:T(8,128)(2,1)} %get-tuple-element.24) | copy-start | bytes 1165828
  116.8 1.1 copy-start.11
  117.3 1.1 copy-start.10
  117.9 1.1 copy-start.9
  118.4 1.1 copy-start.8
  119.0 1.1 copy-start.7
  119.4 1.1 copy-start.6
  120.1 1.1 copy-start.5
  120.5 1.1 copy-start.4
  121.2 1.1 copy-start.3
  121.6 1.1 copy-start.2
  122.3 1.1 copy-start.1
  124.2 1.0 copy-start.14
  124.2 1.2 copy-start.15

commit v10 on v8

--- a/solution.py
+++ b/solution.py
@@ -111,10 +111,22 @@
         [lax.dynamic_slice_in_dim(coadd_low, all_starts[peer], TILE, 1) for peer in range(n_sky)],
         axis=0,
     )
-    strips_here = lax.all_to_all(windows, "sky", split_axis=0, concat_axis=0, tiled=True)
+    me = lax.axis_index("sky")
+    received = [lax.dynamic_index_in_dim(windows, me, 0, keepdims=False)]
+    for shift in range(1, n_sky):
+        outgoing = lax.dynamic_index_in_dim(windows, (me + shift) % n_sky, 0, keepdims=False)
+        received.append(
+            lax.ppermute(
+                outgoing, "sky", perm=[(i, (i + shift) % n_sky) for i in range(n_sky)]
+            )
+        )
+    received = jnp.stack(received, axis=0)
     strips = intersection[0, 0]
     footprint = jnp.concatenate(
-        [lax.dynamic_index_in_dim(strips_here, strips[slot], 0, keepdims=False) for slot in range(NOV)],
+        [
+            lax.dynamic_index_in_dim(received, (me - strips[slot]) % n_sky, 0, keepdims=False)
+            for slot in range(NOV)
+        ],
         axis=0,
     )
     projected = jnp.dot(row_interp[0, 0], footprint, preferred_element_type=jnp.float32).astype(

time: 128 us -> 123 us (0.961)
  between operations: 17 us -> 12.2 us
  waiting for transfers between devices: 2.06 us -> 4.23 us
  starting transfers between devices: 7.24 us -> 5.39 us
    all_to_all x1, waiting for transfers between devices: 0.01 us -> 4.23 us  [shards(): lax.all_to_all(copies, 'visit', split_axis=0, concat_axis=0, tiled=True)]
    all_to_all x1 -> x0, starting transfers between devices: 3.65 us -> none  [shards(): lax.all_to_all(windows, 'sky', split_axis=0, concat_axis=0, tiled=True)]
    all_to_all x1 -> x0, waiting for transfers between devices: 2.06 us -> none  [shards(): lax.all_to_all(windows, 'sky', split_axis=0, concat_axis=0, tiled=True)]
    ppermute x0 -> x3, starting transfers between devices: none -> 1.79 us  [shards(): lax.ppermute(outgoing, 'sky', perm=[(i, (i + shift) % n_sky) for i in ran...]
  transfers between devices with their start and end apart: 2 -> 4, of which waited for: 1 -> 1; matrix products, arithmetic and copies ran while one was open for 12% -> 12% of each run, Pallas kernels for 0% -> 0%
where the time goes in v10:
time: 123 us
  blocking collectives  60.3 us (49%)
  local copies, waits for them, and re-layouts  15.8 us (13%)
  matrix products  15.2 us (12%)
  between operations  12.2 us (10%)
  other arithmetic  9.72 us (8%)
  starting transfers between devices  5.39 us (4%)
  waiting for transfers between devices  4.23 us (3%)
    all_to_all x1, blocking collectives, shards(): lax.all_to_all(stacked, 'visit', split_axis=2, concat_axis=1, tiled=True)  55.3 us
    squeeze x1, local copies, waits for them, and re-layouts, psf_bands(): banded_all[r, c]  6.51 us
    dot_general x16, matrix products, psf_match(): jnp.einsum('rc,acl->arl', cols_window, bands[row_block * blocks + col_blo...  6.3 us
    dot_general x1, matrix products, psf_bands(): jnp.einsum('xyab,bcl->xyacl', tap_rows, diagonal, preferred_element_type=...  5.99 us
    unnamed x1, blocking collectives  4.97 us
    unnamed x40, local copies, waits for them, and re-layouts  4.63 us
    all_to_all x1, waiting for transfers between devices, shards(): lax.all_to_all(copies, 'visit', split_axis=0, concat_axis=0, tiled=True)  4.23 us
    reduce_sum x3, other arithmetic, local_coadd(): coadd_field = jnp.sum(cauchy * values, axis=0) / jnp.sum(cauchy, axis=0)  3.96 us
  transfers between devices with their start and end apart: 4, of which 1 were waited for; matrix products, arithmetic and copies ran while one was open for 12% of the time, Pallas kernels for 0%

profile of v10, /device:TPU:0, one launch (start us, length us, event | category | flops | bytes accessed | tf_op | source)
XLA Modules:
  0.0 122.8 jit_solution(17626333360137401010)
XLA Ops:
  0.6 0.8 eq.36
  1.5 0.9 convolution_convert_fusion.3
  2.3 0.1 reshape.128
  2.4 1.7 %pad_maximum_fusion = bf16[2,2,128,2048]{3,2,1,0:T(8,128)(2,1)S(1)} fusion(bf16[1,2,128,2048]{3,2,1,0:T(8,128)(2,1)} %bitcast.222, bf16[1,2,128,2048]{3,2,1,0:T(8,128)(2,1)} %bitcast.223), kind=kLoop, calls=%fused_computation.29 | loop fusion | flops 1048576 | bytes 4194304 | tf_op jit(solution)/shard_map/stack | solution.py:95
  4.2 0.2 copy.60
  4.4 55.3 %all_to_all.20 = bf16[2,2,8,16,2048]{4,3,1,0,2:T(8,128)(2,1)S(1)} all-to-all(bf16[2,2,8,16,2048]{4,3,1,0,2:T(8,128)(2,1)S(1)} %copy.60), channel_id=1, replica_groups=mesh['visit'=8,'sky'=4] {'visit'}, dimensions={2} | all-to-all | bytes 4194304 | tf_op jit(solution)/shard_map/all_to_all | solution.py:100
  59.7 0.4 convert_reduce_fusion
  60.2 1.3 %fusion.23 = (f32[16,2048]{1,0:T(8,128)S(1)}, f32[16,2048]{1,0:T(8,128)S(1)}) fusion(f32[16,2048]{1,0:T(8,128)S(1)} %div.62, bf16[2,8,2,1,16,2048]{5,4,2,0,1,3:T(8,128)(2,1)S(1)} %bitcast.217), kind=kLoop, calls=%fused_computation.69 | loop fusion | flops 5701632 | bytes 2490368 | tf_op jit(solution)/shard_map/reduce_sum | solution.py:25
  61.5 1.3 %fusion.24 = (f32[16,2048]{1,0:T(8,128)S(1)}, f32[16,2048]{1,0:T(8,128)S(1)}) fusion(f32[16,2048]{1,0:T(8,128)S(1)} %div.65, bf16[2,8,2,1,16,2048]{5,4,2,0,1,3:T(8,128)(2,1)S(1)} %bitcast.218), kind=kLoop, calls=%fused_computation.70 | loop fusion | flops 5701632 | bytes 2490368 | tf_op jit(solution)/shard_map/reduce_sum | solution.py:25
  62.9 1.3 %fusion.25 = (f32[16,2048]{1,0:T(8,128)S(1)}, f32[16,2048]{1,0:T(8,128)S(1)}) fusion(f32[16,2048]{1,0:T(8,128)S(1)} %div.68, bf16[2,8,2,1,16,2048]{5,4,2,0,1,3:T(8,128)(2,1)S(1)} %bitcast.219), kind=kLoop, calls=%fused_computation.71 | loop fusion | flops 5701632 | bytes 2490368 | tf_op jit(solution)/shard_map/reduce_sum | solution.py:25
  64.2 1.1 broadcast_in_dim.2
  65.3 3.6 %all-to-all-start.1 = ((f32[8,16,2048]{2,1,0:T(8,128)}), f32[8,16,2048]{2,1,0:T(8,128)S(1)}, u32[]{:S(2)}, u32[]{:S(2)}) async-start(f32[8,16,2048]{2,1,0:T(8,128)} %broadcast_in_dim.2), calls=%async_computation.1 | async-start | bytes 2097152 | tf_op jit(solution)/shard_map/all_to_all | solution.py:104
  69.6 0.6 dynamic-slice
  70.2 0.7 bitcast_dynamic-update-slice_fusion
  70.8 5.0 %all-reduce.1 = s32[4]{0:T(128)S(1)} all-reduce(s32[4]{0:T(128)S(1)} %bitcast_dynamic-update-slice_fusion), channel_id=2, replica_groups=mesh['visit'=8,'sky'=4] {'sky'}, use_global_device_ids=true, to_apply=%add.1 | all-reduce | flops 4 | bytes 32
  75.8 0.7 fusion.118
  84.3 6.0 %convolution_convert_fusion = bf16[4,4,11,138,128]{4,2,3,1,0:T(8,128)(2,1)} fusion(s32[138,128]{1,0:T(8,128)S(1)} %iota_subtract_fusion, bf16[4,4,11,11]{3,2,1,0:T(8,128)(2,1)S(1)} %reshape.128), kind=kOutput, calls=%fused_computation | convolution fusion | flops 71698176 | bytes 6292256 | tf_op jit(solution)/shard_map/xyab,bcl->xyacl/dot_general | solution.py:46
  90.2 4.2 %all-to-all-done.1 = f32[8,16,2048]{2,1,0:T(8,128)S(1)} async-done(((f32[8,16,2048]{2,1,0:T(8,128)}), f32[8,16,2048]{2,1,0:T(8,128)S(1)}, u32[]{:S(2)}, u32[]{:S(2)}) %all-to-all-start.1) | async-done | bytes 1048608 | tf_op jit(solution)/shard_map/all_to_all | solution.py:104
  94.5 0.3 dynamic-slice_bitcast_fusion.10
  94.9 0.1 pad_maximum_fusion.1
  95.0 1.6 %collective-permute-start.1 = (bf16[128,512]{1,0:T(8,128)(2,1)S(1)}, bf16[128,512]{1,0:T(8,128)(2,1)S(1)}, u32[]{:S(2)}, u32[]{:S(2)}) collective-permute-start(bf16[128,512]{1,0:T(8,128)(2,1)S(1)} %get-tuple-element.36), channel_id=1, source_target_pairs={{0,2},{1,3},{2,0},{3,1},{4,6},{5,7},{6,4},{7,5},{8,10},{9,11},{10,... | collective-permute-start | bytes 393224 | tf_op jit(solution)/shard_map/ppermute | solution.py:119
  96.6 0.2 collective-permute-start
  96.8 6.5 %slice_bitcast_fusion.15 = (bf16[11,138,128]{2,0,1:T(8,128)(2,1)}, bf16[11,138,128]{2,0,1:T(8,128)(2,1)}, bf16[11,138,128]{2,0,1:T(8,128)(2,1)}, bf16[11,138,128...) fusion(bf16[4,4,11,138,128]{4,2,3,1,0:T(8,128)(2,1)} %convoluti, ...), kind=kLoop, calls=%fused_computation.87 | loop fusion | bytes 12435456 | tf_op jit(solution)/shard_map/squeeze | solution.py:49
  103.3 0.7 fusion.117
  106.6 1.0 pad_maximum_fusion.2
  107.6 0.7 dynamic-slice_bitcast_fusion.3
  108.4 2.0 %convolution_convert_fusion.1 = bf16[512,512]{1,0:T(8,128)(2,1)S(1)} fusion(bf16[128,512]{1,0:T(8,128)(2,1)S(1)} %get-tuple-element.31, bf16[128,512]{1,0:T(8,128)(2,1)} %get-tuple-element.32, bf16[128,512]{1,0:T(8,128)(2,1)} %get-tuple-element.33, bf16[128,512]{1,0:T(8,128)(2,1)S(1)} %get-tuple-element.30, bf16[1,1,512,512]{3,2,1,0:T(8,128)(2,1)S(1)} %copy-done, ...), kind=kOutput, calls=%fused_computation.46 | convolution fusion | flops 539492352 | bytes 2097152 | tf_op jit(solution)/shard_map/dot_general | solution.py:135
  110.4 1.5 %convolution_bitcast_fusion.15 = f32[11,138,128]{2,1,0:T(8,128)S(1)} fusion(bf16[11,138,128]{2,0,1:T(8,128)(2,1)} %get-tuple-element.14, bf16[512,512]{1,0:T(8,128)(2,1)S(1)} %convolution_convert_fusion.1), kind=kOutput, calls=%fused_computation.45 | convolution fusion | flops 53627904 | bytes 1690112 | tf_op jit(solution)/shard_map/rc,acl->arl/dot_general | solution.py:66
  111.9 0.1 fusion.99
  112.0 0.3 convolution_bitcast_fusion
  112.3 0.1 fusion.84
  112.4 0.3 convolution_bitcast_fusion.1
  112.7 0.1 fusion.85
  112.8 0.2 copy-done.11
  113.0 0.3 convolution_bitcast_fusion.2
  113.3 0.1 fusion.86
  113.5 0.3 convolution_bitcast_fusion.3
  113.8 0.1 fusion.87
  113.9 0.2 copy-done.9
  114.1 0.3 convolution_bitcast_fusion.4
  114.5 0.1 fusion.88
  114.6 0.3 convolution_bitcast_fusion.5
  114.9 0.1 fusion.89
  115.0 0.2 copy-done.7
  115.2 0.3 convolution_bitcast_fusion.6
  115.5 0.1 fusion.90
  115.6 0.3 convolution_bitcast_fusion.7
  116.0 0.1 fusion.91
  116.0 0.3 copy-done.5
  116.3 0.3 convolution_bitcast_fusion.8
  116.7 0.1 fusion.92
  116.7 0.3 convolution_bitcast_fusion.9
  117.1 0.3 copy-done.3
  117.4 0.3 convolution_bitcast_fusion.10
  117.8 0.3 convolution_bitcast_fusion.11
  118.2 0.3 copy-done.1
  118.5 0.3 convolution_bitcast_fusion.12
  118.9 0.3 convolution_bitcast_fusion.13
  119.3 0.3 convolution_bitcast_fusion.14
  119.7 0.1 fusion.98
  119.8 0.5 copy-done.14
  120.4 0.2 copy-done.15
  120.5 1.3 %fusion.22 = f32[1,1,512,512]{3,2,1,0:T(8,128)} fusion(f32[1,1,128,512]{3,2,1,0:T(8,128)S(1)} %get-tuple-element.53, f32[1,1,128,512]{3,2,1,0:T(8,128)S(1)} %get-tuple-element.52, f32[1,1,128,512]{3,2,1,0:T(8,128)S(1)} %get-tuple-element.51, f32[1,1,128,512]{3,2,1,0:T(8,128)S(1)} %get-tuple-element.50, bf16[1,1,512,512]{3,2,1,0:T(8,128)(2,1)S(1)} %copy-done.14, ...), kind=kLoop, calls=%fused_computation.56 | loop fusion | flops 2883584 | bytes 3145728 | tf_op jit(solution)/shard_map/div | solution.py:144
  121.8 1.0 copy.114
  (47 shorter events, 0.9 us)
Async XLA Ops:
  0.6 107.7 %copy-start = (bf16[1,1,512,512]{3,2,1,0:T(8,128)(2,1)S(1)}, bf16[1,1,512,512]{3,2,1,0:T(8,128)(2,1)}, u32[]{:S(2)}) copy-start(bf16[1,1,512,512]{3,2,1,0:T(8,128)(2,1)} %param.15) | copy-start | bytes 1572868
  64.2 5.4 %copy-start.17 = (u32[32]{0:T(128)S(1)}, u32[32]{0:T(128)}, u32[]{:S(2)}) copy-start(u32[32]{0:T(128)} %constant.96) | copy-start | bytes 388
  65.3 29.2 %all-to-all-start.1 = ((f32[8,16,2048]{2,1,0:T(8,128)}), f32[8,16,2048]{2,1,0:T(8,128)S(1)}, u32[]{:S(2)}, u32[]{:S(2)}) async-start(f32[8,16,2048]{2,1,0:T(8,128)} %broadcast_in_dim.2), calls=%async_computation.1 | async-start | bytes 2097152 | tf_op jit(solution)/shard_map/all_to_all | solution.py:104
  95.0 11.6 %collective-permute-start.2 = (bf16[128,512]{1,0:T(8,128)(2,1)S(1)}, bf16[128,512]{1,0:T(8,128)(2,1)S(1)}, u32[]{:S(2)}, u32[]{:S(2)}) collective-permute-start(bf16[128,512]{1,0:T(8,128)(2,1)S(1)} %get-tuple-element.35), channel_id=1, source_target_pairs={{0,3},{1,0},{2,1},{3,2},{4,7},{5,4},{6,5},{7,6},{8,11},{9,8},{10,9... | collective-permute-start | bytes 393224 | tf_op jit(solution)/shard_map/ppermute | solution.py:119
  95.0 11.6 %collective-permute-start.1 = (bf16[128,512]{1,0:T(8,128)(2,1)S(1)}, bf16[128,512]{1,0:T(8,128)(2,1)S(1)}, u32[]{:S(2)}, u32[]{:S(2)}) collective-permute-start(bf16[128,512]{1,0:T(8,128)(2,1)S(1)} %get-tuple-element.36), channel_id=1, source_target_pairs={{0,2},{1,3},{2,0},{3,1},{4,6},{5,7},{6,4},{7,5},{8,10},{9,11},{10,... | collective-permute-start | bytes 393224 | tf_op jit(solution)/shard_map/ppermute | solution.py:119
  96.6 6.7 %copy-start.16 = (s32[1,1,4]{2,1,0:T(1,128)S(1)}, s32[1,1,4]{2,1,0:T(1,128)}, u32[]{:S(2)}) copy-start(s32[1,1,4]{2,1,0:T(1,128)} %param.12) | copy-start | bytes 52
  96.6 10.0 %collective-permute-start = (bf16[128,512]{1,0:T(8,128)(2,1)S(1)}, bf16[128,512]{1,0:T(8,128)(2,1)}, u32[]{:S(2)}, u32[]{:S(2)}) collective-permute-start(bf16[128,512]{1,0:T(8,128)(2,1)S(1)} %get-tuple-element.37), channel_id=1, source_target_pairs={{0,1},{1,2},{2,3},{3,0},{4,5},{5,6},{6,7},{7,4},{8,9},{9,10},{10,1... | collective-permute-start | bytes 393224 | tf_op jit(solution)/shard_map/ppermute | solution.py:119
  110.4 1.6 %copy-start.13 = (bf16[11,138,128]{2,0,1:T(8,128)(2,1)S(1)}, bf16[11,138,128]{2,0,1:T(8,128)(2,1)}, u32[]{:S(2)}) copy-start(bf16[11,138,128]{2,0,1:T(8,128)(2,1)} %get-tuple-element.15) | copy-start | bytes 1165828
  110.4 2.0 %copy-start.12 = (bf16[11,138,128]{2,0,1:T(8,128)(2,1)S(1)}, bf16[11,138,128]{2,0,1:T(8,128)(2,1)}, u32[]{:S(2)}) copy-start(bf16[11,138,128]{2,0,1:T(8,128)(2,1)} %get-tuple-element.16) | copy-start | bytes 1165828
  112.0 1.1 copy-start.11
  112.4 1.1 copy-start.10
  113.0 1.1 copy-start.9
  113.5 1.1 copy-start.8
  114.1 1.1 copy-start.7
  114.5 1.1 copy-start.6
  115.2 1.1 copy-start.5
  115.6 1.1 copy-start.4
  116.3 1.1 copy-start.3
  116.7 1.1 copy-start.2
  117.4 1.1 copy-start.1
  119.3 1.0 copy-start.14
  119.3 1.2 copy-start.15

commit v11 on v10

--- a/solution.py
+++ b/solution.py
@@ -100,8 +100,17 @@
     gathered = lax.all_to_all(stacked, "visit", split_axis=2, concat_axis=1, tiled=True)
     gathered = gathered.reshape(2, local_visits * n_visit, chunk, sky_w)
     row_share = local_coadd(gathered[0].astype(jnp.float32), gathered[1].astype(jnp.float32))
-    copies = jnp.broadcast_to(row_share[None], (n_visit,) + row_share.shape)
-    coadd_field = lax.all_to_all(copies, "visit", split_axis=0, concat_axis=0, tiled=True)
+    visit_me = lax.axis_index("visit")
+    pieces = [row_share]
+    for shift in range(1, n_visit):
+        pieces.append(
+            lax.ppermute(
+                row_share, "visit", perm=[(i, (i + shift) % n_visit) for i in range(n_visit)]
+            )
+        )
+    pieces = jnp.stack(pieces, axis=0)
+    order = (visit_me - jnp.arange(n_visit, dtype=jnp.int32)) % n_visit
+    coadd_field = jnp.take(pieces, order, axis=0)
     bands = psf_bands(tap_rows)
     coadd_field = coadd_field.reshape(n_visit * chunk, sky_w)
     coadd_low = coadd_field.astype(jnp.bfloat16)

time: 123 us -> 134 us (1.089)
  the two profiles are of different devices: /device:TPU:0 before, /device:TPU:11 now
where the time goes in v11:
time: 134 us
  waiting for transfers between devices  52.4 us (39%)
  starting transfers between devices  22.2 us (17%)
  local copies, waits for them, and re-layouts  15.5 us (12%)
  matrix products  15.3 us (11%)
  between operations  12.2 us (9%)
  other arithmetic  10.9 us (8%)
  blocking collectives  5.14 us (4%)
    all_to_all x1, waiting for transfers between devices, shards(): lax.all_to_all(stacked, 'visit', split_axis=2, concat_axis=1, tiled=True)  31.9 us
    ppermute x7, waiting for transfers between devices, shards(): lax.ppermute(row_share, 'visit', perm=[(i, (i + shift) % n_visit) for i i...  20.5 us
    ppermute x7, starting transfers between devices, shards(): lax.ppermute(row_share, 'visit', perm=[(i, (i + shift) % n_visit) for i i...  13 us
    squeeze x1, local copies, waits for them, and re-layouts, psf_bands(): banded_all[r, c]  6.46 us
    dot_general x16, matrix products, psf_match(): jnp.einsum('rc,acl->arl', cols_window, bands[row_block * blocks + col_blo...  6.3 us
    dot_general x1, matrix products, psf_bands(): jnp.einsum('xyab,bcl->xyacl', tap_rows, diagonal, preferred_element_type=...  6.01 us
    all_to_all x1, starting transfers between devices, shards(): lax.all_to_all(stacked, 'visit', split_axis=2, concat_axis=1, tiled=True)  5.79 us
    unnamed x1, blocking collectives  5.14 us
  transfers between devices with their start and end apart: 11, of which 3 were waited for; matrix products, arithmetic and copies ran while one was open for 11% of the time, Pallas kernels for 0%

profile of v11, /device:TPU:11, one launch (start us, length us, event | category | flops | bytes accessed | tf_op | source)
XLA Modules:
  0.0 133.7 jit_solution(11298203539548035688)
XLA Ops:
  0.6 0.8 eq.38
  1.5 0.9 convolution_convert_fusion.3
  2.3 0.1 reshape.189
  2.4 1.7 %pad_maximum_fusion = bf16[2,2,128,2048]{3,2,1,0:T(8,128)(2,1)S(1)} fusion(bf16[1,2,128,2048]{3,2,1,0:T(8,128)(2,1)} %bitcast.240, bf16[1,2,128,2048]{3,2,1,0:T(8,128)(2,1)} %bitcast.241), kind=kLoop, calls=%fused_computation.30 | loop fusion | flops 1048576 | bytes 4194304 | tf_op jit(solution)/shard_map/stack | solution.py:95
  4.2 1.4 %copy.60 = bf16[2,2,8,16,2048]{4,3,1,0,2:T(8,128)(2,1)} copy(bf16[2,2,8,16,2048]{4,3,2,1,0:T(8,128)(2,1)S(1)} %bitcast.239) | data formatting | bytes 4194304 | tf_op jit(solution)/shard_map/reshape | solution.py:99
  5.6 5.8 %all-to-all-start = ((bf16[2,2,8,16,2048]{4,3,1,0,2:T(8,128)(2,1)}), bf16[2,2,8,16,2048]{4,3,1,0,2:T(8,128)(2,1)S(1)}, u32[]{:S(2)}, u32[]{:S(2)}) async-start(bf16[2,2,8,16,2048]{4,3,1,0,2:T(8,128)(2,1)} %copy.60), calls=%async_computation | async-start | bytes 4194304 | tf_op jit(solution)/shard_map/all_to_all | solution.py:100
  12.1 0.6 dynamic-slice
  12.7 0.7 bitcast_dynamic-update-slice_fusion.8
  13.4 5.1 %all-reduce.1 = s32[4]{0:T(128)S(1)} all-reduce(s32[4]{0:T(128)S(1)} %bitcast_dynamic-update-slice_fusion.8), channel_id=2, replica_groups=mesh['visit'=8,'sky'=4] {'sky'}, use_global_device_ids=true, to_apply=%add.1 | all-reduce | flops 4 | bytes 32
  18.5 0.7 fusion.122
  19.2 6.0 %convolution_convert_fusion = bf16[4,4,11,138,128]{4,2,3,1,0:T(8,128)(2,1)} fusion(s32[138,128]{1,0:T(8,128)S(1)} %iota_subtract_fusion, bf16[4,4,11,11]{3,2,1,0:T(8,128)(2,1)S(1)} %reshape.189), kind=kOutput, calls=%fused_computation.1 | convolution fusion | flops 71698176 | bytes 6292256 | tf_op jit(solution)/shard_map/xyab,bcl->xyacl/dot_general | solution.py:46
  25.2 31.9 %all-to-all-done = bf16[2,2,8,16,2048]{4,3,1,0,2:T(8,128)(2,1)S(1)} async-done(((bf16[2,2,8,16,2048]{4,3,1,0,2:T(8,128)(2,1)}), bf16[2,2,8,16,2048]{4,3,1,0,2:T(8,128)(2,1)S(1)}, u32[]{:S(2)}, u32[]{:S(2)}) %all-to-all-start) | async-done | bytes 2097184 | tf_op jit(solution)/shard_map/all_to_all | solution.py:100
  57.1 0.4 convert_reduce_fusion
  57.6 1.3 fusion.23
  58.9 1.3 fusion.24
  60.3 1.3 fusion.25
  66.9 0.1 broadcast_in_dim.14
  67.0 0.1 broadcast_in_dim.24
  69.7 2.3 %collective-permute-start.5 = (f32[16,2048]{1,0:T(8,128)S(1)}, f32[16,2048]{1,0:T(8,128)S(1)}, u32[]{:S(2)}, u32[]{:S(2)}) collective-permute-start(f32[16,2048]{1,0:T(8,128)S(1)} %get-tuple-element.17), channel_id=1, source_target_pairs={{0,24},{4,28},{8,0},{12,4},{16,8},{20,12},{24,16},{28,20},{1,25},{... | collective-permute-start | bytes 393224 | tf_op jit(solution)/shard_map/ppermute | solution.py:107
  72.0 3.1 %collective-permute-start.4 = (f32[16,2048]{1,0:T(8,128)S(1)}, f32[16,2048]{1,0:T(8,128)S(1)}, u32[]{:S(2)}, u32[]{:S(2)}) collective-permute-start(f32[16,2048]{1,0:T(8,128)S(1)} %get-tuple-element.17), channel_id=1, source_target_pairs={{0,20},{4,24},{8,28},{12,0},{16,4},{20,8},{24,12},{28,16},{1,21},{... | collective-permute-start | bytes 393224 | tf_op jit(solution)/shard_map/ppermute | solution.py:107
  75.1 3.2 %collective-permute-start.2 = (f32[16,2048]{1,0:T(8,128)S(1)}, f32[16,2048]{1,0:T(8,128)S(1)}, u32[]{:S(2)}, u32[]{:S(2)}) collective-permute-start(f32[16,2048]{1,0:T(8,128)S(1)} %get-tuple-element.17), channel_id=1, source_target_pairs={{0,12},{4,16},{8,20},{12,24},{16,28},{20,0},{24,4},{28,8},{1,13},{... | collective-permute-start | bytes 393224 | tf_op jit(solution)/shard_map/ppermute | solution.py:107
  78.3 0.9 collective-permute-start.1
  79.2 15.3 %collective-permute-done.1 = f32[16,2048]{1,0:T(8,128)S(1)} collective-permute-done((f32[16,2048]{1,0:T(8,128)S(1)}, f32[16,2048]{1,0:T(8,128)S(1)}, u32[]{:S(2)}, u32[]{:S(2)}) %collective-permute-start.1) | collective-permute-done | bytes 131104 | tf_op jit(solution)/shard_map/ppermute | solution.py:107
  94.5 3.5 %collective-permute-start.6 = (f32[16,2048]{1,0:T(8,128)S(1)}, f32[16,2048]{1,0:T(8,128)S(1)}, u32[]{:S(2)}, u32[]{:S(2)}) collective-permute-start(f32[16,2048]{1,0:T(8,128)S(1)} %get-tuple-element.17), channel_id=1, source_target_pairs={{0,28},{4,0},{8,4},{12,8},{16,12},{20,16},{24,20},{28,24},{1,29},{... | collective-permute-start | bytes 393224 | tf_op jit(solution)/shard_map/ppermute | solution.py:107
  98.2 5.2 %collective-permute-done.6 = f32[16,2048]{1,0:T(8,128)S(1)} collective-permute-done((f32[16,2048]{1,0:T(8,128)S(1)}, f32[16,2048]{1,0:T(8,128)S(1)}, u32[]{:S(2)}, u32[]{:S(2)}) %collective-permute-start.6) | collective-permute-done | bytes 131104 | tf_op jit(solution)/shard_map/ppermute | solution.py:107
  103.3 0.6 gather_fusion
  104.0 1.1 fusion.120
  105.1 0.3 dynamic-slice_bitcast_fusion.10
  105.4 0.1 pad_maximum_fusion.1
  105.5 1.1 collective-permute-start.9
  106.7 1.2 collective-permute-start.8
  107.9 1.0 collective-permute-start.7
  108.9 6.5 %slice_bitcast_fusion.15 = (bf16[11,138,128]{2,0,1:T(8,128)(2,1)}, bf16[11,138,128]{2,0,1:T(8,128)(2,1)}, bf16[11,138,128]{2,0,1:T(8,128)(2,1)}, bf16[11,138,128...) fusion(bf16[4,4,11,138,128]{4,2,3,1,0:T(8,128)(2,1)} %convoluti, ...), kind=kLoop, calls=%fused_computation.89 | loop fusion | bytes 12435456 | tf_op jit(solution)/shard_map/squeeze | solution.py:49
  115.3 0.7 fusion.121
  118.6 1.0 pad_maximum_fusion.2
  119.6 0.8 dynamic-slice_bitcast_fusion.3
  120.4 2.1 %convolution_convert_fusion.1 = bf16[512,512]{1,0:T(8,128)(2,1)S(1)} fusion(bf16[128,512]{1,0:T(8,128)(2,1)} %get-tuple-element.35, bf16[128,512]{1,0:T(8,128)(2,1)} %get-tuple-element.36, bf16[128,512]{1,0:T(8,128)(2,1)} %get-tuple-element.37, bf16[128,512]{1,0:T(8,128)(2,1)S(1)} %get-tuple-element.34, bf16[1,1,512,512]{3,2,1,0:T(8,128)(2,1)S(1)} %copy-done, ...), kind=kOutput, calls=%fused_computation.47 | convolution fusion | flops 539492352 | bytes 2097152 | tf_op jit(solution)/shard_map/dot_general | solution.py:144
  122.5 1.5 %convolution_bitcast_fusion.15 = f32[11,138,128]{2,1,0:T(8,128)S(1)} fusion(bf16[11,138,128]{2,0,1:T(8,128)(2,1)} %get-tuple-element.18, bf16[512,512]{1,0:T(8,128)(2,1)S(1)} %convolution_convert_fusion.1), kind=kOutput, calls=%fused_computation.46 | convolution fusion | flops 53627904 | bytes 1690112 | tf_op jit(solution)/shard_map/rc,acl->arl/dot_general | solution.py:66
  124.0 0.1 fusion.99
  124.1 0.3 convolution_bitcast_fusion
  124.4 0.1 fusion.84
  124.5 0.3 convolution_bitcast_fusion.1
  124.9 0.1 fusion.85
  124.9 0.2 copy-done.9
  125.2 0.3 convolution_bitcast_fusion.2
  125.6 0.3 convolution_bitcast_fusion.3
  126.0 0.2 copy-done.7
  126.3 0.3 convolution_bitcast_fusion.4
  126.7 0.3 convolution_bitcast_fusion.5
  127.1 0.2 copy-done.5
  127.4 0.3 convolution_bitcast_fusion.6
  127.8 0.3 convolution_bitcast_fusion.7
  128.2 0.3 copy-done.3
  128.5 0.3 convolution_bitcast_fusion.8
  128.9 0.3 convolution_bitcast_fusion.9
  129.3 0.3 copy-done.1
  129.6 0.3 convolution_bitcast_fusion.10
  130.0 0.3 convolution_bitcast_fusion.11
  130.4 0.3 convolution_bitcast_fusion.12
  130.8 0.3 convolution_bitcast_fusion.13
  131.2 0.3 convolution_bitcast_fusion.14
  131.7 0.5 copy-done.12
  132.2 0.2 copy-done.13
  132.4 1.3 fusion.22
  (67 shorter events, 1.5 us)
Async XLA Ops:
  0.6 119.8 %copy-start = (bf16[1,1,512,512]{3,2,1,0:T(8,128)(2,1)S(1)}, bf16[1,1,512,512]{3,2,1,0:T(8,128)(2,1)}, u32[]{:S(2)}) copy-start(bf16[1,1,512,512]{3,2,1,0:T(8,128)(2,1)} %param.15) | copy-start | bytes 1572868
  5.6 6.5 %copy-start.15 = (u32[32]{0:T(128)S(1)}, u32[32]{0:T(128)}, u32[]{:S(2)}) copy-start(u32[32]{0:T(128)} %constant.130) | copy-start | bytes 388
  5.6 51.5 %all-to-all-start = ((bf16[2,2,8,16,2048]{4,3,1,0,2:T(8,128)(2,1)}), bf16[2,2,8,16,2048]{4,3,1,0,2:T(8,128)(2,1)S(1)}, u32[]{:S(2)}, u32[]{:S(2)}) async-start(bf16[2,2,8,16,2048]{4,3,1,0,2:T(8,128)(2,1)} %copy.60), calls=%async_computation | async-start | bytes 4194304 | tf_op jit(solution)/shard_map/all_to_all | solution.py:100
  61.6 16.7 %collective-permute-start = (f32[16,2048]{1,0:T(8,128)S(1)}, f32[16,2048]{1,0:T(8,128)S(1)}, u32[]{:S(2)}, u32[]{:S(2)}) collective-permute-start(f32[16,2048]{1,0:T(8,128)S(1)} %get-tuple-element.17), channel_id=1, source_target_pairs={{0,4},{4,8},{8,12},{12,16},{16,20},{20,24},{24,28},{28,0},{1,5},{5... | collective-permute-start | bytes 393224 | tf_op jit(solution)/shard_map/ppermute | solution.py:107
  69.7 28.4 %collective-permute-start.5 = (f32[16,2048]{1,0:T(8,128)S(1)}, f32[16,2048]{1,0:T(8,128)S(1)}, u32[]{:S(2)}, u32[]{:S(2)}) collective-permute-start(f32[16,2048]{1,0:T(8,128)S(1)} %get-tuple-element.17), channel_id=1, source_target_pairs={{0,24},{4,28},{8,0},{12,4},{16,8},{20,12},{24,16},{28,20},{1,25},{... | collective-permute-start | bytes 393224 | tf_op jit(solution)/shard_map/ppermute | solution.py:107
  72.0 26.1 %collective-permute-start.4 = (f32[16,2048]{1,0:T(8,128)S(1)}, f32[16,2048]{1,0:T(8,128)S(1)}, u32[]{:S(2)}, u32[]{:S(2)}) collective-permute-start(f32[16,2048]{1,0:T(8,128)S(1)} %get-tuple-element.17), channel_id=1, source_target_pairs={{0,20},{4,24},{8,28},{12,0},{16,4},{20,8},{24,12},{28,16},{1,21},{... | collective-permute-start | bytes 393224 | tf_op jit(solution)/shard_map/ppermute | solution.py:107
  75.1 23.0 %collective-permute-start.3 = (f32[16,2048]{1,0:T(8,128)S(1)}, f32[16,2048]{1,0:T(8,128)S(1)}, u32[]{:S(2)}, u32[]{:S(2)}) collective-permute-start(f32[16,2048]{1,0:T(8,128)S(1)} %get-tuple-element.17), channel_id=1, source_target_pairs={{0,16},{4,20},{8,24},{12,28},{16,0},{20,4},{24,8},{28,12},{1,17},{... | collective-permute-start | bytes 393224 | tf_op jit(solution)/shard_map/ppermute | solution.py:107
  75.1 22.9 %collective-permute-start.2 = (f32[16,2048]{1,0:T(8,128)S(1)}, f32[16,2048]{1,0:T(8,128)S(1)}, u32[]{:S(2)}, u32[]{:S(2)}) collective-permute-start(f32[16,2048]{1,0:T(8,128)S(1)} %get-tuple-element.17), channel_id=1, source_target_pairs={{0,12},{4,16},{8,20},{12,24},{16,28},{20,0},{24,4},{28,8},{1,13},{... | collective-permute-start | bytes 393224 | tf_op jit(solution)/shard_map/ppermute | solution.py:107
  78.3 16.2 %collective-permute-start.1 = (f32[16,2048]{1,0:T(8,128)S(1)}, f32[16,2048]{1,0:T(8,128)S(1)}, u32[]{:S(2)}, u32[]{:S(2)}) collective-permute-start(f32[16,2048]{1,0:T(8,128)S(1)} %get-tuple-element.17), channel_id=1, source_target_pairs={{0,8},{4,12},{8,16},{12,20},{16,24},{20,28},{24,0},{28,4},{1,9},{5... | collective-permute-start | bytes 393224 | tf_op jit(solution)/shard_map/ppermute | solution.py:107
  94.5 8.8 %collective-permute-start.6 = (f32[16,2048]{1,0:T(8,128)S(1)}, f32[16,2048]{1,0:T(8,128)S(1)}, u32[]{:S(2)}, u32[]{:S(2)}) collective-permute-start(f32[16,2048]{1,0:T(8,128)S(1)} %get-tuple-element.17), channel_id=1, source_target_pairs={{0,28},{4,0},{8,4},{12,8},{16,12},{20,16},{24,20},{28,24},{1,29},{... | collective-permute-start | bytes 393224 | tf_op jit(solution)/shard_map/ppermute | solution.py:107
  105.5 13.0 %collective-permute-start.9 = (bf16[128,512]{1,0:T(8,128)(2,1)S(1)}, bf16[128,512]{1,0:T(8,128)(2,1)S(1)}, u32[]{:S(2)}, u32[]{:S(2)}) collective-permute-start(bf16[128,512]{1,0:T(8,128)(2,1)S(1)} %get-tuple-element.39), channel_id=1, source_target_pairs={{0,3},{1,0},{2,1},{3,2},{4,7},{5,4},{6,5},{7,6},{8,11},{9,8},{10,9... | collective-permute-start | bytes 393224 | tf_op jit(solution)/shard_map/ppermute | solution.py:128
  106.7 11.9 %collective-permute-start.8 = (bf16[128,512]{1,0:T(8,128)(2,1)S(1)}, bf16[128,512]{1,0:T(8,128)(2,1)}, u32[]{:S(2)}, u32[]{:S(2)}) collective-permute-start(bf16[128,512]{1,0:T(8,128)(2,1)S(1)} %get-tuple-element.40), channel_id=1, source_target_pairs={{0,2},{1,3},{2,0},{3,1},{4,6},{5,7},{6,4},{7,5},{8,10},{9,11},{10,... | collective-permute-start | bytes 393224 | tf_op jit(solution)/shard_map/ppermute | solution.py:128
  107.9 7.4 %copy-start.14 = (s32[1,1,4]{2,1,0:T(1,128)S(1)}, s32[1,1,4]{2,1,0:T(1,128)}, u32[]{:S(2)}) copy-start(s32[1,1,4]{2,1,0:T(1,128)} %param.12) | copy-start | bytes 52
  107.9 10.7 %collective-permute-start.7 = (bf16[128,512]{1,0:T(8,128)(2,1)S(1)}, bf16[128,512]{1,0:T(8,128)(2,1)}, u32[]{:S(2)}, u32[]{:S(2)}) collective-permute-start(bf16[128,512]{1,0:T(8,128)(2,1)S(1)} %get-tuple-element.41), channel_id=1, source_target_pairs={{0,1},{1,2},{2,3},{3,0},{4,5},{5,6},{6,7},{7,4},{8,9},{9,10},{10,1... | collective-permute-start | bytes 393224 | tf_op jit(solution)/shard_map/ppermute | solution.py:128
  122.5 1.6 %copy-start.11 = (bf16[11,138,128]{2,0,1:T(8,128)(2,1)S(1)}, bf16[11,138,128]{2,0,1:T(8,128)(2,1)}, u32[]{:S(2)}) copy-start(bf16[11,138,128]{2,0,1:T(8,128)(2,1)} %get-tuple-element.19) | copy-start | bytes 1165828
  122.5 2.0 %copy-start.10 = (bf16[11,138,128]{2,0,1:T(8,128)(2,1)S(1)}, bf16[11,138,128]{2,0,1:T(8,128)(2,1)}, u32[]{:S(2)}) copy-start(bf16[11,138,128]{2,0,1:T(8,128)(2,1)} %get-tuple-element.20) | copy-start | bytes 1165828
  124.1 1.1 copy-start.9
  124.5 1.1 copy-start.8
  125.2 1.1 copy-start.7
  125.6 1.1 copy-start.6
  126.3 1.1 copy-start.5
  126.7 1.1 copy-start.4
  127.4 1.1 copy-start.3
  127.8 1.1 copy-start.2
  128.5 1.1 copy-start.1
  131.2 1.0 copy-start.12
  131.2 1.2 copy-start.13

commit v12 on v10

--- a/solution.py
+++ b/solution.py
@@ -17,11 +17,11 @@
 
 
 def local_coadd(values, weights):
-    root_weight = jnp.sqrt(weights)
     coadd_field = jnp.sum(weights * values, axis=0) / jnp.sum(weights, axis=0)
+    square = CAUCHY * CAUCHY
     for _ in range(PASSES):
-        scaled = (values - coadd_field[None]) * root_weight / CAUCHY
-        cauchy = weights / (1.0 + scaled * scaled)
+        offset = values - coadd_field[None]
+        cauchy = (square * weights) / (square + offset * offset * weights)
         coadd_field = jnp.sum(cauchy * values, axis=0) / jnp.sum(cauchy, axis=0)
     return coadd_field
 
@@ -49,7 +49,7 @@
     return tuple(banded_all[r, c] for r in range(blocks) for c in range(blocks))
 
 
-def psf_match(blotted, bands):
+def psf_outlier(blotted, bands, science_tile, sigma_tile):
     tile_side = blotted.shape[1]
     blocks = tile_side // CELL
     half_width = KSIZE // 2
@@ -72,7 +72,14 @@
             summed = horizontal[0, 0:CELL, :]
             for tap_row in range(1, KSIZE):
                 summed = summed + horizontal[tap_row, tap_row : tap_row + CELL, :]
-            col_parts.append(summed)
+            rows = slice(row_block * CELL, (row_block + 1) * CELL)
+            cols = slice(col_block * CELL, (col_block + 1) * CELL)
+            residual = (
+                (science_tile[rows, cols].astype(jnp.float32) - summed)
+                * sigma_tile[rows, cols].astype(jnp.float32)
+                / OUTLIER
+            )
+            col_parts.append(1.0 / (1.0 + residual * residual))
         row_parts.append(jnp.concatenate(col_parts, axis=1))
     return jnp.concatenate(row_parts, axis=0)
 
@@ -135,13 +142,7 @@
     blotted = jnp.dot(projected, col_interp[0, 0], preferred_element_type=jnp.float32).astype(
         jnp.bfloat16
     )
-    matched = psf_match(blotted, bands)
-    residual = (
-        (science[0, 0].astype(jnp.float32) - matched)
-        * inv_sigma[0, 0].astype(jnp.float32)
-        / OUTLIER
-    )
-    outlier = 1.0 / (1.0 + residual * residual)
+    outlier = psf_outlier(blotted, bands, science[0, 0], inv_sigma[0, 0])
     return (coadd_field, outlier[None, None])
 
 

time: 123 us -> 123 us (level)
  other arithmetic: 9.72 us -> 8.41 us
    reduce_sum x3, other arithmetic: 3.96 us -> 2.59 us  [local_coadd(): coadd_field = jnp.sum(cauchy * values, axis=0) / jnp.sum(cauchy, axis=0)]
    unnamed x40 -> x38, local copies, waits for them, and re-layouts: 4.63 us -> 4.47 us
where the time goes in v12:
time: 123 us; the launch traced here: 122 us
  blocking collectives  60.3 us (49%)
  matrix products  16.3 us (13%)
  local copies, waits for them, and re-layouts  15.7 us (13%)
  between operations  11.7 us (10%)
  other arithmetic  8.41 us (7%)
  starting transfers between devices  5.39 us (4%)
  waiting for transfers between devices  4.63 us (4%)
    all_to_all x1, blocking collectives, shards(): lax.all_to_all(stacked, 'visit', split_axis=2, concat_axis=1, tiled=True)  55.3 us
    dot_general x16, matrix products, psf_outlier(): jnp.einsum('rc,acl->arl', cols_window, bands[row_block * blocks + col_blo...  7.42 us
    squeeze x1, local copies, waits for them, and re-layouts, psf_bands(): banded_all[r, c]  6.52 us
    dot_general x1, matrix products, psf_bands(): jnp.einsum('xyab,bcl->xyacl', tap_rows, diagonal, preferred_element_type=...  5.97 us
    unnamed x1, blocking collectives  4.97 us
    all_to_all x1, waiting for transfers between devices, shards(): lax.all_to_all(copies, 'visit', split_axis=0, concat_axis=0, tiled=True)  4.63 us
    unnamed x38, local copies, waits for them, and re-layouts  4.47 us
    all_to_all x1, starting transfers between devices, shards(): lax.all_to_all(copies, 'visit', split_axis=0, concat_axis=0, tiled=True)  3.59 us
  transfers between devices with their start and end apart: 4, of which 1 were waited for; matrix products, arithmetic and copies ran while one was open for 12% of the time, Pallas kernels for 0%

profile of v12, /device:TPU:0, one launch (start us, length us, event | category | flops | bytes accessed | tf_op | source)
XLA Modules:
  0.0 122.4 jit_solution(11809329229682959563)
XLA Ops:
  0.6 0.8 eq.36
  1.5 0.9 convolution_convert_fusion.3
  2.3 0.1 reshape.124
  2.4 1.7 %pad_maximum_fusion = bf16[2,2,128,2048]{3,2,1,0:T(8,128)(2,1)S(1)} fusion(bf16[1,2,128,2048]{3,2,1,0:T(8,128)(2,1)} %bitcast.410, bf16[1,2,128,2048]{3,2,1,0:T(8,128)(2,1)} %bitcast.411), kind=kLoop, calls=%fused_computation.26 | loop fusion | flops 1048576 | bytes 4194304 | tf_op jit(solution)/shard_map/stack | solution.py:102
  4.2 0.2 copy.60
  4.4 55.3 %all_to_all.20 = bf16[2,2,8,16,2048]{4,3,1,0,2:T(8,128)(2,1)S(1)} all-to-all(bf16[2,2,8,16,2048]{4,3,1,0,2:T(8,128)(2,1)S(1)} %copy.60), channel_id=1, replica_groups=mesh['visit'=8,'sky'=4] {'visit'}, dimensions={2} | all-to-all | bytes 4194304 | tf_op jit(solution)/shard_map/all_to_all | solution.py:107
  59.7 0.4 convert_reduce_fusion
  60.2 0.9 fusion.15
  61.1 0.9 fusion.16
  62.0 0.9 fusion.17
  62.9 1.1 broadcast_in_dim.4
  64.0 3.6 %all-to-all-start.1 = ((f32[8,16,2048]{2,1,0:T(8,128)}), f32[8,16,2048]{2,1,0:T(8,128)S(1)}, u32[]{:S(2)}, u32[]{:S(2)}) async-start(f32[8,16,2048]{2,1,0:T(8,128)} %broadcast_in_dim.4), calls=%async_computation.1 | async-start | bytes 2097152 | tf_op jit(solution)/shard_map/all_to_all | solution.py:111
  68.2 0.6 dynamic-slice
  68.8 0.7 bitcast_dynamic-update-slice_fusion
  69.5 5.0 %all-reduce.1 = s32[4]{0:T(128)S(1)} all-reduce(s32[4]{0:T(128)S(1)} %bitcast_dynamic-update-slice_fusion), channel_id=2, replica_groups=mesh['visit'=8,'sky'=4] {'sky'}, use_global_device_ids=true, to_apply=%add.1 | all-reduce | flops 4 | bytes 32
  74.5 0.7 fusion.206
  82.5 6.0 %convolution_convert_fusion = bf16[4,4,11,138,128]{4,2,3,1,0:T(8,128)(2,1)} fusion(s32[138,128]{1,0:T(8,128)S(1)} %iota_subtract_fusion, bf16[4,4,11,11]{3,2,1,0:T(8,128)(2,1)S(1)} %reshape.124), kind=kOutput, calls=%fused_computation | convolution fusion | flops 71698176 | bytes 6292256 | tf_op jit(solution)/shard_map/xyab,bcl->xyacl/dot_general | solution.py:46
  88.5 4.6 %all-to-all-done.1 = f32[8,16,2048]{2,1,0:T(8,128)S(1)} async-done(((f32[8,16,2048]{2,1,0:T(8,128)}), f32[8,16,2048]{2,1,0:T(8,128)S(1)}, u32[]{:S(2)}, u32[]{:S(2)}) %all-to-all-start.1) | async-done | bytes 1048608 | tf_op jit(solution)/shard_map/all_to_all | solution.py:111
  93.2 0.3 dynamic-slice_bitcast_fusion.10
  93.7 1.6 %collective-permute-start.1 = (bf16[128,512]{1,0:T(8,128)(2,1)S(1)}, bf16[128,512]{1,0:T(8,128)(2,1)S(1)}, u32[]{:S(2)}, u32[]{:S(2)}) collective-permute-start(bf16[128,512]{1,0:T(8,128)(2,1)S(1)} %get-tuple-element.36), channel_id=1, source_target_pairs={{0,2},{1,3},{2,0},{3,1},{4,6},{5,7},{6,4},{7,5},{8,10},{9,11},{10,... | collective-permute-start | bytes 393224 | tf_op jit(solution)/shard_map/ppermute | solution.py:126
  95.3 0.2 collective-permute-start
  95.4 6.5 %slice_bitcast_fusion.15 = (bf16[11,138,128]{2,0,1:T(8,128)(2,1)}, bf16[11,138,128]{2,0,1:T(8,128)(2,1)}, bf16[11,138,128]{2,0,1:T(8,128)(2,1)}, bf16[11,138,128...) fusion(bf16[4,4,11,138,128]{4,2,3,1,0:T(8,128)(2,1)} %convoluti, ...), kind=kLoop, calls=%fused_computation.79 | loop fusion | bytes 12435456 | tf_op jit(solution)/shard_map/squeeze | solution.py:49
  102.0 0.7 fusion.205
  105.2 1.0 pad_maximum_fusion.2
  106.2 0.7 dynamic-slice_bitcast_fusion.3
  107.0 2.0 %convolution_convert_fusion.1 = bf16[512,512]{1,0:T(8,128)(2,1)S(1)} fusion(bf16[128,512]{1,0:T(8,128)(2,1)S(1)} %get-tuple-element.31, bf16[128,512]{1,0:T(8,128)(2,1)} %get-tuple-element.32, bf16[128,512]{1,0:T(8,128)(2,1)} %get-tuple-element.33, bf16[128,512]{1,0:T(8,128)(2,1)S(1)} %get-tuple-element.30, bf16[1,1,512,512]{3,2,1,0:T(8,128)(2,1)S(1)} %copy-done, ...), kind=kOutput, calls=%fused_computation.43 | convolution fusion | flops 539492352 | bytes 2097152 | tf_op jit(solution)/shard_map/dot_general | solution.py:142
  109.0 1.5 %convolution_bitcast_fusion.15 = f32[11,138,128]{2,1,0:T(8,128)S(1)} fusion(bf16[11,138,128]{2,0,1:T(8,128)(2,1)} %get-tuple-element.14, bf16[512,512]{1,0:T(8,128)(2,1)S(1)} %convolution_convert_fusion.1), kind=kOutput, calls=%fused_computation.42 | convolution fusion | flops 53627904 | bytes 1690112 | tf_op jit(solution)/shard_map/rc,acl->arl/dot_general | solution.py:66
  110.5 1.4 %convolution_bitcast_fusion = f32[11,138,128]{2,1,0:T(8,128)S(1)} fusion(bf16[11,138,128]{2,0,1:T(8,128)(2,1)} %get-tuple-element.15, bf16[512,512]{1,0:T(8,128)(2,1)S(1)} %convolution_convert_fusion.1), kind=kOutput, calls=%fused_computation.27 | convolution fusion | flops 53627904 | bytes 1690112 | tf_op jit(solution)/shard_map/rc,acl->arl/dot_general | solution.py:66
  112.0 0.1 fusion.187
  112.1 0.1 fusion.82
  112.2 0.3 convolution_bitcast_fusion.1
  112.5 0.1 fusion.89
  112.6 0.4 copy-done.11
  113.0 0.3 convolution_bitcast_fusion.2
  113.4 0.1 fusion.96
  113.5 0.2 copy-done.10
  113.6 0.3 convolution_bitcast_fusion.3
  113.9 0.1 fusion.103
  114.0 0.4 copy-done.9
  114.5 0.3 convolution_bitcast_fusion.4
  114.8 0.1 fusion.110
  114.9 0.2 copy-done.8
  115.0 0.3 convolution_bitcast_fusion.5
  115.4 0.1 fusion.117
  115.6 0.3 convolution_bitcast_fusion.6
  115.9 0.1 fusion.124
  116.0 0.2 copy-done.6
  116.1 0.3 convolution_bitcast_fusion.7
  116.5 0.1 fusion.131
  116.7 0.3 convolution_bitcast_fusion.8
  117.0 0.1 fusion.138
  117.1 0.5 copy-done.4
  117.6 0.3 convolution_bitcast_fusion.9
  117.9 0.1 fusion.145
  118.0 0.3 convolution_bitcast_fusion.10
  118.3 0.1 fusion.152
  118.4 0.2 copy-done.2
  118.7 0.3 convolution_bitcast_fusion.11
  119.0 0.1 fusion.159
  119.1 0.3 convolution_bitcast_fusion.12
  119.5 0.3 convolution_bitcast_fusion.13
  120.0 0.3 convolution_bitcast_fusion.14
  120.4 1.0 maximum_bitcast_fusion
  121.4 1.0 copy.114
  (43 shorter events, 0.9 us)
Async XLA Ops:
  0.6 106.3 %copy-start = (bf16[1,1,512,512]{3,2,1,0:T(8,128)(2,1)S(1)}, bf16[1,1,512,512]{3,2,1,0:T(8,128)(2,1)}, u32[]{:S(2)}) copy-start(bf16[1,1,512,512]{3,2,1,0:T(8,128)(2,1)} %param.15) | copy-start | bytes 1572868
  62.8 5.4 %copy-start.16 = (u32[32]{0:T(128)S(1)}, u32[32]{0:T(128)}, u32[]{:S(2)}) copy-start(u32[32]{0:T(128)} %constant.107) | copy-start | bytes 388
  64.0 29.2 %all-to-all-start.1 = ((f32[8,16,2048]{2,1,0:T(8,128)}), f32[8,16,2048]{2,1,0:T(8,128)S(1)}, u32[]{:S(2)}, u32[]{:S(2)}) async-start(f32[8,16,2048]{2,1,0:T(8,128)} %broadcast_in_dim.4), calls=%async_computation.1 | async-start | bytes 2097152 | tf_op jit(solution)/shard_map/all_to_all | solution.py:111
  93.6 11.6 %collective-permute-start.2 = (bf16[128,512]{1,0:T(8,128)(2,1)S(1)}, bf16[128,512]{1,0:T(8,128)(2,1)S(1)}, u32[]{:S(2)}, u32[]{:S(2)}) collective-permute-start(bf16[128,512]{1,0:T(8,128)(2,1)S(1)} %get-tuple-element.35), channel_id=1, source_target_pairs={{0,3},{1,0},{2,1},{3,2},{4,7},{5,4},{6,5},{7,6},{8,11},{9,8},{10,9... | collective-permute-start | bytes 393224 | tf_op jit(solution)/shard_map/ppermute | solution.py:126
  93.7 11.5 %collective-permute-start.1 = (bf16[128,512]{1,0:T(8,128)(2,1)S(1)}, bf16[128,512]{1,0:T(8,128)(2,1)S(1)}, u32[]{:S(2)}, u32[]{:S(2)}) collective-permute-start(bf16[128,512]{1,0:T(8,128)(2,1)S(1)} %get-tuple-element.36), channel_id=1, source_target_pairs={{0,2},{1,3},{2,0},{3,1},{4,6},{5,7},{6,4},{7,5},{8,10},{9,11},{10,... | collective-permute-start | bytes 393224 | tf_op jit(solution)/shard_map/ppermute | solution.py:126
  95.3 6.7 %copy-start.15 = (s32[1,1,4]{2,1,0:T(1,128)S(1)}, s32[1,1,4]{2,1,0:T(1,128)}, u32[]{:S(2)}) copy-start(s32[1,1,4]{2,1,0:T(1,128)} %param.12) | copy-start | bytes 52
  95.3 10.0 %collective-permute-start = (bf16[128,512]{1,0:T(8,128)(2,1)S(1)}, bf16[128,512]{1,0:T(8,128)(2,1)}, u32[]{:S(2)}, u32[]{:S(2)}) collective-permute-start(bf16[128,512]{1,0:T(8,128)(2,1)S(1)} %get-tuple-element.37), channel_id=1, source_target_pairs={{0,1},{1,2},{2,3},{3,0},{4,5},{5,6},{6,7},{7,4},{8,9},{9,10},{10,1... | collective-permute-start | bytes 393224 | tf_op jit(solution)/shard_map/ppermute | solution.py:126
  109.0 3.0 %copy-start.13 = (bf16[1,1,512,512]{3,2,1,0:T(8,128)(2,1)S(1)}, bf16[1,1,512,512]{3,2,1,0:T(8,128)(2,1)}, u32[]{:S(2)}) copy-start(bf16[1,1,512,512]{3,2,1,0:T(8,128)(2,1)} %param.19) | copy-start | bytes 1572868
  109.0 3.0 %copy-start.14 = (bf16[1,1,512,512]{3,2,1,0:T(8,128)(2,1)S(1)}, bf16[1,1,512,512]{3,2,1,0:T(8,128)(2,1)}, u32[]{:S(2)}) copy-start(bf16[1,1,512,512]{3,2,1,0:T(8,128)(2,1)} %param.18) | copy-start | bytes 1572868
  110.5 1.7 %copy-start.12 = (bf16[11,138,128]{2,0,1:T(8,128)(2,1)S(1)}, bf16[11,138,128]{2,0,1:T(8,128)(2,1)}, u32[]{:S(2)}) copy-start(bf16[11,138,128]{2,0,1:T(8,128)(2,1)} %get-tuple-element.16) | copy-start | bytes 1165828
  112.0 1.1 copy-start.11
  112.5 1.1 copy-start.10
  113.4 1.1 copy-start.9
  113.9 1.1 copy-start.8
  114.5 1.1 copy-start.7
  115.0 1.1 copy-start.6
  115.5 1.1 copy-start.5
  116.5 1.1 copy-start.4
  116.6 1.3 %copy-start.3 = (bf16[11,138,128]{2,0,1:T(8,128)(2,1)S(1)}, bf16[11,138,128]{2,0,1:T(8,128)(2,1)}, u32[]{:S(2)}) copy-start(bf16[11,138,128]{2,0,1:T(8,128)(2,1)} %get-tuple-element.25) | copy-start | bytes 1165828
  117.6 1.1 copy-start.2
  118.0 1.1 copy-start.1

commit v13 on v12

--- a/solution.py
+++ b/solution.py
@@ -55,10 +55,9 @@
     half_width = KSIZE // 2
     window = CELL + KSIZE - 1
     padded = jnp.pad(blotted, ((half_width, half_width), (half_width, half_width)))
-    row_parts = []
+    outlier = jnp.zeros((tile_side, tile_side), jnp.float32)
     for row_block in range(blocks):
         rows_window = lax.slice_in_dim(padded, row_block * CELL, row_block * CELL + window, axis=0)
-        col_parts = []
         for col_block in range(blocks):
             cols_window = lax.slice_in_dim(
                 rows_window, col_block * CELL, col_block * CELL + window, axis=1
@@ -79,9 +78,10 @@
                 * sigma_tile[rows, cols].astype(jnp.float32)
                 / OUTLIER
             )
-            col_parts.append(1.0 / (1.0 + residual * residual))
-        row_parts.append(jnp.concatenate(col_parts, axis=1))
-    return jnp.concatenate(row_parts, axis=0)
+            outlier = lax.dynamic_update_slice(
+                outlier, 1.0 / (1.0 + residual * residual), (row_block * CELL, col_block * CELL)
+            )
+    return outlier
 
 
 def shards(
@@ -127,15 +127,15 @@
                 outgoing, "sky", perm=[(i, (i + shift) % n_sky) for i in range(n_sky)]
             )
         )
-    received = jnp.stack(received, axis=0)
     strips = intersection[0, 0]
-    footprint = jnp.concatenate(
-        [
-            lax.dynamic_index_in_dim(received, (me - strips[slot]) % n_sky, 0, keepdims=False)
-            for slot in range(NOV)
-        ],
-        axis=0,
-    )
+    slots = []
+    for slot in range(NOV):
+        shift_of = (me - strips[slot]) % n_sky
+        chosen = received[0]
+        for shift in range(1, n_sky):
+            chosen = jnp.where(shift_of == shift, received[shift], chosen)
+        slots.append(chosen)
+    footprint = jnp.concatenate(slots, axis=0)
     projected = jnp.dot(row_interp[0, 0], footprint, preferred_element_type=jnp.float32).astype(
         jnp.bfloat16
     )

time: 123 us -> 124 us (level)
    select_n x0 -> x1, other arithmetic: none -> 1.8 us  [shards(): chosen = jnp.where(shift_of == shift, received[shift], chosen)]
    dynamic_update_slice x0 -> x15, other arithmetic: none -> 1.37 us  [psf_outlier(): lax.dynamic_update_slice(outlier, 1.0 / (1.0 + residual * residual), (row...]
    div x16 -> x1, other arithmetic: 1.45 us -> 0.09 us  [psf_outlier(): 1.0 / (1.0 + residual * residual)]
    unnamed x38 -> x40, local copies, waits for them, and re-layouts: 4.47 us -> 3.94 us
where the time goes in v13:
time: 124 us; the launch traced here: 123 us
  blocking collectives  60.3 us (49%)
  matrix products  16.3 us (13%)
  local copies, waits for them, and re-layouts  15.1 us (12%)
  between operations  12.1 us (10%)
  other arithmetic  8.2 us (7%)
  starting transfers between devices  6.58 us (5%)
  waiting for transfers between devices  4.26 us (3%)
    all_to_all x1, blocking collectives, shards(): lax.all_to_all(stacked, 'visit', split_axis=2, concat_axis=1, tiled=True)  55.3 us
    dot_general x16, matrix products, psf_outlier(): jnp.einsum('rc,acl->arl', cols_window, bands[row_block * blocks + col_blo...  7.39 us
    squeeze x1, local copies, waits for them, and re-layouts, psf_bands(): banded_all[r, c]  6.52 us
    dot_general x1, matrix products, psf_bands(): jnp.einsum('xyab,bcl->xyacl', tap_rows, diagonal, preferred_element_type=...  5.98 us
    unnamed x1, blocking collectives  4.97 us
    all_to_all x1, waiting for transfers between devices, shards(): lax.all_to_all(copies, 'visit', split_axis=0, concat_axis=0, tiled=True)  4.25 us
    unnamed x40, local copies, waits for them, and re-layouts  3.94 us
    all_to_all x1, starting transfers between devices, shards(): lax.all_to_all(copies, 'visit', split_axis=0, concat_axis=0, tiled=True)  3.59 us
  transfers between devices with their start and end apart: 4, of which 1 were waited for; matrix products, arithmetic and copies ran while one was open for 12% of the time, Pallas kernels for 0%

profile of v13, /device:TPU:0, one launch (start us, length us, event | category | flops | bytes accessed | tf_op | source)
XLA Modules:
  0.0 122.9 jit_solution(11973358074918394093)
XLA Ops:
  0.6 0.8 eq.72
  1.5 0.9 convolution_convert_fusion.3
  2.3 0.1 reshape.154
  2.4 1.7 %pad_maximum_fusion = bf16[2,2,128,2048]{3,2,1,0:T(8,128)(2,1)S(1)} fusion(bf16[1,2,128,2048]{3,2,1,0:T(8,128)(2,1)} %bitcast.480, bf16[1,2,128,2048]{3,2,1,0:T(8,128)(2,1)} %bitcast.481), kind=kLoop, calls=%fused_computation.26 | loop fusion | flops 1048576 | bytes 4194304 | tf_op jit(solution)/shard_map/stack | solution.py:102
  4.2 0.2 copy.60
  4.4 55.3 %all_to_all.20 = bf16[2,2,8,16,2048]{4,3,1,0,2:T(8,128)(2,1)S(1)} all-to-all(bf16[2,2,8,16,2048]{4,3,1,0,2:T(8,128)(2,1)S(1)} %copy.60), channel_id=1, replica_groups=mesh['visit'=8,'sky'=4] {'visit'}, dimensions={2} | all-to-all | bytes 4194304 | tf_op jit(solution)/shard_map/all_to_all | solution.py:107
  59.7 0.4 convert_reduce_fusion
  60.2 0.9 fusion.15
  61.1 0.9 fusion.16
  62.0 0.9 fusion.17
  62.9 1.1 broadcast_in_dim.48
  64.0 3.6 %all-to-all-start.1 = ((f32[8,16,2048]{2,1,0:T(8,128)}), f32[8,16,2048]{2,1,0:T(8,128)S(1)}, u32[]{:S(2)}, u32[]{:S(2)}) async-start(f32[8,16,2048]{2,1,0:T(8,128)} %broadcast_in_dim.48), calls=%async_computation.1 | async-start | bytes 2097152 | tf_op jit(solution)/shard_map/all_to_all | solution.py:111
  68.2 0.6 dynamic-slice
  68.8 0.7 bitcast_dynamic-update-slice_fusion.15
  69.5 5.0 %all-reduce.2 = s32[4]{0:T(128)S(1)} all-reduce(s32[4]{0:T(128)S(1)} %bitcast_dynamic-update-slice_fusion.15), channel_id=2, replica_groups=mesh['visit'=8,'sky'=4] {'sky'}, use_global_device_ids=true, to_apply=%add.2 | all-reduce | flops 4 | bytes 32
  74.5 0.7 fusion.214
  82.9 6.0 %convolution_convert_fusion = bf16[4,4,11,138,128]{4,2,3,1,0:T(8,128)(2,1)} fusion(s32[138,128]{1,0:T(8,128)S(1)} %iota_subtract_fusion, bf16[4,4,11,11]{3,2,1,0:T(8,128)(2,1)S(1)} %reshape.154), kind=kOutput, calls=%fused_computation | convolution fusion | flops 71698176 | bytes 6292256 | tf_op jit(solution)/shard_map/xyab,bcl->xyacl/dot_general | solution.py:46
  88.9 4.3 %all-to-all-done.1 = f32[8,16,2048]{2,1,0:T(8,128)S(1)} async-done(((f32[8,16,2048]{2,1,0:T(8,128)}), f32[8,16,2048]{2,1,0:T(8,128)S(1)}, u32[]{:S(2)}, u32[]{:S(2)}) %all-to-all-start.1) | async-done | bytes 1048608 | tf_op jit(solution)/shard_map/all_to_all | solution.py:111
  93.2 0.3 dynamic-slice_bitcast_fusion.6
  93.6 0.7 dynamic-slice_bitcast_fusion
  94.3 1.5 %collective-permute-start.1 = (bf16[128,512]{1,0:T(8,128)(2,1)S(1)}, bf16[128,512]{1,0:T(8,128)(2,1)}, u32[]{:S(2)}, u32[]{:S(2)}) collective-permute-start(bf16[128,512]{1,0:T(8,128)(2,1)S(1)} %get-tuple-element.35), channel_id=1, source_target_pairs={{0,2},{1,3},{2,0},{3,1},{4,6},{5,7},{6,4},{7,5},{8,10},{9,11},{10,... | collective-permute-start | bytes 393224 | tf_op jit(solution)/shard_map/ppermute | solution.py:126
  95.8 1.5 %collective-permute-start = (bf16[128,512]{1,0:T(8,128)(2,1)S(1)}, bf16[128,512]{1,0:T(8,128)(2,1)}, u32[]{:S(2)}, u32[]{:S(2)}) collective-permute-start(bf16[128,512]{1,0:T(8,128)(2,1)S(1)} %get-tuple-element.36), channel_id=1, source_target_pairs={{0,3},{1,0},{2,1},{3,2},{4,7},{5,4},{6,5},{7,6},{8,11},{9,8},{10,9... | collective-permute-start | bytes 393224 | tf_op jit(solution)/shard_map/ppermute | solution.py:126
  97.3 6.5 %slice_bitcast_fusion = (bf16[11,138,128]{2,0,1:T(8,128)(2,1)}, bf16[11,138,128]{2,0,1:T(8,128)(2,1)}, bf16[11,138,128]{2,0,1:T(8,128)(2,1)}, bf16[11,138,128]{2...) fusion(bf16[4,4,11,138,128]{4,2,3,1,0:T(8,128)(2,1)} %convoluti, ...), kind=kLoop, calls=%fused_computation.64 | loop fusion | bytes 12435456 | tf_op jit(solution)/shard_map/squeeze | solution.py:49
  103.8 0.7 fusion.213
  107.1 1.8 %fusion.53 = (bf16[128,512]{1,0:T(8,128)(2,1)S(1)}, bf16[128,512]{1,0:T(8,128)(2,1)S(1)}, bf16[128,512]{1,0:T(8,128)(2,1)}, bf16[128,512]{1,0:T(8,128)(2,1)}) fusion(bf16[128,512]{1,0:T(8,128)(2,1)} %collective-permute-done, bf16[128,512]{1,0:T(8,128)(2,1)} %collective-permute-done.1, bf16[128,512]{1,0:T(8,128)(2,1)} %collective-permute-done.2, ...), kind=kLoop, calls=%fused_computation.112 | loop fusion | flops 786432 | bytes 1048592 | tf_op jit(solution)/shard_map/jit(_where)/select_n | solution.py:136
  108.9 2.0 %convolution_convert_fusion.1 = bf16[512,512]{1,0:T(8,128)(2,1)S(1)} fusion(bf16[128,512]{1,0:T(8,128)(2,1)S(1)} %get-tuple-element.31, bf16[128,512]{1,0:T(8,128)(2,1)} %get-tuple-element.32, bf16[128,512]{1,0:T(8,128)(2,1)} %get-tuple-element.33, bf16[128,512]{1,0:T(8,128)(2,1)S(1)} %get-tuple-element.30, bf16[1,1,512,512]{3,2,1,0:T(8,128)(2,1)S(1)} %copy-done, ...), kind=kOutput, calls=%fused_computation.43 | convolution fusion | flops 539492352 | bytes 2097152 | tf_op jit(solution)/shard_map/dot_general | solution.py:142
  111.0 1.4 %convolution_bitcast_fusion = f32[11,138,128]{2,1,0:T(8,128)S(1)} fusion(bf16[11,138,128]{2,0,1:T(8,128)(2,1)} %get-tuple-element.14, bf16[512,512]{1,0:T(8,128)(2,1)S(1)} %convolution_convert_fusion.1), kind=kOutput, calls=%fused_computation.27 | convolution fusion | flops 53627904 | bytes 1690112 | tf_op jit(solution)/shard_map/rc,acl->arl/dot_general | solution.py:65
  112.4 1.4 %convolution_bitcast_fusion.1 = f32[11,138,128]{2,1,0:T(8,128)S(1)} fusion(bf16[11,138,128]{2,0,1:T(8,128)(2,1)} %get-tuple-element.15, bf16[512,512]{1,0:T(8,128)(2,1)S(1)} %convolution_convert_fusion.1), kind=kOutput, calls=%fused_computation.28 | convolution fusion | flops 53627904 | bytes 1690112 | tf_op jit(solution)/shard_map/rc,acl->arl/dot_general | solution.py:65
  113.9 0.3 convolution_bitcast_fusion.2
  114.2 0.3 convolution_bitcast_fusion.3
  114.6 0.4 copy-done.10
  114.9 0.3 convolution_bitcast_fusion.4
  115.3 0.3 convolution_bitcast_fusion.5
  115.7 0.3 convolution_bitcast_fusion.6
  116.1 0.3 convolution_bitcast_fusion.7
  116.5 0.3 convolution_bitcast_fusion.8
  116.8 0.3 convolution_bitcast_fusion.9
  117.2 0.3 convolution_bitcast_fusion.10
  117.6 0.3 convolution_bitcast_fusion.11
  117.9 0.3 convolution_bitcast_fusion.12
  118.3 0.3 convolution_bitcast_fusion.13
  118.7 0.3 convolution_bitcast_fusion.14
  119.0 0.3 convolution_bitcast_fusion.15
  119.4 0.4 copy-done.14
  119.7 0.2 copy-done.15
  119.9 0.1 fusion.195
  120.0 0.1 pad_bitcast_fusion
  120.1 0.1 bitcast_dynamic-update-slice_fusion.14
  120.2 0.1 bitcast_dynamic-update-slice_fusion.13
  120.3 0.1 bitcast_dynamic-update-slice_fusion.12
  120.4 0.1 bitcast_dynamic-update-slice_fusion.11
  120.5 0.1 bitcast_dynamic-update-slice_fusion.10
  120.6 0.1 bitcast_dynamic-update-slice_fusion.9
  120.7 0.1 bitcast_dynamic-update-slice_fusion.8
  120.8 0.1 bitcast_dynamic-update-slice_fusion.7
  120.9 0.1 bitcast_dynamic-update-slice_fusion.6
  121.0 0.1 bitcast_dynamic-update-slice_fusion.5
  121.1 0.1 bitcast_dynamic-update-slice_fusion.4
  121.2 0.1 bitcast_dynamic-update-slice_fusion.3
  121.3 0.1 bitcast_dynamic-update-slice_fusion.2
  121.4 0.1 bitcast_dynamic-update-slice_fusion.1
  121.5 0.1 bitcast_dynamic-update-slice_fusion
  121.6 1.0 copy.129
  122.6 0.3 copy-done.13
  (44 shorter events, 0.7 us)
Async XLA Ops:
  0.6 108.3 %copy-start = (bf16[1,1,512,512]{3,2,1,0:T(8,128)(2,1)S(1)}, bf16[1,1,512,512]{3,2,1,0:T(8,128)(2,1)}, u32[]{:S(2)}) copy-start(bf16[1,1,512,512]{3,2,1,0:T(8,128)(2,1)} %param.15) | copy-start | bytes 1572868
  62.8 5.4 %copy-start.17 = (u32[32]{0:T(128)S(1)}, u32[32]{0:T(128)}, u32[]{:S(2)}) copy-start(u32[32]{0:T(128)} %constant.123) | copy-start | bytes 388
  64.0 29.2 %all-to-all-start.1 = ((f32[8,16,2048]{2,1,0:T(8,128)}), f32[8,16,2048]{2,1,0:T(8,128)S(1)}, u32[]{:S(2)}, u32[]{:S(2)}) async-start(f32[8,16,2048]{2,1,0:T(8,128)} %broadcast_in_dim.48), calls=%async_computation.1 | async-start | bytes 2097152 | tf_op jit(solution)/shard_map/all_to_all | solution.py:111
  94.3 12.8 %collective-permute-start.2 = (bf16[128,512]{1,0:T(8,128)(2,1)}, bf16[128,512]{1,0:T(8,128)(2,1)}, u32[]{:S(2)}, u32[]{:S(2)}) collective-permute-start(bf16[128,512]{1,0:T(8,128)(2,1)} %get-tuple-element.34), channel_id=1, source_target_pairs={{0,1},{1,2},{2,3},{3,0},{4,5},{5,6},{6,7},{7,4},{8,9},{9,10},{10,1... | collective-permute-start | bytes 393224 | tf_op jit(solution)/shard_map/ppermute | solution.py:126
  94.3 12.8 %collective-permute-start.1 = (bf16[128,512]{1,0:T(8,128)(2,1)S(1)}, bf16[128,512]{1,0:T(8,128)(2,1)}, u32[]{:S(2)}, u32[]{:S(2)}) collective-permute-start(bf16[128,512]{1,0:T(8,128)(2,1)S(1)} %get-tuple-element.35), channel_id=1, source_target_pairs={{0,2},{1,3},{2,0},{3,1},{4,6},{5,7},{6,4},{7,5},{8,10},{9,11},{10,... | collective-permute-start | bytes 393224 | tf_op jit(solution)/shard_map/ppermute | solution.py:126
  95.8 8.0 %copy-start.16 = (s32[1,1,4]{2,1,0:T(1,128)S(1)}, s32[1,1,4]{2,1,0:T(1,128)}, u32[]{:S(2)}) copy-start(s32[1,1,4]{2,1,0:T(1,128)} %param.12) | copy-start | bytes 52
  95.8 11.3 %collective-permute-start = (bf16[128,512]{1,0:T(8,128)(2,1)S(1)}, bf16[128,512]{1,0:T(8,128)(2,1)}, u32[]{:S(2)}, u32[]{:S(2)}) collective-permute-start(bf16[128,512]{1,0:T(8,128)(2,1)S(1)} %get-tuple-element.36), channel_id=1, source_target_pairs={{0,3},{1,0},{2,1},{3,2},{4,7},{5,4},{6,5},{7,6},{8,11},{9,8},{10,9... | collective-permute-start | bytes 393224 | tf_op jit(solution)/shard_map/ppermute | solution.py:126
  111.0 2.9 %copy-start.12 = (bf16[11,138,128]{2,0,1:T(8,128)(2,1)S(1)}, bf16[11,138,128]{2,0,1:T(8,128)(2,1)}, u32[]{:S(2)}) copy-start(bf16[11,138,128]{2,0,1:T(8,128)(2,1)} %get-tuple-element.16) | copy-start | bytes 1165828
  112.4 1.8 %copy-start.11 = (bf16[11,138,128]{2,0,1:T(8,128)(2,1)S(1)}, bf16[11,138,128]{2,0,1:T(8,128)(2,1)}, u32[]{:S(2)}) copy-start(bf16[11,138,128]{2,0,1:T(8,128)(2,1)} %get-tuple-element.17) | copy-start | bytes 1165828
  113.9 1.1 copy-start.10
  114.2 1.1 copy-start.9
  114.2 1.4 %copy-start.8 = (bf16[11,138,128]{2,0,1:T(8,128)(2,1)S(1)}, bf16[11,138,128]{2,0,1:T(8,128)(2,1)}, u32[]{:S(2)}) copy-start(bf16[11,138,128]{2,0,1:T(8,128)(2,1)} %get-tuple-element.20) | copy-start | bytes 1165828
  114.9 1.1 copy-start.7
  115.3 1.1 copy-start.6
  115.6 1.1 copy-start.5
  116.1 1.1 copy-start.4
  116.5 1.1 copy-start.3
  116.8 1.1 copy-start.2
  117.2 1.1 copy-start.1
  118.7 1.0 copy-start.14
  118.7 1.2 copy-start.15
  121.6 1.3 %copy-start.13 = (f32[1,1,512,512]{3,2,1,0:T(8,128)}, f32[1,1,512,512]{3,2,1,0:T(8,128)S(1)}, u32[]{:S(2)}) copy-start(f32[1,1,512,512]{3,2,1,0:T(8,128)S(1)} %bitcast_dynamic-update-slice_fusion) | copy-start | bytes 3145732

commit v14 on v12

--- a/solution.py
+++ b/solution.py
@@ -55,10 +55,9 @@
     half_width = KSIZE // 2
     window = CELL + KSIZE - 1
     padded = jnp.pad(blotted, ((half_width, half_width), (half_width, half_width)))
-    row_parts = []
+    outlier = jnp.zeros((tile_side, tile_side), jnp.float32)
     for row_block in range(blocks):
         rows_window = lax.slice_in_dim(padded, row_block * CELL, row_block * CELL + window, axis=0)
-        col_parts = []
         for col_block in range(blocks):
             cols_window = lax.slice_in_dim(
                 rows_window, col_block * CELL, col_block * CELL + window, axis=1
@@ -79,9 +78,10 @@
                 * sigma_tile[rows, cols].astype(jnp.float32)
                 / OUTLIER
             )
-            col_parts.append(1.0 / (1.0 + residual * residual))
-        row_parts.append(jnp.concatenate(col_parts, axis=1))
-    return jnp.concatenate(row_parts, axis=0)
+            outlier = lax.dynamic_update_slice(
+                outlier, 1.0 / (1.0 + residual * residual), (row_block * CELL, col_block * CELL)
+            )
+    return outlier
 
 
 def shards(
@@ -127,6 +127,8 @@
                 outgoing, "sky", perm=[(i, (i + shift) % n_sky) for i in range(n_sky)]
             )
         )
+    coadd_out = jnp.where(coadd_field == coadd_field, coadd_field, 0.0)
+    received, coadd_out = lax.optimization_barrier((received, coadd_out))
     received = jnp.stack(received, axis=0)
     strips = intersection[0, 0]
     footprint = jnp.concatenate(
@@ -143,7 +145,7 @@
         jnp.bfloat16
     )
     outlier = psf_outlier(blotted, bands, science[0, 0], inv_sigma[0, 0])
-    return (coadd_field, outlier[None, None])
+    return (coadd_out, outlier[None, None])
 
 
 def solution(mesh):

time: 123 us -> 117 us (0.951)
  local copies, waits for them, and re-layouts: 15.7 us -> 10.7 us
  matrix products: 16.3 us -> 12.7 us
  waiting for transfers between devices: 4.63 us -> 7.52 us
    ppermute x3, waiting for transfers between devices: 0.01 us -> 5.88 us  [shards(): lax.ppermute(outgoing, 'sky', perm=[(i, (i + shift) % n_sky) for i in ran...]
    dot_general x1, matrix products: 5.97 us -> 2.49 us  [psf_bands(): jnp.einsum('xyab,bcl->xyacl', tap_rows, diagonal, preferred_element_type=...]
    squeeze x1, local copies, waits for them, and re-layouts: 6.52 us -> 3.13 us  [psf_bands(): banded_all[r, c]]
    all_to_all x1, waiting for transfers between devices: 4.63 us -> 1.64 us  [shards(): lax.all_to_all(copies, 'visit', split_axis=0, concat_axis=0, tiled=True)]
    dynamic_update_slice x0 -> x15, other arithmetic: none -> 1.41 us  [psf_outlier(): lax.dynamic_update_slice(outlier, 1.0 / (1.0 + residual * residual), (row...]
    div x16 -> x1, other arithmetic: 1.45 us -> 0.09 us  [psf_outlier(): 1.0 / (1.0 + residual * residual)]
    unnamed x38 -> x37, local copies, waits for them, and re-layouts: 4.47 us -> 3.5 us
  transfers between devices with their start and end apart: 4 -> 4, of which waited for: 1 -> 2; matrix products, arithmetic and copies ran while one was open for 12% -> 8% of each run, Pallas kernels for 0% -> 0%
where the time goes in v14:
time: 117 us; the launch traced here: 116 us
  blocking collectives  60.3 us (52%)
  matrix products  12.7 us (11%)
  between operations  11.8 us (10%)
  local copies, waits for them, and re-layouts  10.7 us (9%)
  other arithmetic  7.55 us (6%)
  waiting for transfers between devices  7.52 us (6%)
  starting transfers between devices  5.39 us (5%)
    all_to_all x1, blocking collectives, shards(): lax.all_to_all(stacked, 'visit', split_axis=2, concat_axis=1, tiled=True)  55.3 us
    dot_general x16, matrix products, psf_outlier(): jnp.einsum('rc,acl->arl', cols_window, bands[row_block * blocks + col_blo...  7.39 us
    ppermute x3, waiting for transfers between devices, shards(): lax.ppermute(outgoing, 'sky', perm=[(i, (i + shift) % n_sky) for i in ran...  5.88 us
    unnamed x1, blocking collectives  4.97 us
    all_to_all x1, starting transfers between devices, shards(): lax.all_to_all(copies, 'visit', split_axis=0, concat_axis=0, tiled=True)  3.59 us
    unnamed x37, local copies, waits for them, and re-layouts  3.5 us
    squeeze x1, local copies, waits for them, and re-layouts, psf_bands(): banded_all[r, c]  3.13 us
    reduce_sum x3, other arithmetic, local_coadd(): coadd_field = jnp.sum(cauchy * values, axis=0) / jnp.sum(cauchy, axis=0)  2.59 us
  transfers between devices with their start and end apart: 4, of which 2 were waited for; matrix products, arithmetic and copies ran while one was open for 8% of the time, Pallas kernels for 0%

profile of v14, /device:TPU:0, one launch (start us, length us, event | category | flops | bytes accessed | tf_op | source)
XLA Modules:
  0.0 115.9 jit_solution(7300980360163519323)
XLA Ops:
  0.6 0.8 eq.39
  1.5 0.9 convolution_convert_fusion.3
  2.3 0.1 reshape.154
  2.4 1.7 %pad_maximum_fusion = bf16[2,2,128,2048]{3,2,1,0:T(8,128)(2,1)S(1)} fusion(bf16[1,2,128,2048]{3,2,1,0:T(8,128)(2,1)} %bitcast.473, bf16[1,2,128,2048]{3,2,1,0:T(8,128)(2,1)} %bitcast.474), kind=kLoop, calls=%fused_computation.27 | loop fusion | flops 1048576 | bytes 4194304 | tf_op jit(solution)/shard_map/stack | solution.py:102
  4.2 0.2 copy.60
  4.4 55.3 %all_to_all.20 = bf16[2,2,8,16,2048]{4,3,1,0,2:T(8,128)(2,1)S(1)} all-to-all(bf16[2,2,8,16,2048]{4,3,1,0,2:T(8,128)(2,1)S(1)} %copy.60), channel_id=1, replica_groups=mesh['visit'=8,'sky'=4] {'visit'}, dimensions={2} | all-to-all | bytes 4194304 | tf_op jit(solution)/shard_map/all_to_all | solution.py:107
  59.7 0.4 convert_reduce_fusion
  60.2 0.9 fusion.15
  61.1 0.9 fusion.16
  62.0 0.9 fusion.17
  62.9 1.1 broadcast_in_dim.52
  64.0 3.6 %all-to-all-start.1 = ((f32[8,16,2048]{2,1,0:T(8,128)}), f32[8,16,2048]{2,1,0:T(8,128)S(1)}, u32[]{:S(2)}, u32[]{:S(2)}) async-start(f32[8,16,2048]{2,1,0:T(8,128)} %broadcast_in_dim.52), calls=%async_computation.1 | async-start | bytes 2097152 | tf_op jit(solution)/shard_map/all_to_all | solution.py:111
  68.2 0.6 dynamic-slice
  68.8 0.7 bitcast_dynamic-update-slice_fusion.15
  69.5 5.0 %all-reduce.2 = s32[4]{0:T(128)S(1)} all-reduce(s32[4]{0:T(128)S(1)} %bitcast_dynamic-update-slice_fusion.15), channel_id=2, replica_groups=mesh['visit'=8,'sky'=4] {'sky'}, use_global_device_ids=true, to_apply=%add.2 | all-reduce | flops 4 | bytes 32
  74.5 0.7 fusion.206
  80.1 0.7 fusion.205
  85.9 2.5 %convolution_convert_fusion = bf16[4,4,11,138,128]{4,2,3,1,0:T(8,128)(2,1)S(1)} fusion(s32[138,128]{1,0:T(8,128)S(1)} %iota_subtract_fusion, bf16[4,4,11,11]{3,2,1,0:T(8,128)(2,1)S(1)} %reshape.154), kind=kOutput, calls=%fused_computation | convolution fusion | flops 71698176 | bytes 6292256 | tf_op jit(solution)/shard_map/xyab,bcl->xyacl/dot_general | solution.py:46
  88.4 3.1 %slice_bitcast_fusion = (bf16[11,138,128]{2,0,1:T(8,128)(2,1)}, bf16[11,138,128]{2,0,1:T(8,128)(2,1)}, bf16[11,138,128]{2,0,1:T(8,128)(2,1)}, bf16[11,138,128]{2...) fusion(bf16[4,4,11,138,128]{4,2,3,1,0:T(8,128)(2,1)S(1)} %convo, ...), kind=kLoop, calls=%fused_computation.66 | loop fusion | bytes 12435456 | tf_op jit(solution)/shard_map/squeeze | solution.py:49
  91.5 1.6 %all-to-all-done.1 = f32[8,16,2048]{2,1,0:T(8,128)S(1)} async-done(((f32[8,16,2048]{2,1,0:T(8,128)}), f32[8,16,2048]{2,1,0:T(8,128)S(1)}, u32[]{:S(2)}, u32[]{:S(2)}) %all-to-all-start.1) | async-done | bytes 1048608 | tf_op jit(solution)/shard_map/all_to_all | solution.py:111
  93.2 0.3 dynamic-slice_bitcast_fusion.11
  93.7 1.6 %collective-permute-start.1 = (bf16[128,512]{1,0:T(8,128)(2,1)S(1)}, bf16[128,512]{1,0:T(8,128)(2,1)S(1)}, u32[]{:S(2)}, u32[]{:S(2)}) collective-permute-start(bf16[128,512]{1,0:T(8,128)(2,1)S(1)} %get-tuple-element.45), channel_id=1, source_target_pairs={{0,2},{1,3},{2,0},{3,1},{4,6},{5,7},{6,4},{7,5},{8,10},{9,11},{10,... | collective-permute-start | bytes 393224 | tf_op jit(solution)/shard_map/ppermute | solution.py:126
  95.3 0.2 collective-permute-start
  95.4 1.0 compare_select_fusion
  96.5 5.8 %collective-permute-done.1 = bf16[128,512]{1,0:T(8,128)(2,1)S(1)} collective-permute-done((bf16[128,512]{1,0:T(8,128)(2,1)S(1)}, bf16[128,512]{1,0:T(8,128)(2,1)S(1)}, u32[]{:S(2)}, u32[]{:S(2)}) %collective-permute-start.1) | collective-permute-done | bytes 131104 | tf_op jit(solution)/shard_map/ppermute | solution.py:126
  102.5 1.9 %convolution_convert_fusion.1 = bf16[512,512]{1,0:T(8,128)(2,1)S(1)} fusion(bf16[128,512]{1,0:T(8,128)(2,1)S(1)} %get-tuple-element.41, bf16[128,512]{1,0:T(8,128)(2,1)S(1)} %get-tuple-element.42, bf16[128,512]{1,0:T(8,128)(2,1)S(1)} %get-tuple-element.43, bf16[128,512]{1,0:T(8,128)(2,1)S(1)} %get-tuple-element.40, ...), kind=kOutput, calls=%fused_computation.44 | convolution fusion | flops 539492352 | bytes 2097152 | tf_op jit(solution)/shard_map/dot_general | solution.py:144
  104.4 1.4 %convolution_bitcast_fusion = f32[11,138,128]{2,1,0:T(8,128)S(1)} fusion(bf16[11,138,128]{2,0,1:T(8,128)(2,1)} %get-tuple-element.24, bf16[512,512]{1,0:T(8,128)(2,1)S(1)} %convolution_convert_fusion.1), kind=kOutput, calls=%fused_computation.28 | convolution fusion | flops 53627904 | bytes 1690112 | tf_op jit(solution)/shard_map/rc,acl->arl/dot_general | solution.py:65
  105.9 1.4 %convolution_bitcast_fusion.1 = f32[11,138,128]{2,1,0:T(8,128)S(1)} fusion(bf16[11,138,128]{2,0,1:T(8,128)(2,1)} %get-tuple-element.25, bf16[512,512]{1,0:T(8,128)(2,1)S(1)} %convolution_convert_fusion.1), kind=kOutput, calls=%fused_computation.29 | convolution fusion | flops 53627904 | bytes 1690112 | tf_op jit(solution)/shard_map/rc,acl->arl/dot_general | solution.py:65
  107.3 0.3 convolution_bitcast_fusion.2
  107.7 0.3 convolution_bitcast_fusion.3
  108.0 0.4 copy-done.9
  108.4 0.3 convolution_bitcast_fusion.4
  108.8 0.3 convolution_bitcast_fusion.5
  109.1 0.3 convolution_bitcast_fusion.6
  109.4 0.1 copy-done.6
  109.5 0.3 convolution_bitcast_fusion.7
  109.9 0.3 convolution_bitcast_fusion.8
  110.2 0.3 convolution_bitcast_fusion.9
  110.6 0.3 convolution_bitcast_fusion.10
  111.0 0.3 convolution_bitcast_fusion.11
  111.4 0.3 convolution_bitcast_fusion.12
  111.7 0.3 convolution_bitcast_fusion.13
  112.1 0.3 convolution_bitcast_fusion.14
  112.4 0.3 convolution_bitcast_fusion.15
  112.7 0.4 copy-done.13
  113.1 0.2 copy-done.14
  113.2 0.1 fusion.187
  113.3 0.1 pad_bitcast_fusion
  113.5 0.1 bitcast_dynamic-update-slice_fusion.14
  113.6 0.1 bitcast_dynamic-update-slice_fusion.13
  113.7 0.1 bitcast_dynamic-update-slice_fusion.12
  113.7 0.1 bitcast_dynamic-update-slice_fusion.11
  113.8 0.1 bitcast_dynamic-update-slice_fusion.10
  113.9 0.1 bitcast_dynamic-update-slice_fusion.9
  114.0 0.1 bitcast_dynamic-update-slice_fusion.8
  114.1 0.1 bitcast_dynamic-update-slice_fusion.7
  114.2 0.1 bitcast_dynamic-update-slice_fusion.6
  114.3 0.1 bitcast_dynamic-update-slice_fusion.5
  114.4 0.1 bitcast_dynamic-update-slice_fusion.4
  114.5 0.1 bitcast_dynamic-update-slice_fusion.3
  114.6 0.1 bitcast_dynamic-update-slice_fusion.2
  114.7 0.1 bitcast_dynamic-update-slice_fusion.1
  114.8 0.1 bitcast_dynamic-update-slice_fusion
  114.9 1.0 copy-done.12
  (43 shorter events, 0.9 us)
Async XLA Ops:
  0.6 101.9 %copy-start = (bf16[1,1,512,512]{3,2,1,0:T(8,128)(2,1)S(1)}, bf16[1,1,512,512]{3,2,1,0:T(8,128)(2,1)}, u32[]{:S(2)}) copy-start(bf16[1,1,512,512]{3,2,1,0:T(8,128)(2,1)} %param.15) | copy-start | bytes 1572868
  62.8 5.4 %copy-start.16 = (u32[32]{0:T(128)S(1)}, u32[32]{0:T(128)}, u32[]{:S(2)}) copy-start(u32[32]{0:T(128)} %constant.131) | copy-start | bytes 388
  62.9 17.2 %copy-start.15 = (s32[1,1,4]{2,1,0:T(1,128)S(1)}, s32[1,1,4]{2,1,0:T(1,128)}, u32[]{:S(2)}) copy-start(s32[1,1,4]{2,1,0:T(1,128)} %param.12) | copy-start | bytes 52
  64.0 29.2 %all-to-all-start.1 = ((f32[8,16,2048]{2,1,0:T(8,128)}), f32[8,16,2048]{2,1,0:T(8,128)S(1)}, u32[]{:S(2)}, u32[]{:S(2)}) async-start(f32[8,16,2048]{2,1,0:T(8,128)} %broadcast_in_dim.52), calls=%async_computation.1 | async-start | bytes 2097152 | tf_op jit(solution)/shard_map/all_to_all | solution.py:111
  93.6 2.9 %collective-permute-start.2 = (bf16[128,512]{1,0:T(8,128)(2,1)S(1)}, bf16[128,512]{1,0:T(8,128)(2,1)S(1)}, u32[]{:S(2)}, u32[]{:S(2)}) collective-permute-start(bf16[128,512]{1,0:T(8,128)(2,1)S(1)} %get-tuple-element.44), channel_id=1, source_target_pairs={{0,3},{1,0},{2,1},{3,2},{4,7},{5,4},{6,5},{7,6},{8,11},{9,8},{10,9... | collective-permute-start | bytes 393224 | tf_op jit(solution)/shard_map/ppermute | solution.py:126
  93.7 8.6 %collective-permute-start.1 = (bf16[128,512]{1,0:T(8,128)(2,1)S(1)}, bf16[128,512]{1,0:T(8,128)(2,1)S(1)}, u32[]{:S(2)}, u32[]{:S(2)}) collective-permute-start(bf16[128,512]{1,0:T(8,128)(2,1)S(1)} %get-tuple-element.45), channel_id=1, source_target_pairs={{0,2},{1,3},{2,0},{3,1},{4,6},{5,7},{6,4},{7,5},{8,10},{9,11},{10,... | collective-permute-start | bytes 393224 | tf_op jit(solution)/shard_map/ppermute | solution.py:126
  95.3 7.1 %collective-permute-start = (bf16[128,512]{1,0:T(8,128)(2,1)S(1)}, bf16[128,512]{1,0:T(8,128)(2,1)S(1)}, u32[]{:S(2)}, u32[]{:S(2)}) collective-permute-start(bf16[128,512]{1,0:T(8,128)(2,1)S(1)} %get-tuple-element.46), channel_id=1, source_target_pairs={{0,1},{1,2},{2,3},{3,0},{4,5},{5,6},{6,7},{7,4},{8,9},{9,10},{10,1... | collective-permute-start | bytes 393224 | tf_op jit(solution)/shard_map/ppermute | solution.py:126
  104.4 2.9 %copy-start.11 = (bf16[11,138,128]{2,0,1:T(8,128)(2,1)S(1)}, bf16[11,138,128]{2,0,1:T(8,128)(2,1)}, u32[]{:S(2)}) copy-start(bf16[11,138,128]{2,0,1:T(8,128)(2,1)} %get-tuple-element.26) | copy-start | bytes 1165828
  105.9 1.8 %copy-start.10 = (bf16[11,138,128]{2,0,1:T(8,128)(2,1)S(1)}, bf16[11,138,128]{2,0,1:T(8,128)(2,1)}, u32[]{:S(2)}) copy-start(bf16[11,138,128]{2,0,1:T(8,128)(2,1)} %get-tuple-element.27) | copy-start | bytes 1165828
  107.3 1.1 copy-start.9
  107.7 1.1 copy-start.8
  107.7 1.4 %copy-start.7 = (bf16[11,138,128]{2,0,1:T(8,128)(2,1)S(1)}, bf16[11,138,128]{2,0,1:T(8,128)(2,1)}, u32[]{:S(2)}) copy-start(bf16[11,138,128]{2,0,1:T(8,128)(2,1)} %get-tuple-element.30) | copy-start | bytes 1165828
  108.4 1.1 copy-start.6
  108.7 1.1 copy-start.5
  109.1 1.1 copy-start.4
  109.5 1.1 copy-start.3
  109.9 1.1 copy-start.2
  110.2 1.1 copy-start.1
  112.0 1.0 copy-start.13
  112.0 1.2 %copy-start.14 = (bf16[1,1,512,512]{3,2,1,0:T(8,128)(2,1)S(1)}, bf16[1,1,512,512]{3,2,1,0:T(8,128)(2,1)}, u32[]{:S(2)}) copy-start(bf16[1,1,512,512]{3,2,1,0:T(8,128)(2,1)} %param.18) | copy-start | bytes 1572868
  114.9 1.0 copy-start.12

commit v15 on v14

--- a/solution.py
+++ b/solution.py
@@ -8,7 +8,6 @@
 TILE = 512
 KSIZE = 11
 CELL = 128
-NCELL = 16
 PASSES = 3
 
 
@@ -28,11 +27,8 @@
 
 def psf_taps(cell_grid, kernel_table):
     blocks = TILE // CELL
-    picker = (cell_grid.reshape(-1)[:, None] == jnp.arange(NCELL, dtype=jnp.int32)[None, :]).astype(
-        jnp.bfloat16
-    )
-    tap_rows = jnp.dot(picker, kernel_table, preferred_element_type=jnp.float32)
-    return tap_rows.astype(jnp.bfloat16).reshape(blocks, blocks, KSIZE, KSIZE)
+    tap_rows = jnp.take(kernel_table, cell_grid.reshape(-1), axis=0, mode="clip")
+    return tap_rows.reshape(blocks, blocks, KSIZE, KSIZE)
 
 
 def psf_bands(tap_rows):

time: 117 us -> 117 us (level)
  local copies, waits for them, and re-layouts: 10.7 us -> 12 us
    gather x0 -> x1, local copies, waits for them, and re-layouts: none -> 1.26 us  [psf_taps(): jnp.take(kernel_table, cell_grid.reshape(-1), axis=0, mode='clip')]
where the time goes in v15:
time: 117 us; the launch traced here: 116 us
  blocking collectives  60.3 us (52%)
  local copies, waits for them, and re-layouts  12 us (10%)
  matrix products  11.8 us (10%)
  between operations  11.8 us (10%)
  other arithmetic  7.56 us (6%)
  waiting for transfers between devices  7.53 us (6%)
  starting transfers between devices  5.39 us (5%)
    all_to_all x1, blocking collectives, shards(): lax.all_to_all(stacked, 'visit', split_axis=2, concat_axis=1, tiled=True)  55.3 us
    dot_general x16, matrix products, psf_outlier(): jnp.einsum('rc,acl->arl', cols_window, bands[row_block * blocks + col_blo...  7.39 us
    ppermute x3, waiting for transfers between devices, shards(): lax.ppermute(outgoing, 'sky', perm=[(i, (i + shift) % n_sky) for i in ran...  5.88 us
    unnamed x1, blocking collectives  4.97 us
    all_to_all x1, starting transfers between devices, shards(): lax.all_to_all(copies, 'visit', split_axis=0, concat_axis=0, tiled=True)  3.59 us
    unnamed x37, local copies, waits for them, and re-layouts  3.51 us
    squeeze x1, local copies, waits for them, and re-layouts, psf_bands(): banded_all[r, c]  3.13 us
    reduce_sum x3, other arithmetic, local_coadd(): coadd_field = jnp.sum(cauchy * values, axis=0) / jnp.sum(cauchy, axis=0)  2.59 us
  transfers between devices with their start and end apart: 4, of which 2 were waited for; matrix products, arithmetic and copies ran while one was open for 8% of the time, Pallas kernels for 0%

profile of v15, /device:TPU:0, one launch (start us, length us, event | category | flops | bytes accessed | tf_op | source)
XLA Modules:
  0.0 116.3 jit_solution(14259173905210628833)
XLA Ops:
  0.6 0.8 reshape.223
  1.5 1.3 %gather_fusion = bf16[16,121]{1,0:T(8,128)(2,1)S(1)} fusion(bf16[16,121]{1,0:T(8,128)(2,1)} %bitcast.506, s32[1024]{0:T(1024)S(1)} %pad_clamp_fusion), kind=kCustom, calls=%fused_computation | custom fusion | bytes 7808 | tf_op jit(solution)/shard_map/jit(_take)/gather | solution.py:30
  2.7 0.1 reshape.154
  2.8 1.7 %pad_maximum_fusion = bf16[2,2,128,2048]{3,2,1,0:T(8,128)(2,1)S(1)} fusion(bf16[1,2,128,2048]{3,2,1,0:T(8,128)(2,1)} %bitcast.471, bf16[1,2,128,2048]{3,2,1,0:T(8,128)(2,1)} %bitcast.472), kind=kLoop, calls=%fused_computation.28 | loop fusion | flops 1048576 | bytes 4194304 | tf_op jit(solution)/shard_map/stack | solution.py:98
  4.6 0.2 copy.60
  4.8 55.3 %all_to_all.20 = bf16[2,2,8,16,2048]{4,3,1,0,2:T(8,128)(2,1)S(1)} all-to-all(bf16[2,2,8,16,2048]{4,3,1,0,2:T(8,128)(2,1)S(1)} %copy.60), channel_id=1, replica_groups=mesh['visit'=8,'sky'=4] {'visit'}, dimensions={2} | all-to-all | bytes 4194304 | tf_op jit(solution)/shard_map/all_to_all | solution.py:103
  60.1 0.4 convert_reduce_fusion
  60.6 0.9 fusion.15
  61.5 0.9 fusion.16
  62.4 0.9 fusion.17
  63.3 1.1 broadcast_in_dim.56
  64.4 3.6 %all-to-all-start.1 = ((f32[8,16,2048]{2,1,0:T(8,128)}), f32[8,16,2048]{2,1,0:T(8,128)S(1)}, u32[]{:S(2)}, u32[]{:S(2)}) async-start(f32[8,16,2048]{2,1,0:T(8,128)} %broadcast_in_dim.56), calls=%async_computation.1 | async-start | bytes 2097152 | tf_op jit(solution)/shard_map/all_to_all | solution.py:107
  68.6 0.6 dynamic-slice
  69.2 0.7 bitcast_dynamic-update-slice_fusion.15
  69.9 5.0 %all-reduce.2 = s32[4]{0:T(128)S(1)} all-reduce(s32[4]{0:T(128)S(1)} %bitcast_dynamic-update-slice_fusion.15), channel_id=2, replica_groups=mesh['visit'=8,'sky'=4] {'sky'}, use_global_device_ids=true, to_apply=%add.2 | all-reduce | flops 4 | bytes 32
  74.9 0.7 fusion.204
  80.5 0.7 fusion.203
  86.2 2.5 %convolution_convert_fusion = bf16[4,4,11,138,128]{4,2,3,1,0:T(8,128)(2,1)S(1)} fusion(s32[138,128]{1,0:T(8,128)S(1)} %iota_subtract_fusion, bf16[4,4,11,11]{3,2,1,0:T(8,128)(2,1)S(1)} %reshape.154), kind=kOutput, calls=%fused_computation.1 | convolution fusion | flops 71698176 | bytes 6292256 | tf_op jit(solution)/shard_map/xyab,bcl->xyacl/dot_general | solution.py:42
  88.7 3.1 %slice_bitcast_fusion = (bf16[11,138,128]{2,0,1:T(8,128)(2,1)}, bf16[11,138,128]{2,0,1:T(8,128)(2,1)}, bf16[11,138,128]{2,0,1:T(8,128)(2,1)}, bf16[11,138,128]{2...) fusion(bf16[4,4,11,138,128]{4,2,3,1,0:T(8,128)(2,1)S(1)} %convo, ...), kind=kLoop, calls=%fused_computation.66 | loop fusion | bytes 12435456 | tf_op jit(solution)/shard_map/squeeze | solution.py:45
  91.9 1.6 %all-to-all-done.1 = f32[8,16,2048]{2,1,0:T(8,128)S(1)} async-done(((f32[8,16,2048]{2,1,0:T(8,128)}), f32[8,16,2048]{2,1,0:T(8,128)S(1)}, u32[]{:S(2)}, u32[]{:S(2)}) %all-to-all-start.1) | async-done | bytes 1048608 | tf_op jit(solution)/shard_map/all_to_all | solution.py:107
  93.6 0.3 dynamic-slice_bitcast_fusion.11
  94.1 1.6 %collective-permute-start.1 = (bf16[128,512]{1,0:T(8,128)(2,1)S(1)}, bf16[128,512]{1,0:T(8,128)(2,1)S(1)}, u32[]{:S(2)}, u32[]{:S(2)}) collective-permute-start(bf16[128,512]{1,0:T(8,128)(2,1)S(1)} %get-tuple-element.45), channel_id=1, source_target_pairs={{0,2},{1,3},{2,0},{3,1},{4,6},{5,7},{6,4},{7,5},{8,10},{9,11},{10,... | collective-permute-start | bytes 393224 | tf_op jit(solution)/shard_map/ppermute | solution.py:122
  95.7 0.2 collective-permute-start
  95.8 1.0 compare_select_fusion
  96.9 5.8 %collective-permute-done.1 = bf16[128,512]{1,0:T(8,128)(2,1)S(1)} collective-permute-done((bf16[128,512]{1,0:T(8,128)(2,1)S(1)}, bf16[128,512]{1,0:T(8,128)(2,1)S(1)}, u32[]{:S(2)}, u32[]{:S(2)}) %collective-permute-start.1) | collective-permute-done | bytes 131104 | tf_op jit(solution)/shard_map/ppermute | solution.py:122
  102.9 1.9 %convolution_convert_fusion.1 = bf16[512,512]{1,0:T(8,128)(2,1)S(1)} fusion(bf16[128,512]{1,0:T(8,128)(2,1)S(1)} %get-tuple-element.41, bf16[128,512]{1,0:T(8,128)(2,1)S(1)} %get-tuple-element.42, bf16[128,512]{1,0:T(8,128)(2,1)S(1)} %get-tuple-element.43, bf16[128,512]{1,0:T(8,128)(2,1)S(1)} %get-tuple-element.40, ...), kind=kOutput, calls=%fused_computation.45 | convolution fusion | flops 539492352 | bytes 2097152 | tf_op jit(solution)/shard_map/dot_general | solution.py:140
  104.8 1.4 %convolution_bitcast_fusion = f32[11,138,128]{2,1,0:T(8,128)S(1)} fusion(bf16[11,138,128]{2,0,1:T(8,128)(2,1)} %get-tuple-element.24, bf16[512,512]{1,0:T(8,128)(2,1)S(1)} %convolution_convert_fusion.1), kind=kOutput, calls=%fused_computation.29 | convolution fusion | flops 53627904 | bytes 1690112 | tf_op jit(solution)/shard_map/rc,acl->arl/dot_general | solution.py:61
  106.3 1.4 %convolution_bitcast_fusion.1 = f32[11,138,128]{2,1,0:T(8,128)S(1)} fusion(bf16[11,138,128]{2,0,1:T(8,128)(2,1)} %get-tuple-element.25, bf16[512,512]{1,0:T(8,128)(2,1)S(1)} %convolution_convert_fusion.1), kind=kOutput, calls=%fused_computation.30 | convolution fusion | flops 53627904 | bytes 1690112 | tf_op jit(solution)/shard_map/rc,acl->arl/dot_general | solution.py:61
  107.7 0.3 convolution_bitcast_fusion.2
  108.1 0.3 convolution_bitcast_fusion.3
  108.4 0.4 copy-done.9
  108.8 0.3 convolution_bitcast_fusion.4
  109.1 0.3 convolution_bitcast_fusion.5
  109.5 0.3 convolution_bitcast_fusion.6
  109.9 0.3 convolution_bitcast_fusion.7
  110.3 0.3 convolution_bitcast_fusion.8
  110.6 0.3 convolution_bitcast_fusion.9
  111.0 0.1 copy-done.3
  111.0 0.3 convolution_bitcast_fusion.10
  111.4 0.3 convolution_bitcast_fusion.11
  111.8 0.3 convolution_bitcast_fusion.12
  112.1 0.3 convolution_bitcast_fusion.13
  112.5 0.3 convolution_bitcast_fusion.14
  112.8 0.3 convolution_bitcast_fusion.15
  113.1 0.4 copy-done.13
  113.5 0.2 copy-done.14
  113.6 0.1 fusion.187
  113.7 0.1 pad_bitcast_fusion
  113.9 0.1 bitcast_dynamic-update-slice_fusion.14
  113.9 0.1 bitcast_dynamic-update-slice_fusion.13
  114.0 0.1 bitcast_dynamic-update-slice_fusion.12
  114.1 0.1 bitcast_dynamic-update-slice_fusion.11
  114.2 0.1 bitcast_dynamic-update-slice_fusion.10
  114.3 0.1 bitcast_dynamic-update-slice_fusion.9
  114.4 0.1 bitcast_dynamic-update-slice_fusion.8
  114.5 0.1 bitcast_dynamic-update-slice_fusion.7
  114.6 0.1 bitcast_dynamic-update-slice_fusion.6
  114.7 0.1 bitcast_dynamic-update-slice_fusion.5
  114.8 0.1 bitcast_dynamic-update-slice_fusion.4
  114.9 0.1 bitcast_dynamic-update-slice_fusion.3
  115.0 0.1 bitcast_dynamic-update-slice_fusion.2
  115.1 0.1 bitcast_dynamic-update-slice_fusion.1
  115.2 0.1 bitcast_dynamic-update-slice_fusion
  115.3 1.0 copy-done.12
  (44 shorter events, 0.9 us)
Async XLA Ops:
  0.6 102.3 %copy-start = (bf16[1,1,512,512]{3,2,1,0:T(8,128)(2,1)S(1)}, bf16[1,1,512,512]{3,2,1,0:T(8,128)(2,1)}, u32[]{:S(2)}) copy-start(bf16[1,1,512,512]{3,2,1,0:T(8,128)(2,1)} %param.15) | copy-start | bytes 1572868
  63.2 5.4 %copy-start.16 = (u32[32]{0:T(128)S(1)}, u32[32]{0:T(128)}, u32[]{:S(2)}) copy-start(u32[32]{0:T(128)} %constant.131) | copy-start | bytes 388
  63.2 17.2 %copy-start.15 = (s32[1,1,4]{2,1,0:T(1,128)S(1)}, s32[1,1,4]{2,1,0:T(1,128)}, u32[]{:S(2)}) copy-start(s32[1,1,4]{2,1,0:T(1,128)} %param.12) | copy-start | bytes 52
  64.4 29.2 %all-to-all-start.1 = ((f32[8,16,2048]{2,1,0:T(8,128)}), f32[8,16,2048]{2,1,0:T(8,128)S(1)}, u32[]{:S(2)}, u32[]{:S(2)}) async-start(f32[8,16,2048]{2,1,0:T(8,128)} %broadcast_in_dim.56), calls=%async_computation.1 | async-start | bytes 2097152 | tf_op jit(solution)/shard_map/all_to_all | solution.py:107
  94.0 2.9 %collective-permute-start.2 = (bf16[128,512]{1,0:T(8,128)(2,1)S(1)}, bf16[128,512]{1,0:T(8,128)(2,1)S(1)}, u32[]{:S(2)}, u32[]{:S(2)}) collective-permute-start(bf16[128,512]{1,0:T(8,128)(2,1)S(1)} %get-tuple-element.44), channel_id=1, source_target_pairs={{0,3},{1,0},{2,1},{3,2},{4,7},{5,4},{6,5},{7,6},{8,11},{9,8},{10,9... | collective-permute-start | bytes 393224 | tf_op jit(solution)/shard_map/ppermute | solution.py:122
  94.1 8.6 %collective-permute-start.1 = (bf16[128,512]{1,0:T(8,128)(2,1)S(1)}, bf16[128,512]{1,0:T(8,128)(2,1)S(1)}, u32[]{:S(2)}, u32[]{:S(2)}) collective-permute-start(bf16[128,512]{1,0:T(8,128)(2,1)S(1)} %get-tuple-element.45), channel_id=1, source_target_pairs={{0,2},{1,3},{2,0},{3,1},{4,6},{5,7},{6,4},{7,5},{8,10},{9,11},{10,... | collective-permute-start | bytes 393224 | tf_op jit(solution)/shard_map/ppermute | solution.py:122
  95.7 7.1 %collective-permute-start = (bf16[128,512]{1,0:T(8,128)(2,1)S(1)}, bf16[128,512]{1,0:T(8,128)(2,1)S(1)}, u32[]{:S(2)}, u32[]{:S(2)}) collective-permute-start(bf16[128,512]{1,0:T(8,128)(2,1)S(1)} %get-tuple-element.46), channel_id=1, source_target_pairs={{0,1},{1,2},{2,3},{3,0},{4,5},{5,6},{6,7},{7,4},{8,9},{9,10},{10,1... | collective-permute-start | bytes 393224 | tf_op jit(solution)/shard_map/ppermute | solution.py:122
  104.8 2.9 %copy-start.11 = (bf16[11,138,128]{2,0,1:T(8,128)(2,1)S(1)}, bf16[11,138,128]{2,0,1:T(8,128)(2,1)}, u32[]{:S(2)}) copy-start(bf16[11,138,128]{2,0,1:T(8,128)(2,1)} %get-tuple-element.26) | copy-start | bytes 1165828
  106.3 1.8 %copy-start.10 = (bf16[11,138,128]{2,0,1:T(8,128)(2,1)S(1)}, bf16[11,138,128]{2,0,1:T(8,128)(2,1)}, u32[]{:S(2)}) copy-start(bf16[11,138,128]{2,0,1:T(8,128)(2,1)} %get-tuple-element.27) | copy-start | bytes 1165828
  107.7 1.1 copy-start.9
  108.0 1.1 copy-start.8
  108.1 1.4 %copy-start.7 = (bf16[11,138,128]{2,0,1:T(8,128)(2,1)S(1)}, bf16[11,138,128]{2,0,1:T(8,128)(2,1)}, u32[]{:S(2)}) copy-start(bf16[11,138,128]{2,0,1:T(8,128)(2,1)} %get-tuple-element.30) | copy-start | bytes 1165828
  108.8 1.1 copy-start.6
  109.1 1.1 copy-start.5
  109.5 1.1 copy-start.4
  109.9 1.1 copy-start.3
  110.3 1.1 copy-start.2
  110.6 1.1 copy-start.1
  112.4 1.0 copy-start.13
  112.4 1.2 %copy-start.14 = (bf16[1,1,512,512]{3,2,1,0:T(8,128)(2,1)S(1)}, bf16[1,1,512,512]{3,2,1,0:T(8,128)(2,1)}, u32[]{:S(2)}) copy-start(bf16[1,1,512,512]{3,2,1,0:T(8,128)(2,1)} %param.18) | copy-start | bytes 1572868
  115.3 1.0 copy-start.12

commit v16 on v14

--- a/solution.py
+++ b/solution.py
@@ -113,15 +113,13 @@
     coadd_field = coadd_field.reshape(n_visit * chunk, sky_w)
     coadd_low = coadd_field.astype(jnp.bfloat16)
 
-    all_starts = lax.all_gather(col_start[0], "sky", axis=0, tiled=True)
-    windows = jnp.stack(
-        [lax.dynamic_slice_in_dim(coadd_low, all_starts[peer], TILE, 1) for peer in range(n_sky)],
-        axis=0,
-    )
     me = lax.axis_index("sky")
-    received = [lax.dynamic_index_in_dim(windows, me, 0, keepdims=False)]
+    received = [lax.dynamic_slice_in_dim(coadd_low, col_start[0, 0], TILE, 1)]
     for shift in range(1, n_sky):
-        outgoing = lax.dynamic_index_in_dim(windows, (me + shift) % n_sky, 0, keepdims=False)
+        peer_start = lax.ppermute(
+            col_start[0], "sky", perm=[(i, (i - shift) % n_sky) for i in range(n_sky)]
+        )
+        outgoing = lax.dynamic_slice_in_dim(coadd_low, peer_start[0], TILE, 1)
         received.append(
             lax.ppermute(
                 outgoing, "sky", perm=[(i, (i + shift) % n_sky) for i in range(n_sky)]

time: 117 us -> 116 us (level)
  waiting for transfers between devices: 7.52 us -> 13 us
  blocking collectives: 60.3 us -> 55.3 us
  starting transfers between devices: 5.39 us -> 8.4 us
  local copies, waits for them, and re-layouts: 10.7 us -> 8.73 us
  between operations: 11.8 us -> 10.2 us
    all_to_all x1, waiting for transfers between devices: 1.64 us -> 7.07 us  [shards(): lax.all_to_all(copies, 'visit', split_axis=0, concat_axis=0, tiled=True)]
    unnamed x1 -> x0, blocking collectives: 4.97 us -> none
    ppermute x0 -> x3, starting transfers between devices: none -> 3.01 us  [shards(): lax.ppermute(col_start[0], 'sky', perm=[(i, (i - shift) % n_sky) for i in...]
    unnamed x37 -> x32, local copies, waits for them, and re-layouts: 3.5 us -> 2.24 us
  transfers between devices with their start and end apart: 4 -> 7, of which waited for: 2 -> 2; matrix products, arithmetic and copies ran while one was open for 8% -> 6% of each run, Pallas kernels for 0% -> 0%
where the time goes in v16:
time: 116 us
  blocking collectives  55.3 us (48%)
  waiting for transfers between devices  13 us (11%)
  matrix products  12.6 us (11%)
  between operations  10.2 us (9%)
  local copies, waits for them, and re-layouts  8.73 us (8%)
  starting transfers between devices  8.4 us (7%)
  other arithmetic  7.48 us (6%)
    all_to_all x1, blocking collectives, shards(): lax.all_to_all(stacked, 'visit', split_axis=2, concat_axis=1, tiled=True)  55.3 us
    dot_general x16, matrix products, psf_outlier(): jnp.einsum('rc,acl->arl', cols_window, bands[row_block * blocks + col_blo...  7.39 us
    all_to_all x1, waiting for transfers between devices, shards(): lax.all_to_all(copies, 'visit', split_axis=0, concat_axis=0, tiled=True)  7.07 us
    ppermute x3, waiting for transfers between devices, shards(): lax.ppermute(outgoing, 'sky', perm=[(i, (i + shift) % n_sky) for i in ran...  5.88 us
    all_to_all x1, starting transfers between devices, shards(): lax.all_to_all(copies, 'visit', split_axis=0, concat_axis=0, tiled=True)  3.59 us
    squeeze x1, local copies, waits for them, and re-layouts, psf_bands(): banded_all[r, c]  3.13 us
    ppermute x3, starting transfers between devices, shards(): lax.ppermute(col_start[0], 'sky', perm=[(i, (i - shift) % n_sky) for i in...  3.01 us
    reduce_sum x3, other arithmetic, local_coadd(): coadd_field = jnp.sum(cauchy * values, axis=0) / jnp.sum(cauchy, axis=0)  2.59 us
  transfers between devices with their start and end apart: 7, of which 2 were waited for; matrix products, arithmetic and copies ran while one was open for 6% of the time, Pallas kernels for 0%

profile of v16, /device:TPU:0, one launch (start us, length us, event | category | flops | bytes accessed | tf_op | source)
XLA Modules:
  0.0 115.7 jit_solution(435712660736340071)
XLA Ops:
  0.6 0.8 eq.36
  1.5 0.9 convolution_convert_fusion.3
  2.3 0.1 reshape.154
  2.4 1.7 %pad_maximum_fusion = bf16[2,2,128,2048]{3,2,1,0:T(8,128)(2,1)S(1)} fusion(bf16[1,2,128,2048]{3,2,1,0:T(8,128)(2,1)} %bitcast.458, bf16[1,2,128,2048]{3,2,1,0:T(8,128)(2,1)} %bitcast.459), kind=kLoop, calls=%fused_computation.27 | loop fusion | flops 1048576 | bytes 4194304 | tf_op jit(solution)/shard_map/stack | solution.py:102
  4.2 0.2 copy.60
  4.4 55.3 %all_to_all.20 = bf16[2,2,8,16,2048]{4,3,1,0,2:T(8,128)(2,1)S(1)} all-to-all(bf16[2,2,8,16,2048]{4,3,1,0,2:T(8,128)(2,1)S(1)} %copy.60), channel_id=1, replica_groups=mesh['visit'=8,'sky'=4] {'visit'}, dimensions={2} | all-to-all | bytes 4194304 | tf_op jit(solution)/shard_map/all_to_all | solution.py:107
  59.7 0.4 convert_reduce_fusion
  60.2 0.9 fusion.15
  61.1 0.9 fusion.16
  62.0 0.9 fusion.17
  62.9 1.1 broadcast_in_dim.52
  64.0 3.6 %all-to-all-start.1 = ((f32[8,16,2048]{2,1,0:T(8,128)}), f32[8,16,2048]{2,1,0:T(8,128)S(1)}, u32[]{:S(2)}, u32[]{:S(2)}) async-start(f32[8,16,2048]{2,1,0:T(8,128)} %broadcast_in_dim.52), calls=%async_computation.1 | async-start | bytes 2097152 | tf_op jit(solution)/shard_map/all_to_all | solution.py:111
  67.6 1.6 %collective-permute-start.2 = (s32[1]{0:T(128)}, s32[1]{0:T(128)}, u32[]{:S(2)}, u32[]{:S(2)}) collective-permute-start(s32[1]{0:T(128)} %bitcast.9), channel_id=1, source_target_pairs={{0,2},{1,3},{2,0},{3,1},{4,6},{5,7},{6,4},{7,5},{8,10},{9,11},{10,... | collective-permute-start | bytes 20 | tf_op jit(solution)/shard_map/ppermute | solution.py:119
  69.2 1.4 %collective-permute-start = (s32[1]{0:T(128)}, s32[1]{0:T(128)}, u32[]{:S(2)}, u32[]{:S(2)}) collective-permute-start(s32[1]{0:T(128)} %bitcast.9), channel_id=1, source_target_pairs={{0,3},{1,0},{2,1},{3,2},{4,7},{5,4},{6,5},{7,6},{8,11},{9,8},{10,9... | collective-permute-start | bytes 20 | tf_op jit(solution)/shard_map/ppermute | solution.py:119
  71.3 0.7 fusion.205
  74.6 2.5 %convolution_convert_fusion = bf16[4,4,11,138,128]{4,2,3,1,0:T(8,128)(2,1)S(1)} fusion(s32[138,128]{1,0:T(8,128)S(1)} %iota_subtract_fusion, bf16[4,4,11,11]{3,2,1,0:T(8,128)(2,1)S(1)} %reshape.154), kind=kOutput, calls=%fused_computation | convolution fusion | flops 71698176 | bytes 6292256 | tf_op jit(solution)/shard_map/xyab,bcl->xyacl/dot_general | solution.py:46
  77.1 3.1 %slice_bitcast_fusion = (bf16[11,138,128]{2,0,1:T(8,128)(2,1)}, bf16[11,138,128]{2,0,1:T(8,128)(2,1)}, bf16[11,138,128]{2,0,1:T(8,128)(2,1)}, bf16[11,138,128]{2...) fusion(bf16[4,4,11,138,128]{4,2,3,1,0:T(8,128)(2,1)S(1)} %convo, ...), kind=kLoop, calls=%fused_computation.66 | loop fusion | bytes 12435456 | tf_op jit(solution)/shard_map/squeeze | solution.py:49
  86.1 7.1 %all-to-all-done.1 = f32[8,16,2048]{2,1,0:T(8,128)S(1)} async-done(((f32[8,16,2048]{2,1,0:T(8,128)}), f32[8,16,2048]{2,1,0:T(8,128)S(1)}, u32[]{:S(2)}, u32[]{:S(2)}) %all-to-all-start.1) | async-done | bytes 1048608 | tf_op jit(solution)/shard_map/all_to_all | solution.py:111
  93.2 0.3 constant_dynamic-slice_fusion
  93.6 1.6 %collective-permute-start.3 = (bf16[128,512]{1,0:T(8,128)(2,1)S(1)}, bf16[128,512]{1,0:T(8,128)(2,1)S(1)}, u32[]{:S(2)}, u32[]{:S(2)}) collective-permute-start(bf16[128,512]{1,0:T(8,128)(2,1)S(1)} %get-tuple-element.45), channel_id=1, source_target_pairs={{0,2},{1,3},{2,0},{3,1},{4,6},{5,7},{6,4},{7,5},{8,10},{9,11},{10,... | collective-permute-start | bytes 393224 | tf_op jit(solution)/shard_map/ppermute | solution.py:124
  95.1 0.2 collective-permute-start.1
  95.3 1.0 compare_select_fusion
  96.4 5.8 %collective-permute-done.3 = bf16[128,512]{1,0:T(8,128)(2,1)S(1)} collective-permute-done((bf16[128,512]{1,0:T(8,128)(2,1)S(1)}, bf16[128,512]{1,0:T(8,128)(2,1)S(1)}, u32[]{:S(2)}, u32[]{:S(2)}) %collective-permute-start.3) | collective-permute-done | bytes 131104 | tf_op jit(solution)/shard_map/ppermute | solution.py:124
  102.2 0.1 pad_maximum_fusion.1
  102.4 1.9 %convolution_convert_fusion.1 = bf16[512,512]{1,0:T(8,128)(2,1)S(1)} fusion(bf16[128,512]{1,0:T(8,128)(2,1)S(1)} %get-tuple-element.41, bf16[128,512]{1,0:T(8,128)(2,1)S(1)} %get-tuple-element.42, bf16[128,512]{1,0:T(8,128)(2,1)S(1)} %get-tuple-element.43, bf16[128,512]{1,0:T(8,128)(2,1)S(1)} %get-tuple-element.40, ...), kind=kOutput, calls=%fused_computation.44 | convolution fusion | flops 539492352 | bytes 2097152 | tf_op jit(solution)/shard_map/dot_general | solution.py:142
  104.3 1.4 %convolution_bitcast_fusion = f32[11,138,128]{2,1,0:T(8,128)S(1)} fusion(bf16[11,138,128]{2,0,1:T(8,128)(2,1)} %get-tuple-element.24, bf16[512,512]{1,0:T(8,128)(2,1)S(1)} %convolution_convert_fusion.1), kind=kOutput, calls=%fused_computation.28 | convolution fusion | flops 53627904 | bytes 1690112 | tf_op jit(solution)/shard_map/rc,acl->arl/dot_general | solution.py:65
  105.7 1.4 %convolution_bitcast_fusion.1 = f32[11,138,128]{2,1,0:T(8,128)S(1)} fusion(bf16[11,138,128]{2,0,1:T(8,128)(2,1)} %get-tuple-element.25, bf16[512,512]{1,0:T(8,128)(2,1)S(1)} %convolution_convert_fusion.1), kind=kOutput, calls=%fused_computation.29 | convolution fusion | flops 53627904 | bytes 1690112 | tf_op jit(solution)/shard_map/rc,acl->arl/dot_general | solution.py:65
  107.2 0.3 convolution_bitcast_fusion.2
  107.5 0.3 convolution_bitcast_fusion.3
  107.9 0.4 copy-done.9
  108.2 0.3 convolution_bitcast_fusion.4
  108.6 0.3 convolution_bitcast_fusion.5
  109.0 0.3 convolution_bitcast_fusion.6
  109.3 0.1 copy-done.6
  109.4 0.3 convolution_bitcast_fusion.7
  109.7 0.3 convolution_bitcast_fusion.8
  110.1 0.3 convolution_bitcast_fusion.9
  110.4 0.1 copy-done.3
  110.5 0.3 convolution_bitcast_fusion.10
  110.9 0.3 convolution_bitcast_fusion.11
  111.2 0.3 convolution_bitcast_fusion.12
  111.6 0.3 convolution_bitcast_fusion.13
  111.9 0.3 convolution_bitcast_fusion.14
  112.2 0.3 convolution_bitcast_fusion.15
  112.6 0.4 copy-done.13
  112.9 0.2 copy-done.14
  113.1 0.1 fusion.187
  113.2 0.1 pad_bitcast_fusion
  113.3 0.1 bitcast_dynamic-update-slice_fusion.14
  113.4 0.1 bitcast_dynamic-update-slice_fusion.13
  113.5 0.1 bitcast_dynamic-update-slice_fusion.12
  113.6 0.1 bitcast_dynamic-update-slice_fusion.11
  113.7 0.1 bitcast_dynamic-update-slice_fusion.10
  113.8 0.1 bitcast_dynamic-update-slice_fusion.9
  113.9 0.1 bitcast_dynamic-update-slice_fusion.8
  114.0 0.1 bitcast_dynamic-update-slice_fusion.7
  114.1 0.1 bitcast_dynamic-update-slice_fusion.6
  114.2 0.1 bitcast_dynamic-update-slice_fusion.5
  114.3 0.1 bitcast_dynamic-update-slice_fusion.4
  114.4 0.1 bitcast_dynamic-update-slice_fusion.3
  114.5 0.1 bitcast_dynamic-update-slice_fusion.2
  114.6 0.1 bitcast_dynamic-update-slice_fusion.1
  114.7 0.1 bitcast_dynamic-update-slice_fusion
  114.8 1.0 copy-done.12
  (40 shorter events, 0.6 us)
Async XLA Ops:
  0.6 101.7 %copy-start = (bf16[1,1,512,512]{3,2,1,0:T(8,128)(2,1)S(1)}, bf16[1,1,512,512]{3,2,1,0:T(8,128)(2,1)}, u32[]{:S(2)}) copy-start(bf16[1,1,512,512]{3,2,1,0:T(8,128)(2,1)} %param.15) | copy-start | bytes 1572868
  62.8 8.4 %copy-start.15 = (s32[1,1,4]{2,1,0:T(1,128)S(1)}, s32[1,1,4]{2,1,0:T(1,128)}, u32[]{:S(2)}) copy-start(s32[1,1,4]{2,1,0:T(1,128)} %param.12) | copy-start | bytes 52
  64.0 29.2 %all-to-all-start.1 = ((f32[8,16,2048]{2,1,0:T(8,128)}), f32[8,16,2048]{2,1,0:T(8,128)S(1)}, u32[]{:S(2)}, u32[]{:S(2)}) async-start(f32[8,16,2048]{2,1,0:T(8,128)} %broadcast_in_dim.52), calls=%async_computation.1 | async-start | bytes 2097152 | tf_op jit(solution)/shard_map/all_to_all | solution.py:111
  67.6 12.7 %collective-permute-start.4 = (s32[1]{0:T(128)}, s32[1]{0:T(128)}, u32[]{:S(2)}, u32[]{:S(2)}) collective-permute-start(s32[1]{0:T(128)} %bitcast.9), channel_id=1, source_target_pairs={{0,1},{1,2},{2,3},{3,0},{4,5},{5,6},{6,7},{7,4},{8,9},{9,10},{10,1... | collective-permute-start | bytes 20 | tf_op jit(solution)/shard_map/ppermute | solution.py:119
  67.6 14.0 %collective-permute-start.2 = (s32[1]{0:T(128)}, s32[1]{0:T(128)}, u32[]{:S(2)}, u32[]{:S(2)}) collective-permute-start(s32[1]{0:T(128)} %bitcast.9), channel_id=1, source_target_pairs={{0,2},{1,3},{2,0},{3,1},{4,6},{5,7},{6,4},{7,5},{8,10},{9,11},{10,... | collective-permute-start | bytes 20 | tf_op jit(solution)/shard_map/ppermute | solution.py:119
  69.2 13.7 %collective-permute-start = (s32[1]{0:T(128)}, s32[1]{0:T(128)}, u32[]{:S(2)}, u32[]{:S(2)}) collective-permute-start(s32[1]{0:T(128)} %bitcast.9), channel_id=1, source_target_pairs={{0,3},{1,0},{2,1},{3,2},{4,7},{5,4},{6,5},{7,6},{8,11},{9,8},{10,9... | collective-permute-start | bytes 20 | tf_op jit(solution)/shard_map/ppermute | solution.py:119
  93.5 2.9 %collective-permute-start.5 = (bf16[128,512]{1,0:T(8,128)(2,1)S(1)}, bf16[128,512]{1,0:T(8,128)(2,1)S(1)}, u32[]{:S(2)}, u32[]{:S(2)}) collective-permute-start(bf16[128,512]{1,0:T(8,128)(2,1)S(1)} %get-tuple-element.44), channel_id=1, source_target_pairs={{0,3},{1,0},{2,1},{3,2},{4,7},{5,4},{6,5},{7,6},{8,11},{9,8},{10,9... | collective-permute-start | bytes 393224 | tf_op jit(solution)/shard_map/ppermute | solution.py:124
  93.6 8.6 %collective-permute-start.3 = (bf16[128,512]{1,0:T(8,128)(2,1)S(1)}, bf16[128,512]{1,0:T(8,128)(2,1)S(1)}, u32[]{:S(2)}, u32[]{:S(2)}) collective-permute-start(bf16[128,512]{1,0:T(8,128)(2,1)S(1)} %get-tuple-element.45), channel_id=1, source_target_pairs={{0,2},{1,3},{2,0},{3,1},{4,6},{5,7},{6,4},{7,5},{8,10},{9,11},{10,... | collective-permute-start | bytes 393224 | tf_op jit(solution)/shard_map/ppermute | solution.py:124
  95.1 7.1 %collective-permute-start.1 = (bf16[128,512]{1,0:T(8,128)(2,1)S(1)}, bf16[128,512]{1,0:T(8,128)(2,1)S(1)}, u32[]{:S(2)}, u32[]{:S(2)}) collective-permute-start(bf16[128,512]{1,0:T(8,128)(2,1)S(1)} %get-tuple-element.46), channel_id=1, source_target_pairs={{0,1},{1,2},{2,3},{3,0},{4,5},{5,6},{6,7},{7,4},{8,9},{9,10},{10,1... | collective-permute-start | bytes 393224 | tf_op jit(solution)/shard_map/ppermute | solution.py:124
  104.3 2.9 %copy-start.11 = (bf16[11,138,128]{2,0,1:T(8,128)(2,1)S(1)}, bf16[11,138,128]{2,0,1:T(8,128)(2,1)}, u32[]{:S(2)}) copy-start(bf16[11,138,128]{2,0,1:T(8,128)(2,1)} %get-tuple-element.26) | copy-start | bytes 1165828
  105.7 1.8 %copy-start.10 = (bf16[11,138,128]{2,0,1:T(8,128)(2,1)S(1)}, bf16[11,138,128]{2,0,1:T(8,128)(2,1)}, u32[]{:S(2)}) copy-start(bf16[11,138,128]{2,0,1:T(8,128)(2,1)} %get-tuple-element.27) | copy-start | bytes 1165828
  107.2 1.1 copy-start.9
  107.5 1.1 copy-start.8
  107.5 1.4 %copy-start.7 = (bf16[11,138,128]{2,0,1:T(8,128)(2,1)S(1)}, bf16[11,138,128]{2,0,1:T(8,128)(2,1)}, u32[]{:S(2)}) copy-start(bf16[11,138,128]{2,0,1:T(8,128)(2,1)} %get-tuple-element.30) | copy-start | bytes 1165828
  108.2 1.1 copy-start.6
  108.6 1.1 copy-start.5
  108.9 1.1 copy-start.4
  109.4 1.1 copy-start.3
  109.7 1.1 copy-start.2
  110.1 1.1 copy-start.1
  111.9 1.0 copy-start.13
  111.9 1.2 %copy-start.14 = (bf16[1,1,512,512]{3,2,1,0:T(8,128)(2,1)S(1)}, bf16[1,1,512,512]{3,2,1,0:T(8,128)(2,1)}, u32[]{:S(2)}) copy-start(bf16[1,1,512,512]{3,2,1,0:T(8,128)(2,1)} %param.18) | copy-start | bytes 1572868
  114.8 1.0 copy-start.12

commit v17 on v16

--- a/solution.py
+++ b/solution.py
@@ -100,16 +100,31 @@
     n_sky = lax.axis_size("sky")
     local_visits, strip_rows, sky_w = warped.shape
     stacked = jnp.stack([warped, inv_var], axis=0)
-    tap_rows = psf_taps(cell_ids[0, 0], kernels[0, 0])
-    stacked, tap_rows = lax.optimization_barrier((stacked, tap_rows))
     chunk = strip_rows // n_visit
     stacked = stacked.reshape(2, local_visits, n_visit, chunk, sky_w)
     gathered = lax.all_to_all(stacked, "visit", split_axis=2, concat_axis=1, tiled=True)
     gathered = gathered.reshape(2, local_visits * n_visit, chunk, sky_w)
     row_share = local_coadd(gathered[0].astype(jnp.float32), gathered[1].astype(jnp.float32))
-    copies = jnp.broadcast_to(row_share[None], (n_visit,) + row_share.shape)
-    coadd_field = lax.all_to_all(copies, "visit", split_axis=0, concat_axis=0, tiled=True)
-    bands = psf_bands(tap_rows)
+    outer = n_visit // 2
+    visit_me = lax.axis_index("visit")
+    outer_me, inner_me = visit_me // 2, visit_me % 2
+    same = [row_share]
+    for shift in range(1, outer):
+        same.append(
+            lax.ppermute(
+                row_share,
+                "visit",
+                perm=[(v, ((v // 2 + shift) % outer) * 2 + v % 2) for v in range(n_visit)],
+            )
+        )
+    same = jnp.stack(same, axis=0)
+    other = lax.ppermute(same, "visit", perm=[(v, v ^ 1) for v in range(n_visit)])
+    both = jnp.stack([same, other], axis=0)
+    pick_inner = jnp.arange(2, dtype=jnp.int32) ^ inner_me
+    pick_outer = (outer_me - jnp.arange(outer, dtype=jnp.int32)) % outer
+    coadd_field = jnp.take(jnp.take(both, pick_inner, axis=0), pick_outer, axis=1)
+    coadd_field = coadd_field.transpose(1, 0, 2, 3)
+    bands = psf_bands(psf_taps(cell_ids[0, 0], kernels[0, 0]))
     coadd_field = coadd_field.reshape(n_visit * chunk, sky_w)
     coadd_low = coadd_field.astype(jnp.bfloat16)
 

time: 116 us -> 115 us (level)
  blocking collectives: 55.3 us -> 0 us
  waiting for transfers between devices: 13 us -> 52.6 us
  starting transfers between devices: 8.4 us -> 15.1 us
  local copies, waits for them, and re-layouts: 8.73 us -> 14 us
  other arithmetic: 7.48 us -> 9.12 us
    all_to_all x1 -> x0, blocking collectives: 55.3 us -> none  [shards(): lax.all_to_all(stacked, 'visit', split_axis=2, concat_axis=1, tiled=True)]
    all_to_all x1, waiting for transfers between devices: 7.07 us -> 39.5 us  [shards(): lax.all_to_all(stacked, 'visit', split_axis=2, concat_axis=1, tiled=True)]
    ppermute x0 -> x4, waiting for transfers between devices: none -> 7.22 us  [the longest x3 7 us: shards(): lax.ppermute(row_share, 'visit', perm=[(v, (v // 2 + shift) % outer * 2 +...]
    all_to_all x1, starting transfers between devices: 3.59 us -> 7.41 us  [shards(): lax.all_to_all(stacked, 'visit', split_axis=2, concat_axis=1, tiled=True)]
    ppermute x0 -> x4, starting transfers between devices: none -> 3.68 us  [the longest x3 2.97 us: shards(): lax.ppermute(row_share, 'visit', perm=[(v, (v // 2 + shift) % outer * 2 +...]
    dot_general x1, matrix products: 2.49 us -> 6 us  [psf_bands(): jnp.einsum('xyab,bcl->xyacl', tap_rows, diagonal, preferred_element_type=...]
    squeeze x1, local copies, waits for them, and re-layouts: 3.13 us -> 6.58 us  [psf_bands(): banded_all[r, c]]
    dot_general x16, matrix products: 7.39 us -> 5.16 us  [psf_outlier(): jnp.einsum('rc,acl->arl', cols_window, bands[row_block * blocks + col_blo...]
  transfers between devices with their start and end apart: 7 -> 11, of which waited for: 2 -> 5; matrix products, arithmetic and copies ran while one was open for 6% -> 16% of each run, Pallas kernels for 0% -> 0%
where the time goes in v17:
time: 115 us; the launch traced here: 114 us
  waiting for transfers between devices  52.6 us (46%)
  starting transfers between devices  15.1 us (13%)
  local copies, waits for them, and re-layouts  14 us (12%)
  matrix products  13.3 us (12%)
  between operations  10.3 us (9%)
  other arithmetic  9.12 us (8%)
    all_to_all x1, waiting for transfers between devices, shards(): lax.all_to_all(stacked, 'visit', split_axis=2, concat_axis=1, tiled=True)  39.5 us
    all_to_all x1, starting transfers between devices, shards(): lax.all_to_all(stacked, 'visit', split_axis=2, concat_axis=1, tiled=True)  7.41 us
    ppermute x3, waiting for transfers between devices, shards(): lax.ppermute(row_share, 'visit', perm=[(v, (v // 2 + shift) % outer * 2 +...  7 us
    squeeze x1, local copies, waits for them, and re-layouts, psf_bands(): banded_all[r, c]  6.58 us
    dot_general x1, matrix products, psf_bands(): jnp.einsum('xyab,bcl->xyacl', tap_rows, diagonal, preferred_element_type=...  6 us
    ppermute x3, waiting for transfers between devices, shards(): lax.ppermute(outgoing, 'sky', perm=[(i, (i + shift) % n_sky) for i in ran...  5.88 us
    dot_general x16, matrix products, psf_outlier(): jnp.einsum('rc,acl->arl', cols_window, bands[row_block * blocks + col_blo...  5.16 us
    unnamed x46, local copies, waits for them, and re-layouts  3.45 us
  transfers between devices with their start and end apart: 11, of which 5 were waited for; matrix products, arithmetic and copies ran while one was open for 16% of the time, Pallas kernels for 0%

profile of v17, /device:TPU:0, one launch (start us, length us, event | category | flops | bytes accessed | tf_op | source)
XLA Modules:
  0.0 114.5 jit_solution(2742370353581931708)
XLA Ops:
  0.6 1.8 %pad_maximum_fusion = bf16[2,2,8,16,2048]{4,3,2,1,0:T(8,128)(2,1)S(1)} fusion(bf16[1,2,8,16,2048]{4,3,2,1,0:T(8,128)(2,1)} %bitcast.465, bf16[1,2,8,16,2048]{4,3,2,1,0:T(8,128)(2,1)} %bitcast.466), kind=kLoop, calls=%fused_computation.29 | loop fusion | flops 1048576 | bytes 4194304 | tf_op jit(solution)/shard_map/stack | solution.py:102
  2.4 1.5 %copy.60 = bf16[2,2,8,16,2048]{4,3,1,0,2:T(8,128)(2,1)} copy(bf16[2,2,8,16,2048]{4,3,2,1,0:T(8,128)(2,1)S(1)} %pad_maximum_fusion) | data formatting | bytes 4194304 | tf_op jit(solution)/shard_map/stack | solution.py:102
  3.9 7.4 %all-to-all-start = ((bf16[2,2,8,16,2048]{4,3,1,0,2:T(8,128)(2,1)}), bf16[2,2,8,16,2048]{4,3,1,0,2:T(8,128)(2,1)S(1)}, u32[]{:S(2)}, u32[]{:S(2)}) async-start(bf16[2,2,8,16,2048]{4,3,1,0,2:T(8,128)(2,1)} %copy.60), calls=%async_computation | async-start | bytes 4194304 | tf_op jit(solution)/shard_map/all_to_all | solution.py:105
  11.3 1.6 %collective-permute-start.6 = (s32[1]{0:T(128)}, s32[1]{0:T(128)}, u32[]{:S(2)}, u32[]{:S(2)}) collective-permute-start(s32[1]{0:T(128)} %bitcast.15), channel_id=1, source_target_pairs={{0,2},{1,3},{2,0},{3,1},{4,6},{5,7},{6,4},{7,5},{8,10},{9,11},{10,... | collective-permute-start | bytes 20 | tf_op jit(solution)/shard_map/ppermute | solution.py:134
  13.0 0.2 convolution_convert_fusion.3
  13.2 0.1 reshape.352
  13.4 0.7 fusion.210
  14.0 6.0 %convolution_convert_fusion = bf16[4,4,11,138,128]{4,2,3,1,0:T(8,128)(2,1)} fusion(s32[138,128]{1,0:T(8,128)S(1)} %iota_subtract_fusion, bf16[4,4,11,11,1]{3,2,1,0,4:T(8,128)(2,1)S(1)} %reshape.352), kind=kOutput, calls=%fused_computation.2 | convolution fusion | flops 71698176 | bytes 6292256 | tf_op jit(solution)/shard_map/xyab,bcl->xyacl/dot_general | solution.py:46
  20.0 39.5 %all-to-all-done = bf16[2,2,8,16,2048]{4,3,1,0,2:T(8,128)(2,1)S(1)} async-done(((bf16[2,2,8,16,2048]{4,3,1,0,2:T(8,128)(2,1)}), bf16[2,2,8,16,2048]{4,3,1,0,2:T(8,128)(2,1)S(1)}, u32[]{:S(2)}, u32[]{:S(2)}) %all-to-all-start) | async-done | bytes 2097184 | tf_op jit(solution)/shard_map/all_to_all | solution.py:105
  59.5 0.4 convert_reduce_fusion
  60.0 0.9 fusion.15
  60.9 0.9 fusion.16
  61.8 0.9 fusion.17
  62.7 2.3 %collective-permute-start.2 = (f32[16,2048]{1,0:T(8,128)S(1)}, f32[16,2048]{1,0:T(8,128)S(1)}, u32[]{:S(2)}, u32[]{:S(2)}) collective-permute-start(f32[16,2048]{1,0:T(8,128)S(1)} %div.162), channel_id=1, source_target_pairs={{0,24},{4,28},{8,0},{12,4},{16,8},{20,12},{24,16},{28,20},{1,25},{... | collective-permute-start | bytes 393224 | tf_op jit(solution)/shard_map/ppermute | solution.py:114
  65.0 0.6 collective-permute-start
  69.0 0.6 collective-permute-start.4
  69.6 7.0 %collective-permute-done.1 = f32[16,2048]{1,0:T(8,128)S(1)} collective-permute-done((f32[16,2048]{1,0:T(8,128)S(1)}, f32[16,2048]{1,0:T(8,128)S(1)}, u32[]{:S(2)}, u32[]{:S(2)}) %collective-permute-start.1) | collective-permute-done | bytes 131104 | tf_op jit(solution)/shard_map/ppermute | solution.py:114
  76.6 0.1 fusion.209
  76.7 0.7 collective-permute-start.3
  77.4 6.6 %slice_bitcast_fusion = (bf16[11,138,128]{2,0,1:T(8,128)(2,1)}, bf16[11,138,128]{2,0,1:T(8,128)(2,1)}, bf16[11,138,128]{2,0,1:T(8,128)(2,1)}, bf16[11,138,128]{2...) fusion(bf16[4,4,11,138,128]{4,2,3,1,0:T(8,128)(2,1)} %convoluti, ...), kind=kLoop, calls=%fused_computation.69 | loop fusion | bytes 12435456 | tf_op jit(solution)/shard_map/squeeze | solution.py:49
  89.8 0.2 collective-permute-done.3
  90.0 0.8 copy-done.17
  90.8 1.1 pad_maximum_fusion.1
  91.9 0.6 gather_fusion
  92.5 0.2 broadcast_select_fusion.1
  92.7 0.6 gather_fusion.1
  93.3 0.2 broadcast_select_fusion
  93.6 0.3 constant_dynamic-slice_fusion
  93.9 0.2 collective-permute-start.9
  94.1 1.5 %collective-permute-start.7 = (bf16[128,512]{1,0:T(8,128)(2,1)S(1)}, bf16[128,512]{1,0:T(8,128)(2,1)S(1)}, u32[]{:S(2)}, u32[]{:S(2)}) collective-permute-start(bf16[128,512]{1,0:T(8,128)(2,1)S(1)} %get-tuple-element.41), channel_id=1, source_target_pairs={{0,2},{1,3},{2,0},{3,1},{4,6},{5,7},{6,4},{7,5},{8,10},{9,11},{10,... | collective-permute-start | bytes 393224 | tf_op jit(solution)/shard_map/ppermute | solution.py:139
  95.6 0.2 collective-permute-start.5
  95.7 1.1 compare_select_fusion
  96.8 0.2 collective-permute-done.9
  97.0 5.6 %collective-permute-done.7 = bf16[128,512]{1,0:T(8,128)(2,1)S(1)} collective-permute-done((bf16[128,512]{1,0:T(8,128)(2,1)S(1)}, bf16[128,512]{1,0:T(8,128)(2,1)S(1)}, u32[]{:S(2)}, u32[]{:S(2)}) %collective-permute-start.7) | collective-permute-done | bytes 131104 | tf_op jit(solution)/shard_map/ppermute | solution.py:139
  102.8 2.0 %convolution_convert_fusion.1 = bf16[512,512]{1,0:T(8,128)(2,1)S(1)} fusion(bf16[128,512]{1,0:T(8,128)(2,1)S(1)} %get-tuple-element.37, bf16[128,512]{1,0:T(8,128)(2,1)S(1)} %get-tuple-element.38, bf16[128,512]{1,0:T(8,128)(2,1)S(1)} %get-tuple-element.39, bf16[128,512]{1,0:T(8,128)(2,1)S(1)} %get-tuple-element.36, ...), kind=kOutput, calls=%fused_computation.46 | convolution fusion | flops 539492352 | bytes 2097152 | tf_op jit(solution)/shard_map/dot_general | solution.py:157
  104.8 0.3 convolution_bitcast_fusion
  105.2 0.3 convolution_bitcast_fusion.1
  105.5 0.4 copy-done.13
  105.9 0.3 convolution_bitcast_fusion.2
  106.2 0.3 convolution_bitcast_fusion.3
  106.6 0.3 convolution_bitcast_fusion.4
  107.0 0.3 copy-done.10
  107.3 0.3 convolution_bitcast_fusion.5
  107.6 0.3 convolution_bitcast_fusion.6
  108.0 0.3 convolution_bitcast_fusion.7
  108.3 0.1 copy-done.7
  108.4 0.3 convolution_bitcast_fusion.8
  108.8 0.3 convolution_bitcast_fusion.9
  109.1 0.3 convolution_bitcast_fusion.10
  109.5 0.1 copy-done.4
  109.6 0.3 convolution_bitcast_fusion.11
  109.9 0.3 convolution_bitcast_fusion.12
  110.3 0.3 convolution_bitcast_fusion.13
  110.6 0.4 copy-done.1
  111.0 0.3 convolution_bitcast_fusion.14
  111.3 0.3 convolution_bitcast_fusion.15
  111.7 0.2 copy-done.19
  111.9 0.1 pad_bitcast_fusion
  112.1 0.1 bitcast_dynamic-update-slice_fusion.14
  112.1 0.1 bitcast_dynamic-update-slice_fusion.13
  112.3 0.1 bitcast_dynamic-update-slice_fusion.11
  112.5 0.1 bitcast_dynamic-update-slice_fusion.9
  112.7 0.1 bitcast_dynamic-update-slice_fusion.7
  113.5 1.0 copy-done.16
  (72 shorter events, 1.7 us)
Async XLA Ops:
  0.6 102.2 %copy-start = (bf16[1,1,512,512]{3,2,1,0:T(8,128)(2,1)S(1)}, bf16[1,1,512,512]{3,2,1,0:T(8,128)(2,1)}, u32[]{:S(2)}) copy-start(bf16[1,1,512,512]{3,2,1,0:T(8,128)(2,1)} %param.15) | copy-start | bytes 1572868
  3.9 9.0 %copy-start.21 = (s32[1,1,4,4]{3,2,1,0:T(4,128)S(1)}, s32[1,1,4,4]{3,2,1,0:T(4,128)}, u32[]{:S(2)}) copy-start(s32[1,1,4,4]{3,2,1,0:T(4,128)} %param.16) | copy-start | bytes 196
  3.9 9.1 %copy-start.22 = (bf16[1,1,16,121]{3,2,1,0:T(8,128)(2,1)S(1)}, bf16[1,1,16,121]{3,2,1,0:T(8,128)(2,1)}, u32[]{:S(2)}) copy-start(bf16[1,1,16,121]{3,2,1,0:T(8,128)(2,1)} %param.17) | copy-start | bytes 11620
  3.9 9.5 %copy-start.20 = (s32[1,1,4]{2,1,0:T(1,128)S(1)}, s32[1,1,4]{2,1,0:T(1,128)}, u32[]{:S(2)}) copy-start(s32[1,1,4]{2,1,0:T(1,128)} %param.12) | copy-start | bytes 52
  3.9 55.7 %all-to-all-start = ((bf16[2,2,8,16,2048]{4,3,1,0,2:T(8,128)(2,1)}), bf16[2,2,8,16,2048]{4,3,1,0,2:T(8,128)(2,1)S(1)}, u32[]{:S(2)}, u32[]{:S(2)}) async-start(bf16[2,2,8,16,2048]{4,3,1,0,2:T(8,128)(2,1)} %copy.60), calls=%async_computation | async-start | bytes 4194304 | tf_op jit(solution)/shard_map/all_to_all | solution.py:105
  11.3 72.7 %collective-permute-start.8 = (s32[1]{0:T(128)}, s32[1]{0:T(128)}, u32[]{:S(2)}, u32[]{:S(2)}) collective-permute-start(s32[1]{0:T(128)} %bitcast.15), channel_id=1, source_target_pairs={{0,1},{1,2},{2,3},{3,0},{4,5},{5,6},{6,7},{7,4},{8,9},{9,10},{10,1... | collective-permute-start | bytes 20 | tf_op jit(solution)/shard_map/ppermute | solution.py:134
  11.3 74.0 %collective-permute-start.6 = (s32[1]{0:T(128)}, s32[1]{0:T(128)}, u32[]{:S(2)}, u32[]{:S(2)}) collective-permute-start(s32[1]{0:T(128)} %bitcast.15), channel_id=1, source_target_pairs={{0,2},{1,3},{2,0},{3,1},{4,6},{5,7},{6,4},{7,5},{8,10},{9,11},{10,... | collective-permute-start | bytes 20 | tf_op jit(solution)/shard_map/ppermute | solution.py:134
  62.7 6.3 %collective-permute-start.2 = (f32[16,2048]{1,0:T(8,128)S(1)}, f32[16,2048]{1,0:T(8,128)S(1)}, u32[]{:S(2)}, u32[]{:S(2)}) collective-permute-start(f32[16,2048]{1,0:T(8,128)S(1)} %div.162), channel_id=1, source_target_pairs={{0,24},{4,28},{8,0},{12,4},{16,8},{20,12},{24,16},{28,20},{1,25},{... | collective-permute-start | bytes 393224 | tf_op jit(solution)/shard_map/ppermute | solution.py:114
  65.0 11.5 %collective-permute-start.1 = (f32[16,2048]{1,0:T(8,128)S(1)}, f32[16,2048]{1,0:T(8,128)S(1)}, u32[]{:S(2)}, u32[]{:S(2)}) collective-permute-start(f32[16,2048]{1,0:T(8,128)S(1)} %div.162), channel_id=1, source_target_pairs={{0,16},{4,20},{8,24},{12,28},{16,0},{20,4},{24,8},{28,12},{1,17},{... | collective-permute-start | bytes 393224 | tf_op jit(solution)/shard_map/ppermute | solution.py:114
  65.0 11.5 %collective-permute-start = (f32[16,2048]{1,0:T(8,128)S(1)}, f32[16,2048]{1,0:T(8,128)S(1)}, u32[]{:S(2)}, u32[]{:S(2)}) collective-permute-start(f32[16,2048]{1,0:T(8,128)S(1)} %div.162), channel_id=1, source_target_pairs={{0,8},{4,12},{8,16},{12,20},{16,24},{20,28},{24,0},{28,4},{1,9},{5... | collective-permute-start | bytes 393224 | tf_op jit(solution)/shard_map/ppermute | solution.py:114
  69.0 17.6 %collective-permute-start.4 = (s32[1]{0:T(128)}, s32[1]{0:T(128)}, u32[]{:S(2)}, u32[]{:S(2)}) collective-permute-start(s32[1]{0:T(128)} %bitcast.15), channel_id=1, source_target_pairs={{0,3},{1,0},{2,1},{3,2},{4,7},{5,4},{6,5},{7,6},{8,11},{9,8},{10,9... | collective-permute-start | bytes 20 | tf_op jit(solution)/shard_map/ppermute | solution.py:134
  76.7 13.4 %collective-permute-start.3 = (f32[4,16,2048]{2,1,0:T(8,128)S(1)}, f32[4,16,2048]{2,1,0:T(8,128)S(1)}, u32[]{:S(2)}, u32[]{:S(2)}) collective-permute-start(f32[4,16,2048]{2,1,0:T(8,128)S(1)} %get-tuple-element.45), channel_id=1, source_target_pairs={{0,4},{4,0},{8,12},{12,8},{16,20},{20,16},{24,28},{28,24},{1,5},{5... | collective-permute-start | bytes 1572872 | tf_op jit(solution)/shard_map/ppermute | solution.py:121
  90.0 0.8 copy-start.17
  93.9 3.1 %collective-permute-start.9 = (bf16[128,512]{1,0:T(8,128)(2,1)S(1)}, bf16[128,512]{1,0:T(8,128)(2,1)S(1)}, u32[]{:S(2)}, u32[]{:S(2)}) collective-permute-start(bf16[128,512]{1,0:T(8,128)(2,1)S(1)} %get-tuple-element.40), channel_id=1, source_target_pairs={{0,3},{1,0},{2,1},{3,2},{4,7},{5,4},{6,5},{7,6},{8,11},{9,8},{10,9... | collective-permute-start | bytes 393224 | tf_op jit(solution)/shard_map/ppermute | solution.py:139
  94.1 8.5 %collective-permute-start.7 = (bf16[128,512]{1,0:T(8,128)(2,1)S(1)}, bf16[128,512]{1,0:T(8,128)(2,1)S(1)}, u32[]{:S(2)}, u32[]{:S(2)}) collective-permute-start(bf16[128,512]{1,0:T(8,128)(2,1)S(1)} %get-tuple-element.41), channel_id=1, source_target_pairs={{0,2},{1,3},{2,0},{3,1},{4,6},{5,7},{6,4},{7,5},{8,10},{9,11},{10,... | collective-permute-start | bytes 393224 | tf_op jit(solution)/shard_map/ppermute | solution.py:139
  95.6 7.1 %collective-permute-start.5 = (bf16[128,512]{1,0:T(8,128)(2,1)S(1)}, bf16[128,512]{1,0:T(8,128)(2,1)S(1)}, u32[]{:S(2)}, u32[]{:S(2)}) collective-permute-start(bf16[128,512]{1,0:T(8,128)(2,1)S(1)} %get-tuple-element.42), channel_id=1, source_target_pairs={{0,1},{1,2},{2,3},{3,0},{4,5},{5,6},{6,7},{7,4},{8,9},{9,10},{10,1... | collective-permute-start | bytes 393224 | tf_op jit(solution)/shard_map/ppermute | solution.py:139
  102.8 2.0 %copy-start.15 = (bf16[11,138,128]{2,0,1:T(8,128)(2,1)S(1)}, bf16[11,138,128]{2,0,1:T(8,128)(2,1)}, u32[]{:S(2)}) copy-start(bf16[11,138,128]{2,0,1:T(8,128)(2,1)} %get-tuple-element.20) | copy-start | bytes 1165828
  102.8 2.4 %copy-start.14 = (bf16[11,138,128]{2,0,1:T(8,128)(2,1)S(1)}, bf16[11,138,128]{2,0,1:T(8,128)(2,1)}, u32[]{:S(2)}) copy-start(bf16[11,138,128]{2,0,1:T(8,128)(2,1)} %get-tuple-element.21) | copy-start | bytes 1165828
  104.8 1.1 copy-start.13
  105.1 1.1 copy-start.12
  105.5 1.1 copy-start.11
  106.2 1.1 copy-start.10
  106.2 1.4 %copy-start.9 = (bf16[11,138,128]{2,0,1:T(8,128)(2,1)S(1)}, bf16[11,138,128]{2,0,1:T(8,128)(2,1)}, u32[]{:S(2)}) copy-start(bf16[11,138,128]{2,0,1:T(8,128)(2,1)} %get-tuple-element.26) | copy-start | bytes 1165828
  106.6 1.3 %copy-start.8 = (bf16[11,138,128]{2,0,1:T(8,128)(2,1)S(1)}, bf16[11,138,128]{2,0,1:T(8,128)(2,1)}, u32[]{:S(2)}) copy-start(bf16[11,138,128]{2,0,1:T(8,128)(2,1)} %get-tuple-element.27) | copy-start | bytes 1165828
  107.3 1.1 copy-start.7
  107.6 1.1 copy-start.6
  108.0 1.1 copy-start.5
  108.4 1.1 copy-start.4
  108.8 1.1 copy-start.3
  109.1 1.1 copy-start.2
  109.9 1.1 copy-start.1
  110.6 1.1 copy-start.18
  110.6 1.2 %copy-start.19 = (bf16[1,1,512,512]{3,2,1,0:T(8,128)(2,1)S(1)}, bf16[1,1,512,512]{3,2,1,0:T(8,128)(2,1)}, u32[]{:S(2)}) copy-start(bf16[1,1,512,512]{3,2,1,0:T(8,128)(2,1)} %param.18) | copy-start | bytes 1572868
  113.5 1.0 copy-start.16

commit v18 on v16

--- a/solution.py
+++ b/solution.py
@@ -100,16 +100,43 @@
     n_sky = lax.axis_size("sky")
     local_visits, strip_rows, sky_w = warped.shape
     stacked = jnp.stack([warped, inv_var], axis=0)
-    tap_rows = psf_taps(cell_ids[0, 0], kernels[0, 0])
-    stacked, tap_rows = lax.optimization_barrier((stacked, tap_rows))
     chunk = strip_rows // n_visit
     stacked = stacked.reshape(2, local_visits, n_visit, chunk, sky_w)
     gathered = lax.all_to_all(stacked, "visit", split_axis=2, concat_axis=1, tiled=True)
     gathered = gathered.reshape(2, local_visits * n_visit, chunk, sky_w)
     row_share = local_coadd(gathered[0].astype(jnp.float32), gathered[1].astype(jnp.float32))
-    copies = jnp.broadcast_to(row_share[None], (n_visit,) + row_share.shape)
-    coadd_field = lax.all_to_all(copies, "visit", split_axis=0, concat_axis=0, tiled=True)
-    bands = psf_bands(tap_rows)
+    outer = n_visit // 2
+    visit_me = lax.axis_index("visit")
+    outer_me, inner_me = visit_me // 2, visit_me % 2
+    pick_inner = jnp.arange(2, dtype=jnp.int32) ^ inner_me
+    pick_outer = (outer_me - jnp.arange(outer, dtype=jnp.int32)) % outer
+
+    def outer_stage(part):
+        same = [part]
+        for shift in range(1, outer):
+            same.append(
+                lax.ppermute(
+                    part,
+                    "visit",
+                    perm=[(v, ((v // 2 + shift) % outer) * 2 + v % 2) for v in range(n_visit)],
+                )
+            )
+        return jnp.stack(same, axis=0)
+
+    def inner_stage(same):
+        other = lax.ppermute(same, "visit", perm=[(v, v ^ 1) for v in range(n_visit)])
+        both = jnp.stack([same, other], axis=0)
+        return jnp.take(jnp.take(both, pick_inner, axis=0), pick_outer, axis=1)
+
+    half = chunk // 2
+    same_first = outer_stage(row_share[:half])
+    second, same_first = lax.optimization_barrier((row_share[half:], same_first))
+    same_second = outer_stage(second)
+    coadd_field = jnp.concatenate(
+        [inner_stage(same_first), inner_stage(same_second)], axis=2
+    )
+    coadd_field = coadd_field.transpose(1, 0, 2, 3)
+    bands = psf_bands(psf_taps(cell_ids[0, 0], kernels[0, 0]))
     coadd_field = coadd_field.reshape(n_visit * chunk, sky_w)
     coadd_low = coadd_field.astype(jnp.bfloat16)
 

time: 116 us -> 115 us (level)
  blocking collectives: 55.3 us -> 0 us
  waiting for transfers between devices: 13 us -> 55.6 us
  starting transfers between devices: 8.4 us -> 20.4 us
  matrix products: 12.6 us -> 9.84 us
  local copies, waits for them, and re-layouts: 8.73 us -> 11.1 us
    all_to_all x1 -> x0, blocking collectives: 55.3 us -> none  [shards(): lax.all_to_all(stacked, 'visit', split_axis=2, concat_axis=1, tiled=True)]
    all_to_all x1, waiting for transfers between devices: 7.07 us -> 39.7 us  [shards(): lax.all_to_all(stacked, 'visit', split_axis=2, concat_axis=1, tiled=True)]
    ppermute x0 -> x8, waiting for transfers between devices: none -> 10 us  [the longest x6 9.06 us: outer_stage(): lax.ppermute(part, 'visit', perm=[(v, (v // 2 + shift) % outer * 2 + v %...]
    ppermute x0 -> x8, starting transfers between devices: none -> 9.62 us  [the longest x6 7.52 us: outer_stage(): lax.ppermute(part, 'visit', perm=[(v, (v // 2 + shift) % outer * 2 + v %...]
    all_to_all x1, starting transfers between devices: 3.59 us -> 7.41 us  [shards(): lax.all_to_all(stacked, 'visit', split_axis=2, concat_axis=1, tiled=True)]
    gather x0 -> x4, local copies, waits for them, and re-layouts: none -> 2.32 us  [inner_stage(): return jnp.take(jnp.take(both, pick_inner, axis=0), pick_outer, axis=1)]
    dot_general x16, matrix products: 7.39 us -> 5.16 us  [psf_outlier(): jnp.einsum('rc,acl->arl', cols_window, bands[row_block * blocks + col_blo...]
    another operation x0 -> x2, local copies, waits for them, and re-layouts: none -> 1.48 us  [the longest x1 1.47 us: shards(): stacked = jnp.stack([warped, inv_var], axis=0)]
  transfers between devices with their start and end apart: 7 -> 15, of which waited for: 2 -> 7; matrix products, arithmetic and copies ran while one was open for 6% -> 10% of each run, Pallas kernels for 0% -> 0%
where the time goes in v18:
time: 115 us
  waiting for transfers between devices  55.6 us (48%)
  starting transfers between devices  20.4 us (18%)
  local copies, waits for them, and re-layouts  11.1 us (10%)
  matrix products  9.84 us (9%)
  between operations  9.68 us (8%)
  other arithmetic  8.11 us (7%)
    all_to_all x1, waiting for transfers between devices, shards(): lax.all_to_all(stacked, 'visit', split_axis=2, concat_axis=1, tiled=True)  39.7 us
    ppermute x6, waiting for transfers between devices, outer_stage(): lax.ppermute(part, 'visit', perm=[(v, (v // 2 + shift) % outer * 2 + v %...  9.06 us
    ppermute x6, starting transfers between devices, outer_stage(): lax.ppermute(part, 'visit', perm=[(v, (v // 2 + shift) % outer * 2 + v %...  7.52 us
    all_to_all x1, starting transfers between devices, shards(): lax.all_to_all(stacked, 'visit', split_axis=2, concat_axis=1, tiled=True)  7.41 us
    ppermute x3, waiting for transfers between devices, shards(): lax.ppermute(outgoing, 'sky', perm=[(i, (i + shift) % n_sky) for i in ran...  5.88 us
    dot_general x16, matrix products, psf_outlier(): jnp.einsum('rc,acl->arl', cols_window, bands[row_block * blocks + col_blo...  5.16 us
    squeeze x1, local copies, waits for them, and re-layouts, psf_bands(): banded_all[r, c]  3.35 us
    unnamed x44, local copies, waits for them, and re-layouts  2.66 us
  transfers between devices with their start and end apart: 15, of which 7 were waited for; matrix products, arithmetic and copies ran while one was open for 10% of the time, Pallas kernels for 0%

profile of v18, /device:TPU:0, one launch (start us, length us, event | category | flops | bytes accessed | tf_op | source)
XLA Modules:
  0.0 114.7 jit_solution(6742157618025870167)
XLA Ops:
  0.6 1.8 %pad_maximum_fusion = bf16[2,2,8,16,2048]{4,3,2,1,0:T(8,128)(2,1)S(1)} fusion(bf16[1,2,8,16,2048]{4,3,2,1,0:T(8,128)(2,1)} %bitcast.475, bf16[1,2,8,16,2048]{4,3,2,1,0:T(8,128)(2,1)} %bitcast.476), kind=kLoop, calls=%fused_computation.31 | loop fusion | flops 1048576 | bytes 4194304 | tf_op jit(solution)/shard_map/stack | solution.py:102
  2.4 1.5 %copy.60 = bf16[2,2,8,16,2048]{4,3,1,0,2:T(8,128)(2,1)} copy(bf16[2,2,8,16,2048]{4,3,2,1,0:T(8,128)(2,1)S(1)} %pad_maximum_fusion) | data formatting | bytes 4194304 | tf_op jit(solution)/shard_map/stack | solution.py:102
  3.9 7.4 %all-to-all-start = ((bf16[2,2,8,16,2048]{4,3,1,0,2:T(8,128)(2,1)}), bf16[2,2,8,16,2048]{4,3,1,0,2:T(8,128)(2,1)S(1)}, u32[]{:S(2)}, u32[]{:S(2)}) async-start(bf16[2,2,8,16,2048]{4,3,1,0,2:T(8,128)(2,1)} %copy.60), calls=%async_computation | async-start | bytes 4194304 | tf_op jit(solution)/shard_map/all_to_all | solution.py:105
  11.3 1.6 %collective-permute-start.10 = (s32[1]{0:T(128)}, s32[1]{0:T(128)}, u32[]{:S(2)}, u32[]{:S(2)}) collective-permute-start(s32[1]{0:T(128)} %bitcast.22), channel_id=1, source_target_pairs={{0,2},{1,3},{2,0},{3,1},{4,6},{5,7},{6,4},{7,5},{8,10},{9,11},{10,... | collective-permute-start | bytes 20 | tf_op jit(solution)/shard_map/ppermute | solution.py:146
  13.0 0.2 convolution_convert_fusion.3
  13.2 0.1 reshape.303
  13.4 0.7 fusion.207
  14.1 2.5 %convolution_convert_fusion = bf16[4,4,11,138,128]{4,2,3,1,0:T(8,128)(2,1)S(1)} fusion(s32[138,128]{1,0:T(8,128)S(1)} %iota_subtract_fusion, bf16[4,4,11,11,1]{3,2,1,0,4:T(8,128)(2,1)S(1)} %reshape.303), kind=kOutput, calls=%fused_computation.4 | convolution fusion | flops 71698176 | bytes 6292256 | tf_op jit(solution)/shard_map/xyab,bcl->xyacl/dot_general | solution.py:46
  16.6 3.4 %slice_bitcast_fusion = (bf16[11,138,128]{2,0,1:T(8,128)(2,1)}, bf16[11,138,128]{2,0,1:T(8,128)(2,1)}, bf16[11,138,128]{2,0,1:T(8,128)(2,1)}, bf16[11,138,128]{2...) fusion(bf16[4,4,11,138,128]{4,2,3,1,0:T(8,128)(2,1)S(1)} %convo, ...), kind=kLoop, calls=%fused_computation.71 | loop fusion | bytes 12435456 | tf_op jit(solution)/shard_map/squeeze | solution.py:49
  19.9 39.7 %all-to-all-done = bf16[2,2,8,16,2048]{4,3,1,0,2:T(8,128)(2,1)S(1)} async-done(((bf16[2,2,8,16,2048]{4,3,1,0,2:T(8,128)(2,1)}), bf16[2,2,8,16,2048]{4,3,1,0,2:T(8,128)(2,1)S(1)}, u32[]{:S(2)}, u32[]{:S(2)}) %all-to-all-start) | async-done | bytes 2097184 | tf_op jit(solution)/shard_map/all_to_all | solution.py:105
  59.6 0.4 convert_reduce_fusion
  60.0 0.9 fusion.15
  60.9 0.9 fusion.16
  61.8 0.9 fusion.17
  62.8 2.8 %collective-permute-start = (f32[8,2048]{1,0:T(8,128)S(1)}, f32[8,2048]{1,0:T(8,128)S(1)}, u32[]{:S(2)}, u32[]{:S(2)}) collective-permute-start(f32[8,2048]{1,0:T(8,128)S(1)} %get-tuple-element.53), channel_id=1, source_target_pairs={{0,8},{4,12},{8,16},{12,20},{16,24},{20,28},{24,0},{28,4},{1,9},{5... | collective-permute-start | bytes 196616 | tf_op jit(solution)/shard_map/ppermute | solution.py:118
  65.6 1.1 collective-permute-start.2
  66.7 3.4 %collective-permute-done.1 = f32[8,2048]{1,0:T(8,128)S(1)} collective-permute-done((f32[8,2048]{1,0:T(8,128)S(1)}, f32[8,2048]{1,0:T(8,128)S(1)}, u32[]{:S(2)}, u32[]{:S(2)}) %collective-permute-start.1) | collective-permute-done | bytes 65568 | tf_op jit(solution)/shard_map/ppermute | solution.py:118
  70.1 0.5 collective-permute-done.2
  70.7 2.2 %collective-permute-start.6 = (f32[8,2048]{1,0:T(8,128)S(1)}, f32[8,2048]{1,0:T(8,128)S(1)}, u32[]{:S(2)}, u32[]{:S(2)}) collective-permute-start(f32[8,2048]{1,0:T(8,128)S(1)} %get-tuple-element.12), channel_id=1, source_target_pairs={{0,24},{4,28},{8,0},{12,4},{16,8},{20,12},{24,16},{28,20},{1,25},{... | collective-permute-start | bytes 196616 | tf_op jit(solution)/shard_map/ppermute | solution.py:118
  72.9 1.3 %collective-permute-start.4 = (f32[8,2048]{1,0:T(8,128)S(1)}, f32[8,2048]{1,0:T(8,128)S(1)}, u32[]{:S(2)}, u32[]{:S(2)}) collective-permute-start(f32[8,2048]{1,0:T(8,128)S(1)} %get-tuple-element.12), channel_id=1, source_target_pairs={{0,8},{4,12},{8,16},{12,20},{16,24},{20,28},{24,0},{28,4},{1,9},{5... | collective-permute-start | bytes 196616 | tf_op jit(solution)/shard_map/ppermute | solution.py:118
  74.3 1.1 collective-permute-done.6
  75.4 4.0 %collective-permute-done.5 = f32[8,2048]{1,0:T(8,128)S(1)} collective-permute-done((f32[8,2048]{1,0:T(8,128)S(1)}, f32[8,2048]{1,0:T(8,128)S(1)}, u32[]{:S(2)}, u32[]{:S(2)}) %collective-permute-start.5) | collective-permute-done | bytes 65568 | tf_op jit(solution)/shard_map/ppermute | solution.py:118
  79.4 1.6 %collective-permute-start.3 = (f32[4,8,2048]{2,1,0:T(8,128)S(1)}, f32[4,8,2048]{2,1,0:T(8,128)S(1)}, u32[]{:S(2)}, u32[]{:S(2)}) collective-permute-start(f32[4,8,2048]{2,1,0:T(8,128)S(1)} %pad_maximum_fusion.5), channel_id=1, source_target_pairs={{0,4},{4,0},{8,12},{12,8},{16,20},{20,16},{24,28},{28,24},{1,5},{5... | collective-permute-start | bytes 786440 | tf_op jit(solution)/shard_map/ppermute | solution.py:127
  81.0 0.4 collective-permute-start.7
  90.0 0.6 gather_fusion
  90.6 1.0 collective-permute-done.7
  91.6 0.6 gather_fusion.2
  92.2 0.2 broadcast_select_fusion.1
  92.3 0.6 gather_fusion.1
  92.9 0.6 gather_fusion.3
  93.5 0.1 select_bitcast_fusion.1
  93.7 0.1 pad_maximum_fusion.1
  93.8 0.3 constant_dynamic-slice_fusion
  94.2 1.6 %collective-permute-start.11 = (bf16[128,512]{1,0:T(8,128)(2,1)S(1)}, bf16[128,512]{1,0:T(8,128)(2,1)S(1)}, u32[]{:S(2)}, u32[]{:S(2)}) collective-permute-start(bf16[128,512]{1,0:T(8,128)(2,1)S(1)} %get-tuple-element.47), channel_id=1, source_target_pairs={{0,2},{1,3},{2,0},{3,1},{4,6},{5,7},{6,4},{7,5},{8,10},{9,11},{10,... | collective-permute-start | bytes 393224 | tf_op jit(solution)/shard_map/ppermute | solution.py:151
  95.8 0.2 collective-permute-start.9
  96.0 1.1 compare_select_fusion
  97.1 5.8 %collective-permute-done.11 = bf16[128,512]{1,0:T(8,128)(2,1)S(1)} collective-permute-done((bf16[128,512]{1,0:T(8,128)(2,1)S(1)}, bf16[128,512]{1,0:T(8,128)(2,1)S(1)}, u32[]{:S(2)}, u32[]{:S(2)}) %collective-permute-start.11) | collective-permute-done | bytes 131104 | tf_op jit(solution)/shard_map/ppermute | solution.py:151
  103.0 2.0 %convolution_convert_fusion.1 = bf16[512,512]{1,0:T(8,128)(2,1)S(1)} fusion(bf16[128,512]{1,0:T(8,128)(2,1)S(1)} %get-tuple-element.43, bf16[128,512]{1,0:T(8,128)(2,1)S(1)} %get-tuple-element.44, bf16[128,512]{1,0:T(8,128)(2,1)S(1)} %get-tuple-element.45, bf16[128,512]{1,0:T(8,128)(2,1)S(1)} %get-tuple-element.42, ...), kind=kOutput, calls=%fused_computation.48 | convolution fusion | flops 539492352 | bytes 2097152 | tf_op jit(solution)/shard_map/dot_general | solution.py:169
  105.1 0.3 convolution_bitcast_fusion
  105.4 0.3 convolution_bitcast_fusion.1
  105.7 0.4 copy-done.13
  106.1 0.3 convolution_bitcast_fusion.2
  106.5 0.3 convolution_bitcast_fusion.3
  106.9 0.3 convolution_bitcast_fusion.4
  107.2 0.3 copy-done.10
  107.5 0.3 convolution_bitcast_fusion.5
  107.9 0.3 convolution_bitcast_fusion.6
  108.2 0.3 convolution_bitcast_fusion.7
  108.6 0.1 copy-done.7
  108.7 0.3 convolution_bitcast_fusion.8
  109.0 0.3 convolution_bitcast_fusion.9
  109.4 0.3 convolution_bitcast_fusion.10
  109.7 0.1 copy-done.4
  109.8 0.3 convolution_bitcast_fusion.11
  110.2 0.3 convolution_bitcast_fusion.12
  110.5 0.3 convolution_bitcast_fusion.13
  110.9 0.4 copy-done.1
  111.2 0.3 convolution_bitcast_fusion.14
  111.6 0.3 convolution_bitcast_fusion.15
  111.9 0.2 copy-done.18
  112.2 0.1 pad_bitcast_fusion
  112.3 0.1 bitcast_dynamic-update-slice_fusion.14
  112.5 0.1 bitcast_dynamic-update-slice_fusion.12
  113.8 1.0 copy-done.16
  (84 shorter events, 2.4 us)
Async XLA Ops:
  0.6 102.4 %copy-start = (bf16[1,1,512,512]{3,2,1,0:T(8,128)(2,1)S(1)}, bf16[1,1,512,512]{3,2,1,0:T(8,128)(2,1)}, u32[]{:S(2)}) copy-start(bf16[1,1,512,512]{3,2,1,0:T(8,128)(2,1)} %param.19) | copy-start | bytes 1572868
  3.9 9.0 %copy-start.20 = (s32[1,1,4,4]{3,2,1,0:T(4,128)S(1)}, s32[1,1,4,4]{3,2,1,0:T(4,128)}, u32[]{:S(2)}) copy-start(s32[1,1,4,4]{3,2,1,0:T(4,128)} %param.20) | copy-start | bytes 196
  3.9 9.1 %copy-start.21 = (bf16[1,1,16,121]{3,2,1,0:T(8,128)(2,1)S(1)}, bf16[1,1,16,121]{3,2,1,0:T(8,128)(2,1)}, u32[]{:S(2)}) copy-start(bf16[1,1,16,121]{3,2,1,0:T(8,128)(2,1)} %param.21) | copy-start | bytes 11620
  3.9 9.5 %copy-start.19 = (s32[1,1,4]{2,1,0:T(1,128)S(1)}, s32[1,1,4]{2,1,0:T(1,128)}, u32[]{:S(2)}) copy-start(s32[1,1,4]{2,1,0:T(1,128)} %param.16) | copy-start | bytes 52
  3.9 55.7 %all-to-all-start = ((bf16[2,2,8,16,2048]{4,3,1,0,2:T(8,128)(2,1)}), bf16[2,2,8,16,2048]{4,3,1,0,2:T(8,128)(2,1)S(1)}, u32[]{:S(2)}, u32[]{:S(2)}) async-start(bf16[2,2,8,16,2048]{4,3,1,0,2:T(8,128)(2,1)} %copy.60), calls=%async_computation | async-start | bytes 4194304 | tf_op jit(solution)/shard_map/all_to_all | solution.py:105
  11.3 73.3 %collective-permute-start.12 = (s32[1]{0:T(128)}, s32[1]{0:T(128)}, u32[]{:S(2)}, u32[]{:S(2)}) collective-permute-start(s32[1]{0:T(128)} %bitcast.22), channel_id=1, source_target_pairs={{0,1},{1,2},{2,3},{3,0},{4,5},{5,6},{6,7},{7,4},{8,9},{9,10},{10,1... | collective-permute-start | bytes 20 | tf_op jit(solution)/shard_map/ppermute | solution.py:146
  11.3 74.5 %collective-permute-start.10 = (s32[1]{0:T(128)}, s32[1]{0:T(128)}, u32[]{:S(2)}, u32[]{:S(2)}) collective-permute-start(s32[1]{0:T(128)} %bitcast.22), channel_id=1, source_target_pairs={{0,2},{1,3},{2,0},{3,1},{4,6},{5,7},{6,4},{7,5},{8,10},{9,11},{10,... | collective-permute-start | bytes 20 | tf_op jit(solution)/shard_map/ppermute | solution.py:146
  62.7 7.4 %collective-permute-start.1 = (f32[8,2048]{1,0:T(8,128)S(1)}, f32[8,2048]{1,0:T(8,128)S(1)}, u32[]{:S(2)}, u32[]{:S(2)}) collective-permute-start(f32[8,2048]{1,0:T(8,128)S(1)} %get-tuple-element.53), channel_id=1, source_target_pairs={{0,16},{4,20},{8,24},{12,28},{16,0},{20,4},{24,8},{28,12},{1,17},{... | collective-permute-start | bytes 196616 | tf_op jit(solution)/shard_map/ppermute | solution.py:118
  62.8 7.3 %collective-permute-start = (f32[8,2048]{1,0:T(8,128)S(1)}, f32[8,2048]{1,0:T(8,128)S(1)}, u32[]{:S(2)}, u32[]{:S(2)}) collective-permute-start(f32[8,2048]{1,0:T(8,128)S(1)} %get-tuple-element.53), channel_id=1, source_target_pairs={{0,8},{4,12},{8,16},{12,20},{16,24},{20,28},{24,0},{28,4},{1,9},{5... | collective-permute-start | bytes 196616 | tf_op jit(solution)/shard_map/ppermute | solution.py:118
  65.6 5.1 %collective-permute-start.2 = (f32[8,2048]{1,0:T(8,128)S(1)}, f32[8,2048]{1,0:T(8,128)S(1)}, u32[]{:S(2)}, u32[]{:S(2)}) collective-permute-start(f32[8,2048]{1,0:T(8,128)S(1)} %get-tuple-element.53), channel_id=1, source_target_pairs={{0,24},{4,28},{8,0},{12,4},{16,8},{20,12},{24,16},{28,20},{1,25},{... | collective-permute-start | bytes 196616 | tf_op jit(solution)/shard_map/ppermute | solution.py:118
  70.7 4.7 %collective-permute-start.6 = (f32[8,2048]{1,0:T(8,128)S(1)}, f32[8,2048]{1,0:T(8,128)S(1)}, u32[]{:S(2)}, u32[]{:S(2)}) collective-permute-start(f32[8,2048]{1,0:T(8,128)S(1)} %get-tuple-element.12), channel_id=1, source_target_pairs={{0,24},{4,28},{8,0},{12,4},{16,8},{20,12},{24,16},{28,20},{1,25},{... | collective-permute-start | bytes 196616 | tf_op jit(solution)/shard_map/ppermute | solution.py:118
  72.9 6.4 %collective-permute-start.5 = (f32[8,2048]{1,0:T(8,128)S(1)}, f32[8,2048]{1,0:T(8,128)S(1)}, u32[]{:S(2)}, u32[]{:S(2)}) collective-permute-start(f32[8,2048]{1,0:T(8,128)S(1)} %get-tuple-element.12), channel_id=1, source_target_pairs={{0,16},{4,20},{8,24},{12,28},{16,0},{20,4},{24,8},{28,12},{1,17},{... | collective-permute-start | bytes 196616 | tf_op jit(solution)/shard_map/ppermute | solution.py:118
  72.9 8.1 %collective-permute-start.4 = (f32[8,2048]{1,0:T(8,128)S(1)}, f32[8,2048]{1,0:T(8,128)S(1)}, u32[]{:S(2)}, u32[]{:S(2)}) collective-permute-start(f32[8,2048]{1,0:T(8,128)S(1)} %get-tuple-element.12), channel_id=1, source_target_pairs={{0,8},{4,12},{8,16},{12,20},{16,24},{20,28},{24,0},{28,4},{1,9},{5... | collective-permute-start | bytes 196616 | tf_op jit(solution)/shard_map/ppermute | solution.py:118
  75.4 11.7 %collective-permute-start.8 = (s32[1]{0:T(128)}, s32[1]{0:T(128)}, u32[]{:S(2)}, u32[]{:S(2)}) collective-permute-start(s32[1]{0:T(128)} %bitcast.22), channel_id=1, source_target_pairs={{0,3},{1,0},{2,1},{3,2},{4,7},{5,4},{6,5},{7,6},{8,11},{9,8},{10,9... | collective-permute-start | bytes 20 | tf_op jit(solution)/shard_map/ppermute | solution.py:146
  79.4 10.6 %collective-permute-start.3 = (f32[4,8,2048]{2,1,0:T(8,128)S(1)}, f32[4,8,2048]{2,1,0:T(8,128)S(1)}, u32[]{:S(2)}, u32[]{:S(2)}) collective-permute-start(f32[4,8,2048]{2,1,0:T(8,128)S(1)} %pad_maximum_fusion.5), channel_id=1, source_target_pairs={{0,4},{4,0},{8,12},{12,8},{16,20},{20,16},{24,28},{28,24},{1,5},{5... | collective-permute-start | bytes 786440 | tf_op jit(solution)/shard_map/ppermute | solution.py:127
  81.0 10.5 %collective-permute-start.7 = (f32[4,8,2048]{2,1,0:T(8,128)S(1)}, f32[4,8,2048]{2,1,0:T(8,128)S(1)}, u32[]{:S(2)}, u32[]{:S(2)}) collective-permute-start(f32[4,8,2048]{2,1,0:T(8,128)S(1)} %get-tuple-element.51), channel_id=1, source_target_pairs={{0,4},{4,0},{8,12},{12,8},{16,20},{20,16},{24,28},{28,24},{1,5},{5... | collective-permute-start | bytes 786440 | tf_op jit(solution)/shard_map/ppermute | solution.py:127
  94.2 2.9 %collective-permute-start.13 = (bf16[128,512]{1,0:T(8,128)(2,1)S(1)}, bf16[128,512]{1,0:T(8,128)(2,1)S(1)}, u32[]{:S(2)}, u32[]{:S(2)}) collective-permute-start(bf16[128,512]{1,0:T(8,128)(2,1)S(1)} %get-tuple-element.46), channel_id=1, source_target_pairs={{0,3},{1,0},{2,1},{3,2},{4,7},{5,4},{6,5},{7,6},{8,11},{9,8},{10,9... | collective-permute-start | bytes 393224 | tf_op jit(solution)/shard_map/ppermute | solution.py:151
  94.2 8.6 %collective-permute-start.11 = (bf16[128,512]{1,0:T(8,128)(2,1)S(1)}, bf16[128,512]{1,0:T(8,128)(2,1)S(1)}, u32[]{:S(2)}, u32[]{:S(2)}) collective-permute-start(bf16[128,512]{1,0:T(8,128)(2,1)S(1)} %get-tuple-element.47), channel_id=1, source_target_pairs={{0,2},{1,3},{2,0},{3,1},{4,6},{5,7},{6,4},{7,5},{8,10},{9,11},{10,... | collective-permute-start | bytes 393224 | tf_op jit(solution)/shard_map/ppermute | solution.py:151
  95.8 7.1 %collective-permute-start.9 = (bf16[128,512]{1,0:T(8,128)(2,1)S(1)}, bf16[128,512]{1,0:T(8,128)(2,1)S(1)}, u32[]{:S(2)}, u32[]{:S(2)}) collective-permute-start(bf16[128,512]{1,0:T(8,128)(2,1)S(1)} %get-tuple-element.48), channel_id=1, source_target_pairs={{0,1},{1,2},{2,3},{3,0},{4,5},{5,6},{6,7},{7,4},{8,9},{9,10},{10,1... | collective-permute-start | bytes 393224 | tf_op jit(solution)/shard_map/ppermute | solution.py:151
  103.0 2.0 %copy-start.15 = (bf16[11,138,128]{2,0,1:T(8,128)(2,1)S(1)}, bf16[11,138,128]{2,0,1:T(8,128)(2,1)}, u32[]{:S(2)}) copy-start(bf16[11,138,128]{2,0,1:T(8,128)(2,1)} %get-tuple-element.26) | copy-start | bytes 1165828
  103.0 2.4 %copy-start.14 = (bf16[11,138,128]{2,0,1:T(8,128)(2,1)S(1)}, bf16[11,138,128]{2,0,1:T(8,128)(2,1)}, u32[]{:S(2)}) copy-start(bf16[11,138,128]{2,0,1:T(8,128)(2,1)} %get-tuple-element.27) | copy-start | bytes 1165828
  105.0 1.1 copy-start.13
  105.4 1.1 copy-start.12
  105.7 1.1 copy-start.11
  106.4 1.1 copy-start.10
  106.5 1.4 %copy-start.9 = (bf16[11,138,128]{2,0,1:T(8,128)(2,1)S(1)}, bf16[11,138,128]{2,0,1:T(8,128)(2,1)}, u32[]{:S(2)}) copy-start(bf16[11,138,128]{2,0,1:T(8,128)(2,1)} %get-tuple-element.32) | copy-start | bytes 1165828
  106.9 1.3 %copy-start.8 = (bf16[11,138,128]{2,0,1:T(8,128)(2,1)S(1)}, bf16[11,138,128]{2,0,1:T(8,128)(2,1)}, u32[]{:S(2)}) copy-start(bf16[11,138,128]{2,0,1:T(8,128)(2,1)} %get-tuple-element.33) | copy-start | bytes 1165828
  107.5 1.1 copy-start.7
  107.9 1.1 copy-start.6
  108.2 1.1 copy-start.5
  108.7 1.1 copy-start.4
  109.0 1.1 copy-start.3
  109.4 1.1 copy-start.2
  110.1 1.1 copy-start.1
  110.8 1.1 copy-start.17
  110.8 1.2 %copy-start.18 = (bf16[1,1,512,512]{3,2,1,0:T(8,128)(2,1)S(1)}, bf16[1,1,512,512]{3,2,1,0:T(8,128)(2,1)}, u32[]{:S(2)}) copy-start(bf16[1,1,512,512]{3,2,1,0:T(8,128)(2,1)} %param.22) | copy-start | bytes 1572868
  113.8 1.0 copy-start.16

commit v19 on v16

--- a/solution.py
+++ b/solution.py
@@ -55,6 +55,7 @@
     half_width = KSIZE // 2
     window = CELL + KSIZE - 1
     padded = jnp.pad(blotted, ((half_width, half_width), (half_width, half_width)))
+    padded = lax.optimization_barrier(padded)
     outlier = jnp.zeros((tile_side, tile_side), jnp.float32)
     for row_block in range(blocks):
         rows_window = lax.slice_in_dim(padded, row_block * CELL, row_block * CELL + window, axis=0)
@@ -100,8 +101,6 @@
     n_sky = lax.axis_size("sky")
     local_visits, strip_rows, sky_w = warped.shape
     stacked = jnp.stack([warped, inv_var], axis=0)
-    tap_rows = psf_taps(cell_ids[0, 0], kernels[0, 0])
-    stacked, tap_rows = lax.optimization_barrier((stacked, tap_rows))
     chunk = strip_rows // n_visit
     stacked = stacked.reshape(2, local_visits, n_visit, chunk, sky_w)
     gathered = lax.all_to_all(stacked, "visit", split_axis=2, concat_axis=1, tiled=True)
@@ -109,7 +108,7 @@
     row_share = local_coadd(gathered[0].astype(jnp.float32), gathered[1].astype(jnp.float32))
     copies = jnp.broadcast_to(row_share[None], (n_visit,) + row_share.shape)
     coadd_field = lax.all_to_all(copies, "visit", split_axis=0, concat_axis=0, tiled=True)
-    bands = psf_bands(tap_rows)
+    bands = psf_bands(psf_taps(cell_ids[0, 0], kernels[0, 0]))
     coadd_field = coadd_field.reshape(n_visit * chunk, sky_w)
     coadd_low = coadd_field.astype(jnp.bfloat16)
 
@@ -139,6 +138,7 @@
     projected = jnp.dot(row_interp[0, 0], footprint, preferred_element_type=jnp.float32).astype(
         jnp.bfloat16
     )
+    projected = lax.optimization_barrier(projected)
     blotted = jnp.dot(projected, col_interp[0, 0], preferred_element_type=jnp.float32).astype(
         jnp.bfloat16
     )

time: 116 us -> 111 us (0.957)
  matrix products: 12.6 us -> 8.01 us
  waiting for transfers between devices: 13 us -> 10.6 us
  starting transfers between devices: 8.4 us -> 9.64 us
    dot_general x16, matrix products: 7.39 us -> 4.38 us  [psf_outlier(): jnp.einsum('rc,acl->arl', cols_window, bands[row_block * blocks + col_blo...]
    ppermute x3, waiting for transfers between devices: 5.88 us -> 3.61 us  [shards(): lax.ppermute(outgoing, 'sky', perm=[(i, (i + shift) % n_sky) for i in ran...]
    dot_general x1, matrix products: 1.89 us -> 0.46 us  [shards(): jnp.dot(projected, col_interp[0, 0], preferred_element_type=jnp.float32)]
    ppermute x3, starting transfers between devices: 1.8 us -> 3.03 us  [shards(): lax.ppermute(outgoing, 'sky', perm=[(i, (i + shift) % n_sky) for i in ran...]
    unnamed x32 -> x42, local copies, waits for them, and re-layouts: 2.24 us -> 2.56 us
  transfers between devices with their start and end apart: 7 -> 7, of which waited for: 2 -> 4; matrix products, arithmetic and copies ran while one was open for 6% -> 7% of each run, Pallas kernels for 0% -> 0%
where the time goes in v19:
time: 111 us; the launch traced here: 110 us
  blocking collectives  55.3 us (50%)
  waiting for transfers between devices  10.6 us (10%)
  between operations  10.1 us (9%)
  starting transfers between devices  9.64 us (9%)
  local copies, waits for them, and re-layouts  8.71 us (8%)
  matrix products  8.01 us (7%)
  other arithmetic  7.5 us (7%)
    all_to_all x1, blocking collectives, shards(): lax.all_to_all(stacked, 'visit', split_axis=2, concat_axis=1, tiled=True)  55.3 us
    all_to_all x1, waiting for transfers between devices, shards(): lax.all_to_all(copies, 'visit', split_axis=0, concat_axis=0, tiled=True)  6.97 us
    dot_general x16, matrix products, psf_outlier(): jnp.einsum('rc,acl->arl', cols_window, bands[row_block * blocks + col_blo...  4.38 us
    ppermute x3, waiting for transfers between devices, shards(): lax.ppermute(outgoing, 'sky', perm=[(i, (i + shift) % n_sky) for i in ran...  3.61 us
    all_to_all x1, starting transfers between devices, shards(): lax.all_to_all(copies, 'visit', split_axis=0, concat_axis=0, tiled=True)  3.59 us
    squeeze x1, local copies, waits for them, and re-layouts, psf_bands(): banded_all[r, c]  3.1 us
    ppermute x3, starting transfers between devices, shards(): lax.ppermute(outgoing, 'sky', perm=[(i, (i + shift) % n_sky) for i in ran...  3.03 us
    ppermute x3, starting transfers between devices, shards(): lax.ppermute(col_start[0], 'sky', perm=[(i, (i - shift) % n_sky) for i in...  3.01 us
  transfers between devices with their start and end apart: 7, of which 4 were waited for; matrix products, arithmetic and copies ran while one was open for 7% of the time, Pallas kernels for 0%

profile of v19, /device:TPU:0, one launch (start us, length us, event | category | flops | bytes accessed | tf_op | source)
XLA Modules:
  0.0 109.8 jit_solution(1670266981062022261)
XLA Ops:
  0.6 1.8 %pad_maximum_fusion = bf16[2,2,8,16,2048]{4,3,2,1,0:T(8,128)(2,1)S(1)} fusion(bf16[1,2,8,16,2048]{4,3,2,1,0:T(8,128)(2,1)} %bitcast.456, bf16[1,2,8,16,2048]{4,3,2,1,0:T(8,128)(2,1)} %bitcast.457), kind=kLoop, calls=%fused_computation.27 | loop fusion | flops 1048576 | bytes 4194304 | tf_op jit(solution)/shard_map/stack | solution.py:103
  2.4 0.2 copy.60
  2.7 55.3 %all_to_all.20 = bf16[2,2,8,16,2048]{4,3,1,0,2:T(8,128)(2,1)S(1)} all-to-all(bf16[2,2,8,16,2048]{4,3,1,0,2:T(8,128)(2,1)S(1)} %copy.60), channel_id=1, replica_groups=mesh['visit'=8,'sky'=4] {'visit'}, dimensions={2} | all-to-all | bytes 4194304 | tf_op jit(solution)/shard_map/all_to_all | solution.py:106
  58.0 0.4 convert_reduce_fusion
  58.4 0.9 fusion.16
  59.3 0.9 fusion.17
  60.2 0.9 fusion.18
  61.2 1.1 broadcast_in_dim.52
  62.2 3.6 %all-to-all-start.1 = ((f32[8,16,2048]{2,1,0:T(8,128)}), f32[8,16,2048]{2,1,0:T(8,128)S(1)}, u32[]{:S(2)}, u32[]{:S(2)}) async-start(f32[8,16,2048]{2,1,0:T(8,128)} %broadcast_in_dim.52), calls=%async_computation.1 | async-start | bytes 2097152 | tf_op jit(solution)/shard_map/all_to_all | solution.py:110
  65.9 1.6 %collective-permute-start.2 = (s32[1]{0:T(128)}, s32[1]{0:T(128)}, u32[]{:S(2)}, u32[]{:S(2)}) collective-permute-start(s32[1]{0:T(128)} %bitcast.7), channel_id=1, source_target_pairs={{0,2},{1,3},{2,0},{3,1},{4,6},{5,7},{6,4},{7,5},{8,10},{9,11},{10,... | collective-permute-start | bytes 20 | tf_op jit(solution)/shard_map/ppermute | solution.py:118
  67.5 1.4 %collective-permute-start = (s32[1]{0:T(128)}, s32[1]{0:T(128)}, u32[]{:S(2)}, u32[]{:S(2)}) collective-permute-start(s32[1]{0:T(128)} %bitcast.7), channel_id=1, source_target_pairs={{0,3},{1,0},{2,1},{3,2},{4,7},{5,4},{6,5},{7,6},{8,11},{9,8},{10,9... | collective-permute-start | bytes 20 | tf_op jit(solution)/shard_map/ppermute | solution.py:118
  69.6 0.7 fusion.161
  72.8 0.2 convolution_convert_fusion.3
  73.0 0.1 reshape.254
  73.2 2.5 %convolution_convert_fusion = bf16[4,4,11,138,128]{4,2,3,1,0:T(8,128)(2,1)S(1)} fusion(s32[138,128]{1,0:T(8,128)S(1)} %iota_subtract_fusion, bf16[4,4,11,11,1]{3,2,1,0,4:T(8,128)(2,1)S(1)} %reshape.254), kind=kOutput, calls=%fused_computation | convolution fusion | flops 71698176 | bytes 6292256 | tf_op jit(solution)/shard_map/xyab,bcl->xyacl/dot_general | solution.py:46
  75.7 3.1 %slice_bitcast_fusion = (bf16[11,138,128]{2,0,1:T(8,128)(2,1)S(1)}, bf16[11,138,128]{2,0,1:T(8,128)(2,1)S(1)}, bf16[11,138,128]{2,0,1:T(8,128)(2,1)S(1)}, bf16[1...) fusion(bf16[4,4,11,138,128]{4,2,3,1,0:T(8,128)(2,1)S(1)} %convo, ...), kind=kLoop, calls=%fused_computation.55 | loop fusion | bytes 12435456 | tf_op jit(solution)/shard_map/squeeze | solution.py:49
  84.4 7.0 %all-to-all-done.1 = f32[8,16,2048]{2,1,0:T(8,128)S(1)} async-done(((f32[8,16,2048]{2,1,0:T(8,128)}), f32[8,16,2048]{2,1,0:T(8,128)S(1)}, u32[]{:S(2)}, u32[]{:S(2)}) %all-to-all-start.1) | async-done | bytes 1048608 | tf_op jit(solution)/shard_map/all_to_all | solution.py:110
  91.5 0.3 constant_dynamic-slice_fusion
  91.8 1.6 %collective-permute-start.3 = (bf16[128,512]{1,0:T(8,128)(2,1)S(1)}, bf16[128,512]{1,0:T(8,128)(2,1)S(1)}, u32[]{:S(2)}, u32[]{:S(2)}) collective-permute-start(bf16[128,512]{1,0:T(8,128)(2,1)S(1)} %get-tuple-element.41), channel_id=1, source_target_pairs={{0,2},{1,3},{2,0},{3,1},{4,6},{5,7},{6,4},{7,5},{8,10},{9,11},{10,... | collective-permute-start | bytes 393224 | tf_op jit(solution)/shard_map/ppermute | solution.py:123
  93.4 1.4 %collective-permute-start.5 = (bf16[128,512]{1,0:T(8,128)(2,1)S(1)}, bf16[128,512]{1,0:T(8,128)(2,1)S(1)}, u32[]{:S(2)}, u32[]{:S(2)}) collective-permute-start(bf16[128,512]{1,0:T(8,128)(2,1)S(1)} %get-tuple-element.40), channel_id=1, source_target_pairs={{0,3},{1,0},{2,1},{3,2},{4,7},{5,4},{6,5},{7,6},{8,11},{9,8},{10,9... | collective-permute-start | bytes 393224 | tf_op jit(solution)/shard_map/ppermute | solution.py:123
  94.8 1.0 compare_select_fusion
  95.9 1.1 %collective-permute-done.1 = bf16[128,512]{1,0:T(8,128)(2,1)S(1)} collective-permute-done((bf16[128,512]{1,0:T(8,128)(2,1)S(1)}, bf16[128,512]{1,0:T(8,128)(2,1)S(1)}, u32[]{:S(2)}, u32[]{:S(2)}) %collective-permute-start.1) | collective-permute-done | bytes 131104 | tf_op jit(solution)/shard_map/ppermute | solution.py:123
  97.0 1.3 %collective-permute-done.3 = bf16[128,512]{1,0:T(8,128)(2,1)S(1)} collective-permute-done((bf16[128,512]{1,0:T(8,128)(2,1)S(1)}, bf16[128,512]{1,0:T(8,128)(2,1)S(1)}, u32[]{:S(2)}, u32[]{:S(2)}) %collective-permute-start.3) | collective-permute-done | bytes 131104 | tf_op jit(solution)/shard_map/ppermute | solution.py:123
  98.3 1.2 %collective-permute-done.5 = bf16[128,512]{1,0:T(8,128)(2,1)S(1)} collective-permute-done((bf16[128,512]{1,0:T(8,128)(2,1)S(1)}, bf16[128,512]{1,0:T(8,128)(2,1)S(1)}, u32[]{:S(2)}, u32[]{:S(2)}) %collective-permute-start.5) | collective-permute-done | bytes 131104 | tf_op jit(solution)/shard_map/ppermute | solution.py:123
  99.6 0.5 fusion.13
  100.1 0.5 copy-done.19
  100.6 0.5 convolution_convert_fusion.1
  101.1 0.4 pad.5
  101.5 0.1 copy-done.13
  101.6 0.3 convolution_bitcast_fusion.15
  102.1 0.1 pad_bitcast_fusion
  102.2 0.3 convolution_bitcast_fusion.14
  102.5 0.3 copy-done.11
  102.8 0.3 convolution_bitcast_fusion.13
  103.1 0.3 convolution_bitcast_fusion.12
  103.4 0.3 convolution_bitcast_fusion.11
  103.7 0.3 convolution_bitcast_fusion.10
  104.0 0.2 copy-done.7
  104.2 0.3 convolution_bitcast_fusion.9
  104.5 0.3 convolution_bitcast_fusion.8
  104.8 0.3 convolution_bitcast_fusion.7
  105.2 0.3 convolution_bitcast_fusion.6
  105.5 0.2 copy-done.3
  105.7 0.3 convolution_bitcast_fusion.5
  106.0 0.3 convolution_bitcast_fusion.4
  106.3 0.3 convolution_bitcast_fusion.3
  106.6 0.3 convolution_bitcast_fusion.2
  106.8 0.3 convolution_bitcast_fusion.1
  107.1 0.3 convolution_bitcast_fusion
  107.4 0.1 bitcast_dynamic-update-slice_fusion.14
  107.5 0.1 bitcast_dynamic-update-slice_fusion.13
  107.6 0.1 bitcast_dynamic-update-slice_fusion.12
  107.7 0.1 bitcast_dynamic-update-slice_fusion.11
  107.8 0.1 bitcast_dynamic-update-slice_fusion.10
  107.9 0.1 bitcast_dynamic-update-slice_fusion.9
  108.0 0.1 bitcast_dynamic-update-slice_fusion.8
  108.1 0.1 bitcast_dynamic-update-slice_fusion.7
  108.2 0.1 bitcast_dynamic-update-slice_fusion.6
  108.3 0.1 bitcast_dynamic-update-slice_fusion.5
  108.4 0.1 bitcast_dynamic-update-slice_fusion.4
  108.5 0.1 bitcast_dynamic-update-slice_fusion.3
  108.6 0.1 bitcast_dynamic-update-slice_fusion.2
  108.7 0.1 bitcast_dynamic-update-slice_fusion.1
  108.9 1.0 copy-done.14
  (52 shorter events, 0.9 us)
Async XLA Ops:
  0.6 99.0 %copy-start = (bf16[1,1,512,512]{3,2,1,0:T(8,128)(2,1)S(1)}, bf16[1,1,512,512]{3,2,1,0:T(8,128)(2,1)}, u32[]{:S(2)}) copy-start(bf16[1,1,512,512]{3,2,1,0:T(8,128)(2,1)} %param.14) | copy-start | bytes 1572868
  61.1 8.5 %copy-start.17 = (s32[1,1,4]{2,1,0:T(1,128)S(1)}, s32[1,1,4]{2,1,0:T(1,128)}, u32[]{:S(2)}) copy-start(s32[1,1,4]{2,1,0:T(1,128)} %param.12) | copy-start | bytes 52
  61.1 11.6 %copy-start.18 = (s32[1,1,4,4]{3,2,1,0:T(4,128)S(1)}, s32[1,1,4,4]{3,2,1,0:T(4,128)}, u32[]{:S(2)}) copy-start(s32[1,1,4,4]{3,2,1,0:T(4,128)} %param.16) | copy-start | bytes 196
  61.1 11.7 %copy-start.20 = (bf16[1,1,16,121]{3,2,1,0:T(8,128)(2,1)S(1)}, bf16[1,1,16,121]{3,2,1,0:T(8,128)(2,1)}, u32[]{:S(2)}) copy-start(bf16[1,1,16,121]{3,2,1,0:T(8,128)(2,1)} %param.17) | copy-start | bytes 11620
  62.2 29.2 %all-to-all-start.1 = ((f32[8,16,2048]{2,1,0:T(8,128)}), f32[8,16,2048]{2,1,0:T(8,128)S(1)}, u32[]{:S(2)}, u32[]{:S(2)}) async-start(f32[8,16,2048]{2,1,0:T(8,128)} %broadcast_in_dim.52), calls=%async_computation.1 | async-start | bytes 2097152 | tf_op jit(solution)/shard_map/all_to_all | solution.py:110
  65.8 13.0 %collective-permute-start.4 = (s32[1]{0:T(128)}, s32[1]{0:T(128)}, u32[]{:S(2)}, u32[]{:S(2)}) collective-permute-start(s32[1]{0:T(128)} %bitcast.7), channel_id=1, source_target_pairs={{0,1},{1,2},{2,3},{3,0},{4,5},{5,6},{6,7},{7,4},{8,9},{9,10},{10,1... | collective-permute-start | bytes 20 | tf_op jit(solution)/shard_map/ppermute | solution.py:118
  65.9 14.2 %collective-permute-start.2 = (s32[1]{0:T(128)}, s32[1]{0:T(128)}, u32[]{:S(2)}, u32[]{:S(2)}) collective-permute-start(s32[1]{0:T(128)} %bitcast.7), channel_id=1, source_target_pairs={{0,2},{1,3},{2,0},{3,1},{4,6},{5,7},{6,4},{7,5},{8,10},{9,11},{10,... | collective-permute-start | bytes 20 | tf_op jit(solution)/shard_map/ppermute | solution.py:118
  67.5 13.7 %collective-permute-start = (s32[1]{0:T(128)}, s32[1]{0:T(128)}, u32[]{:S(2)}, u32[]{:S(2)}) collective-permute-start(s32[1]{0:T(128)} %bitcast.7), channel_id=1, source_target_pairs={{0,3},{1,0},{2,1},{3,2},{4,7},{5,4},{6,5},{7,6},{8,11},{9,8},{10,9... | collective-permute-start | bytes 20 | tf_op jit(solution)/shard_map/ppermute | solution.py:118
  91.8 5.2 %collective-permute-start.1 = (bf16[128,512]{1,0:T(8,128)(2,1)S(1)}, bf16[128,512]{1,0:T(8,128)(2,1)S(1)}, u32[]{:S(2)}, u32[]{:S(2)}) collective-permute-start(bf16[128,512]{1,0:T(8,128)(2,1)S(1)} %get-tuple-element.42), channel_id=1, source_target_pairs={{0,1},{1,2},{2,3},{3,0},{4,5},{5,6},{6,7},{7,4},{8,9},{9,10},{10,1... | collective-permute-start | bytes 393224 | tf_op jit(solution)/shard_map/ppermute | solution.py:123
  91.8 6.4 %collective-permute-start.3 = (bf16[128,512]{1,0:T(8,128)(2,1)S(1)}, bf16[128,512]{1,0:T(8,128)(2,1)S(1)}, u32[]{:S(2)}, u32[]{:S(2)}) collective-permute-start(bf16[128,512]{1,0:T(8,128)(2,1)S(1)} %get-tuple-element.41), channel_id=1, source_target_pairs={{0,2},{1,3},{2,0},{3,1},{4,6},{5,7},{6,4},{7,5},{8,10},{9,11},{10,... | collective-permute-start | bytes 393224 | tf_op jit(solution)/shard_map/ppermute | solution.py:123
  93.4 6.0 %collective-permute-start.5 = (bf16[128,512]{1,0:T(8,128)(2,1)S(1)}, bf16[128,512]{1,0:T(8,128)(2,1)S(1)}, u32[]{:S(2)}, u32[]{:S(2)}) collective-permute-start(bf16[128,512]{1,0:T(8,128)(2,1)S(1)} %get-tuple-element.40), channel_id=1, source_target_pairs={{0,3},{1,0},{2,1},{3,2},{4,7},{5,4},{6,5},{7,6},{8,11},{9,8},{10,9... | collective-permute-start | bytes 393224 | tf_op jit(solution)/shard_map/ppermute | solution.py:123
  99.5 1.0 copy-start.19
  100.6 1.1 copy-start.13
  100.6 1.3 %copy-start.15 = (bf16[1,1,512,512]{3,2,1,0:T(8,128)(2,1)S(1)}, bf16[1,1,512,512]{3,2,1,0:T(8,128)(2,1)}, u32[]{:S(2)}) copy-start(bf16[1,1,512,512]{3,2,1,0:T(8,128)(2,1)} %param.19) | copy-start | bytes 1572868
  100.6 1.4 %copy-start.16 = (bf16[1,1,512,512]{3,2,1,0:T(8,128)(2,1)S(1)}, bf16[1,1,512,512]{3,2,1,0:T(8,128)(2,1)}, u32[]{:S(2)}) copy-start(bf16[1,1,512,512]{3,2,1,0:T(8,128)(2,1)} %param.18) | copy-start | bytes 1572868
  101.1 1.2 %copy-start.12 = (bf16[11,138,128]{2,0,1:T(8,128)(2,1)S(1)}, bf16[11,138,128]{2,0,1:T(8,128)(2,1)}, u32[]{:S(2)}) copy-start(bf16[11,138,128]{2,0,1:T(8,128)(2,1)} %get-tuple-element.34) | copy-start | bytes 1165828
  101.6 1.2 %copy-start.11 = (bf16[11,138,128]{2,0,1:T(8,128)(2,1)S(1)}, bf16[11,138,128]{2,0,1:T(8,128)(2,1)}, u32[]{:S(2)}) copy-start(bf16[11,138,128]{2,0,1:T(8,128)(2,1)} %get-tuple-element.33) | copy-start | bytes 1165828
  102.0 1.2 %copy-start.10 = (bf16[11,138,128]{2,0,1:T(8,128)(2,1)S(1)}, bf16[11,138,128]{2,0,1:T(8,128)(2,1)}, u32[]{:S(2)}) copy-start(bf16[11,138,128]{2,0,1:T(8,128)(2,1)} %get-tuple-element.32) | copy-start | bytes 1165828
  102.2 1.2 %copy-start.9 = (bf16[11,138,128]{2,0,1:T(8,128)(2,1)S(1)}, bf16[11,138,128]{2,0,1:T(8,128)(2,1)}, u32[]{:S(2)}) copy-start(bf16[11,138,128]{2,0,1:T(8,128)(2,1)} %get-tuple-element.31) | copy-start | bytes 1165828
  102.5 1.2 %copy-start.8 = (bf16[11,138,128]{2,0,1:T(8,128)(2,1)S(1)}, bf16[11,138,128]{2,0,1:T(8,128)(2,1)}, u32[]{:S(2)}) copy-start(bf16[11,138,128]{2,0,1:T(8,128)(2,1)} %get-tuple-element.30) | copy-start | bytes 1165828
  103.1 1.1 %copy-start.7 = (bf16[11,138,128]{2,0,1:T(8,128)(2,1)S(1)}, bf16[11,138,128]{2,0,1:T(8,128)(2,1)}, u32[]{:S(2)}) copy-start(bf16[11,138,128]{2,0,1:T(8,128)(2,1)} %get-tuple-element.29) | copy-start | bytes 1165828
  103.4 1.1 %copy-start.6 = (bf16[11,138,128]{2,0,1:T(8,128)(2,1)S(1)}, bf16[11,138,128]{2,0,1:T(8,128)(2,1)}, u32[]{:S(2)}) copy-start(bf16[11,138,128]{2,0,1:T(8,128)(2,1)} %get-tuple-element.28) | copy-start | bytes 1165828
  103.7 1.1 %copy-start.5 = (bf16[11,138,128]{2,0,1:T(8,128)(2,1)S(1)}, bf16[11,138,128]{2,0,1:T(8,128)(2,1)}, u32[]{:S(2)}) copy-start(bf16[11,138,128]{2,0,1:T(8,128)(2,1)} %get-tuple-element.27) | copy-start | bytes 1165828
  104.0 1.2 %copy-start.4 = (bf16[11,138,128]{2,0,1:T(8,128)(2,1)S(1)}, bf16[11,138,128]{2,0,1:T(8,128)(2,1)}, u32[]{:S(2)}) copy-start(bf16[11,138,128]{2,0,1:T(8,128)(2,1)} %get-tuple-element.26) | copy-start | bytes 1165828
  104.5 1.1 %copy-start.3 = (bf16[11,138,128]{2,0,1:T(8,128)(2,1)S(1)}, bf16[11,138,128]{2,0,1:T(8,128)(2,1)}, u32[]{:S(2)}) copy-start(bf16[11,138,128]{2,0,1:T(8,128)(2,1)} %get-tuple-element.25) | copy-start | bytes 1165828
  104.8 1.1 %copy-start.2 = (bf16[11,138,128]{2,0,1:T(8,128)(2,1)S(1)}, bf16[11,138,128]{2,0,1:T(8,128)(2,1)}, u32[]{:S(2)}) copy-start(bf16[11,138,128]{2,0,1:T(8,128)(2,1)} %get-tuple-element.24) | copy-start | bytes 1165828
  105.1 1.2 %copy-start.1 = (bf16[11,138,128]{2,0,1:T(8,128)(2,1)S(1)}, bf16[11,138,128]{2,0,1:T(8,128)(2,1)}, u32[]{:S(2)}) copy-start(bf16[11,138,128]{2,0,1:T(8,128)(2,1)} %get-tuple-element.23) | copy-start | bytes 1165828
  108.9 1.0 copy-start.14
